TPU v7x, 128 devices: a whole 4x4x4 slice. The times are simulated.
128 devices in a mesh: flow: 32 (over y, z, core), grp: 4 (over x).
Axes of the slice: x: 4, y: 4, z: 4, core: 2. Of those that a mesh axis runs over, the one named last changes fastest.
Arguments:
- velocity: float32 [3, 256, 128, 256], P(None, 'flow', 'grp'), may hold values from -6 to 6
- eddy_visc: float32 [256, 128, 256], P('flow', 'grp'), may hold values from 0.05 to 0.4
- projection: bfloat16 [125, 512], replicated, may hold values from -0.25 to 0.25
- acoustic_state: float32 [4, 125, 16384], P(None, None, ('flow', 'grp')), may hold values from -6 to 6
- route_send: int32 [128, 128, 2], P(('flow', 'grp')), may hold values from -1 to 127, as said below
- route_place: int32 [128, 128], P(('flow', 'grp')), may hold values from 0 to 255, as said below
Outputs:
- velocity_out: float32 [3, 256, 128, 256], P(None, 'flow', 'grp')
- acoustic_out: float32 [4, 125, 16384], P(None, None, ('flow', 'grp'))
Inputs may be any that keep to these rules, and one draw needn't show every extreme that they name: `route_send`: row h lists, for each owner o, the local indices of home h's elements that o holds in 2 slots, -1 in an empty slot; every local element of h stands exactly once in row h; an owner holds elements of 64 home devices, all 2 slots of each filled. `route_place`: row o is a permutation of the filled slots h * 2 + k of owner o; position j of owner o holds home h's element route_send[h, o, k].
All inputs are finite; a program needn't handle non-finite values.
Results may differ from a plain program's by a relative error of at most 0.0003.
Values sent between devices are 32-bit elements; how exact they have to be, the bound alone decides.
No kernel may reach another device: no remote copies, remote signals or barrier semaphores. Data moves between devices by JAX's collectives and lax.ppermute only.
A program may use at most 64 MiB of HBM per device.

v0:
```python
import math

import jax
import jax.numpy as jnp
import numpy as np
from jax import lax
from jax.experimental import pallas as pl
from jax.experimental.pallas import tpu as pltpu
from jax.sharding import PartitionSpec as P

LES_SECTIONS = 2
AC_SECTIONS = 2


TIME_STEP_LES = 0.15
TIME_STEP_ACOUSTIC = 0.02
GEOMETRY = 2.0
LIFT_FACTOR = 20.0
HIGH = lax.Precision.HIGHEST


def gll_derivative():
    gll_nodes = np.array([-1.0, -math.sqrt(3.0 / 7.0), 0.0, math.sqrt(3.0 / 7.0), 1.0])
    bary_weights = np.array(
        [
            1.0
            / np.prod([gll_nodes[first] - gll_nodes[other] for other in range(5) if other != first])
            for first in range(5)
        ]
    )
    matrix = np.zeros((5, 5))
    for row_id in range(5):
        for col_id in range(5):
            if row_id != col_id:
                matrix[row_id, col_id] = (
                    bary_weights[col_id]
                    / bary_weights[row_id]
                    / (gll_nodes[row_id] - gll_nodes[col_id])
                )
    for row_id in range(5):
        matrix[row_id, row_id] = -matrix[row_id].sum()
    return matrix


def node_id(coords):
    return coords[0] * 25 + coords[1] * 5 + coords[2]


def face_nodes(dim, at):
    ids = []
    for first in range(5):
        for second in range(5):
            coords = [first, second]
            coords.insert(dim, at)
            ids.append(node_id(coords))
    return ids


def dg_matrices():
    dmat = gll_derivative()
    own = np.zeros((500, 500))
    for a in range(5):
        for b in range(5):
            for c in range(5):
                row = node_id((a, b, c))
                pos = (a, b, c)
                for dim in range(3):
                    for k in range(5):
                        col_pos = list(pos)
                        col_pos[dim] = k
                        col = node_id(col_pos)
                        weight = -GEOMETRY * dmat[pos[dim], k]
                        own[row, (1 + dim) * 125 + col] += weight
                        own[(1 + dim) * 125 + row, col] += weight
    half = LIFT_FACTOR * 0.5
    other = np.zeros((500, 600))
    face_order = []
    for dim in range(3):
        for sign, at in ((-1.0, 0), (1.0, 4)):
            face_order.append((dim, sign, at))
    for slot, (dim, sign, at) in enumerate(face_order):
        for t, node in enumerate(face_nodes(dim, at)):
            col = lambda comp: slot * 100 + comp * 25 + t
            own[node, (1 + dim) * 125 + node] += half * sign
            own[node, node] += -half
            other[node, col(1 + dim)] += -half * sign
            other[node, col(0)] += half
            for k in range(3):
                own[(1 + k) * 125 + node, (1 + k) * 125 + node] += -half
                other[(1 + k) * 125 + node, col(1 + k)] += half
            own[(1 + dim) * 125 + node, node] += half * sign
            other[(1 + dim) * 125 + node, col(0)] += -half * sign
    return own.astype(np.float32), other.astype(np.float32)


def face_rows(state, dim, at):
    elems = state.shape[-1]
    cube = state.reshape(4, 5, 5, 5, elems)
    face = lax.index_in_dim(cube, at, axis=1 + dim, keepdims=False)
    return face.reshape(100, elems)


def les_kernel(want_lamb, vel_ref, nu_ref, vxlo_ref, vxhi_ref, vylo_ref, vyhi_ref,
               nxlo_ref, nxhi_ref, nylo_ref, nyhi_ref, out_ref, *rest):
    size_x, size_y, size_z = vel_ref.shape[1], vel_ref.shape[2], vel_ref.shape[3]
    row = lax.broadcasted_iota(jnp.int32, (size_y, size_z), 0)
    lane = lax.broadcasted_iota(jnp.int32, (size_y, size_z), 1)

    def yp(f, halo):
        return jnp.where(row == size_y - 1, halo, pltpu.roll(f, size_y - 1, 0))

    def ym(f, halo):
        return jnp.where(row == 0, halo, pltpu.roll(f, 1, 0))

    def zp(f):
        return jnp.where(lane == size_z - 1, 0.0, pltpu.roll(f, size_z - 1, 1))

    def zm(f):
        return jnp.where(lane == 0, 0.0, pltpu.roll(f, 1, 1))

    def step(x, carry):
        lo = jnp.maximum(x - 1, 0)
        hi = jnp.minimum(x + 1, size_x - 1)
        u = [vel_ref[c, x] for c in range(3)]
        uxm = [jnp.where(x == 0, vxlo_ref[c], vel_ref[c, lo]) for c in range(3)]
        uxp = [jnp.where(x == size_x - 1, vxhi_ref[c], vel_ref[c, hi]) for c in range(3)]
        uym = [ym(u[c], vylo_ref[c, x]) for c in range(3)]
        uyp = [yp(u[c], vyhi_ref[c, x]) for c in range(3)]
        uzm = [zm(u[c]) for c in range(3)]
        uzp = [zp(u[c]) for c in range(3)]
        nu = nu_ref[x]
        nxm = jnp.where(x == 0, nxlo_ref[...], nu_ref[lo])
        nxp = jnp.where(x == size_x - 1, nxhi_ref[...], nu_ref[hi])
        nym = ym(nu, nylo_ref[x])
        nyp = yp(nu, nyhi_ref[x])
        nzm = zm(nu)
        nzp = zp(nu)
        plus = (uxp, uyp, uzp)
        minus = (uxm, uym, uzm)

        def d(c, axis):
            return 0.5 * (plus[axis][c] - minus[axis][c])

        wx = d(2, 1) - d(1, 2)
        wy = d(0, 2) - d(2, 0)
        wz = d(1, 0) - d(0, 1)
        lamb = (wy * u[2] - wz * u[1], wz * u[0] - wx * u[2], wx * u[1] - wy * u[0])
        ups = (0.5 * (nu + nxp), 0.5 * (nu + nyp), 0.5 * (nu + nzp))
        downs = (0.5 * (nu + nxm), 0.5 * (nu + nym), 0.5 * (nu + nzm))
        for c in range(3):
            total = None
            for axis in range(3):
                term = ups[axis] * (plus[axis][c] - u[c]) - downs[axis] * (u[c] - minus[axis][c])
                total = term if total is None else total + term
            out_ref[c, x] = u[c] + TIME_STEP_LES * (total - lamb[c])
            if want_lamb:
                rest[0][c, x] = lamb[c].astype(rest[0].dtype)
        return carry

    lax.fori_loop(0, size_x, step, 0)


def les_section(vel, nu, vhalo, nhalo, want_lamb):
    out_shape = [jax.ShapeDtypeStruct(vel.shape, jnp.float32)]
    if want_lamb:
        out_shape.append(jax.ShapeDtypeStruct(vel.shape, jnp.bfloat16))
    res = pl.pallas_call(
        lambda *refs: les_kernel(want_lamb, *refs),
        out_shape=tuple(out_shape),
    )(vel, nu, *vhalo, *nhalo)
    return res


def halos(field, lead):
    flow_n = lax.axis_size("flow")
    grp_n = lax.axis_size("grp")
    up_f = [(i, i + 1) for i in range(flow_n - 1)]
    down_f = [(i + 1, i) for i in range(flow_n - 1)]
    up_g = [(i, i + 1) for i in range(grp_n - 1)]
    down_g = [(i + 1, i) for i in range(grp_n - 1)]
    size_x, size_y = field.shape[lead], field.shape[lead + 1]
    xlo = lax.ppermute(lax.index_in_dim(field, size_x - 1, lead, keepdims=False), "flow", up_f)
    xhi = lax.ppermute(lax.index_in_dim(field, 0, lead, keepdims=False), "flow", down_f)
    ylo = lax.ppermute(lax.slice_in_dim(field, size_y - 1, size_y, axis=lead + 1), "grp", up_g)
    yhi = lax.ppermute(lax.slice_in_dim(field, 0, 1, axis=lead + 1), "grp", down_g)
    return xlo, xhi, ylo, yhi


def project(lamb, projection):
    size_x, size_y, size_z = (lamb.shape[1], lamb.shape[2], lamb.shape[3])
    blocks = lamb.reshape(3, size_x // 8, 8, size_y // 8, 8, size_z // 8, 8)
    blocks = blocks.transpose(2, 4, 6, 0, 1, 3, 5).reshape(512, -1)
    source = jnp.dot(projection, blocks, preferred_element_type=jnp.float32)
    source = source.reshape(125, 3, -1).transpose(1, 0, 2)
    return source.reshape(375, -1)


def body(velocity, eddy_visc, projection, acoustic_state, route_send, route_place):
    nhalo = halos(eddy_visc, 0)
    vel = velocity
    lamb = None
    for turn in range(LES_SECTIONS):
        vhalo = halos(vel, 1)
        last = turn == LES_SECTIONS - 1
        res = les_section(vel, eddy_visc, vhalo, nhalo, last)
        vel = res[0]
        if last:
            lamb = res[1]
    source = project(lamb, projection)
    flow_size = lax.axis_size("flow")
    grp_size = lax.axis_size("grp")
    slot_cap = route_send.shape[2]
    elem_count = acoustic_state.shape[2]
    total_slots = flow_size * grp_size * slot_cap
    placing = route_place.reshape(-1)
    outgoing = (
        jnp.zeros((500, total_slots), jnp.float32)
        .at[:, placing]
        .set(acoustic_state.reshape(500, elem_count))
    )
    arrived = lax.all_to_all(outgoing, ("flow", "grp"), split_axis=1, concat_axis=1, tiled=True)
    sending = route_send.reshape(-1)
    filled = sending >= 0
    target = jnp.where(filled, sending, elem_count)
    state = jnp.zeros((500, elem_count), jnp.float32).at[:, target].set(arrived, mode="drop")

    block_y = velocity.shape[2] // 8
    block_z = velocity.shape[3] // 8
    own_np, other_np = dg_matrices()
    own_mat = jnp.asarray(own_np)
    other_mat = jnp.asarray(other_np)
    src_full = jnp.concatenate([jnp.zeros((125, elem_count), jnp.float32), source], axis=0)
    lane = lax.broadcasted_iota(jnp.int32, (1, elem_count), 1)
    ez = lane % block_z
    flow_n = lax.axis_size("flow")
    grp_n = lax.axis_size("grp")
    up_f = [(i, i + 1) for i in range(flow_n - 1)]
    down_f = [(i + 1, i) for i in range(flow_n - 1)]
    up_g = [(i, i + 1) for i in range(grp_n - 1)]
    down_g = [(i + 1, i) for i in range(grp_n - 1)]
    row_len = block_z
    for turn in range(AC_SECTIONS):
        fx0 = face_rows(state, 0, 0)
        fx4 = face_rows(state, 0, 4)
        fy0 = face_rows(state, 1, 0)
        fy4 = face_rows(state, 1, 4)
        fz0 = face_rows(state, 2, 0)
        fz4 = face_rows(state, 2, 4)
        oxlo = lax.ppermute(fx4, "flow", up_f)
        oxhi = lax.ppermute(fx0, "flow", down_f)
        ylo_recv = lax.ppermute(fy4[:, elem_count - row_len:], "grp", up_g)
        yhi_recv = lax.ppermute(fy0[:, :row_len], "grp", down_g)
        oylo = jnp.concatenate([ylo_recv, fy4[:, : elem_count - row_len]], axis=1)
        oyhi = jnp.concatenate([fy0[:, row_len:], yhi_recv], axis=1)
        zero_col = jnp.zeros((100, 1), jnp.float32)
        ozlo = jnp.where(ez == 0, 0.0, jnp.concatenate([zero_col, fz4[:, :-1]], axis=1))
        ozhi = jnp.where(ez == block_z - 1, 0.0, jnp.concatenate([fz0[:, 1:], zero_col], axis=1))
        others = jnp.concatenate([oxlo, oxhi, oylo, oyhi, ozlo, ozhi], axis=0)
        rate = (
            jnp.dot(own_mat, state, precision=HIGH)
            + jnp.dot(other_mat, others, precision=HIGH)
            - src_full
        )
        state = state + TIME_STEP_ACOUSTIC * rate
    flat_state = state
    leaving = jnp.where(filled[None, :], flat_state[:, jnp.where(filled, sending, 0)], 0.0)
    returned = lax.all_to_all(leaving, ("flow", "grp"), split_axis=1, concat_axis=1, tiled=True)
    acoustic_out = returned[:, placing].reshape(4, 125, elem_count)
    return (vel, acoustic_out)


def solution(mesh):
    placed = (
        P(None, "flow", "grp", None),
        P("flow", "grp", None),
        P(),
        P(None, None, ("flow", "grp")),
        P(("flow", "grp"), None, None),
        P(("flow", "grp"), None),
    )
    return jax.shard_map(
        body,
        mesh=mesh,
        in_specs=placed,
        out_specs=(P(None, "flow", "grp", None), P(None, None, ("flow", "grp"))),
        check_vma=False,
    )
```

profile of v0, /device:TPU:1, one launch (start us, length us, event | category | flops | bytes accessed | tf_op | source)
XLA Modules:
  0.0 174.7 jit_solution(17060840336376209253)
XLA Ops:
  1.5 4.9 %collective-permute-start.4 = (f32[32,256]{1,0:T(8,128)S(1)}, f32[32,256]{1,0:T(8,128)S(1)}, u32[]{:S(2)}, u32[]{:S(2)}) collective-permute-start(f32[32,256]{1,0:T(8,128)S(1)} %get-tuple-element.33), channel_id=1, source_target_pairs={{0,4},{4,8},{8,12},{12,16},{16,20},{20,24},{24,28},{28,32},{32,36}... | collective-permute-start | bytes 98312 | tf_op jit(solution)/shard_map/ppermute | solution.py:182
  6.4 1.9 %collective-permute-start.5 = (f32[32,256]{1,0:T(8,128)S(1)}, f32[32,256]{1,0:T(8,128)S(1)}, u32[]{:S(2)}, u32[]{:S(2)}) collective-permute-start(f32[32,256]{1,0:T(8,128)S(1)} %get-tuple-element.32), channel_id=1, source_target_pairs={{4,0},{8,4},{12,8},{16,12},{20,16},{24,20},{28,24},{32,28},{36,32}... | collective-permute-start | bytes 98312 | tf_op jit(solution)/shard_map/ppermute | solution.py:183
  9.2 3.1 %collective-permute-start.6 = (f32[8,1,256]{2,1,0:T(1,128)S(1)}, f32[8,1,256]{2,1,0:T(1,128)S(1)}, u32[]{:S(2)}, u32[]{:S(2)}) collective-permute-start(f32[8,1,256]{2,1,0:T(1,128)S(1)} %get-tuple-element.31), channel_id=1, source_target_pairs={{0,1},{1,2},{2,3},{4,5},{5,6},{6,7},{8,9},{9,10},{10,11},{12,13},{... | collective-permute-start | bytes 24584 | tf_op jit(solution)/shard_map/ppermute | solution.py:184
  14.7 4.0 %collective-permute-start.2 = (f32[3,8,1,256]{3,2,1,0:T(1,128)S(1)}, f32[3,8,1,256]{3,2,1,0:T(1,128)S(1)}, u32[]{:S(2)}, u32[]{:S(2)}) collective-permute-start(f32[3,8,1,256]{3,2,1,0:T(1,128)S(1)} %get-tuple-element.19), channel_id=1, source_target_pairs={{0,1},{1,2},{2,3},{4,5},{5,6},{6,7},{8,9},{9,10},{10,11},{12,13},{... | collective-permute-start | bytes 73736 | tf_op jit(solution)/shard_map/ppermute | solution.py:184
  22.8 10.8 %all-to-all-start = ((f32[500,128,2]{0,2,1:T(2,128)}), f32[500,128,2]{0,2,1:T(2,128)S(1)}, u32[]{:S(2)}, u32[]{:S(2)}) async-start(f32[500,128,2]{0,2,1:T(2,128)} %all_to_all.14), calls=%async_computation | async-start | bytes 1048576 | tf_op jit(solution)/shard_map/all_to_all | solution.py:221
  36.2 3.7 %collective-permute-start = (f32[3,32,256]{2,1,0:T(8,128)S(1)}, f32[3,32,256]{2,1,0:T(8,128)S(1)}, u32[]{:S(2)}, u32[]{:S(2)}) collective-permute-start(f32[3,32,256]{2,1,0:T(8,128)S(1)} %get-tuple-element.21), channel_id=1, source_target_pairs={{0,4},{4,8},{8,12},{12,16},{16,20},{20,24},{24,28},{28,32},{32,36}... | collective-permute-start | bytes 294920 | tf_op jit(solution)/shard_map/ppermute | solution.py:182
  39.9 1.9 %collective-permute-start.1 = (f32[3,32,256]{2,1,0:T(8,128)S(1)}, f32[3,32,256]{2,1,0:T(8,128)S(1)}, u32[]{:S(2)}, u32[]{:S(2)}) collective-permute-start(f32[3,32,256]{2,1,0:T(8,128)S(1)} %get-tuple-element.20), channel_id=1, source_target_pairs={{4,0},{8,4},{12,8},{16,12},{20,16},{24,20},{28,24},{32,28},{36,32}... | collective-permute-start | bytes 294920 | tf_op jit(solution)/shard_map/ppermute | solution.py:183
  43.1 3.6 %collective-permute-done.3.refs_5_ = f32[3,8,1,256]{3,2,1,0:T(1,128)S(1)} collective-permute-done((f32[3,8,1,256]{3,2,1,0:T(1,128)S(1)}, f32[3,8,1,256]{3,2,1,0:T(1,128)S(1)}, u32[]{:S(2)}, u32[]{:S(2)}) %collective-permute-start.3) | collective-permute-done | bytes 24608 | tf_op jit(solution)/shard_map/ppermute | solution.py:185
  48.0 3.8 %shard_map.95.refs_0_ = f32[3,8,32,256]{3,2,1,0:T(8,128)} custom-call(f32[3,8,32,256]{3,2,1,0:T(8,128)} %refs_0_.1, f32[8,32,256]{2,1,0:T(8,128)} %refs_1_.3, f32[3,32,256]{2,1,0:T(8,128)} %copy-done.7, f32[3,32,256]{2,1,0:T(8,128)} %copy-done.8, f32[3,8,1,256]{3,2,1,0:T(1,128)} %copy-done.14, f32[3,8,1,256]{3,2,1,0:T(1,128)} %copy-done.15, ...), custom_call_target="tpu_custom_call" | custom-call | tf_op jit(solution)/shard_map/pallas_call | solution.py:167
  52.8 4.5 %collective-permute-start.8 = (f32[3,32,256]{2,1,0:T(8,128)S(1)}, f32[3,32,256]{2,1,0:T(8,128)S(1)}, u32[]{:S(2)}, u32[]{:S(2)}) collective-permute-start(f32[3,32,256]{2,1,0:T(8,128)S(1)} %get-tuple-element.17), channel_id=1, source_target_pairs={{0,4},{4,8},{8,12},{12,16},{16,20},{20,24},{24,28},{28,32},{32,36}... | collective-permute-start | bytes 294920 | tf_op jit(solution)/shard_map/ppermute | solution.py:182
  57.3 1.9 %collective-permute-start.9 = (f32[3,32,256]{2,1,0:T(8,128)S(1)}, f32[3,32,256]{2,1,0:T(8,128)S(1)}, u32[]{:S(2)}, u32[]{:S(2)}) collective-permute-start(f32[3,32,256]{2,1,0:T(8,128)S(1)} %get-tuple-element.16), channel_id=1, source_target_pairs={{4,0},{8,4},{12,8},{16,12},{20,16},{24,20},{28,24},{32,28},{36,32}... | collective-permute-start | bytes 294920 | tf_op jit(solution)/shard_map/ppermute | solution.py:183
  60.3 3.1 %collective-permute-start.10 = (f32[3,8,1,256]{3,2,1,0:T(1,128)S(1)}, f32[3,8,1,256]{3,2,1,0:T(1,128)S(1)}, u32[]{:S(2)}, u32[]{:S(2)}) collective-permute-start(f32[3,8,1,256]{3,2,1,0:T(1,128)S(1)} %get-tuple-element.15), channel_id=1, source_target_pairs={{0,1},{1,2},{2,3},{4,5},{5,6},{6,7},{8,9},{9,10},{10,11},{12,13},{... | collective-permute-start | bytes 73736 | tf_op jit(solution)/shard_map/ppermute | solution.py:184
  64.9 3.1 %collective-permute-done.11.refs_5_ = f32[3,8,1,256]{3,2,1,0:T(1,128)S(1)} collective-permute-done((f32[3,8,1,256]{3,2,1,0:T(1,128)S(1)}, f32[3,8,1,256]{3,2,1,0:T(1,128)S(1)}, u32[]{:S(2)}, u32[]{:S(2)}) %collective-permute-start.11) | collective-permute-done | bytes 24608 | tf_op jit(solution)/shard_map/ppermute | solution.py:185
  69.3 3.9 %shard_map.96 = (f32[3,8,32,256]{3,2,1,0:T(8,128)}, bf16[3,8,32,256]{3,2,1,0:T(8,128)(2,1)}) custom-call(f32[3,8,32,256]{3,2,1,0:T(8,128)} %shard_map.95.refs_0_, f32[8,32,256]{2,1,0:T(8,128)} %refs_1_.3, f32[3,32,256]{2,1,0:T(8,128)} %copy-done.9, f32[3,32,256]{2,1,0:T(8,128)} %copy-done.10, f32[3,8,1,256]{3,2,1,0:T(1,128)} %copy-done.16, ...), custom_call_target="tpu_custom_call" | custom-call | tf_op jit(solution)/shard_map/pallas_call | solution.py:167
  73.2 9.4 %reshape.163 = bf16[3,1,8,4,8,32,8]{6,5,4,3,2,0,1:T(8,128)(2,1)} reshape(bf16[3,8,32,256]{3,2,1,0:T(8,128)(2,1)} %get-tuple-element.5) | data formatting | bytes 786432 | tf_op jit(solution)/shard_map/reshape | solution.py:191
  82.6 5.6 %copy.30 = bf16[8,8,8,3,1,4,32]{6,5,3,2,1,0,4:T(4,128)(2,1)S(1)} copy(bf16[8,8,8,3,1,4,32]{2,6,1,5,0,3,4:T(8,128)(2,1)} %bitcast.97) | data formatting | bytes 786432 | tf_op jit(solution)/shard_map/transpose | solution.py:192
  88.2 1.6 reshape.164
  91.8 1.5 scatter_custom_fusion.1
  95.1 3.1 %collective-permute-start.14 = (f32[100,32]{1,0:T(8,128)}, f32[100,32]{1,0:T(8,128)S(1)}, u32[]{:S(2)}, u32[]{:S(2)}) collective-permute-start(f32[100,32]{1,0:T(8,128)} %slice.167), channel_id=1, source_target_pairs={{0,1},{1,2},{2,3},{4,5},{5,6},{6,7},{8,9},{9,10},{10,11},{12,13},{... | collective-permute-start | bytes 38408 | tf_op jit(solution)/shard_map/ppermute | solution.py:251
  101.7 1.9 %collective-permute-start.13 = (f32[100,128]{1,0:T(8,128)}, f32[100,128]{1,0:T(8,128)}, u32[]{:S(2)}, u32[]{:S(2)}) collective-permute-start(f32[100,128]{1,0:T(8,128)} %reshape_squeeze.37), channel_id=1, source_target_pairs={{4,0},{8,4},{12,8},{16,12},{20,16},{24,20},{28,24},{32,28},{36,32}... | collective-permute-start | bytes 153608 | tf_op jit(solution)/shard_map/ppermute | solution.py:250
  104.2 5.5 %collective-permute-start.12 = (f32[100,128]{1,0:T(8,128)}, f32[100,128]{1,0:T(8,128)}, u32[]{:S(2)}, u32[]{:S(2)}) collective-permute-start(f32[100,128]{1,0:T(8,128)} %reshape_squeeze.36), channel_id=1, source_target_pairs={{0,4},{4,8},{8,12},{12,16},{16,20},{20,24},{24,28},{28,32},{32,36}... | collective-permute-start | bytes 153608 | tf_op jit(solution)/shard_map/ppermute | solution.py:249
  109.7 1.7 fusion.71
  111.4 1.6 fusion.44
  117.6 1.5 fusion.72
  120.6 1.7 fusion.12
  123.6 4.3 %collective-permute-start.18 = (f32[100,32]{1,0:T(8,128)S(1)}, f32[100,32]{1,0:T(8,128)S(1)}, u32[]{:S(2)}, u32[]{:S(2)}) collective-permute-start(f32[100,32]{1,0:T(8,128)S(1)} %slice.179), channel_id=1, source_target_pairs={{0,1},{1,2},{2,3},{4,5},{5,6},{6,7},{8,9},{9,10},{10,11},{12,13},{... | collective-permute-start | bytes 38408 | tf_op jit(solution)/shard_map/ppermute | solution.py:251
  129.3 1.6 fusion.39
  131.0 1.9 %collective-permute-start.17 = (f32[100,128]{1,0:T(8,128)S(1)}, f32[100,128]{1,0:T(8,128)S(1)}, u32[]{:S(2)}, u32[]{:S(2)}) collective-permute-start(f32[100,128]{1,0:T(8,128)S(1)} %reshape_squeeze.43), channel_id=1, source_target_pairs={{4,0},{8,4},{12,8},{16,12},{20,16},{24,20},{28,24},{32,28},{36,32}... | collective-permute-start | bytes 153608 | tf_op jit(solution)/shard_map/ppermute | solution.py:250
  132.9 3.6 %collective-permute-start.16 = (f32[100,128]{1,0:T(8,128)S(1)}, f32[100,128]{1,0:T(8,128)S(1)}, u32[]{:S(2)}, u32[]{:S(2)}) collective-permute-start(f32[100,128]{1,0:T(8,128)S(1)} %reshape_squeeze.42), channel_id=1, source_target_pairs={{0,4},{4,8},{8,12},{12,16},{16,20},{20,24},{24,28},{28,32},{32,36}... | collective-permute-start | bytes 153608 | tf_op jit(solution)/shard_map/ppermute | solution.py:249
  140.1 1.5 fusion.15
  144.2 14.2 %all-to-all-start.1 = ((f32[500,128,2]{0,2,1:T(2,128)}), f32[500,128,2]{0,2,1:T(2,128)S(1)}, u32[]{:S(2)}, u32[]{:S(2)}) async-start(f32[500,128,2]{0,2,1:T(2,128)} %broadcast_select_fusion), calls=%async_computation.1 | async-start | bytes 1048576 | tf_op jit(solution)/shard_map/all_to_all | solution.py:267
  158.4 14.1 %all-to-all-done.1 = f32[500,128,2]{0,2,1:T(2,128)S(1)} async-done(((f32[500,128,2]{0,2,1:T(2,128)}), f32[500,128,2]{0,2,1:T(2,128)S(1)}, u32[]{:S(2)}, u32[]{:S(2)}) %all-to-all-start.1) | async-done | bytes 512032 | tf_op jit(solution)/shard_map/all_to_all | solution.py:267
  (128 shorter events, 42.7 us)
Async XLA Ops:
  0.6 89.2 %copy-start = (bf16[125,512]{1,0:T(8,128)(2,1)S(1)}, bf16[125,512]{1,0:T(8,128)(2,1)}, u32[]{:S(2)}) copy-start(bf16[125,512]{1,0:T(8,128)(2,1)} %param.10) | copy-start | bytes 384004
  1.5 45.2 %collective-permute-start.4 = (f32[32,256]{1,0:T(8,128)S(1)}, f32[32,256]{1,0:T(8,128)S(1)}, u32[]{:S(2)}, u32[]{:S(2)}) collective-permute-start(f32[32,256]{1,0:T(8,128)S(1)} %get-tuple-element.33), channel_id=1, source_target_pairs={{0,4},{4,8},{8,12},{12,16},{16,20},{20,24},{24,28},{28,32},{32,36}... | collective-permute-start | bytes 98312 | tf_op jit(solution)/shard_map/ppermute | solution.py:182
  6.4 40.3 %collective-permute-start.5 = (f32[32,256]{1,0:T(8,128)S(1)}, f32[32,256]{1,0:T(8,128)S(1)}, u32[]{:S(2)}, u32[]{:S(2)}) collective-permute-start(f32[32,256]{1,0:T(8,128)S(1)} %get-tuple-element.32), channel_id=1, source_target_pairs={{4,0},{8,4},{12,8},{16,12},{20,16},{24,20},{28,24},{32,28},{36,32}... | collective-permute-start | bytes 98312 | tf_op jit(solution)/shard_map/ppermute | solution.py:183
  9.2 26.9 %collective-permute-start.6 = (f32[8,1,256]{2,1,0:T(1,128)S(1)}, f32[8,1,256]{2,1,0:T(1,128)S(1)}, u32[]{:S(2)}, u32[]{:S(2)}) collective-permute-start(f32[8,1,256]{2,1,0:T(1,128)S(1)} %get-tuple-element.31), channel_id=1, source_target_pairs={{0,1},{1,2},{2,3},{4,5},{5,6},{6,7},{8,9},{9,10},{10,11},{12,13},{... | collective-permute-start | bytes 24584 | tf_op jit(solution)/shard_map/ppermute | solution.py:184
  12.3 27.5 %collective-permute-start.7 = (f32[8,1,256]{2,1,0:T(1,128)S(1)}, f32[8,1,256]{2,1,0:T(1,128)S(1)}, u32[]{:S(2)}, u32[]{:S(2)}) collective-permute-start(f32[8,1,256]{2,1,0:T(1,128)S(1)} %get-tuple-element.30), channel_id=1, source_target_pairs={{1,0},{2,1},{3,2},{5,4},{6,5},{7,6},{9,8},{10,9},{11,10},{13,12},{... | collective-permute-start | bytes 24584 | tf_op jit(solution)/shard_map/ppermute | solution.py:185
  14.7 27.1 %collective-permute-start.2 = (f32[3,8,1,256]{3,2,1,0:T(1,128)S(1)}, f32[3,8,1,256]{3,2,1,0:T(1,128)S(1)}, u32[]{:S(2)}, u32[]{:S(2)}) collective-permute-start(f32[3,8,1,256]{3,2,1,0:T(1,128)S(1)} %get-tuple-element.19), channel_id=1, source_target_pairs={{0,1},{1,2},{2,3},{4,5},{5,6},{6,7},{8,9},{9,10},{10,11},{12,13},{... | collective-permute-start | bytes 73736 | tf_op jit(solution)/shard_map/ppermute | solution.py:184
  22.8 68.6 %all-to-all-start = ((f32[500,128,2]{0,2,1:T(2,128)}), f32[500,128,2]{0,2,1:T(2,128)S(1)}, u32[]{:S(2)}, u32[]{:S(2)}) async-start(f32[500,128,2]{0,2,1:T(2,128)} %all_to_all.14), calls=%async_computation | async-start | bytes 1048576 | tf_op jit(solution)/shard_map/all_to_all | solution.py:221
  36.2 10.6 %copy-start.12 = (f32[8,1,256]{2,1,0:T(1,128)}, f32[8,1,256]{2,1,0:T(1,128)S(1)}, u32[]{:S(2)}) copy-start(f32[8,1,256]{2,1,0:T(1,128)S(1)} %collective-permute-done.6.refs_8_) | copy-start | bytes 24580
  36.2 10.5 %collective-permute-start = (f32[3,32,256]{2,1,0:T(8,128)S(1)}, f32[3,32,256]{2,1,0:T(8,128)S(1)}, u32[]{:S(2)}, u32[]{:S(2)}) collective-permute-start(f32[3,32,256]{2,1,0:T(8,128)S(1)} %get-tuple-element.21), channel_id=1, source_target_pairs={{0,4},{4,8},{8,12},{12,16},{16,20},{20,24},{24,28},{28,32},{32,36}... | collective-permute-start | bytes 294920 | tf_op jit(solution)/shard_map/ppermute | solution.py:182
  39.8 6.9 %copy-start.13 = (f32[8,1,256]{2,1,0:T(1,128)}, f32[8,1,256]{2,1,0:T(1,128)S(1)}, u32[]{:S(2)}) copy-start(f32[8,1,256]{2,1,0:T(1,128)S(1)} %collective-permute-done.7.refs_9_) | copy-start | bytes 24580
  39.9 6.9 %collective-permute-start.1 = (f32[3,32,256]{2,1,0:T(8,128)S(1)}, f32[3,32,256]{2,1,0:T(8,128)S(1)}, u32[]{:S(2)}, u32[]{:S(2)}) collective-permute-start(f32[3,32,256]{2,1,0:T(8,128)S(1)} %get-tuple-element.20), channel_id=1, source_target_pairs={{4,0},{8,4},{12,8},{16,12},{20,16},{24,20},{28,24},{32,28},{36,32}... | collective-permute-start | bytes 294920 | tf_op jit(solution)/shard_map/ppermute | solution.py:183
  41.8 5.0 %copy-start.14 = (f32[3,8,1,256]{3,2,1,0:T(1,128)}, f32[3,8,1,256]{3,2,1,0:T(1,128)S(1)}, u32[]{:S(2)}) copy-start(f32[3,8,1,256]{3,2,1,0:T(1,128)S(1)} %collective-permute-done.2.refs_4_) | copy-start | bytes 73732
  41.8 4.9 %collective-permute-start.3 = (f32[3,8,1,256]{3,2,1,0:T(1,128)S(1)}, f32[3,8,1,256]{3,2,1,0:T(1,128)S(1)}, u32[]{:S(2)}, u32[]{:S(2)}) collective-permute-start(f32[3,8,1,256]{3,2,1,0:T(1,128)S(1)} %get-tuple-element.18), channel_id=1, source_target_pairs={{1,0},{2,1},{3,2},{5,4},{6,5},{7,6},{9,8},{10,9},{11,10},{13,12},{... | collective-permute-start | bytes 73736 | tf_op jit(solution)/shard_map/ppermute | solution.py:185
  52.8 15.2 %collective-permute-start.8 = (f32[3,32,256]{2,1,0:T(8,128)S(1)}, f32[3,32,256]{2,1,0:T(8,128)S(1)}, u32[]{:S(2)}, u32[]{:S(2)}) collective-permute-start(f32[3,32,256]{2,1,0:T(8,128)S(1)} %get-tuple-element.17), channel_id=1, source_target_pairs={{0,4},{4,8},{8,12},{12,16},{16,20},{20,24},{24,28},{28,32},{32,36}... | collective-permute-start | bytes 294920 | tf_op jit(solution)/shard_map/ppermute | solution.py:182
  57.3 10.7 %collective-permute-start.9 = (f32[3,32,256]{2,1,0:T(8,128)S(1)}, f32[3,32,256]{2,1,0:T(8,128)S(1)}, u32[]{:S(2)}, u32[]{:S(2)}) collective-permute-start(f32[3,32,256]{2,1,0:T(8,128)S(1)} %get-tuple-element.16), channel_id=1, source_target_pairs={{4,0},{8,4},{12,8},{16,12},{20,16},{24,20},{28,24},{32,28},{36,32}... | collective-permute-start | bytes 294920 | tf_op jit(solution)/shard_map/ppermute | solution.py:183
  60.3 4.6 %collective-permute-start.10 = (f32[3,8,1,256]{3,2,1,0:T(1,128)S(1)}, f32[3,8,1,256]{3,2,1,0:T(1,128)S(1)}, u32[]{:S(2)}, u32[]{:S(2)}) collective-permute-start(f32[3,8,1,256]{3,2,1,0:T(1,128)S(1)} %get-tuple-element.15), channel_id=1, source_target_pairs={{0,1},{1,2},{2,3},{4,5},{5,6},{6,7},{8,9},{9,10},{10,11},{12,13},{... | collective-permute-start | bytes 73736 | tf_op jit(solution)/shard_map/ppermute | solution.py:184
  63.4 4.6 %collective-permute-start.11 = (f32[3,8,1,256]{3,2,1,0:T(1,128)S(1)}, f32[3,8,1,256]{3,2,1,0:T(1,128)S(1)}, u32[]{:S(2)}, u32[]{:S(2)}) collective-permute-start(f32[3,8,1,256]{3,2,1,0:T(1,128)S(1)} %get-tuple-element.14), channel_id=1, source_target_pairs={{1,0},{2,1},{3,2},{5,4},{6,5},{7,6},{9,8},{10,9},{11,10},{13,12},{... | collective-permute-start | bytes 73736 | tf_op jit(solution)/shard_map/ppermute | solution.py:185
  64.9 3.1 %copy-start.16 = (f32[3,8,1,256]{3,2,1,0:T(1,128)}, f32[3,8,1,256]{3,2,1,0:T(1,128)S(1)}, u32[]{:S(2)}) copy-start(f32[3,8,1,256]{3,2,1,0:T(1,128)S(1)} %collective-permute-done.10.refs_4_) | copy-start | bytes 73732
  68.6 0.6 copy-start.10
  82.6 27.2 %copy-start.1 = (f32[500,500]{1,0:T(8,128)S(1)}, f32[500,500]{1,0:T(8,128)}, u32[]{:S(2)}) copy-start(f32[500,500]{1,0:T(8,128)} %constant.18.clone) | copy-start | bytes 3000004
  89.8 24.8 %copy-start.4 = (f32[500,100]{1,0:T(8,128)S(1)}, f32[500,100]{1,0:T(8,128)}, u32[]{:S(2)}) copy-start(f32[500,100]{1,0:T(8,128)} %constant.56) | copy-start | bytes 600004
  89.8 26.3 %copy-start.3 = (f32[500,100]{1,0:T(8,128)S(1)}, f32[500,100]{1,0:T(8,128)}, u32[]{:S(2)}) copy-start(f32[500,100]{1,0:T(8,128)} %constant.57) | copy-start | bytes 600004
  89.8 29.3 %copy-start.2 = (f32[500,100]{1,0:T(8,128)S(1)}, f32[500,100]{1,0:T(8,128)}, u32[]{:S(2)}) copy-start(f32[500,100]{1,0:T(8,128)} %constant.54) | copy-start | bytes 600004
  95.1 18.9 %collective-permute-start.14 = (f32[100,32]{1,0:T(8,128)}, f32[100,32]{1,0:T(8,128)S(1)}, u32[]{:S(2)}, u32[]{:S(2)}) collective-permute-start(f32[100,32]{1,0:T(8,128)} %slice.167), channel_id=1, source_target_pairs={{0,1},{1,2},{2,3},{4,5},{5,6},{6,7},{8,9},{9,10},{10,11},{12,13},{... | collective-permute-start | bytes 38408 | tf_op jit(solution)/shard_map/ppermute | solution.py:251
  98.9 17.2 %collective-permute-start.15 = (f32[100,32]{1,0:T(8,128)}, f32[100,32]{1,0:T(8,128)}, u32[]{:S(2)}, u32[]{:S(2)}) collective-permute-start(f32[100,32]{1,0:T(8,128)} %bitcast.92), channel_id=1, source_target_pairs={{1,0},{2,1},{3,2},{5,4},{6,5},{7,6},{9,8},{10,9},{11,10},{13,12},{... | collective-permute-start | bytes 38408 | tf_op jit(solution)/shard_map/ppermute | solution.py:252
  101.7 15.9 %collective-permute-start.13 = (f32[100,128]{1,0:T(8,128)}, f32[100,128]{1,0:T(8,128)}, u32[]{:S(2)}, u32[]{:S(2)}) collective-permute-start(f32[100,128]{1,0:T(8,128)} %reshape_squeeze.37), channel_id=1, source_target_pairs={{4,0},{8,4},{12,8},{16,12},{20,16},{24,20},{28,24},{32,28},{36,32}... | collective-permute-start | bytes 153608 | tf_op jit(solution)/shard_map/ppermute | solution.py:250
  104.2 14.9 %collective-permute-start.12 = (f32[100,128]{1,0:T(8,128)}, f32[100,128]{1,0:T(8,128)}, u32[]{:S(2)}, u32[]{:S(2)}) collective-permute-start(f32[100,128]{1,0:T(8,128)} %reshape_squeeze.36), channel_id=1, source_target_pairs={{0,4},{4,8},{8,12},{12,16},{16,20},{20,24},{24,28},{28,32},{32,36}... | collective-permute-start | bytes 153608 | tf_op jit(solution)/shard_map/ppermute | solution.py:249
  123.6 13.0 %collective-permute-start.18 = (f32[100,32]{1,0:T(8,128)S(1)}, f32[100,32]{1,0:T(8,128)S(1)}, u32[]{:S(2)}, u32[]{:S(2)}) collective-permute-start(f32[100,32]{1,0:T(8,128)S(1)} %slice.179), channel_id=1, source_target_pairs={{0,1},{1,2},{2,3},{4,5},{5,6},{6,7},{8,9},{9,10},{10,11},{12,13},{... | collective-permute-start | bytes 38408 | tf_op jit(solution)/shard_map/ppermute | solution.py:251
  128.0 9.3 %collective-permute-start.19 = (f32[100,32]{1,0:T(8,128)S(1)}, f32[100,32]{1,0:T(8,128)S(1)}, u32[]{:S(2)}, u32[]{:S(2)}) collective-permute-start(f32[100,32]{1,0:T(8,128)S(1)} %bitcast.105), channel_id=1, source_target_pairs={{1,0},{2,1},{3,2},{5,4},{6,5},{7,6},{9,8},{10,9},{11,10},{13,12},{... | collective-permute-start | bytes 38408 | tf_op jit(solution)/shard_map/ppermute | solution.py:252
  131.0 7.0 %collective-permute-start.17 = (f32[100,128]{1,0:T(8,128)S(1)}, f32[100,128]{1,0:T(8,128)S(1)}, u32[]{:S(2)}, u32[]{:S(2)}) collective-permute-start(f32[100,128]{1,0:T(8,128)S(1)} %reshape_squeeze.43), channel_id=1, source_target_pairs={{4,0},{8,4},{12,8},{16,12},{20,16},{24,20},{28,24},{32,28},{36,32}... | collective-permute-start | bytes 153608 | tf_op jit(solution)/shard_map/ppermute | solution.py:250
  132.9 6.6 %collective-permute-start.16 = (f32[100,128]{1,0:T(8,128)S(1)}, f32[100,128]{1,0:T(8,128)S(1)}, u32[]{:S(2)}, u32[]{:S(2)}) collective-permute-start(f32[100,128]{1,0:T(8,128)S(1)} %reshape_squeeze.42), channel_id=1, source_target_pairs={{0,4},{4,8},{8,12},{12,16},{16,20},{20,24},{24,28},{28,32},{32,36}... | collective-permute-start | bytes 153608 | tf_op jit(solution)/shard_map/ppermute | solution.py:249
  144.2 28.3 %all-to-all-start.1 = ((f32[500,128,2]{0,2,1:T(2,128)}), f32[500,128,2]{0,2,1:T(2,128)S(1)}, u32[]{:S(2)}, u32[]{:S(2)}) async-start(f32[500,128,2]{0,2,1:T(2,128)} %broadcast_select_fusion), calls=%async_computation.1 | async-start | bytes 1048576 | tf_op jit(solution)/shard_map/all_to_all | solution.py:267
  (8 other events, 5.0 us)
where the time goes:
time: 176 us; the launch traced here: 175 us
  starting transfers between devices  80.8 us (46%)
  local copies, waits for them, and re-layouts  41.8 us (24%)
  waiting for transfers between devices  20.8 us (12%)
  matrix products  19.6 us (11%)
  Pallas kernels  7.79 us (4%)
  other arithmetic  2.49 us (1%)
    dot_general x12, matrix products, body(): jnp.dot(other_mat, others, precision=HIGH)  15.6 us
    all_to_all x1, starting transfers between devices, body(): lax.all_to_all(leaving, ('flow', 'grp'), split_axis=1, concat_axis=1, til...  14.2 us
    all_to_all x1, waiting for transfers between devices, body(): lax.all_to_all(leaving, ('flow', 'grp'), split_axis=1, concat_axis=1, til...  14.1 us
    ppermute x3, starting transfers between devices, halos(): lax.ppermute(lax.index_in_dim(field, size_x - 1, lead, keepdims=False), '...  13.1 us
    all_to_all x1, starting transfers between devices, body(): lax.all_to_all(outgoing, ('flow', 'grp'), split_axis=1, concat_axis=1, ti...  10.8 us
    ppermute x3, starting transfers between devices, halos(): lax.ppermute(lax.slice_in_dim(field, size_y - 1, size_y, axis=lead + 1),...  10.2 us
    reshape x1, local copies, waits for them, and re-layouts, project(): blocks = lamb.reshape(3, size_x // 8, 8, size_y // 8, 8, size_z // 8, 8)  9.37 us
    ppermute x2, starting transfers between devices, body(): oxlo = lax.ppermute(fx4, 'flow', up_f)  9.16 us
  transfers between devices with their start and end apart: 22, of which 3 were waited for; matrix products, arithmetic and copies ran while one was open for 25% of the time, Pallas kernels for 4%

commit v1 on v0

--- a/solution.py
+++ b/solution.py
@@ -195,13 +195,26 @@
     return source.reshape(375, -1)
 
 
+def two_stage_all_to_all(value, flow_size, grp_size):
+    rows, cols = value.shape
+    cube = value.reshape(rows, flow_size, grp_size, cols // (flow_size * grp_size))
+    cube = lax.all_to_all(cube, "grp", split_axis=2, concat_axis=2, tiled=True)
+    cube = lax.all_to_all(cube, "flow", split_axis=1, concat_axis=1, tiled=True)
+    return cube.reshape(rows, cols)
+
+
 def body(velocity, eddy_visc, projection, acoustic_state, route_send, route_place):
-    nhalo = halos(eddy_visc, 0)
     vel = velocity
     lamb = None
+    nhalo = None
     for turn in range(LES_SECTIONS):
-        vhalo = halos(vel, 1)
         last = turn == LES_SECTIONS - 1
+        if nhalo is None:
+            joint = halos(jnp.concatenate([vel, eddy_visc[None]], axis=0), 1)
+            vhalo = [part[:3] for part in joint]
+            nhalo = [part[3] for part in joint]
+        else:
+            vhalo = halos(vel, 1)
         res = les_section(vel, eddy_visc, vhalo, nhalo, last)
         vel = res[0]
         if last:
@@ -218,7 +231,7 @@
         .at[:, placing]
         .set(acoustic_state.reshape(500, elem_count))
     )
-    arrived = lax.all_to_all(outgoing, ("flow", "grp"), split_axis=1, concat_axis=1, tiled=True)
+    arrived = two_stage_all_to_all(outgoing, flow_size, grp_size)
     sending = route_send.reshape(-1)
     filled = sending >= 0
     target = jnp.where(filled, sending, elem_count)
@@ -264,7 +277,7 @@
         state = state + TIME_STEP_ACOUSTIC * rate
     flat_state = state
     leaving = jnp.where(filled[None, :], flat_state[:, jnp.where(filled, sending, 0)], 0.0)
-    returned = lax.all_to_all(leaving, ("flow", "grp"), split_axis=1, concat_axis=1, tiled=True)
+    returned = two_stage_all_to_all(leaving, flow_size, grp_size)
     acoustic_out = returned[:, placing].reshape(4, 125, elem_count)
     return (vel, acoustic_out)
 

time: 176 us -> 172 us (0.977)
  starting transfers between devices: 80.8 us -> 66.6 us
  blocking collectives: 0 us -> 13.7 us
  waiting for transfers between devices: 20.8 us -> 15.1 us
    all_to_all x0 -> x1, blocking collectives: none -> 13.7 us  [two_stage_all_to_all(): cube = lax.all_to_all(cube, 'grp', split_axis=2, concat_axis=2, tiled=True)]
    ppermute x3 -> x2, starting transfers between devices: 13.1 us -> 6.77 us  [halos(): lax.ppermute(lax.index_in_dim(field, size_x - 1, lead, keepdims=False), '...]
    ppermute x3 -> x2, waiting for transfers between devices: 6.66 us -> 3.4 us  [halos(): lax.ppermute(lax.slice_in_dim(field, 0, 1, axis=lead + 1), 'grp', down_g)]
    all_to_all x2 -> x3, starting transfers between devices: 24.9 us -> 21.9 us  [the longest x2 17.9 us: two_stage_all_to_all(): cube = lax.all_to_all(cube, 'flow', split_axis=1, concat_axis=1, tiled=True)]
    ppermute x3 -> x2, starting transfers between devices: 10.2 us -> 7.64 us  [halos(): lax.ppermute(lax.slice_in_dim(field, size_y - 1, size_y, axis=lead + 1),...]
    all_to_all x2 -> x3, waiting for transfers between devices: 14.1 us -> 11.6 us  [the longest x2 11.6 us: two_stage_all_to_all(): cube = lax.all_to_all(cube, 'flow', split_axis=1, concat_axis=1, tiled=True)]
    slice x0 -> x4, local copies, waits for them, and re-layouts: none -> 2.48 us  [body(): vhalo = [part[:3] for part in joint]]
    squeeze x0 -> x4, local copies, waits for them, and re-layouts: none -> 2.4 us  [body(): nhalo = [part[3] for part in joint]]
  transfers between devices with their start and end apart: 22 -> 19, of which waited for: 3 -> 2; matrix products, arithmetic and copies ran while one was open for 25% -> 28% of each run, Pallas kernels for 4% -> 5%
where the time goes in v1:
time: 172 us; the launch traced here: 170 us
  starting transfers between devices  66.6 us (39%)
  local copies, waits for them, and re-layouts  42.8 us (25%)
  matrix products  19.6 us (11%)
  waiting for transfers between devices  15.1 us (9%)
  blocking collectives  13.7 us (8%)
  Pallas kernels  7.79 us (5%)
  other arithmetic  3.2 us (2%)
    all_to_all x2, starting transfers between devices, two_stage_all_to_all(): cube = lax.all_to_all(cube, 'flow', split_axis=1, concat_axis=1, tiled=True)  17.9 us
    dot_general x12, matrix products, body(): jnp.dot(other_mat, others, precision=HIGH)  15.6 us
    all_to_all x1, blocking collectives, two_stage_all_to_all(): cube = lax.all_to_all(cube, 'grp', split_axis=2, concat_axis=2, tiled=True)  13.7 us
    all_to_all x2, waiting for transfers between devices, two_stage_all_to_all(): cube = lax.all_to_all(cube, 'flow', split_axis=1, concat_axis=1, tiled=True)  11.6 us
    reshape x1, local copies, waits for them, and re-layouts, project(): blocks = lamb.reshape(3, size_x // 8, 8, size_y // 8, 8, size_z // 8, 8)  9.35 us
    pallas_call x2, Pallas kernels, les_section(): pl.pallas_call(lambda *refs: les_kernel(want_lamb, *refs), out_shape=tupl...  7.79 us
    ppermute x2, starting transfers between devices, halos(): lax.ppermute(lax.slice_in_dim(field, size_y - 1, size_y, axis=lead + 1),...  7.64 us
    ppermute x2, starting transfers between devices, body(): ylo_recv = lax.ppermute(fy4[:, elem_count - row_len:], 'grp', up_g)  7.34 us
  transfers between devices with their start and end apart: 19, of which 2 were waited for; matrix products, arithmetic and copies ran while one was open for 28% of the time, Pallas kernels for 5%

profile of v1, /device:TPU:1, one launch (start us, length us, event | category | flops | bytes accessed | tf_op | source)
XLA Modules:
  0.0 170.1 jit_solution(12249051717501850270)
XLA Ops:
  1.7 3.3 %collective-permute-start.1 = (f32[4,32,256]{2,1,0:T(8,128)S(1)}, f32[4,32,256]{2,1,0:T(8,128)S(1)}, u32[]{:S(2)}, u32[]{:S(2)}) collective-permute-start(f32[4,32,256]{2,1,0:T(8,128)S(1)} %get-tuple-element.20), channel_id=1, source_target_pairs={{4,0},{8,4},{12,8},{16,12},{20,16},{24,20},{28,24},{32,28},{36,32}... | collective-permute-start | bytes 393224 | tf_op jit(solution)/shard_map/ppermute | solution.py:183
  5.0 3.5 %collective-permute-start = (f32[4,32,256]{2,1,0:T(8,128)S(1)}, f32[4,32,256]{2,1,0:T(8,128)S(1)}, u32[]{:S(2)}, u32[]{:S(2)}) collective-permute-start(f32[4,32,256]{2,1,0:T(8,128)S(1)} %get-tuple-element.21), channel_id=1, source_target_pairs={{0,4},{4,8},{8,12},{12,16},{16,20},{20,24},{24,28},{28,32},{32,36}... | collective-permute-start | bytes 393224 | tf_op jit(solution)/shard_map/ppermute | solution.py:182
  11.0 4.0 %collective-permute-start.2 = (f32[4,8,1,256]{3,2,1,0:T(1,128)S(1)}, f32[4,8,1,256]{3,2,1,0:T(1,128)S(1)}, u32[]{:S(2)}, u32[]{:S(2)}) collective-permute-start(f32[4,8,1,256]{3,2,1,0:T(1,128)S(1)} %get-tuple-element.19), channel_id=1, source_target_pairs={{0,1},{1,2},{2,3},{4,5},{5,6},{6,7},{8,9},{9,10},{10,11},{12,13},{... | collective-permute-start | bytes 98312 | tf_op jit(solution)/shard_map/ppermute | solution.py:184
  19.1 4.0 %all-to-all-start = ((f32[500,32,4,2]{0,3,1,2:T(2,128)}), f32[500,32,4,2]{0,3,1,2:T(2,128)S(1)}, u32[]{:S(2)}, u32[]{:S(2)}) async-start(f32[500,32,4,2]{0,3,1,2:T(2,128)} %copy.55), calls=%async_computation | async-start | bytes 1048576 | tf_op jit(solution)/shard_map/all_to_all | solution.py:201
  28.4 3.8 %shard_map.95.refs_0_ = f32[3,8,32,256]{3,2,1,0:T(8,128)} custom-call(f32[3,8,32,256]{3,2,1,0:T(8,128)} %refs_0_.1, f32[8,32,256]{2,1,0:T(8,128)} %refs_1_.3, f32[3,32,256]{2,1,0:T(8,128)} %slice.176.refs_2_, f32[3,32,256]{2,1,0:T(8,128)} %slice.177.refs_3_, f32[3,8,1,256]{3,2,1,0:T(1,128)} %slice.178.refs_4_, f32[3,8,1,256]{3,2,1,0:T(1,128)} %slice.179.refs_5_, ...), custom_call_target="tpu_custom_call" | custom-call | tf_op jit(solution)/shard_map/pallas_call | solution.py:167
  33.2 3.2 %collective-permute-start.4 = (f32[3,32,256]{2,1,0:T(8,128)S(1)}, f32[3,32,256]{2,1,0:T(8,128)S(1)}, u32[]{:S(2)}, u32[]{:S(2)}) collective-permute-start(f32[3,32,256]{2,1,0:T(8,128)S(1)} %get-tuple-element.25), channel_id=1, source_target_pairs={{0,4},{4,8},{8,12},{12,16},{16,20},{20,24},{24,28},{28,32},{32,36}... | collective-permute-start | bytes 294920 | tf_op jit(solution)/shard_map/ppermute | solution.py:182
  36.4 1.9 %collective-permute-start.5 = (f32[3,32,256]{2,1,0:T(8,128)S(1)}, f32[3,32,256]{2,1,0:T(8,128)S(1)}, u32[]{:S(2)}, u32[]{:S(2)}) collective-permute-start(f32[3,32,256]{2,1,0:T(8,128)S(1)} %get-tuple-element.24), channel_id=1, source_target_pairs={{4,0},{8,4},{12,8},{16,12},{20,16},{24,20},{28,24},{32,28},{36,32}... | collective-permute-start | bytes 294920 | tf_op jit(solution)/shard_map/ppermute | solution.py:183
  39.2 9.9 %all-to-all-start.1 = ((f32[500,32,4,2]{0,3,2,1:T(2,128)}), f32[500,32,4,2]{0,3,2,1:T(2,128)S(1)}, u32[]{:S(2)}, u32[]{:S(2)}) async-start(f32[500,32,4,2]{0,3,2,1:T(2,128)} %copy.56), calls=%async_computation.1 | async-start | bytes 1048576 | tf_op jit(solution)/shard_map/all_to_all | solution.py:202
  50.2 3.6 %collective-permute-start.6 = (f32[3,8,1,256]{3,2,1,0:T(1,128)S(1)}, f32[3,8,1,256]{3,2,1,0:T(1,128)S(1)}, u32[]{:S(2)}, u32[]{:S(2)}) collective-permute-start(f32[3,8,1,256]{3,2,1,0:T(1,128)S(1)} %get-tuple-element.23), channel_id=1, source_target_pairs={{0,1},{1,2},{2,3},{4,5},{5,6},{6,7},{8,9},{9,10},{10,11},{12,13},{... | collective-permute-start | bytes 73736 | tf_op jit(solution)/shard_map/ppermute | solution.py:184
  55.4 3.4 %collective-permute-done.7.refs_5_ = f32[3,8,1,256]{3,2,1,0:T(1,128)S(1)} collective-permute-done((f32[3,8,1,256]{3,2,1,0:T(1,128)S(1)}, f32[3,8,1,256]{3,2,1,0:T(1,128)S(1)}, u32[]{:S(2)}, u32[]{:S(2)}) %collective-permute-start.7) | collective-permute-done | bytes 24608 | tf_op jit(solution)/shard_map/ppermute | solution.py:185
  60.0 3.9 %shard_map.96 = (f32[3,8,32,256]{3,2,1,0:T(8,128)}, bf16[3,8,32,256]{3,2,1,0:T(8,128)(2,1)}) custom-call(f32[3,8,32,256]{3,2,1,0:T(8,128)} %shard_map.95.refs_0_, f32[8,32,256]{2,1,0:T(8,128)} %refs_1_.3, f32[3,32,256]{2,1,0:T(8,128)} %copy-done.5, f32[3,32,256]{2,1,0:T(8,128)} %copy-done.6, f32[3,8,1,256]{3,2,1,0:T(1,128)} %copy-done.8, ...), custom_call_target="tpu_custom_call" | custom-call | tf_op jit(solution)/shard_map/pallas_call | solution.py:167
  64.0 9.3 %reshape.171 = bf16[3,1,8,4,8,32,8]{6,5,4,3,2,0,1:T(8,128)(2,1)} reshape(bf16[3,8,32,256]{3,2,1,0:T(8,128)(2,1)} %get-tuple-element.5) | data formatting | bytes 786432 | tf_op jit(solution)/shard_map/reshape | solution.py:191
  73.3 5.6 %copy.58 = bf16[8,8,8,3,1,4,32]{6,5,3,2,1,0,4:T(4,128)(2,1)S(1)} copy(bf16[8,8,8,3,1,4,32]{2,6,1,5,0,3,4:T(8,128)(2,1)} %bitcast.97) | data formatting | bytes 786432 | tf_op jit(solution)/shard_map/transpose | solution.py:192
  78.9 1.6 reshape.172
  82.5 1.5 scatter_custom_fusion.1
  85.9 3.1 %collective-permute-start.10 = (f32[100,32]{1,0:T(8,128)}, f32[100,32]{1,0:T(8,128)S(1)}, u32[]{:S(2)}, u32[]{:S(2)}) collective-permute-start(f32[100,32]{1,0:T(8,128)} %slice.191), channel_id=1, source_target_pairs={{0,1},{1,2},{2,3},{4,5},{5,6},{6,7},{8,9},{9,10},{10,11},{12,13},{... | collective-permute-start | bytes 38408 | tf_op jit(solution)/shard_map/ppermute | solution.py:264
  92.4 3.5 %collective-permute-start.9 = (f32[100,128]{1,0:T(8,128)}, f32[100,128]{1,0:T(8,128)}, u32[]{:S(2)}, u32[]{:S(2)}) collective-permute-start(f32[100,128]{1,0:T(8,128)} %reshape_squeeze.37), channel_id=1, source_target_pairs={{4,0},{8,4},{12,8},{16,12},{20,16},{24,20},{28,24},{32,28},{36,32}... | collective-permute-start | bytes 153608 | tf_op jit(solution)/shard_map/ppermute | solution.py:263
  96.6 3.5 %collective-permute-start.8 = (f32[100,128]{1,0:T(8,128)}, f32[100,128]{1,0:T(8,128)}, u32[]{:S(2)}, u32[]{:S(2)}) collective-permute-start(f32[100,128]{1,0:T(8,128)} %reshape_squeeze.36), channel_id=1, source_target_pairs={{0,4},{4,8},{8,12},{12,16},{16,20},{20,24},{24,28},{28,32},{32,36}... | collective-permute-start | bytes 153608 | tf_op jit(solution)/shard_map/ppermute | solution.py:262
  100.1 1.7 fusion.69
  101.8 1.6 fusion.44
  105.0 1.4 fusion.21
  107.9 1.5 fusion.70
  110.9 1.7 fusion.12
  114.0 4.3 %collective-permute-start.14 = (f32[100,32]{1,0:T(8,128)S(1)}, f32[100,32]{1,0:T(8,128)S(1)}, u32[]{:S(2)}, u32[]{:S(2)}) collective-permute-start(f32[100,32]{1,0:T(8,128)S(1)} %slice.203), channel_id=1, source_target_pairs={{0,1},{1,2},{2,3},{4,5},{5,6},{6,7},{8,9},{9,10},{10,11},{12,13},{... | collective-permute-start | bytes 38408 | tf_op jit(solution)/shard_map/ppermute | solution.py:264
  119.7 1.9 %collective-permute-start.13 = (f32[100,128]{1,0:T(8,128)S(1)}, f32[100,128]{1,0:T(8,128)S(1)}, u32[]{:S(2)}, u32[]{:S(2)}) collective-permute-start(f32[100,128]{1,0:T(8,128)S(1)} %reshape_squeeze.43), channel_id=1, source_target_pairs={{4,0},{8,4},{12,8},{16,12},{20,16},{24,20},{28,24},{32,28},{36,32}... | collective-permute-start | bytes 153608 | tf_op jit(solution)/shard_map/ppermute | solution.py:263
  121.6 1.6 fusion.39
  123.2 3.6 %collective-permute-start.12 = (f32[100,128]{1,0:T(8,128)S(1)}, f32[100,128]{1,0:T(8,128)S(1)}, u32[]{:S(2)}, u32[]{:S(2)}) collective-permute-start(f32[100,128]{1,0:T(8,128)S(1)} %reshape_squeeze.42), channel_id=1, source_target_pairs={{0,4},{4,8},{8,12},{12,16},{16,20},{20,24},{24,28},{28,32},{32,36}... | collective-permute-start | bytes 153608 | tf_op jit(solution)/shard_map/ppermute | solution.py:262
  128.3 1.5 fusion.73
  130.4 1.5 fusion.15
  133.8 13.7 %all_to_all.20 = f32[500,32,4,2]{0,3,1,2:T(2,128)S(1)} all-to-all(f32[500,32,4,2]{0,3,1,2:T(2,128)S(1)} %copy.62), channel_id=1, replica_groups=mesh['flow'=32,'grp'=4] {'grp'}, dimensions={2} | all-to-all | bytes 1024000 | tf_op jit(solution)/shard_map/all_to_all | solution.py:201
  148.3 7.9 %all-to-all-start.3 = ((f32[500,32,4,2]{0,3,2,1:T(2,128)}), f32[500,32,4,2]{0,3,2,1:T(2,128)S(1)}, u32[]{:S(2)}, u32[]{:S(2)}) async-start(f32[500,32,4,2]{0,3,2,1:T(2,128)} %copy.63), calls=%async_computation.3 | async-start | bytes 1048576 | tf_op jit(solution)/shard_map/all_to_all | solution.py:202
  156.3 11.6 %all-to-all-done.3 = f32[500,32,4,2]{0,3,2,1:T(2,128)S(1)} async-done(((f32[500,32,4,2]{0,3,2,1:T(2,128)}), f32[500,32,4,2]{0,3,2,1:T(2,128)S(1)}, u32[]{:S(2)}, u32[]{:S(2)}) %all-to-all-start.3) | async-done | bytes 512032 | tf_op jit(solution)/shard_map/all_to_all | solution.py:202
  (119 shorter events, 40.2 us)
Async XLA Ops:
  0.6 79.9 %copy-start = (bf16[125,512]{1,0:T(8,128)(2,1)S(1)}, bf16[125,512]{1,0:T(8,128)(2,1)}, u32[]{:S(2)}) copy-start(bf16[125,512]{1,0:T(8,128)(2,1)} %param.10) | copy-start | bytes 384004
  0.6 22.5 %copy-start.10 = (s32[1,128,2]{1,2,0:T(2,128)S(1)}, s32[1,128,2]{1,2,0:T(2,128)}, u32[]{:S(2)}) copy-start(s32[1,128,2]{1,2,0:T(2,128)} %param.12) | copy-start | bytes 3076
  1.7 24.2 %collective-permute-start.1 = (f32[4,32,256]{2,1,0:T(8,128)S(1)}, f32[4,32,256]{2,1,0:T(8,128)S(1)}, u32[]{:S(2)}, u32[]{:S(2)}) collective-permute-start(f32[4,32,256]{2,1,0:T(8,128)S(1)} %get-tuple-element.20), channel_id=1, source_target_pairs={{4,0},{8,4},{12,8},{16,12},{20,16},{24,20},{28,24},{32,28},{36,32}... | collective-permute-start | bytes 393224 | tf_op jit(solution)/shard_map/ppermute | solution.py:183
  5.0 22.1 %collective-permute-start = (f32[4,32,256]{2,1,0:T(8,128)S(1)}, f32[4,32,256]{2,1,0:T(8,128)S(1)}, u32[]{:S(2)}, u32[]{:S(2)}) collective-permute-start(f32[4,32,256]{2,1,0:T(8,128)S(1)} %get-tuple-element.21), channel_id=1, source_target_pairs={{0,4},{4,8},{8,12},{12,16},{16,20},{20,24},{24,28},{28,32},{32,36}... | collective-permute-start | bytes 393224 | tf_op jit(solution)/shard_map/ppermute | solution.py:182
  9.7 13.7 %collective-permute-start.3 = (f32[4,8,1,256]{3,2,1,0:T(1,128)S(1)}, f32[4,8,1,256]{3,2,1,0:T(1,128)S(1)}, u32[]{:S(2)}, u32[]{:S(2)}) collective-permute-start(f32[4,8,1,256]{3,2,1,0:T(1,128)S(1)} %get-tuple-element.18), channel_id=1, source_target_pairs={{1,0},{2,1},{3,2},{5,4},{6,5},{7,6},{9,8},{10,9},{11,10},{13,12},{... | collective-permute-start | bytes 98312 | tf_op jit(solution)/shard_map/ppermute | solution.py:185
  11.0 13.6 %collective-permute-start.2 = (f32[4,8,1,256]{3,2,1,0:T(1,128)S(1)}, f32[4,8,1,256]{3,2,1,0:T(1,128)S(1)}, u32[]{:S(2)}, u32[]{:S(2)}) collective-permute-start(f32[4,8,1,256]{3,2,1,0:T(1,128)S(1)} %get-tuple-element.19), channel_id=1, source_target_pairs={{0,1},{1,2},{2,3},{4,5},{5,6},{6,7},{8,9},{9,10},{10,11},{12,13},{... | collective-permute-start | bytes 98312 | tf_op jit(solution)/shard_map/ppermute | solution.py:184
  19.1 19.2 %all-to-all-start = ((f32[500,32,4,2]{0,3,1,2:T(2,128)}), f32[500,32,4,2]{0,3,1,2:T(2,128)S(1)}, u32[]{:S(2)}, u32[]{:S(2)}) async-start(f32[500,32,4,2]{0,3,1,2:T(2,128)} %copy.55), calls=%async_computation | async-start | bytes 1048576 | tf_op jit(solution)/shard_map/all_to_all | solution.py:201
  33.2 25.6 %collective-permute-start.4 = (f32[3,32,256]{2,1,0:T(8,128)S(1)}, f32[3,32,256]{2,1,0:T(8,128)S(1)}, u32[]{:S(2)}, u32[]{:S(2)}) collective-permute-start(f32[3,32,256]{2,1,0:T(8,128)S(1)} %get-tuple-element.25), channel_id=1, source_target_pairs={{0,4},{4,8},{8,12},{12,16},{16,20},{20,24},{24,28},{28,32},{32,36}... | collective-permute-start | bytes 294920 | tf_op jit(solution)/shard_map/ppermute | solution.py:182
  36.4 22.3 %collective-permute-start.5 = (f32[3,32,256]{2,1,0:T(8,128)S(1)}, f32[3,32,256]{2,1,0:T(8,128)S(1)}, u32[]{:S(2)}, u32[]{:S(2)}) collective-permute-start(f32[3,32,256]{2,1,0:T(8,128)S(1)} %get-tuple-element.24), channel_id=1, source_target_pairs={{4,0},{8,4},{12,8},{16,12},{20,16},{24,20},{28,24},{32,28},{36,32}... | collective-permute-start | bytes 294920 | tf_op jit(solution)/shard_map/ppermute | solution.py:183
  39.2 42.9 %all-to-all-start.1 = ((f32[500,32,4,2]{0,3,2,1:T(2,128)}), f32[500,32,4,2]{0,3,2,1:T(2,128)S(1)}, u32[]{:S(2)}, u32[]{:S(2)}) async-start(f32[500,32,4,2]{0,3,2,1:T(2,128)} %copy.56), calls=%async_computation.1 | async-start | bytes 1048576 | tf_op jit(solution)/shard_map/all_to_all | solution.py:202
  50.2 5.1 %collective-permute-start.6 = (f32[3,8,1,256]{3,2,1,0:T(1,128)S(1)}, f32[3,8,1,256]{3,2,1,0:T(1,128)S(1)}, u32[]{:S(2)}, u32[]{:S(2)}) collective-permute-start(f32[3,8,1,256]{3,2,1,0:T(1,128)S(1)} %get-tuple-element.23), channel_id=1, source_target_pairs={{0,1},{1,2},{2,3},{4,5},{5,6},{6,7},{8,9},{9,10},{10,11},{12,13},{... | collective-permute-start | bytes 73736 | tf_op jit(solution)/shard_map/ppermute | solution.py:184
  53.9 4.9 %collective-permute-start.7 = (f32[3,8,1,256]{3,2,1,0:T(1,128)S(1)}, f32[3,8,1,256]{3,2,1,0:T(1,128)S(1)}, u32[]{:S(2)}, u32[]{:S(2)}) collective-permute-start(f32[3,8,1,256]{3,2,1,0:T(1,128)S(1)} %get-tuple-element.22), channel_id=1, source_target_pairs={{1,0},{2,1},{3,2},{5,4},{6,5},{7,6},{9,8},{10,9},{11,10},{13,12},{... | collective-permute-start | bytes 73736 | tf_op jit(solution)/shard_map/ppermute | solution.py:185
  55.3 3.4 %copy-start.8 = (f32[3,8,1,256]{3,2,1,0:T(1,128)}, f32[3,8,1,256]{3,2,1,0:T(1,128)S(1)}, u32[]{:S(2)}) copy-start(f32[3,8,1,256]{3,2,1,0:T(1,128)S(1)} %collective-permute-done.6.refs_4_) | copy-start | bytes 73732
  58.7 0.6 copy-start.9
  58.8 0.6 copy-start.5
  59.4 0.6 copy-start.6
  73.3 26.7 %copy-start.1 = (f32[500,500]{1,0:T(8,128)S(1)}, f32[500,500]{1,0:T(8,128)}, u32[]{:S(2)}) copy-start(f32[500,500]{1,0:T(8,128)} %constant.18.clone) | copy-start | bytes 3000004
  80.6 24.4 %copy-start.4 = (f32[500,100]{1,0:T(8,128)S(1)}, f32[500,100]{1,0:T(8,128)}, u32[]{:S(2)}) copy-start(f32[500,100]{1,0:T(8,128)} %constant.56) | copy-start | bytes 600004
  80.6 25.9 %copy-start.3 = (f32[500,100]{1,0:T(8,128)S(1)}, f32[500,100]{1,0:T(8,128)}, u32[]{:S(2)}) copy-start(f32[500,100]{1,0:T(8,128)} %constant.57) | copy-start | bytes 600004
  80.6 28.9 %copy-start.2 = (f32[500,100]{1,0:T(8,128)S(1)}, f32[500,100]{1,0:T(8,128)}, u32[]{:S(2)}) copy-start(f32[500,100]{1,0:T(8,128)} %constant.54) | copy-start | bytes 600004
  85.9 18.5 %collective-permute-start.10 = (f32[100,32]{1,0:T(8,128)}, f32[100,32]{1,0:T(8,128)S(1)}, u32[]{:S(2)}, u32[]{:S(2)}) collective-permute-start(f32[100,32]{1,0:T(8,128)} %slice.191), channel_id=1, source_target_pairs={{0,1},{1,2},{2,3},{4,5},{5,6},{6,7},{8,9},{9,10},{10,11},{12,13},{... | collective-permute-start | bytes 38408 | tf_op jit(solution)/shard_map/ppermute | solution.py:264
  89.6 16.8 %collective-permute-start.11 = (f32[100,32]{1,0:T(8,128)}, f32[100,32]{1,0:T(8,128)}, u32[]{:S(2)}, u32[]{:S(2)}) collective-permute-start(f32[100,32]{1,0:T(8,128)} %bitcast.92), channel_id=1, source_target_pairs={{1,0},{2,1},{3,2},{5,4},{6,5},{7,6},{9,8},{10,9},{11,10},{13,12},{... | collective-permute-start | bytes 38408 | tf_op jit(solution)/shard_map/ppermute | solution.py:265
  92.4 15.5 %collective-permute-start.9 = (f32[100,128]{1,0:T(8,128)}, f32[100,128]{1,0:T(8,128)}, u32[]{:S(2)}, u32[]{:S(2)}) collective-permute-start(f32[100,128]{1,0:T(8,128)} %reshape_squeeze.37), channel_id=1, source_target_pairs={{4,0},{8,4},{12,8},{16,12},{20,16},{24,20},{28,24},{32,28},{36,32}... | collective-permute-start | bytes 153608 | tf_op jit(solution)/shard_map/ppermute | solution.py:263
  96.6 12.9 %collective-permute-start.8 = (f32[100,128]{1,0:T(8,128)}, f32[100,128]{1,0:T(8,128)}, u32[]{:S(2)}, u32[]{:S(2)}) collective-permute-start(f32[100,128]{1,0:T(8,128)} %reshape_squeeze.36), channel_id=1, source_target_pairs={{0,4},{4,8},{8,12},{12,16},{16,20},{20,24},{24,28},{28,32},{32,36}... | collective-permute-start | bytes 153608 | tf_op jit(solution)/shard_map/ppermute | solution.py:262
  104.3 0.6 copy-start.7
  114.0 13.0 %collective-permute-start.14 = (f32[100,32]{1,0:T(8,128)S(1)}, f32[100,32]{1,0:T(8,128)S(1)}, u32[]{:S(2)}, u32[]{:S(2)}) collective-permute-start(f32[100,32]{1,0:T(8,128)S(1)} %slice.203), channel_id=1, source_target_pairs={{0,1},{1,2},{2,3},{4,5},{5,6},{6,7},{8,9},{9,10},{10,11},{12,13},{... | collective-permute-start | bytes 38408 | tf_op jit(solution)/shard_map/ppermute | solution.py:264
  118.4 9.3 %collective-permute-start.15 = (f32[100,32]{1,0:T(8,128)S(1)}, f32[100,32]{1,0:T(8,128)S(1)}, u32[]{:S(2)}, u32[]{:S(2)}) collective-permute-start(f32[100,32]{1,0:T(8,128)S(1)} %bitcast.107), channel_id=1, source_target_pairs={{1,0},{2,1},{3,2},{5,4},{6,5},{7,6},{9,8},{10,9},{11,10},{13,12},{... | collective-permute-start | bytes 38408 | tf_op jit(solution)/shard_map/ppermute | solution.py:265
  119.7 8.6 %collective-permute-start.13 = (f32[100,128]{1,0:T(8,128)S(1)}, f32[100,128]{1,0:T(8,128)S(1)}, u32[]{:S(2)}, u32[]{:S(2)}) collective-permute-start(f32[100,128]{1,0:T(8,128)S(1)} %reshape_squeeze.43), channel_id=1, source_target_pairs={{4,0},{8,4},{12,8},{16,12},{20,16},{24,20},{28,24},{32,28},{36,32}... | collective-permute-start | bytes 153608 | tf_op jit(solution)/shard_map/ppermute | solution.py:263
  123.2 6.6 %collective-permute-start.12 = (f32[100,128]{1,0:T(8,128)S(1)}, f32[100,128]{1,0:T(8,128)S(1)}, u32[]{:S(2)}, u32[]{:S(2)}) collective-permute-start(f32[100,128]{1,0:T(8,128)S(1)} %reshape_squeeze.42), channel_id=1, source_target_pairs={{0,4},{4,8},{8,12},{12,16},{16,20},{20,24},{24,28},{28,32},{32,36}... | collective-permute-start | bytes 153608 | tf_op jit(solution)/shard_map/ppermute | solution.py:262
  148.3 19.6 %all-to-all-start.3 = ((f32[500,32,4,2]{0,3,2,1:T(2,128)}), f32[500,32,4,2]{0,3,2,1:T(2,128)S(1)}, u32[]{:S(2)}, u32[]{:S(2)}) async-start(f32[500,32,4,2]{0,3,2,1:T(2,128)} %copy.63), calls=%async_computation.3 | async-start | bytes 1048576 | tf_op jit(solution)/shard_map/all_to_all | solution.py:202

commit v2 on v0

--- a/solution.py
+++ b/solution.py
@@ -188,20 +188,32 @@
 
 def project(lamb, projection):
     size_x, size_y, size_z = (lamb.shape[1], lamb.shape[2], lamb.shape[3])
-    blocks = lamb.reshape(3, size_x // 8, 8, size_y // 8, 8, size_z // 8, 8)
-    blocks = blocks.transpose(2, 4, 6, 0, 1, 3, 5).reshape(512, -1)
+    bx, by, bz = size_x // 8, size_y // 8, size_z // 8
+    perm = np.zeros((size_z, size_z), np.float32)
+    for ez in range(bz):
+        for cz in range(8):
+            perm[ez * 8 + cz, cz * bz + ez] = 1.0
+    rows = lamb.reshape(-1, size_z)
+    moved = jnp.dot(rows, jnp.asarray(perm, jnp.bfloat16), preferred_element_type=jnp.float32)
+    moved = moved.astype(jnp.bfloat16)
+    blocks = moved.reshape(3, bx, 8, by, 8, 8, bz).transpose(2, 4, 5, 0, 1, 3, 6).reshape(512, -1)
     source = jnp.dot(projection, blocks, preferred_element_type=jnp.float32)
     source = source.reshape(125, 3, -1).transpose(1, 0, 2)
     return source.reshape(375, -1)
 
 
 def body(velocity, eddy_visc, projection, acoustic_state, route_send, route_place):
-    nhalo = halos(eddy_visc, 0)
     vel = velocity
     lamb = None
+    nhalo = None
     for turn in range(LES_SECTIONS):
-        vhalo = halos(vel, 1)
         last = turn == LES_SECTIONS - 1
+        if nhalo is None:
+            joint = halos(jnp.concatenate([vel, eddy_visc[None]], axis=0), 1)
+            vhalo = [part[:3] for part in joint]
+            nhalo = [part[3] for part in joint]
+        else:
+            vhalo = halos(vel, 1)
         res = les_section(vel, eddy_visc, vhalo, nhalo, last)
         vel = res[0]
         if last:

time: 176 us -> 147 us (0.84)
  local copies, waits for them, and re-layouts: 41.8 us -> 30.3 us
  starting transfers between devices: 80.8 us -> 70.4 us
  matrix products: 19.6 us -> 15.4 us
  waiting for transfers between devices: 20.8 us -> 17.3 us
    reshape x2 -> x3, local copies, waits for them, and re-layouts: 11 us -> 3.51 us  [project(): moved.reshape(3, bx, 8, by, 8, 8, bz).transpose(2, 4, 5, 0, 1, 3, 6)]
    ppermute x3 -> x2, starting transfers between devices: 13.1 us -> 7.19 us  [halos(): lax.ppermute(lax.index_in_dim(field, size_x - 1, lead, keepdims=False), '...]
    transpose x1 -> x0, local copies, waits for them, and re-layouts: 5.58 us -> none  [project(): blocks = blocks.transpose(2, 4, 6, 0, 1, 3, 5).reshape(512, -1)]
    dot_general x12, matrix products: 15.6 us -> 11.2 us  [body(): jnp.dot(other_mat, others, precision=HIGH)]
    ppermute x3 -> x2, waiting for transfers between devices: 6.66 us -> 3.11 us  [halos(): lax.ppermute(lax.slice_in_dim(field, 0, 1, axis=lead + 1), 'grp', down_g)]
    unnamed x39 -> x55, local copies, waits for them, and re-layouts: 5.78 us -> 2.36 us
    ppermute x3 -> x2, starting transfers between devices: 10.2 us -> 7.09 us  [halos(): lax.ppermute(lax.slice_in_dim(field, size_y - 1, size_y, axis=lead + 1),...]
    slice x0 -> x4, local copies, waits for them, and re-layouts: none -> 2.5 us  [body(): vhalo = [part[:3] for part in joint]]
  transfers between devices with their start and end apart: 22 -> 18, of which waited for: 3 -> 2; matrix products, arithmetic and copies ran while one was open for 25% -> 20% of each run, Pallas kernels for 4% -> 5%
where the time goes in v2:
time: 147 us; the launch traced here: 146 us
  starting transfers between devices  70.4 us (48%)
  local copies, waits for them, and re-layouts  30.3 us (21%)
  waiting for transfers between devices  17.3 us (12%)
  matrix products  15.4 us (10%)
  Pallas kernels  7.83 us (5%)
  other arithmetic  3.64 us (2%)
    all_to_all x1, waiting for transfers between devices, body(): lax.all_to_all(leaving, ('flow', 'grp'), split_axis=1, concat_axis=1, til...  14.1 us
    all_to_all x1, starting transfers between devices, body(): lax.all_to_all(leaving, ('flow', 'grp'), split_axis=1, concat_axis=1, til...  12.3 us
    all_to_all x1, starting transfers between devices, body(): lax.all_to_all(outgoing, ('flow', 'grp'), split_axis=1, concat_axis=1, ti...  12.2 us
    dot_general x12, matrix products, body(): jnp.dot(other_mat, others, precision=HIGH)  11.2 us
    ppermute x2, starting transfers between devices, body(): oxlo = lax.ppermute(fx4, 'flow', up_f)  9.31 us
    ppermute x2, starting transfers between devices, body(): ylo_recv = lax.ppermute(fy4[:, elem_count - row_len:], 'grp', up_g)  7.99 us
    pallas_call x2, Pallas kernels, les_section(): pl.pallas_call(lambda *refs: les_kernel(want_lamb, *refs), out_shape=tupl...  7.83 us
    ppermute x2, starting transfers between devices, halos(): lax.ppermute(lax.index_in_dim(field, size_x - 1, lead, keepdims=False), '...  7.19 us
  transfers between devices with their start and end apart: 18, of which 2 were waited for; matrix products, arithmetic and copies ran while one was open for 20% of the time, Pallas kernels for 5%

profile of v2, /device:TPU:1, one launch (start us, length us, event | category | flops | bytes accessed | tf_op | source)
XLA Modules:
  0.0 146.2 jit_solution(8708387972765877891)
XLA Ops:
  1.8 3.3 %collective-permute-start.1 = (f32[4,32,256]{2,1,0:T(8,128)S(1)}, f32[4,32,256]{2,1,0:T(8,128)S(1)}, u32[]{:S(2)}, u32[]{:S(2)}) collective-permute-start(f32[4,32,256]{2,1,0:T(8,128)S(1)} %get-tuple-element.16), channel_id=1, source_target_pairs={{4,0},{8,4},{12,8},{16,12},{20,16},{24,20},{28,24},{32,28},{36,32}... | collective-permute-start | bytes 393224 | tf_op jit(solution)/shard_map/ppermute | solution.py:183
  5.1 3.5 %collective-permute-start = (f32[4,32,256]{2,1,0:T(8,128)S(1)}, f32[4,32,256]{2,1,0:T(8,128)S(1)}, u32[]{:S(2)}, u32[]{:S(2)}) collective-permute-start(f32[4,32,256]{2,1,0:T(8,128)S(1)} %get-tuple-element.17), channel_id=1, source_target_pairs={{0,4},{4,8},{8,12},{12,16},{16,20},{20,24},{24,28},{28,32},{32,36}... | collective-permute-start | bytes 393224 | tf_op jit(solution)/shard_map/ppermute | solution.py:182
  9.6 1.3 collective-permute-start.3
  10.9 4.0 %collective-permute-start.2 = (f32[4,8,1,256]{3,2,1,0:T(1,128)S(1)}, f32[4,8,1,256]{3,2,1,0:T(1,128)S(1)}, u32[]{:S(2)}, u32[]{:S(2)}) collective-permute-start(f32[4,8,1,256]{3,2,1,0:T(1,128)S(1)} %get-tuple-element.15), channel_id=1, source_target_pairs={{0,1},{1,2},{2,3},{4,5},{5,6},{6,7},{8,9},{9,10},{10,11},{12,13},{... | collective-permute-start | bytes 98312 | tf_op jit(solution)/shard_map/ppermute | solution.py:184
  17.4 12.2 %all-to-all-start = ((f32[500,128,2]{0,2,1:T(2,128)}), f32[500,128,2]{0,2,1:T(2,128)}, u32[]{:S(2)}, u32[]{:S(2)}) async-start(f32[500,128,2]{0,2,1:T(2,128)} %all_to_all.14), calls=%async_computation | async-start | bytes 1048576 | tf_op jit(solution)/shard_map/all_to_all | solution.py:233
  35.4 3.9 %shard_map.104.refs_0_ = f32[3,8,32,256]{3,2,1,0:T(8,128)} custom-call(f32[3,8,32,256]{3,2,1,0:T(8,128)} %refs_0_.1, f32[8,32,256]{2,1,0:T(8,128)} %refs_1_.3, f32[3,32,256]{2,1,0:T(8,128)} %slice.176.refs_2_, f32[3,32,256]{2,1,0:T(8,128)} %slice.177.refs_3_, f32[3,8,1,256]{3,2,1,0:T(1,128)} %slice.178.refs_4_, f32[3,8,1,256]{3,2,1,0:T(1,128)} %slice.179.refs_5_, ...), custom_call_target="tpu_custom_call" | custom-call | tf_op jit(solution)/shard_map/pallas_call | solution.py:167
  41.3 3.7 %collective-permute-start.4 = (f32[3,32,256]{2,1,0:T(8,128)S(1)}, f32[3,32,256]{2,1,0:T(8,128)S(1)}, u32[]{:S(2)}, u32[]{:S(2)}) collective-permute-start(f32[3,32,256]{2,1,0:T(8,128)S(1)} %get-tuple-element.21), channel_id=1, source_target_pairs={{0,4},{4,8},{8,12},{12,16},{16,20},{20,24},{24,28},{28,32},{32,36}... | collective-permute-start | bytes 294920 | tf_op jit(solution)/shard_map/ppermute | solution.py:182
  44.9 1.9 %collective-permute-start.5 = (f32[3,32,256]{2,1,0:T(8,128)S(1)}, f32[3,32,256]{2,1,0:T(8,128)S(1)}, u32[]{:S(2)}, u32[]{:S(2)}) collective-permute-start(f32[3,32,256]{2,1,0:T(8,128)S(1)} %get-tuple-element.20), channel_id=1, source_target_pairs={{4,0},{8,4},{12,8},{16,12},{20,16},{24,20},{28,24},{32,28},{36,32}... | collective-permute-start | bytes 294920 | tf_op jit(solution)/shard_map/ppermute | solution.py:183
  46.9 3.1 %collective-permute-start.6 = (f32[3,8,1,256]{3,2,1,0:T(1,128)S(1)}, f32[3,8,1,256]{3,2,1,0:T(1,128)S(1)}, u32[]{:S(2)}, u32[]{:S(2)}) collective-permute-start(f32[3,8,1,256]{3,2,1,0:T(1,128)S(1)} %get-tuple-element.19), channel_id=1, source_target_pairs={{0,1},{1,2},{2,3},{4,5},{5,6},{6,7},{8,9},{9,10},{10,11},{12,13},{... | collective-permute-start | bytes 73736 | tf_op jit(solution)/shard_map/ppermute | solution.py:184
  50.0 1.3 collective-permute-start.7
  51.5 3.1 %collective-permute-done.7.refs_5_ = f32[3,8,1,256]{3,2,1,0:T(1,128)S(1)} collective-permute-done((f32[3,8,1,256]{3,2,1,0:T(1,128)S(1)}, f32[3,8,1,256]{3,2,1,0:T(1,128)S(1)}, u32[]{:S(2)}, u32[]{:S(2)}) %collective-permute-start.7) | collective-permute-done | bytes 24608 | tf_op jit(solution)/shard_map/ppermute | solution.py:185
  55.8 3.9 %shard_map.105 = (f32[3,8,32,256]{3,2,1,0:T(8,128)}, bf16[3,8,32,256]{3,2,1,0:T(8,128)(2,1)}) custom-call(f32[3,8,32,256]{3,2,1,0:T(8,128)} %shard_map.104.refs_0_, f32[8,32,256]{2,1,0:T(8,128)} %refs_1_.3, f32[3,32,256]{2,1,0:T(8,128)} %copy-done.17, f32[3,32,256]{2,1,0:T(8,128)} %copy-done.18, f32[3,8,1,256]{3,2,1,0:T(1,128)} %copy-done.19, ...), custom_call_target="tpu_custom_call" | custom-call | tf_op jit(solution)/shard_map/pallas_call | solution.py:167
  59.8 1.2 convolution_convert_fusion
  61.7 2.0 %copy.42 = bf16[3,1,8,4,8,8,32]{6,3,0,5,4,2,1:T(4,128)(2,1)S(1)} copy(bf16[3,1,8,4,8,8,32]{6,5,4,3,2,0,1:T(8,128)(2,1)S(1)} %reshape.167) | data formatting | bytes 786432 | tf_op jit(solution)/shard_map/reshape | solution.py:199
  65.1 1.4 reshape.198
  66.5 1.5 %scatter_custom_fusion.1 = f32[500,128]{0,1:T(8,128)S(1)} fusion(s32[256]{0:T(256)S(1)} %bitcast.117, f32[500,256]{0,1:T(8,128)S(1)} %reshape.198, f32[]{:T(128)} %constant.13.clone.1), kind=kCustom, calls=%fused_computation.26 | custom fusion | bytes 780292 | tf_op jit(solution)/shard_map/scatter | solution.py:237
  69.8 3.7 %collective-permute-start.10 = (f32[100,32]{1,0:T(8,128)}, f32[100,32]{1,0:T(8,128)}, u32[]{:S(2)}, u32[]{:S(2)}) collective-permute-start(f32[100,32]{1,0:T(8,128)} %slice.191), channel_id=1, source_target_pairs={{0,1},{1,2},{2,3},{4,5},{5,6},{6,7},{8,9},{9,10},{10,11},{12,13},{... | collective-permute-start | bytes 38408 | tf_op jit(solution)/shard_map/ppermute | solution.py:263
  73.5 1.3 collective-permute-start.11
  76.1 1.9 %collective-permute-start.9 = (f32[100,128]{1,0:T(8,128)}, f32[100,128]{1,0:T(8,128)}, u32[]{:S(2)}, u32[]{:S(2)}) collective-permute-start(f32[100,128]{1,0:T(8,128)} %reshape_squeeze.37), channel_id=1, source_target_pairs={{4,0},{8,4},{12,8},{16,12},{20,16},{24,20},{28,24},{32,28},{36,32}... | collective-permute-start | bytes 153608 | tf_op jit(solution)/shard_map/ppermute | solution.py:262
  78.6 5.7 %collective-permute-start.8 = (f32[100,128]{1,0:T(8,128)}, f32[100,128]{1,0:T(8,128)}, u32[]{:S(2)}, u32[]{:S(2)}) collective-permute-start(f32[100,128]{1,0:T(8,128)} %reshape_squeeze.36), channel_id=1, source_target_pairs={{0,4},{4,8},{8,12},{12,16},{16,20},{20,24},{24,28},{28,32},{32,36}... | collective-permute-start | bytes 153608 | tf_op jit(solution)/shard_map/ppermute | solution.py:261
  84.3 1.7 %fusion.69 = f32[128,500]{0,1:T(8,128)} fusion(f32[500,128]{0,1:T(8,128)S(1)} %scatter_custom_fusion.1, f32[500,500]{1,0:T(8,128)S(1)} %copy-done.2), kind=kOutput, calls=%fused_computation.105 | convolution fusion | flops 384000000 | bytes 1512000 | tf_op jit(solution)/shard_map/dot_general | solution.py:272
  86.0 1.2 fusion.44
  88.3 1.5 %fusion.21 = f32[128,500]{0,1:T(8,128)S(1)} fusion(f32[500,100]{1,0:T(8,128)S(1)} %copy-done.5, f32[100,96]{1,0:T(8,128)S(1)} %bitcast.110, f32[100,32]{1,0:T(8,128)} %collective-permute-done.10), kind=kOutput, calls=%fused_computation.36 | convolution fusion | flops 76812800 | bytes 507200 | tf_op jit(solution)/shard_map/dot_general | solution.py:273
  89.8 1.4 fusion.25
  91.3 1.4 fusion.70
  92.7 1.4 fusion.10
  98.1 4.3 %collective-permute-start.14 = (f32[100,32]{1,0:T(8,128)S(1)}, f32[100,32]{1,0:T(8,128)S(1)}, u32[]{:S(2)}, u32[]{:S(2)}) collective-permute-start(f32[100,32]{1,0:T(8,128)S(1)} %slice.203), channel_id=1, source_target_pairs={{0,1},{1,2},{2,3},{4,5},{5,6},{6,7},{8,9},{9,10},{10,11},{12,13},{... | collective-permute-start | bytes 38408 | tf_op jit(solution)/shard_map/ppermute | solution.py:263
  102.4 1.3 collective-permute-start.15
  103.8 1.9 %collective-permute-start.13 = (f32[100,128]{1,0:T(8,128)S(1)}, f32[100,128]{1,0:T(8,128)S(1)}, u32[]{:S(2)}, u32[]{:S(2)}) collective-permute-start(f32[100,128]{1,0:T(8,128)S(1)} %reshape_squeeze.43), channel_id=1, source_target_pairs={{4,0},{8,4},{12,8},{16,12},{20,16},{24,20},{28,24},{32,28},{36,32}... | collective-permute-start | bytes 153608 | tf_op jit(solution)/shard_map/ppermute | solution.py:262
  107.3 3.6 %collective-permute-start.12 = (f32[100,128]{1,0:T(8,128)S(1)}, f32[100,128]{1,0:T(8,128)S(1)}, u32[]{:S(2)}, u32[]{:S(2)}) collective-permute-start(f32[100,128]{1,0:T(8,128)S(1)} %reshape_squeeze.42), channel_id=1, source_target_pairs={{0,4},{4,8},{8,12},{12,16},{16,20},{20,24},{24,28},{28,32},{32,36}... | collective-permute-start | bytes 153608 | tf_op jit(solution)/shard_map/ppermute | solution.py:261
  117.5 12.3 %all-to-all-start.1 = ((f32[500,128,2]{0,2,1:T(2,128)}), f32[500,128,2]{0,2,1:T(2,128)S(1)}, u32[]{:S(2)}, u32[]{:S(2)}) async-start(f32[500,128,2]{0,2,1:T(2,128)} %broadcast_select_fusion), calls=%async_computation.1 | async-start | bytes 1048576 | tf_op jit(solution)/shard_map/all_to_all | solution.py:279
  129.9 14.1 %all-to-all-done.1 = f32[500,128,2]{0,2,1:T(2,128)S(1)} async-done(((f32[500,128,2]{0,2,1:T(2,128)}), f32[500,128,2]{0,2,1:T(2,128)S(1)}, u32[]{:S(2)}, u32[]{:S(2)}) %all-to-all-start.1) | async-done | bytes 512032 | tf_op jit(solution)/shard_map/all_to_all | solution.py:279
  (143 shorter events, 34.5 us)
Async XLA Ops:
  0.6 63.9 %copy-start = (bf16[125,512]{1,0:T(8,128)(2,1)S(1)}, bf16[125,512]{1,0:T(8,128)(2,1)}, u32[]{:S(2)}) copy-start(bf16[125,512]{1,0:T(8,128)(2,1)} %param.11) | copy-start | bytes 384004
  0.6 8.0 %copy-start.1 = (f32[3,8,32,256]{3,2,1,0:T(8,128)S(1)}, f32[3,8,32,256]{3,2,1,0:T(8,128)}, u32[]{:S(2)}) copy-start(f32[3,8,32,256]{3,2,1,0:T(8,128)} %refs_0_.1) | copy-start | bytes 2359300
  0.7 14.2 %copy-start.25 = (s32[1,128]{1,0:T(1,128)S(1)}, s32[1,128]{1,0:T(1,128)}, u32[]{:S(2)}) copy-start(s32[1,128]{1,0:T(1,128)} %param.14) | copy-start | bytes 1540
  0.7 14.2 %copy-start.14 = (f32[4,125,128]{2,0,1:T(4,128)S(1)}, f32[4,125,128]{2,0,1:T(4,128)}, u32[]{:S(2)}) copy-start(f32[4,125,128]{2,0,1:T(4,128)} %param.12) | copy-start | bytes 768004
  1.8 32.3 %collective-permute-start.1 = (f32[4,32,256]{2,1,0:T(8,128)S(1)}, f32[4,32,256]{2,1,0:T(8,128)S(1)}, u32[]{:S(2)}, u32[]{:S(2)}) collective-permute-start(f32[4,32,256]{2,1,0:T(8,128)S(1)} %get-tuple-element.16), channel_id=1, source_target_pairs={{4,0},{8,4},{12,8},{16,12},{20,16},{24,20},{28,24},{32,28},{36,32}... | collective-permute-start | bytes 393224 | tf_op jit(solution)/shard_map/ppermute | solution.py:183
  5.1 27.7 %collective-permute-start = (f32[4,32,256]{2,1,0:T(8,128)S(1)}, f32[4,32,256]{2,1,0:T(8,128)S(1)}, u32[]{:S(2)}, u32[]{:S(2)}) collective-permute-start(f32[4,32,256]{2,1,0:T(8,128)S(1)} %get-tuple-element.17), channel_id=1, source_target_pairs={{0,4},{4,8},{8,12},{12,16},{16,20},{20,24},{24,28},{28,32},{32,36}... | collective-permute-start | bytes 393224 | tf_op jit(solution)/shard_map/ppermute | solution.py:182
  9.6 20.8 %collective-permute-start.3 = (f32[4,8,1,256]{3,2,1,0:T(1,128)S(1)}, f32[4,8,1,256]{3,2,1,0:T(1,128)S(1)}, u32[]{:S(2)}, u32[]{:S(2)}) collective-permute-start(f32[4,8,1,256]{3,2,1,0:T(1,128)S(1)} %get-tuple-element.14), channel_id=1, source_target_pairs={{1,0},{2,1},{3,2},{5,4},{6,5},{7,6},{9,8},{10,9},{11,10},{13,12},{... | collective-permute-start | bytes 98312 | tf_op jit(solution)/shard_map/ppermute | solution.py:185
  10.9 20.7 %collective-permute-start.2 = (f32[4,8,1,256]{3,2,1,0:T(1,128)S(1)}, f32[4,8,1,256]{3,2,1,0:T(1,128)S(1)}, u32[]{:S(2)}, u32[]{:S(2)}) collective-permute-start(f32[4,8,1,256]{3,2,1,0:T(1,128)S(1)} %get-tuple-element.15), channel_id=1, source_target_pairs={{0,1},{1,2},{2,3},{4,5},{5,6},{6,7},{8,9},{9,10},{10,11},{12,13},{... | collective-permute-start | bytes 98312 | tf_op jit(solution)/shard_map/ppermute | solution.py:184
  15.0 14.7 %copy-start.22 = (s32[1,128,2]{1,2,0:T(2,128)S(1)}, s32[1,128,2]{1,2,0:T(2,128)}, u32[]{:S(2)}) copy-start(s32[1,128,2]{1,2,0:T(2,128)} %param.13) | copy-start | bytes 3076
  17.4 47.6 %all-to-all-start = ((f32[500,128,2]{0,2,1:T(2,128)}), f32[500,128,2]{0,2,1:T(2,128)}, u32[]{:S(2)}, u32[]{:S(2)}) async-start(f32[500,128,2]{0,2,1:T(2,128)} %all_to_all.14), calls=%async_computation | async-start | bytes 1048576 | tf_op jit(solution)/shard_map/all_to_all | solution.py:233
  35.4 24.4 %copy-start.16 = (bf16[256,256]{1,0:T(8,128)(2,1)S(1)}, bf16[256,256]{1,0:T(8,128)(2,1)}, u32[]{:S(2)}) copy-start(bf16[256,256]{1,0:T(8,128)(2,1)} %constant.19.clone) | copy-start | bytes 393220
  41.3 13.3 %collective-permute-start.4 = (f32[3,32,256]{2,1,0:T(8,128)S(1)}, f32[3,32,256]{2,1,0:T(8,128)S(1)}, u32[]{:S(2)}, u32[]{:S(2)}) collective-permute-start(f32[3,32,256]{2,1,0:T(8,128)S(1)} %get-tuple-element.21), channel_id=1, source_target_pairs={{0,4},{4,8},{8,12},{12,16},{16,20},{20,24},{24,28},{28,32},{32,36}... | collective-permute-start | bytes 294920 | tf_op jit(solution)/shard_map/ppermute | solution.py:182
  44.9 9.6 %collective-permute-start.5 = (f32[3,32,256]{2,1,0:T(8,128)S(1)}, f32[3,32,256]{2,1,0:T(8,128)S(1)}, u32[]{:S(2)}, u32[]{:S(2)}) collective-permute-start(f32[3,32,256]{2,1,0:T(8,128)S(1)} %get-tuple-element.20), channel_id=1, source_target_pairs={{4,0},{8,4},{12,8},{16,12},{20,16},{24,20},{28,24},{32,28},{36,32}... | collective-permute-start | bytes 294920 | tf_op jit(solution)/shard_map/ppermute | solution.py:183
  46.9 4.6 %collective-permute-start.6 = (f32[3,8,1,256]{3,2,1,0:T(1,128)S(1)}, f32[3,8,1,256]{3,2,1,0:T(1,128)S(1)}, u32[]{:S(2)}, u32[]{:S(2)}) collective-permute-start(f32[3,8,1,256]{3,2,1,0:T(1,128)S(1)} %get-tuple-element.19), channel_id=1, source_target_pairs={{0,1},{1,2},{2,3},{4,5},{5,6},{6,7},{8,9},{9,10},{10,11},{12,13},{... | collective-permute-start | bytes 73736 | tf_op jit(solution)/shard_map/ppermute | solution.py:184
  50.0 4.6 %collective-permute-start.7 = (f32[3,8,1,256]{3,2,1,0:T(1,128)S(1)}, f32[3,8,1,256]{3,2,1,0:T(1,128)S(1)}, u32[]{:S(2)}, u32[]{:S(2)}) collective-permute-start(f32[3,8,1,256]{3,2,1,0:T(1,128)S(1)} %get-tuple-element.18), channel_id=1, source_target_pairs={{1,0},{2,1},{3,2},{5,4},{6,5},{7,6},{9,8},{10,9},{11,10},{13,12},{... | collective-permute-start | bytes 73736 | tf_op jit(solution)/shard_map/ppermute | solution.py:185
  68.0 16.3 %copy-start.2 = (f32[500,500]{1,0:T(8,128)S(1)}, f32[500,500]{1,0:T(8,128)}, u32[]{:S(2)}) copy-start(f32[500,500]{1,0:T(8,128)} %constant.20.clone) | copy-start | bytes 3000004
  68.2 17.8 %copy-start.7 = (f32[500,100]{1,0:T(8,128)S(1)}, f32[500,100]{1,0:T(8,128)}, u32[]{:S(2)}) copy-start(f32[500,100]{1,0:T(8,128)} %constant.61) | copy-start | bytes 600004
  69.1 19.2 %copy-start.5 = (f32[500,100]{1,0:T(8,128)S(1)}, f32[500,100]{1,0:T(8,128)}, u32[]{:S(2)}) copy-start(f32[500,100]{1,0:T(8,128)} %constant.59) | copy-start | bytes 600004
  69.8 18.5 %collective-permute-start.10 = (f32[100,32]{1,0:T(8,128)}, f32[100,32]{1,0:T(8,128)}, u32[]{:S(2)}, u32[]{:S(2)}) collective-permute-start(f32[100,32]{1,0:T(8,128)} %slice.191), channel_id=1, source_target_pairs={{0,1},{1,2},{2,3},{4,5},{5,6},{6,7},{8,9},{9,10},{10,11},{12,13},{... | collective-permute-start | bytes 38408 | tf_op jit(solution)/shard_map/ppermute | solution.py:263
  73.5 16.3 %collective-permute-start.11 = (f32[100,32]{1,0:T(8,128)S(1)}, f32[100,32]{1,0:T(8,128)}, u32[]{:S(2)}, u32[]{:S(2)}) collective-permute-start(f32[100,32]{1,0:T(8,128)S(1)} %bitcast.113), channel_id=1, source_target_pairs={{1,0},{2,1},{3,2},{5,4},{6,5},{7,6},{9,8},{10,9},{11,10},{13,12},{... | collective-permute-start | bytes 38408 | tf_op jit(solution)/shard_map/ppermute | solution.py:264
  76.1 15.2 %collective-permute-start.9 = (f32[100,128]{1,0:T(8,128)}, f32[100,128]{1,0:T(8,128)}, u32[]{:S(2)}, u32[]{:S(2)}) collective-permute-start(f32[100,128]{1,0:T(8,128)} %reshape_squeeze.37), channel_id=1, source_target_pairs={{4,0},{8,4},{12,8},{16,12},{20,16},{24,20},{28,24},{32,28},{36,32}... | collective-permute-start | bytes 153608 | tf_op jit(solution)/shard_map/ppermute | solution.py:262
  78.6 7.4 %copy-start.15 = (f32[100,128]{1,0:T(8,128)S(1)}, f32[100,128]{1,0:T(8,128)}, u32[]{:S(2)}) copy-start(f32[100,128]{1,0:T(8,128)} %reshape_squeeze.40) | copy-start | bytes 153604
  78.6 11.2 %copy-start.4 = (f32[500,100]{1,0:T(8,128)S(1)}, f32[500,100]{1,0:T(8,128)}, u32[]{:S(2)}) copy-start(f32[500,100]{1,0:T(8,128)} %constant.60) | copy-start | bytes 600004
  78.6 12.7 %copy-start.6 = (f32[500,100]{1,0:T(8,128)S(1)}, f32[500,100]{1,0:T(8,128)}, u32[]{:S(2)}) copy-start(f32[500,100]{1,0:T(8,128)} %constant.58) | copy-start | bytes 600004
  78.6 14.1 %collective-permute-start.8 = (f32[100,128]{1,0:T(8,128)}, f32[100,128]{1,0:T(8,128)}, u32[]{:S(2)}, u32[]{:S(2)}) collective-permute-start(f32[100,128]{1,0:T(8,128)} %reshape_squeeze.36), channel_id=1, source_target_pairs={{0,4},{4,8},{8,12},{12,16},{16,20},{20,24},{24,28},{28,32},{32,36}... | collective-permute-start | bytes 153608 | tf_op jit(solution)/shard_map/ppermute | solution.py:261
  94.8 11.8 %copy-start.21 = (pred[128]{0:T(512)(128)(4,1)S(1)}, pred[128]{0:T(512)(128)(4,1)}, u32[]{:S(2)}) copy-start(pred[128]{0:T(512)(128)(4,1)} %broadcast_compare_fusion) | copy-start | bytes 388
  98.1 13.8 %collective-permute-start.14 = (f32[100,32]{1,0:T(8,128)S(1)}, f32[100,32]{1,0:T(8,128)S(1)}, u32[]{:S(2)}, u32[]{:S(2)}) collective-permute-start(f32[100,32]{1,0:T(8,128)S(1)} %slice.203), channel_id=1, source_target_pairs={{0,1},{1,2},{2,3},{4,5},{5,6},{6,7},{8,9},{9,10},{10,11},{12,13},{... | collective-permute-start | bytes 38408 | tf_op jit(solution)/shard_map/ppermute | solution.py:263
  102.4 10.1 %collective-permute-start.15 = (f32[100,32]{1,0:T(8,128)S(1)}, f32[100,32]{1,0:T(8,128)S(1)}, u32[]{:S(2)}, u32[]{:S(2)}) collective-permute-start(f32[100,32]{1,0:T(8,128)S(1)} %bitcast.112), channel_id=1, source_target_pairs={{1,0},{2,1},{3,2},{5,4},{6,5},{7,6},{9,8},{10,9},{11,10},{13,12},{... | collective-permute-start | bytes 38408 | tf_op jit(solution)/shard_map/ppermute | solution.py:264
  103.8 9.4 %collective-permute-start.13 = (f32[100,128]{1,0:T(8,128)S(1)}, f32[100,128]{1,0:T(8,128)S(1)}, u32[]{:S(2)}, u32[]{:S(2)}) collective-permute-start(f32[100,128]{1,0:T(8,128)S(1)} %reshape_squeeze.43), channel_id=1, source_target_pairs={{4,0},{8,4},{12,8},{16,12},{20,16},{24,20},{28,24},{32,28},{36,32}... | collective-permute-start | bytes 153608 | tf_op jit(solution)/shard_map/ppermute | solution.py:262
  107.3 6.5 %collective-permute-start.12 = (f32[100,128]{1,0:T(8,128)S(1)}, f32[100,128]{1,0:T(8,128)S(1)}, u32[]{:S(2)}, u32[]{:S(2)}) collective-permute-start(f32[100,128]{1,0:T(8,128)S(1)} %reshape_squeeze.42), channel_id=1, source_target_pairs={{0,4},{4,8},{8,12},{12,16},{16,20},{20,24},{24,28},{28,32},{32,36}... | collective-permute-start | bytes 153608 | tf_op jit(solution)/shard_map/ppermute | solution.py:261
  116.1 13.8 %copy-start.24 = (s32[128]{0:T(128)S(1)}, s32[128]{0:T(128)}, u32[]{:S(2)}) copy-start(s32[128]{0:T(128)} %copy-done.23) | copy-start | bytes 1540
  117.5 26.5 %all-to-all-start.1 = ((f32[500,128,2]{0,2,1:T(2,128)}), f32[500,128,2]{0,2,1:T(2,128)S(1)}, u32[]{:S(2)}, u32[]{:S(2)}) async-start(f32[500,128,2]{0,2,1:T(2,128)} %broadcast_select_fusion), calls=%async_computation.1 | async-start | bytes 1048576 | tf_op jit(solution)/shard_map/all_to_all | solution.py:279
  (12 other events, 41.4 us)

commit v3 on v2

--- a/solution.py
+++ b/solution.py
@@ -90,7 +90,14 @@
                 other[(1 + k) * 125 + node, col(1 + k)] += half
             own[(1 + dim) * 125 + node, node] += half * sign
             other[(1 + dim) * 125 + node, col(0)] += -half * sign
-    return own.astype(np.float32), other.astype(np.float32)
+    own_pad = np.zeros((512, 512), np.float32)
+    other_pad = np.zeros((512, 768), np.float32)
+    for ci in range(4):
+        for cj in range(4):
+            own_pad[ci * 128:ci * 128 + 125, cj * 128:cj * 128 + 125] = own[ci * 125:(ci + 1) * 125, cj * 125:(cj + 1) * 125]
+        for slot in range(6):
+            other_pad[ci * 128:ci * 128 + 125, slot * 128:slot * 128 + 100] = other[ci * 125:(ci + 1) * 125, slot * 100:(slot + 1) * 100]
+    return own_pad, other_pad
 
 
 def face_rows(state, dim, at):
@@ -129,10 +136,10 @@
         uzm = [zm(u[c]) for c in range(3)]
         uzp = [zp(u[c]) for c in range(3)]
         nu = nu_ref[x]
-        nxm = jnp.where(x == 0, nxlo_ref[...], nu_ref[lo])
-        nxp = jnp.where(x == size_x - 1, nxhi_ref[...], nu_ref[hi])
-        nym = ym(nu, nylo_ref[x])
-        nyp = yp(nu, nyhi_ref[x])
+        nxm = jnp.where(x == 0, nxlo_ref[3], nu_ref[lo])
+        nxp = jnp.where(x == size_x - 1, nxhi_ref[3], nu_ref[hi])
+        nym = ym(nu, nylo_ref[3, x])
+        nyp = yp(nu, nyhi_ref[3, x])
         nzm = zm(nu)
         nzp = zp(nu)
         plus = (uxp, uyp, uzp)
@@ -197,9 +204,126 @@
     moved = jnp.dot(rows, jnp.asarray(perm, jnp.bfloat16), preferred_element_type=jnp.float32)
     moved = moved.astype(jnp.bfloat16)
     blocks = moved.reshape(3, bx, 8, by, 8, 8, bz).transpose(2, 4, 5, 0, 1, 3, 6).reshape(512, -1)
-    source = jnp.dot(projection, blocks, preferred_element_type=jnp.float32)
-    source = source.reshape(125, 3, -1).transpose(1, 0, 2)
-    return source.reshape(375, -1)
+    padded_proj = jnp.pad(projection, ((0, 3), (0, 0)))
+    source = jnp.dot(padded_proj, blocks, preferred_element_type=jnp.float32)
+    source = source.reshape(128, 3, -1).transpose(1, 0, 2)
+    return source.reshape(384, -1)
+
+
+FACE_ROWS = 104
+
+
+def extract_faces(state_ref, face_ref):
+    for dim in range(3):
+        for side, at in ((0, 0), (1, 4)):
+            f = 2 * dim + side
+            for comp in range(4):
+                base = comp * 128
+                if dim == 0:
+                    face_ref[f, pl.ds(comp * 25, 25), :] = state_ref[pl.ds(base + at * 25, 25), :]
+                elif dim == 1:
+                    for a in range(5):
+                        face_ref[f, pl.ds(comp * 25 + a * 5, 5), :] = state_ref[pl.ds(base + a * 25 + at * 5, 5), :]
+                else:
+                    face_ref[f, pl.ds(comp * 25, 25), :] = state_ref[pl.ds(base + at, 25, stride=5), :]
+
+
+def send_faces(face_ref, sx0_ref, sx4_ref, sy0_ref, sy4_ref, row_len):
+    sx0_ref[...] = face_ref[0]
+    sx4_ref[...] = face_ref[1]
+    sy0_ref[...] = face_ref[2][:, :row_len]
+    last = pltpu.roll(face_ref[3], row_len, 1)
+    sy4_ref[...] = last[:, :row_len]
+
+
+def dg_faces_kernel(state_ref, sx0_ref, sx4_ref, sy0_ref, sy4_ref, face_ref):
+    face_ref[...] = jnp.zeros(face_ref.shape, jnp.float32)
+    extract_faces(state_ref, face_ref)
+    send_faces(face_ref, sx0_ref, sx4_ref, sy0_ref, sy4_ref, sy0_ref.shape[1])
+
+
+def dg_step_kernel(want_faces, state_ref, src_ref, xlo_ref, xhi_ref, ylo_ref, yhi_ref, own_ref, other_ref,
+                   out_ref, *rest):
+    if want_faces:
+        sx0_ref, sx4_ref, sy0_ref, sy4_ref, face_ref, oth_ref, pad_ref = rest
+    else:
+        face_ref, oth_ref, pad_ref = rest
+    elems = state_ref.shape[1]
+    row_len = ylo_ref.shape[1]
+    lane = lax.broadcasted_iota(jnp.int32, (FACE_ROWS, elems), 1)
+    ez = lane % row_len
+    face_ref[...] = jnp.zeros(face_ref.shape, jnp.float32)
+    oth_ref[...] = jnp.zeros(oth_ref.shape, jnp.float32)
+    extract_faces(state_ref, face_ref)
+    oth_ref[pl.ds(0, FACE_ROWS), :] = xlo_ref[...]
+    oth_ref[pl.ds(128, FACE_ROWS), :] = xhi_ref[...]
+    pad_ref[:, pl.ds(0, row_len)] = ylo_ref[...]
+    oth_ref[pl.ds(256, FACE_ROWS), :] = jnp.where(
+        lane < row_len, pad_ref[...], pltpu.roll(face_ref[3], row_len, 1))
+    pad_ref[:, pl.ds(0, row_len)] = yhi_ref[...]
+    oth_ref[pl.ds(384, FACE_ROWS), :] = jnp.where(
+        lane >= elems - row_len, pltpu.roll(pad_ref[...], elems - row_len, 1),
+        pltpu.roll(face_ref[2], elems - row_len, 1))
+    oth_ref[pl.ds(512, FACE_ROWS), :] = jnp.where(ez == 0, 0.0, pltpu.roll(face_ref[5], 1, 1))
+    oth_ref[pl.ds(640, FACE_ROWS), :] = jnp.where(
+        ez == row_len - 1, 0.0, pltpu.roll(face_ref[4], elems - 1, 1))
+    state = state_ref[...]
+    rate = jnp.dot(own_ref[...], state, precision=HIGH, preferred_element_type=jnp.float32)
+    rate = rate + jnp.dot(other_ref[...], oth_ref[...], precision=HIGH, preferred_element_type=jnp.float32)
+    out_ref[pl.ds(0, 128), :] = state[:128] + TIME_STEP_ACOUSTIC * rate[:128]
+    out_ref[pl.ds(128, 384), :] = state[128:] + TIME_STEP_ACOUSTIC * (rate[128:] - src_ref[...])
+    if want_faces:
+        extract_faces(out_ref, face_ref)
+        send_faces(face_ref, sx0_ref, sx4_ref, sy0_ref, sy4_ref, row_len)
+
+
+def face_shapes(elems, row_len):
+    big = jax.ShapeDtypeStruct((FACE_ROWS, elems), jnp.float32)
+    small = jax.ShapeDtypeStruct((FACE_ROWS, row_len), jnp.float32)
+    return [big, big, small, small]
+
+
+def dg_faces(state, row_len):
+    elems = state.shape[1]
+    return pl.pallas_call(
+        dg_faces_kernel,
+        out_shape=tuple(face_shapes(elems, row_len)),
+        scratch_shapes=[pltpu.VMEM((6, FACE_ROWS, elems), jnp.float32)],
+    )(state)
+
+
+def dg_step(state, src, recv, own_mat, other_mat, want_faces):
+    elems = state.shape[1]
+    row_len = recv[2].shape[1]
+    out_shape = [jax.ShapeDtypeStruct(state.shape, jnp.float32)]
+    if want_faces:
+        out_shape += face_shapes(elems, row_len)
+    res = pl.pallas_call(
+        lambda *refs: dg_step_kernel(want_faces, *refs),
+        out_shape=tuple(out_shape),
+        scratch_shapes=[
+            pltpu.VMEM((6, FACE_ROWS, elems), jnp.float32),
+            pltpu.VMEM((768, elems), jnp.float32),
+            pltpu.VMEM((FACE_ROWS, elems), jnp.float32),
+        ],
+    )(state, src, *recv, own_mat, other_mat)
+    return res
+
+
+def exchange_faces(sent):
+    sx0, sx4, sy0, sy4 = sent
+    flow_n = lax.axis_size("flow")
+    grp_n = lax.axis_size("grp")
+    up_f = [(i, i + 1) for i in range(flow_n - 1)]
+    down_f = [(i + 1, i) for i in range(flow_n - 1)]
+    up_g = [(i, i + 1) for i in range(grp_n - 1)]
+    down_g = [(i + 1, i) for i in range(grp_n - 1)]
+    return (
+        lax.ppermute(sx4, "flow", up_f),
+        lax.ppermute(sx0, "flow", down_f),
+        lax.ppermute(sy4, "grp", up_g),
+        lax.ppermute(sy0, "grp", down_g),
+    )
 
 
 def body(velocity, eddy_visc, projection, acoustic_state, route_send, route_place):
@@ -209,9 +333,8 @@
     for turn in range(LES_SECTIONS):
         last = turn == LES_SECTIONS - 1
         if nhalo is None:
-            joint = halos(jnp.concatenate([vel, eddy_visc[None]], axis=0), 1)
-            vhalo = [part[:3] for part in joint]
-            nhalo = [part[3] for part in joint]
+            nhalo = halos(jnp.concatenate([vel, eddy_visc[None]], axis=0), 1)
+            vhalo = nhalo
         else:
             vhalo = halos(vel, 1)
         res = les_section(vel, eddy_visc, vhalo, nhalo, last)
@@ -225,59 +348,30 @@
     elem_count = acoustic_state.shape[2]
     total_slots = flow_size * grp_size * slot_cap
     placing = route_place.reshape(-1)
-    outgoing = (
-        jnp.zeros((500, total_slots), jnp.float32)
-        .at[:, placing]
-        .set(acoustic_state.reshape(500, elem_count))
-    )
+    padded_state = jnp.pad(acoustic_state, ((0, 0), (0, 3), (0, 0))).reshape(512, elem_count)
+    outgoing = jnp.zeros((512, total_slots), jnp.float32).at[:, placing].set(padded_state)
     arrived = lax.all_to_all(outgoing, ("flow", "grp"), split_axis=1, concat_axis=1, tiled=True)
     sending = route_send.reshape(-1)
     filled = sending >= 0
     target = jnp.where(filled, sending, elem_count)
-    state = jnp.zeros((500, elem_count), jnp.float32).at[:, target].set(arrived, mode="drop")
-
-    block_y = velocity.shape[2] // 8
-    block_z = velocity.shape[3] // 8
+    state = jnp.zeros((512, elem_count), jnp.float32).at[:, target].set(arrived, mode="drop")
+
+    row_len = velocity.shape[3] // 8
     own_np, other_np = dg_matrices()
     own_mat = jnp.asarray(own_np)
     other_mat = jnp.asarray(other_np)
-    src_full = jnp.concatenate([jnp.zeros((125, elem_count), jnp.float32), source], axis=0)
-    lane = lax.broadcasted_iota(jnp.int32, (1, elem_count), 1)
-    ez = lane % block_z
-    flow_n = lax.axis_size("flow")
-    grp_n = lax.axis_size("grp")
-    up_f = [(i, i + 1) for i in range(flow_n - 1)]
-    down_f = [(i + 1, i) for i in range(flow_n - 1)]
-    up_g = [(i, i + 1) for i in range(grp_n - 1)]
-    down_g = [(i + 1, i) for i in range(grp_n - 1)]
-    row_len = block_z
+    sent = dg_faces(state, row_len)
     for turn in range(AC_SECTIONS):
-        fx0 = face_rows(state, 0, 0)
-        fx4 = face_rows(state, 0, 4)
-        fy0 = face_rows(state, 1, 0)
-        fy4 = face_rows(state, 1, 4)
-        fz0 = face_rows(state, 2, 0)
-        fz4 = face_rows(state, 2, 4)
-        oxlo = lax.ppermute(fx4, "flow", up_f)
-        oxhi = lax.ppermute(fx0, "flow", down_f)
-        ylo_recv = lax.ppermute(fy4[:, elem_count - row_len:], "grp", up_g)
-        yhi_recv = lax.ppermute(fy0[:, :row_len], "grp", down_g)
-        oylo = jnp.concatenate([ylo_recv, fy4[:, : elem_count - row_len]], axis=1)
-        oyhi = jnp.concatenate([fy0[:, row_len:], yhi_recv], axis=1)
-        zero_col = jnp.zeros((100, 1), jnp.float32)
-        ozlo = jnp.where(ez == 0, 0.0, jnp.concatenate([zero_col, fz4[:, :-1]], axis=1))
-        ozhi = jnp.where(ez == block_z - 1, 0.0, jnp.concatenate([fz0[:, 1:], zero_col], axis=1))
-        others = jnp.concatenate([oxlo, oxhi, oylo, oyhi, ozlo, ozhi], axis=0)
-        rate = (
-            jnp.dot(own_mat, state, precision=HIGH)
-            + jnp.dot(other_mat, others, precision=HIGH)
-            - src_full
-        )
-        state = state + TIME_STEP_ACOUSTIC * rate
+        recv = exchange_faces(sent)
+        last = turn == AC_SECTIONS - 1
+        res = dg_step(state, source, recv, own_mat, other_mat, not last)
+        state = res[0]
+        if not last:
+            sent = res[1:]
     flat_state = state
     leaving = jnp.where(filled[None, :], flat_state[:, jnp.where(filled, sending, 0)], 0.0)
     returned = lax.all_to_all(leaving, ("flow", "grp"), split_axis=1, concat_axis=1, tiled=True)
-    acoustic_out = returned[:, placing].reshape(4, 125, elem_count)
+    acoustic_out = returned[:, placing].reshape(4, 128, elem_count)[:, :125]
     return (vel, acoustic_out)
 
 

time: 147 us -> 139 us (0.946)
  matrix products: 15.4 us -> 2.22 us
  Pallas kernels: 7.83 us -> 19.8 us
  local copies, waits for them, and re-layouts: 30.3 us -> 20.6 us
  waiting for transfers between devices: 17.3 us -> 24.3 us
  starting transfers between devices: 70.4 us -> 66.7 us
    dot_general x15 -> x1, matrix products: 14.1 us -> 0.97 us  [project(): source = jnp.dot(padded_proj, blocks, preferred_element_type=jnp.float32)]
    pallas_call x0 -> x3, Pallas kernels: none -> 11.9 us  [the longest x2 10.2 us: dg_step(): pl.pallas_call(lambda *refs: dg_step_kernel(want_faces, *refs), out_shape...]
    ppermute x8, waiting for transfers between devices: 0.02 us -> 6.92 us  [the longest x2 4.04 us: exchange_faces(): lax.ppermute(sy0, 'grp', down_g)]
    slice x16 -> x0, local copies, waits for them, and re-layouts: 6.62 us -> none  [the longest x6 3.03 us: face_rows(): face = lax.index_in_dim(cube, at, axis=1 + dim, keepdims=False)]
    another operation x12 -> x0, local copies, waits for them, and re-layouts: 4.62 us -> none  [face_rows(): return face.reshape(100, elems)]
    unnamed x55 -> x47, local copies, waits for them, and re-layouts: 2.36 us -> 4.85 us
    squeeze x4 -> x0, local copies, waits for them, and re-layouts: 2.43 us -> none  [body(): nhalo = [part[3] for part in joint]]
    ppermute x8, starting transfers between devices: 23.7 us -> 21.7 us  [the longest x2 7.37 us: exchange_faces(): lax.ppermute(sy4, 'grp', up_g)]
  transfers between devices with their start and end apart: 18 -> 18, of which waited for: 2 -> 5; matrix products, arithmetic and copies ran while one was open for 20% -> 8% of each run, Pallas kernels for 5% -> 6%
where the time goes in v3:
time: 139 us; the launch traced here: 138 us
  starting transfers between devices  66.7 us (48%)
  waiting for transfers between devices  24.3 us (17%)
  local copies, waits for them, and re-layouts  20.6 us (15%)
  Pallas kernels  19.8 us (14%)
  other arithmetic  3.16 us (2%)
  matrix products  2.22 us (2%)
    all_to_all x1, waiting for transfers between devices, body(): lax.all_to_all(leaving, ('flow', 'grp'), split_axis=1, concat_axis=1, til...  14.1 us
    all_to_all x1, starting transfers between devices, body(): lax.all_to_all(outgoing, ('flow', 'grp'), split_axis=1, concat_axis=1, ti...  12.1 us
    all_to_all x1, starting transfers between devices, body(): lax.all_to_all(leaving, ('flow', 'grp'), split_axis=1, concat_axis=1, til...  11.6 us
    pallas_call x2, Pallas kernels, dg_step(): pl.pallas_call(lambda *refs: dg_step_kernel(want_faces, *refs), out_shape...  10.2 us
    ppermute x2, starting transfers between devices, halos(): lax.ppermute(lax.index_in_dim(field, size_x - 1, lead, keepdims=False), '...  8.6 us
    pallas_call x2, Pallas kernels, les_section(): pl.pallas_call(lambda *refs: les_kernel(want_lamb, *refs), out_shape=tupl...  7.99 us
    ppermute x2, starting transfers between devices, exchange_faces(): lax.ppermute(sy4, 'grp', up_g)  7.37 us
    ppermute x2, starting transfers between devices, exchange_faces(): lax.ppermute(sx4, 'flow', up_f)  7.33 us
  transfers between devices with their start and end apart: 18, of which 5 were waited for; matrix products, arithmetic and copies ran while one was open for 8% of the time, Pallas kernels for 6%

profile of v3, /device:TPU:1, one launch (start us, length us, event | category | flops | bytes accessed | tf_op | source)
XLA Modules:
  0.0 138.0 jit_solution(17364093281297539835)
XLA Ops:
  1.8 4.9 %collective-permute-start = (f32[4,32,256]{2,1,0:T(8,128)S(1)}, f32[4,32,256]{2,1,0:T(8,128)S(1)}, u32[]{:S(2)}, u32[]{:S(2)}) collective-permute-start(f32[4,32,256]{2,1,0:T(8,128)S(1)} %get-tuple-element.27), channel_id=1, source_target_pairs={{0,4},{4,8},{8,12},{12,16},{16,20},{20,24},{24,28},{28,32},{32,36}... | collective-permute-start | bytes 393224 | tf_op jit(solution)/shard_map/ppermute | solution.py:189
  6.7 1.9 %collective-permute-start.1 = (f32[4,32,256]{2,1,0:T(8,128)S(1)}, f32[4,32,256]{2,1,0:T(8,128)S(1)}, u32[]{:S(2)}, u32[]{:S(2)}) collective-permute-start(f32[4,32,256]{2,1,0:T(8,128)S(1)} %get-tuple-element.26), channel_id=1, source_target_pairs={{4,0},{8,4},{12,8},{16,12},{20,16},{24,20},{28,24},{32,28},{36,32}... | collective-permute-start | bytes 393224 | tf_op jit(solution)/shard_map/ppermute | solution.py:190
  9.6 3.1 %collective-permute-start.2 = (f32[4,8,1,256]{3,2,1,0:T(1,128)S(1)}, f32[4,8,1,256]{3,2,1,0:T(1,128)S(1)}, u32[]{:S(2)}, u32[]{:S(2)}) collective-permute-start(f32[4,8,1,256]{3,2,1,0:T(1,128)S(1)} %get-tuple-element.25), channel_id=1, source_target_pairs={{0,1},{1,2},{2,3},{4,5},{5,6},{6,7},{8,9},{9,10},{10,11},{12,13},{... | collective-permute-start | bytes 98312 | tf_op jit(solution)/shard_map/ppermute | solution.py:191
  12.7 1.3 collective-permute-start.3
  14.2 1.1 scatter_custom_fusion
  16.5 12.1 %all-to-all-start = ((f32[512,128,2]{0,2,1:T(2,128)}), f32[512,128,2]{0,2,1:T(2,128)}, u32[]{:S(2)}, u32[]{:S(2)}) async-start(f32[512,128,2]{0,2,1:T(2,128)} %all_to_all.14), calls=%async_computation | async-start | bytes 1048576 | tf_op jit(solution)/shard_map/all_to_all | solution.py:353
  30.2 4.0 %shard_map.104.refs_0_ = f32[3,8,32,256]{3,2,1,0:T(8,128)} custom-call(f32[3,8,32,256]{3,2,1,0:T(8,128)} %refs_0_.1, f32[8,32,256]{2,1,0:T(8,128)} %refs_1_.3, f32[4,32,256]{2,1,0:T(8,128)} %copy-done.1, f32[4,32,256]{2,1,0:T(8,128)} %copy-done.2, f32[4,8,1,256]{3,2,1,0:T(1,128)} %copy-done.3, f32[4,8,1,256]{3,2,1,0:T(1,128)} %copy-done.4, ...), custom_call_target="tpu_custom_call" | custom-call | tf_op jit(solution)/shard_map/pallas_call | solution.py:174
  36.2 3.7 %collective-permute-start.4 = (f32[3,32,256]{2,1,0:T(8,128)S(1)}, f32[3,32,256]{2,1,0:T(8,128)S(1)}, u32[]{:S(2)}, u32[]{:S(2)}) collective-permute-start(f32[3,32,256]{2,1,0:T(8,128)S(1)} %get-tuple-element.31), channel_id=1, source_target_pairs={{0,4},{4,8},{8,12},{12,16},{16,20},{20,24},{24,28},{28,32},{32,36}... | collective-permute-start | bytes 294920 | tf_op jit(solution)/shard_map/ppermute | solution.py:189
  39.9 1.9 %collective-permute-start.5 = (f32[3,32,256]{2,1,0:T(8,128)S(1)}, f32[3,32,256]{2,1,0:T(8,128)S(1)}, u32[]{:S(2)}, u32[]{:S(2)}) collective-permute-start(f32[3,32,256]{2,1,0:T(8,128)S(1)} %get-tuple-element.30), channel_id=1, source_target_pairs={{4,0},{8,4},{12,8},{16,12},{20,16},{24,20},{28,24},{32,28},{36,32}... | collective-permute-start | bytes 294920 | tf_op jit(solution)/shard_map/ppermute | solution.py:190
  41.8 3.1 %collective-permute-start.6 = (f32[3,8,1,256]{3,2,1,0:T(1,128)S(1)}, f32[3,8,1,256]{3,2,1,0:T(1,128)S(1)}, u32[]{:S(2)}, u32[]{:S(2)}) collective-permute-start(f32[3,8,1,256]{3,2,1,0:T(1,128)S(1)} %get-tuple-element.29), channel_id=1, source_target_pairs={{0,1},{1,2},{2,3},{4,5},{5,6},{6,7},{8,9},{9,10},{10,11},{12,13},{... | collective-permute-start | bytes 73736 | tf_op jit(solution)/shard_map/ppermute | solution.py:191
  44.9 1.3 collective-permute-start.7
  46.3 3.2 %collective-permute-done.7.refs_5_ = f32[3,8,1,256]{3,2,1,0:T(1,128)S(1)} collective-permute-done((f32[3,8,1,256]{3,2,1,0:T(1,128)S(1)}, f32[3,8,1,256]{3,2,1,0:T(1,128)S(1)}, u32[]{:S(2)}, u32[]{:S(2)}) %collective-permute-start.7) | collective-permute-done | bytes 24608 | tf_op jit(solution)/shard_map/ppermute | solution.py:192
  50.8 4.0 %shard_map.105 = (f32[3,8,32,256]{3,2,1,0:T(8,128)}, bf16[3,8,32,256]{3,2,1,0:T(8,128)(2,1)}) custom-call(f32[3,8,32,256]{3,2,1,0:T(8,128)} %shard_map.104.refs_0_, f32[8,32,256]{2,1,0:T(8,128)} %refs_1_.3, f32[3,32,256]{2,1,0:T(8,128)} %copy-done.8, f32[3,32,256]{2,1,0:T(8,128)} %copy-done.9, f32[3,8,1,256]{3,2,1,0:T(1,128)} %copy-done.18, ...), custom_call_target="tpu_custom_call" | custom-call | tf_op jit(solution)/shard_map/pallas_call | solution.py:174
  54.8 1.2 convolution_convert_fusion
  56.7 2.0 %copy.46 = bf16[3,1,8,4,8,8,32]{6,3,0,5,4,2,1:T(4,128)(2,1)S(1)} copy(bf16[3,1,8,4,8,8,32]{6,5,4,3,2,0,1:T(8,128)(2,1)S(1)} %reshape.129) | data formatting | bytes 786432 | tf_op jit(solution)/shard_map/reshape | solution.py:206
  59.8 1.4 %reshape.158 = f32[512,256]{0,1:T(8,128)S(1)} reshape(f32[512,128,2]{0,2,1:T(2,128)} %all-to-all-done) | data formatting | bytes 1048576 | tf_op jit(solution)/shard_map/all_to_all | solution.py:353
  61.2 1.5 %scatter_custom_fusion.1 = f32[512,128]{0,1:T(8,128)S(1)} fusion(s32[256]{0:T(256)S(1)} %bitcast.70, f32[512,256]{0,1:T(8,128)S(1)} %reshape.158, f32[]{:T(128)} %constant.9.clone.1), kind=kCustom, calls=%fused_computation.6 | custom fusion | bytes 786436 | tf_op jit(solution)/shard_map/scatter | solution.py:357
  63.6 1.7 %shard_map.106 = (f32[104,128]{1,0:T(8,128)}, f32[104,128]{1,0:T(8,128)}, f32[104,32]{1,0:T(8,128)}, f32[104,32]{1,0:T(8,128)}) custom-call(f32[512,128]{1,0:T(8,128)} %copy.39.state_ref.refs_0_), custom_call_target="tpu_custom_call" | custom-call | tf_op jit(solution)/shard_map/pallas_call | solution.py:288
  65.3 3.1 %collective-permute-start.10 = (f32[104,32]{1,0:T(8,128)}, f32[104,32]{1,0:T(8,128)S(1)}, u32[]{:S(2)}, u32[]{:S(2)}) collective-permute-start(f32[104,32]{1,0:T(8,128)} %get-tuple-element.17), channel_id=1, source_target_pairs={{0,1},{1,2},{2,3},{4,5},{5,6},{6,7},{8,9},{9,10},{10,11},{12,13},{... | collective-permute-start | bytes 39944 | tf_op jit(solution)/shard_map/ppermute | solution.py:324
  68.4 1.3 collective-permute-start.11
  69.7 5.4 %collective-permute-start.8 = (f32[104,128]{1,0:T(8,128)}, f32[104,128]{1,0:T(8,128)S(1)}, u32[]{:S(2)}, u32[]{:S(2)}) collective-permute-start(f32[104,128]{1,0:T(8,128)} %get-tuple-element.15), channel_id=1, source_target_pairs={{0,4},{4,8},{8,12},{12,16},{16,20},{20,24},{24,28},{28,32},{32,36}... | collective-permute-start | bytes 159752 | tf_op jit(solution)/shard_map/ppermute | solution.py:322
  75.1 1.9 %collective-permute-start.9 = (f32[104,128]{1,0:T(8,128)}, f32[104,128]{1,0:T(8,128)S(1)}, u32[]{:S(2)}, u32[]{:S(2)}) collective-permute-start(f32[104,128]{1,0:T(8,128)} %get-tuple-element.16), channel_id=1, source_target_pairs={{4,0},{8,4},{12,8},{16,12},{20,16},{24,20},{28,24},{32,28},{36,32}... | collective-permute-start | bytes 159752 | tf_op jit(solution)/shard_map/ppermute | solution.py:323
  78.0 2.7 %collective-permute-done.9.refs_3_ = f32[104,128]{1,0:T(8,128)S(1)} collective-permute-done((f32[104,128]{1,0:T(8,128)}, f32[104,128]{1,0:T(8,128)S(1)}, u32[]{:S(2)}, u32[]{:S(2)}) %collective-permute-start.9) | collective-permute-done | bytes 53280 | tf_op jit(solution)/shard_map/ppermute | solution.py:323
  81.4 5.2 %shard_map.107 = (f32[512,128]{1,0:T(8,128)}, f32[104,128]{1,0:T(8,128)}, f32[104,128]{1,0:T(8,128)}, f32[104,32]{1,0:T(8,128)}, f32[104,32]{1,0:T(8,128)}) custom-call(f32[512,128]{1,0:T(8,128)} %copy.39.state_ref.refs_0_, f32[384,128]{1,0:T(8,128)} %bitcast.61, f32[104,128]{1,0:T(8,128)} %copy-done.16, f32[104,128]{1,0:T(8,128)} %copy-done.17, ...), custom_call_target="tpu_custom_call" | custom-call | tf_op jit(solution)/shard_map/pallas_call | solution.py:301
  86.5 2.0 %collective-permute-start.12 = (f32[104,128]{1,0:T(8,128)}, f32[104,128]{1,0:T(8,128)S(1)}, u32[]{:S(2)}, u32[]{:S(2)}) collective-permute-start(f32[104,128]{1,0:T(8,128)} %get-tuple-element.20), channel_id=1, source_target_pairs={{0,4},{4,8},{8,12},{12,16},{16,20},{20,24},{24,28},{28,32},{32,36}... | collective-permute-start | bytes 159752 | tf_op jit(solution)/shard_map/ppermute | solution.py:322
  88.5 2.3 %collective-permute-start.13 = (f32[104,128]{1,0:T(8,128)}, f32[104,128]{1,0:T(8,128)S(1)}, u32[]{:S(2)}, u32[]{:S(2)}) collective-permute-start(f32[104,128]{1,0:T(8,128)} %get-tuple-element.21), channel_id=1, source_target_pairs={{4,0},{8,4},{12,8},{16,12},{20,16},{24,20},{28,24},{32,28},{36,32}... | collective-permute-start | bytes 159752 | tf_op jit(solution)/shard_map/ppermute | solution.py:323
  90.8 4.3 %collective-permute-start.14 = (f32[104,32]{1,0:T(8,128)}, f32[104,32]{1,0:T(8,128)S(1)}, u32[]{:S(2)}, u32[]{:S(2)}) collective-permute-start(f32[104,32]{1,0:T(8,128)} %get-tuple-element.22), channel_id=1, source_target_pairs={{0,1},{1,2},{2,3},{4,5},{5,6},{6,7},{8,9},{9,10},{10,11},{12,13},{... | collective-permute-start | bytes 39944 | tf_op jit(solution)/shard_map/ppermute | solution.py:324
  95.1 1.5 %collective-permute-start.15 = (f32[104,32]{1,0:T(8,128)}, f32[104,32]{1,0:T(8,128)S(1)}, u32[]{:S(2)}, u32[]{:S(2)}) collective-permute-start(f32[104,32]{1,0:T(8,128)} %get-tuple-element.23), channel_id=1, source_target_pairs={{1,0},{2,1},{3,2},{5,4},{6,5},{7,6},{9,8},{10,9},{11,10},{13,12},{... | collective-permute-start | bytes 39944 | tf_op jit(solution)/shard_map/ppermute | solution.py:325
  96.9 4.0 %collective-permute-done.15.refs_5_ = f32[104,32]{1,0:T(8,128)S(1)} collective-permute-done((f32[104,32]{1,0:T(8,128)}, f32[104,32]{1,0:T(8,128)S(1)}, u32[]{:S(2)}, u32[]{:S(2)}) %collective-permute-start.15) | collective-permute-done | bytes 13344 | tf_op jit(solution)/shard_map/ppermute | solution.py:325
  101.6 5.0 %shard_map.108 = f32[512,128]{1,0:T(8,128)} custom-call(f32[512,128]{1,0:T(8,128)} %get-tuple-element.19.refs_0_, f32[384,128]{1,0:T(8,128)} %bitcast.62, f32[104,128]{1,0:T(8,128)} %copy-done.10, f32[104,128]{1,0:T(8,128)} %copy-done.11, f32[104,32]{1,0:T(8,128)} %copy-done.12, f32[104,32]{1,0:T(8,128)} %copy-done.13, f32[512,512]{1,0:T(8,128)} %constant.7.clone.refs_6_, ...), custom_call_target="tpu_custom_call" | custom-call | tf_op jit(solution)/shard_map/pallas_call | solution.py:301
  110.1 11.6 %all-to-all-start.1 = ((f32[512,128,2]{0,2,1:T(2,128)}), f32[512,128,2]{0,2,1:T(2,128)S(1)}, u32[]{:S(2)}, u32[]{:S(2)}) async-start(f32[512,128,2]{0,2,1:T(2,128)} %broadcast_select_fusion), calls=%async_computation.1 | async-start | bytes 1048576 | tf_op jit(solution)/shard_map/all_to_all | solution.py:373
  121.8 14.1 %all-to-all-done.1 = f32[512,128,2]{0,2,1:T(2,128)S(1)} async-done(((f32[512,128,2]{0,2,1:T(2,128)}), f32[512,128,2]{0,2,1:T(2,128)S(1)}, u32[]{:S(2)}, u32[]{:S(2)}) %all-to-all-start.1) | async-done | bytes 524320 | tf_op jit(solution)/shard_map/all_to_all | solution.py:373
  (87 shorter events, 18.8 us)
Async XLA Ops:
  0.6 8.0 %copy-start = (f32[3,8,32,256]{3,2,1,0:T(8,128)S(1)}, f32[3,8,32,256]{3,2,1,0:T(8,128)}, u32[]{:S(2)}) copy-start(f32[3,8,32,256]{3,2,1,0:T(8,128)} %refs_0_.1) | copy-start | bytes 2359300
  0.6 13.3 %copy-start.21 = (s32[1,128]{1,0:T(1,128)S(1)}, s32[1,128]{1,0:T(1,128)}, u32[]{:S(2)}) copy-start(s32[1,128]{1,0:T(1,128)} %param.14) | copy-start | bytes 1540
  0.7 13.4 %copy-start.5 = (f32[4,125,128]{2,0,1:T(4,128)S(1)}, f32[4,125,128]{2,0,1:T(4,128)}, u32[]{:S(2)}) copy-start(f32[4,125,128]{2,0,1:T(4,128)} %param.12) | copy-start | bytes 768004
  1.8 27.1 %collective-permute-start = (f32[4,32,256]{2,1,0:T(8,128)S(1)}, f32[4,32,256]{2,1,0:T(8,128)S(1)}, u32[]{:S(2)}, u32[]{:S(2)}) collective-permute-start(f32[4,32,256]{2,1,0:T(8,128)S(1)} %get-tuple-element.27), channel_id=1, source_target_pairs={{0,4},{4,8},{8,12},{12,16},{16,20},{20,24},{24,28},{28,32},{32,36}... | collective-permute-start | bytes 393224 | tf_op jit(solution)/shard_map/ppermute | solution.py:189
  6.7 22.2 %collective-permute-start.1 = (f32[4,32,256]{2,1,0:T(8,128)S(1)}, f32[4,32,256]{2,1,0:T(8,128)S(1)}, u32[]{:S(2)}, u32[]{:S(2)}) collective-permute-start(f32[4,32,256]{2,1,0:T(8,128)S(1)} %get-tuple-element.26), channel_id=1, source_target_pairs={{4,0},{8,4},{12,8},{16,12},{20,16},{24,20},{28,24},{32,28},{36,32}... | collective-permute-start | bytes 393224 | tf_op jit(solution)/shard_map/ppermute | solution.py:190
  9.6 19.3 %collective-permute-start.2 = (f32[4,8,1,256]{3,2,1,0:T(1,128)S(1)}, f32[4,8,1,256]{3,2,1,0:T(1,128)S(1)}, u32[]{:S(2)}, u32[]{:S(2)}) collective-permute-start(f32[4,8,1,256]{3,2,1,0:T(1,128)S(1)} %get-tuple-element.25), channel_id=1, source_target_pairs={{0,1},{1,2},{2,3},{4,5},{5,6},{6,7},{8,9},{9,10},{10,11},{12,13},{... | collective-permute-start | bytes 98312 | tf_op jit(solution)/shard_map/ppermute | solution.py:191
  12.7 16.2 %collective-permute-start.3 = (f32[4,8,1,256]{3,2,1,0:T(1,128)S(1)}, f32[4,8,1,256]{3,2,1,0:T(1,128)S(1)}, u32[]{:S(2)}, u32[]{:S(2)}) collective-permute-start(f32[4,8,1,256]{3,2,1,0:T(1,128)S(1)} %get-tuple-element.24), channel_id=1, source_target_pairs={{1,0},{2,1},{3,2},{5,4},{6,5},{7,6},{9,8},{10,9},{11,10},{13,12},{... | collective-permute-start | bytes 98312 | tf_op jit(solution)/shard_map/ppermute | solution.py:192
  14.1 14.5 %copy-start.20 = (s32[1,128,2]{1,2,0:T(2,128)S(1)}, s32[1,128,2]{1,2,0:T(2,128)}, u32[]{:S(2)}) copy-start(s32[1,128,2]{1,2,0:T(2,128)} %param.13) | copy-start | bytes 3076
  16.5 43.4 %all-to-all-start = ((f32[512,128,2]{0,2,1:T(2,128)}), f32[512,128,2]{0,2,1:T(2,128)}, u32[]{:S(2)}, u32[]{:S(2)}) async-start(f32[512,128,2]{0,2,1:T(2,128)} %all_to_all.14), calls=%async_computation | async-start | bytes 1048576 | tf_op jit(solution)/shard_map/all_to_all | solution.py:353
  28.9 0.7 copy-start.1
  29.6 0.7 copy-start.2
  34.2 20.7 %copy-start.6 = (bf16[256,256]{1,0:T(8,128)(2,1)S(1)}, bf16[256,256]{1,0:T(8,128)(2,1)}, u32[]{:S(2)}) copy-start(bf16[256,256]{1,0:T(8,128)(2,1)} %constant.6.clone) | copy-start | bytes 393220
  36.2 13.3 %collective-permute-start.4 = (f32[3,32,256]{2,1,0:T(8,128)S(1)}, f32[3,32,256]{2,1,0:T(8,128)S(1)}, u32[]{:S(2)}, u32[]{:S(2)}) collective-permute-start(f32[3,32,256]{2,1,0:T(8,128)S(1)} %get-tuple-element.31), channel_id=1, source_target_pairs={{0,4},{4,8},{8,12},{12,16},{16,20},{20,24},{24,28},{28,32},{32,36}... | collective-permute-start | bytes 294920 | tf_op jit(solution)/shard_map/ppermute | solution.py:189
  39.9 9.6 %collective-permute-start.5 = (f32[3,32,256]{2,1,0:T(8,128)S(1)}, f32[3,32,256]{2,1,0:T(8,128)S(1)}, u32[]{:S(2)}, u32[]{:S(2)}) collective-permute-start(f32[3,32,256]{2,1,0:T(8,128)S(1)} %get-tuple-element.30), channel_id=1, source_target_pairs={{4,0},{8,4},{12,8},{16,12},{20,16},{24,20},{28,24},{32,28},{36,32}... | collective-permute-start | bytes 294920 | tf_op jit(solution)/shard_map/ppermute | solution.py:190
  41.8 4.4 %collective-permute-start.6 = (f32[3,8,1,256]{3,2,1,0:T(1,128)S(1)}, f32[3,8,1,256]{3,2,1,0:T(1,128)S(1)}, u32[]{:S(2)}, u32[]{:S(2)}) collective-permute-start(f32[3,8,1,256]{3,2,1,0:T(1,128)S(1)} %get-tuple-element.29), channel_id=1, source_target_pairs={{0,1},{1,2},{2,3},{4,5},{5,6},{6,7},{8,9},{9,10},{10,11},{12,13},{... | collective-permute-start | bytes 73736 | tf_op jit(solution)/shard_map/ppermute | solution.py:191
  44.9 4.6 %collective-permute-start.7 = (f32[3,8,1,256]{3,2,1,0:T(1,128)S(1)}, f32[3,8,1,256]{3,2,1,0:T(1,128)S(1)}, u32[]{:S(2)}, u32[]{:S(2)}) collective-permute-start(f32[3,8,1,256]{3,2,1,0:T(1,128)S(1)} %get-tuple-element.28), channel_id=1, source_target_pairs={{1,0},{2,1},{3,2},{5,4},{6,5},{7,6},{9,8},{10,9},{11,10},{13,12},{... | collective-permute-start | bytes 73736 | tf_op jit(solution)/shard_map/ppermute | solution.py:192
  46.3 3.3 %copy-start.18 = (f32[3,8,1,256]{3,2,1,0:T(1,128)}, f32[3,8,1,256]{3,2,1,0:T(1,128)S(1)}, u32[]{:S(2)}) copy-start(f32[3,8,1,256]{3,2,1,0:T(1,128)S(1)} %collective-permute-done.6.refs_4_) | copy-start | bytes 73732
  59.6 17.4 %copy-start.7 = (bf16[125,512]{1,0:T(8,128)(2,1)S(1)}, bf16[125,512]{1,0:T(8,128)(2,1)}, u32[]{:S(2)}) copy-start(bf16[125,512]{1,0:T(8,128)(2,1)} %param.11) | copy-start | bytes 384004
  65.3 12.7 %collective-permute-start.10 = (f32[104,32]{1,0:T(8,128)}, f32[104,32]{1,0:T(8,128)S(1)}, u32[]{:S(2)}, u32[]{:S(2)}) collective-permute-start(f32[104,32]{1,0:T(8,128)} %get-tuple-element.17), channel_id=1, source_target_pairs={{0,1},{1,2},{2,3},{4,5},{5,6},{6,7},{8,9},{9,10},{10,11},{12,13},{... | collective-permute-start | bytes 39944 | tf_op jit(solution)/shard_map/ppermute | solution.py:324
  68.4 9.6 %collective-permute-start.11 = (f32[104,32]{1,0:T(8,128)}, f32[104,32]{1,0:T(8,128)S(1)}, u32[]{:S(2)}, u32[]{:S(2)}) collective-permute-start(f32[104,32]{1,0:T(8,128)} %get-tuple-element.18), channel_id=1, source_target_pairs={{1,0},{2,1},{3,2},{5,4},{6,5},{7,6},{9,8},{10,9},{11,10},{13,12},{... | collective-permute-start | bytes 39944 | tf_op jit(solution)/shard_map/ppermute | solution.py:325
  69.7 8.3 %collective-permute-start.8 = (f32[104,128]{1,0:T(8,128)}, f32[104,128]{1,0:T(8,128)S(1)}, u32[]{:S(2)}, u32[]{:S(2)}) collective-permute-start(f32[104,128]{1,0:T(8,128)} %get-tuple-element.15), channel_id=1, source_target_pairs={{0,4},{4,8},{8,12},{12,16},{16,20},{20,24},{24,28},{28,32},{32,36}... | collective-permute-start | bytes 159752 | tf_op jit(solution)/shard_map/ppermute | solution.py:322
  75.1 5.7 %collective-permute-start.9 = (f32[104,128]{1,0:T(8,128)}, f32[104,128]{1,0:T(8,128)S(1)}, u32[]{:S(2)}, u32[]{:S(2)}) collective-permute-start(f32[104,128]{1,0:T(8,128)} %get-tuple-element.16), channel_id=1, source_target_pairs={{4,0},{8,4},{12,8},{16,12},{20,16},{24,20},{28,24},{32,28},{36,32}... | collective-permute-start | bytes 159752 | tf_op jit(solution)/shard_map/ppermute | solution.py:323
  78.0 2.8 %copy-start.14 = (f32[104,32]{1,0:T(8,128)}, f32[104,32]{1,0:T(8,128)S(1)}, u32[]{:S(2)}) copy-start(f32[104,32]{1,0:T(8,128)S(1)} %collective-permute-done.10.refs_4_) | copy-start | bytes 39940
  78.0 2.7 %copy-start.15 = (f32[104,32]{1,0:T(8,128)}, f32[104,32]{1,0:T(8,128)S(1)}, u32[]{:S(2)}) copy-start(f32[104,32]{1,0:T(8,128)S(1)} %collective-permute-done.11.refs_5_) | copy-start | bytes 39940
  78.0 2.7 %copy-start.16 = (f32[104,128]{1,0:T(8,128)}, f32[104,128]{1,0:T(8,128)S(1)}, u32[]{:S(2)}) copy-start(f32[104,128]{1,0:T(8,128)S(1)} %collective-permute-done.8.refs_2_) | copy-start | bytes 159748
  86.5 14.4 %collective-permute-start.12 = (f32[104,128]{1,0:T(8,128)}, f32[104,128]{1,0:T(8,128)S(1)}, u32[]{:S(2)}, u32[]{:S(2)}) collective-permute-start(f32[104,128]{1,0:T(8,128)} %get-tuple-element.20), channel_id=1, source_target_pairs={{0,4},{4,8},{8,12},{12,16},{16,20},{20,24},{24,28},{28,32},{32,36}... | collective-permute-start | bytes 159752 | tf_op jit(solution)/shard_map/ppermute | solution.py:322
  88.5 12.5 %collective-permute-start.13 = (f32[104,128]{1,0:T(8,128)}, f32[104,128]{1,0:T(8,128)S(1)}, u32[]{:S(2)}, u32[]{:S(2)}) collective-permute-start(f32[104,128]{1,0:T(8,128)} %get-tuple-element.21), channel_id=1, source_target_pairs={{4,0},{8,4},{12,8},{16,12},{20,16},{24,20},{28,24},{32,28},{36,32}... | collective-permute-start | bytes 159752 | tf_op jit(solution)/shard_map/ppermute | solution.py:323
  90.8 6.1 %collective-permute-start.14 = (f32[104,32]{1,0:T(8,128)}, f32[104,32]{1,0:T(8,128)S(1)}, u32[]{:S(2)}, u32[]{:S(2)}) collective-permute-start(f32[104,32]{1,0:T(8,128)} %get-tuple-element.22), channel_id=1, source_target_pairs={{0,1},{1,2},{2,3},{4,5},{5,6},{6,7},{8,9},{9,10},{10,11},{12,13},{... | collective-permute-start | bytes 39944 | tf_op jit(solution)/shard_map/ppermute | solution.py:324
  95.1 5.8 %collective-permute-start.15 = (f32[104,32]{1,0:T(8,128)}, f32[104,32]{1,0:T(8,128)S(1)}, u32[]{:S(2)}, u32[]{:S(2)}) collective-permute-start(f32[104,32]{1,0:T(8,128)} %get-tuple-element.23), channel_id=1, source_target_pairs={{1,0},{2,1},{3,2},{5,4},{6,5},{7,6},{9,8},{10,9},{11,10},{13,12},{... | collective-permute-start | bytes 39944 | tf_op jit(solution)/shard_map/ppermute | solution.py:325
  96.9 4.1 %copy-start.12 = (f32[104,32]{1,0:T(8,128)}, f32[104,32]{1,0:T(8,128)S(1)}, u32[]{:S(2)}) copy-start(f32[104,32]{1,0:T(8,128)S(1)} %collective-permute-done.14.refs_4_) | copy-start | bytes 39940
  101.0 0.7 copy-start.11
  110.1 25.8 %all-to-all-start.1 = ((f32[512,128,2]{0,2,1:T(2,128)}), f32[512,128,2]{0,2,1:T(2,128)S(1)}, u32[]{:S(2)}, u32[]{:S(2)}) async-start(f32[512,128,2]{0,2,1:T(2,128)} %broadcast_select_fusion), calls=%async_computation.1 | async-start | bytes 1048576 | tf_op jit(solution)/shard_map/all_to_all | solution.py:373
  (8 other events, 5.0 us)

commit v4 on v3

--- a/solution.py
+++ b/solution.py
@@ -107,11 +107,48 @@
     return face.reshape(100, elems)
 
 
-def les_kernel(want_lamb, vel_ref, nu_ref, vxlo_ref, vxhi_ref, vylo_ref, vyhi_ref,
-               nxlo_ref, nxhi_ref, nylo_ref, nyhi_ref, out_ref, *rest):
+def les_kernel(mode, vel_ref, nu_ref, vxlo_ref, vxhi_ref, vylo_ref, vyhi_ref,
+               nxlo_ref, nxhi_ref, nylo_ref, nyhi_ref, *rest):
     size_x, size_y, size_z = vel_ref.shape[1], vel_ref.shape[2], vel_ref.shape[3]
+    half = size_z // 2
     row = lax.broadcasted_iota(jnp.int32, (size_y, size_z), 0)
     lane = lax.broadcasted_iota(jnp.int32, (size_y, size_z), 1)
+    if mode == 0:
+        sx0_ref, sx4_ref, sy0_ref, sy4_ref, out_ref, mxup_ref, mxdn_ref, myup_ref, mydn_ref = rest
+
+        def xlo(c):
+            return vxlo_ref[c]
+
+        def xhi(c):
+            return vxhi_ref[c]
+
+        def ylo(c, x):
+            return vylo_ref[c, x]
+
+        def yhi(c, x):
+            return vyhi_ref[c, x]
+    else:
+        out_ref, lamb_ref = rest
+
+        def plane(ref, c):
+            return jnp.concatenate(
+                [ref[pl.ds(c * 2 * size_y, size_y), :], ref[pl.ds(c * 2 * size_y + size_y, size_y), :]], axis=1)
+
+        def line(ref, c, x):
+            return jnp.concatenate(
+                [ref[pl.ds(c * 2 * size_x + x, 1), :], ref[pl.ds(c * 2 * size_x + size_x + x, 1), :]], axis=1)
+
+        def xlo(c):
+            return plane(vxlo_ref, c)
+
+        def xhi(c):
+            return plane(vxhi_ref, c)
+
+        def ylo(c, x):
+            return line(vylo_ref, c, x)
+
+        def yhi(c, x):
+            return line(vyhi_ref, c, x)
 
     def yp(f, halo):
         return jnp.where(row == size_y - 1, halo, pltpu.roll(f, size_y - 1, 0))
@@ -129,10 +166,10 @@
         lo = jnp.maximum(x - 1, 0)
         hi = jnp.minimum(x + 1, size_x - 1)
         u = [vel_ref[c, x] for c in range(3)]
-        uxm = [jnp.where(x == 0, vxlo_ref[c], vel_ref[c, lo]) for c in range(3)]
-        uxp = [jnp.where(x == size_x - 1, vxhi_ref[c], vel_ref[c, hi]) for c in range(3)]
-        uym = [ym(u[c], vylo_ref[c, x]) for c in range(3)]
-        uyp = [yp(u[c], vyhi_ref[c, x]) for c in range(3)]
+        uxm = [jnp.where(x == 0, xlo(c), vel_ref[c, lo]) for c in range(3)]
+        uxp = [jnp.where(x == size_x - 1, xhi(c), vel_ref[c, hi]) for c in range(3)]
+        uym = [ym(u[c], ylo(c, x)) for c in range(3)]
+        uyp = [yp(u[c], yhi(c, x)) for c in range(3)]
         uzm = [zm(u[c]) for c in range(3)]
         uzp = [zp(u[c]) for c in range(3)]
         nu = nu_ref[x]
@@ -160,22 +197,46 @@
                 term = ups[axis] * (plus[axis][c] - u[c]) - downs[axis] * (u[c] - minus[axis][c])
                 total = term if total is None else total + term
             out_ref[c, x] = u[c] + TIME_STEP_LES * (total - lamb[c])
-            if want_lamb:
-                rest[0][c, x] = lamb[c].astype(rest[0].dtype)
+            if mode == 1:
+                lamb_ref[c, x] = lamb[c].astype(lamb_ref.dtype)
         return carry
 
     lax.fori_loop(0, size_x, step, 0)
-
-
-def les_section(vel, nu, vhalo, nhalo, want_lamb):
-    out_shape = [jax.ShapeDtypeStruct(vel.shape, jnp.float32)]
-    if want_lamb:
-        out_shape.append(jax.ShapeDtypeStruct(vel.shape, jnp.bfloat16))
-    res = pl.pallas_call(
-        lambda *refs: les_kernel(want_lamb, *refs),
-        out_shape=tuple(out_shape),
-    )(vel, nu, *vhalo, *nhalo)
-    return res
+    if mode == 0:
+        for c in range(3):
+            for h in range(2):
+                mxup_ref[pl.ds(c * 2 * size_y + h * size_y, size_y), :] = out_ref[c, size_x - 1, :, pl.ds(h * half, half)]
+                mxdn_ref[pl.ds(c * 2 * size_y + h * size_y, size_y), :] = out_ref[c, 0, :, pl.ds(h * half, half)]
+                for x in range(size_x):
+                    at = c * 2 * size_x + h * size_x + x
+                    myup_ref[pl.ds(at, 1), :] = out_ref[c, x, pl.ds(size_y - 1, 1), pl.ds(h * half, half)]
+                    mydn_ref[pl.ds(at, 1), :] = out_ref[c, x, pl.ds(0, 1), pl.ds(h * half, half)]
+        xrows = 3 * 2 * size_y
+        yrows = 3 * 2 * size_x
+        mxup_ref[pl.ds(xrows, FACE_ROWS), :] = sx4_ref[...]
+        mxdn_ref[pl.ds(xrows, FACE_ROWS), :] = sx0_ref[...]
+        zeros = jnp.zeros((FACE_ROWS, half), jnp.float32)
+        myup_ref[pl.ds(yrows, FACE_ROWS), :] = zeros
+        mydn_ref[pl.ds(yrows, FACE_ROWS), :] = zeros
+        myup_ref[pl.ds(yrows, FACE_ROWS), pl.ds(0, sy4_ref.shape[1])] = sy4_ref[...]
+        mydn_ref[pl.ds(yrows, FACE_ROWS), pl.ds(0, sy0_ref.shape[1])] = sy0_ref[...]
+
+
+def les_section_first(vel, nu, joint, faces):
+    size_x, size_y, size_z = vel.shape[1], vel.shape[2], vel.shape[3]
+    xbuf = jax.ShapeDtypeStruct((3 * 2 * size_y + FACE_ROWS, size_z // 2), jnp.float32)
+    ybuf = jax.ShapeDtypeStruct((3 * 2 * size_x + FACE_ROWS, size_z // 2), jnp.float32)
+    return pl.pallas_call(
+        lambda *refs: les_kernel(0, *refs),
+        out_shape=(jax.ShapeDtypeStruct(vel.shape, jnp.float32), xbuf, xbuf, ybuf, ybuf),
+    )(vel, nu, *joint, *joint, *faces)
+
+
+def les_section_last(vel, nu, merged, joint):
+    return pl.pallas_call(
+        lambda *refs: les_kernel(1, *refs),
+        out_shape=(jax.ShapeDtypeStruct(vel.shape, jnp.float32), jax.ShapeDtypeStruct(vel.shape, jnp.bfloat16)),
+    )(vel, nu, *merged, *joint)
 
 
 def halos(field, lead):
@@ -242,25 +303,24 @@
     send_faces(face_ref, sx0_ref, sx4_ref, sy0_ref, sy4_ref, sy0_ref.shape[1])
 
 
-def dg_step_kernel(want_faces, state_ref, src_ref, xlo_ref, xhi_ref, ylo_ref, yhi_ref, own_ref, other_ref,
+def dg_step_kernel(want_faces, xoff, yoff, row_len, state_ref, src_ref, xlo_ref, xhi_ref, ylo_ref, yhi_ref, own_ref, other_ref,
                    out_ref, *rest):
     if want_faces:
         sx0_ref, sx4_ref, sy0_ref, sy4_ref, face_ref, oth_ref, pad_ref = rest
     else:
         face_ref, oth_ref, pad_ref = rest
     elems = state_ref.shape[1]
-    row_len = ylo_ref.shape[1]
     lane = lax.broadcasted_iota(jnp.int32, (FACE_ROWS, elems), 1)
     ez = lane % row_len
     face_ref[...] = jnp.zeros(face_ref.shape, jnp.float32)
     oth_ref[...] = jnp.zeros(oth_ref.shape, jnp.float32)
     extract_faces(state_ref, face_ref)
-    oth_ref[pl.ds(0, FACE_ROWS), :] = xlo_ref[...]
-    oth_ref[pl.ds(128, FACE_ROWS), :] = xhi_ref[...]
-    pad_ref[:, pl.ds(0, row_len)] = ylo_ref[...]
+    oth_ref[pl.ds(0, FACE_ROWS), :] = xlo_ref[pl.ds(xoff, FACE_ROWS), :]
+    oth_ref[pl.ds(128, FACE_ROWS), :] = xhi_ref[pl.ds(xoff, FACE_ROWS), :]
+    pad_ref[:, pl.ds(0, row_len)] = ylo_ref[pl.ds(yoff, FACE_ROWS), pl.ds(0, row_len)]
     oth_ref[pl.ds(256, FACE_ROWS), :] = jnp.where(
         lane < row_len, pad_ref[...], pltpu.roll(face_ref[3], row_len, 1))
-    pad_ref[:, pl.ds(0, row_len)] = yhi_ref[...]
+    pad_ref[:, pl.ds(0, row_len)] = yhi_ref[pl.ds(yoff, FACE_ROWS), pl.ds(0, row_len)]
     oth_ref[pl.ds(384, FACE_ROWS), :] = jnp.where(
         lane >= elems - row_len, pltpu.roll(pad_ref[...], elems - row_len, 1),
         pltpu.roll(face_ref[2], elems - row_len, 1))
@@ -292,14 +352,13 @@
     )(state)
 
 
-def dg_step(state, src, recv, own_mat, other_mat, want_faces):
+def dg_step(state, src, recv, own_mat, other_mat, want_faces, row_len, xoff=0, yoff=0):
     elems = state.shape[1]
-    row_len = recv[2].shape[1]
     out_shape = [jax.ShapeDtypeStruct(state.shape, jnp.float32)]
     if want_faces:
         out_shape += face_shapes(elems, row_len)
     res = pl.pallas_call(
-        lambda *refs: dg_step_kernel(want_faces, *refs),
+        lambda *refs: dg_step_kernel(want_faces, xoff, yoff, row_len, *refs),
         out_shape=tuple(out_shape),
         scratch_shapes=[
             pltpu.VMEM((6, FACE_ROWS, elems), jnp.float32),
@@ -327,21 +386,7 @@
 
 
 def body(velocity, eddy_visc, projection, acoustic_state, route_send, route_place):
-    vel = velocity
-    lamb = None
-    nhalo = None
-    for turn in range(LES_SECTIONS):
-        last = turn == LES_SECTIONS - 1
-        if nhalo is None:
-            nhalo = halos(jnp.concatenate([vel, eddy_visc[None]], axis=0), 1)
-            vhalo = nhalo
-        else:
-            vhalo = halos(vel, 1)
-        res = les_section(vel, eddy_visc, vhalo, nhalo, last)
-        vel = res[0]
-        if last:
-            lamb = res[1]
-    source = project(lamb, projection)
+    joint = halos(jnp.concatenate([velocity, eddy_visc[None]], axis=0), 1)
     flow_size = lax.axis_size("flow")
     grp_size = lax.axis_size("grp")
     slot_cap = route_send.shape[2]
@@ -361,13 +406,16 @@
     own_mat = jnp.asarray(own_np)
     other_mat = jnp.asarray(other_np)
     sent = dg_faces(state, row_len)
-    for turn in range(AC_SECTIONS):
-        recv = exchange_faces(sent)
-        last = turn == AC_SECTIONS - 1
-        res = dg_step(state, source, recv, own_mat, other_mat, not last)
-        state = res[0]
-        if not last:
-            sent = res[1:]
+    vel, mxup, mxdn, myup, mydn = les_section_first(velocity, eddy_visc, joint, sent)
+    merged = exchange_faces((mxdn, mxup, mydn, myup))
+    vel, lamb = les_section_last(vel, eddy_visc, merged, joint)
+    source = project(lamb, projection)
+    xoff = 3 * 2 * velocity.shape[2]
+    yoff = 3 * 2 * velocity.shape[1]
+    res = dg_step(state, source, merged, own_mat, other_mat, True, row_len, xoff, yoff)
+    state = res[0]
+    recv = exchange_faces(res[1:])
+    state = dg_step(state, source, recv, own_mat, other_mat, False, row_len)[0]
     flat_state = state
     leaving = jnp.where(filled[None, :], flat_state[:, jnp.where(filled, sending, 0)], 0.0)
     returned = lax.all_to_all(leaving, ("flow", "grp"), split_axis=1, concat_axis=1, tiled=True)

time: 139 us -> 122 us (0.88)
  starting transfers between devices: 66.7 us -> 52.5 us
  local copies, waits for them, and re-layouts: 20.6 us -> 16.7 us
  waiting for transfers between devices: 24.3 us -> 26.4 us
    ppermute x2 -> x1, starting transfers between devices: 8.6 us -> 3.66 us  [halos(): lax.ppermute(lax.index_in_dim(field, size_x - 1, lead, keepdims=False), '...]
    all_to_all x1, waiting for transfers between devices: 0.01 us -> 3.74 us  [body(): lax.all_to_all(outgoing, ('flow', 'grp'), split_axis=1, concat_axis=1, ti...]
    ppermute x2, waiting for transfers between devices: 4.04 us -> 7.67 us  [exchange_faces(): lax.ppermute(sy0, 'grp', down_g)]
    ppermute x2 -> x1, waiting for transfers between devices: 3.24 us -> 0.01 us  [halos(): lax.ppermute(lax.slice_in_dim(field, 0, 1, axis=lead + 1), 'grp', down_g)]
    ppermute x2 -> x1, starting transfers between devices: 6.22 us -> 3.11 us  [halos(): lax.ppermute(lax.slice_in_dim(field, size_y - 1, size_y, axis=lead + 1),...]
    ppermute x2, waiting for transfers between devices: 2.71 us -> 0.01 us  [exchange_faces(): lax.ppermute(sx0, 'flow', down_f)]
    ppermute x2, starting transfers between devices: 7.37 us -> 4.99 us  [exchange_faces(): lax.ppermute(sy4, 'grp', up_g)]
    ppermute x2 -> x1, starting transfers between devices: 3.84 us -> 1.92 us  [halos(): lax.ppermute(lax.index_in_dim(field, 0, lead, keepdims=False), 'flow', do...]
  transfers between devices with their start and end apart: 18 -> 14, of which waited for: 5 -> 5; matrix products, arithmetic and copies ran while one was open for 8% -> 3% of each run, Pallas kernels for 6% -> 1%
where the time goes in v4:
time: 122 us; the launch traced here: 121 us
  starting transfers between devices  52.5 us (43%)
  waiting for transfers between devices  26.4 us (22%)
  Pallas kernels  20.1 us (16%)
  local copies, waits for them, and re-layouts  16.7 us (14%)
  matrix products  2.22 us (2%)
  other arithmetic  1.87 us (2%)
    all_to_all x1, waiting for transfers between devices, body(): lax.all_to_all(leaving, ('flow', 'grp'), split_axis=1, concat_axis=1, til...  14.1 us
    all_to_all x1, starting transfers between devices, body(): lax.all_to_all(leaving, ('flow', 'grp'), split_axis=1, concat_axis=1, til...  12.8 us
    all_to_all x1, starting transfers between devices, body(): lax.all_to_all(outgoing, ('flow', 'grp'), split_axis=1, concat_axis=1, ti...  11.5 us
    pallas_call x2, Pallas kernels, dg_step(): pl.pallas_call(lambda *refs: dg_step_kernel(want_faces, xoff, yoff, row_l...  10.3 us
    ppermute x2, waiting for transfers between devices, exchange_faces(): lax.ppermute(sy0, 'grp', down_g)  7.67 us
    ppermute x2, starting transfers between devices, exchange_faces(): lax.ppermute(sx4, 'flow', up_f)  6.61 us
    ppermute x2, starting transfers between devices, exchange_faces(): lax.ppermute(sy4, 'grp', up_g)  4.99 us
    pallas_call x1, Pallas kernels, les_section_first(): pl.pallas_call(lambda *refs: les_kernel(0, *refs), out_shape=(jax.ShapeDt...  4.16 us
  transfers between devices with their start and end apart: 14, of which 5 were waited for; matrix products, arithmetic and copies ran while one was open for 3% of the time, Pallas kernels for 1%

profile of v4, /device:TPU:1, one launch (start us, length us, event | category | flops | bytes accessed | tf_op | source)
XLA Modules:
  0.0 120.8 jit_solution(2883844079783686639)
XLA Ops:
  2.4 1.1 scatter_custom_fusion
  3.6 1.1 all_to_all.14
  4.7 11.5 %all-to-all-start = ((f32[512,128,2]{0,2,1:T(2,128)}), f32[512,128,2]{0,2,1:T(2,128)S(1)}, u32[]{:S(2)}, u32[]{:S(2)}) async-start(f32[512,128,2]{0,2,1:T(2,128)} %all_to_all.14), calls=%async_computation | async-start | bytes 1048576 | tf_op jit(solution)/shard_map/all_to_all | solution.py:398
  16.2 3.7 %collective-permute-start = (f32[4,32,256]{2,1,0:T(8,128)S(1)}, f32[4,32,256]{2,1,0:T(8,128)S(1)}, u32[]{:S(2)}, u32[]{:S(2)}) collective-permute-start(f32[4,32,256]{2,1,0:T(8,128)S(1)} %get-tuple-element.37), channel_id=1, source_target_pairs={{0,4},{4,8},{8,12},{12,16},{16,20},{20,24},{24,28},{28,32},{32,36}... | collective-permute-start | bytes 393224 | tf_op jit(solution)/shard_map/ppermute | solution.py:250
  19.9 1.9 %collective-permute-start.1 = (f32[4,32,256]{2,1,0:T(8,128)S(1)}, f32[4,32,256]{2,1,0:T(8,128)S(1)}, u32[]{:S(2)}, u32[]{:S(2)}) collective-permute-start(f32[4,32,256]{2,1,0:T(8,128)S(1)} %get-tuple-element.36), channel_id=1, source_target_pairs={{4,0},{8,4},{12,8},{16,12},{20,16},{24,20},{28,24},{32,28},{36,32}... | collective-permute-start | bytes 393224 | tf_op jit(solution)/shard_map/ppermute | solution.py:251
  21.9 3.1 %collective-permute-start.2 = (f32[4,8,1,256]{3,2,1,0:T(1,128)S(1)}, f32[4,8,1,256]{3,2,1,0:T(1,128)S(1)}, u32[]{:S(2)}, u32[]{:S(2)}) collective-permute-start(f32[4,8,1,256]{3,2,1,0:T(1,128)S(1)} %get-tuple-element.35), channel_id=1, source_target_pairs={{0,1},{1,2},{2,3},{4,5},{5,6},{6,7},{8,9},{9,10},{10,11},{12,13},{... | collective-permute-start | bytes 98312 | tf_op jit(solution)/shard_map/ppermute | solution.py:252
  25.0 1.3 %collective-permute-start.3 = (f32[4,8,1,256]{3,2,1,0:T(1,128)S(1)}, f32[4,8,1,256]{3,2,1,0:T(1,128)S(1)}, u32[]{:S(2)}, u32[]{:S(2)}) collective-permute-start(f32[4,8,1,256]{3,2,1,0:T(1,128)S(1)} %get-tuple-element.34), channel_id=1, source_target_pairs={{1,0},{2,1},{3,2},{5,4},{6,5},{7,6},{9,8},{10,9},{11,10},{13,12},{... | collective-permute-start | bytes 98312 | tf_op jit(solution)/shard_map/ppermute | solution.py:253
  26.6 3.7 %all-to-all-done = f32[512,128,2]{0,2,1:T(2,128)S(1)} async-done(((f32[512,128,2]{0,2,1:T(2,128)}), f32[512,128,2]{0,2,1:T(2,128)S(1)}, u32[]{:S(2)}, u32[]{:S(2)}) %all-to-all-start) | async-done | bytes 524320 | tf_op jit(solution)/shard_map/all_to_all | solution.py:398
  30.7 1.5 %scatter_custom_fusion.1 = f32[512,128]{0,1:T(8,128)S(1)} fusion(s32[256]{0:T(256)S(1)} %bitcast.62, f32[512,256]{0,1:T(8,128)S(1)} %reshape.158, f32[]{:T(128)} %constant.8.clone.1), kind=kCustom, calls=%fused_computation.6 | custom fusion | bytes 786436 | tf_op jit(solution)/shard_map/scatter | solution.py:402
  33.1 1.7 %shard_map.104 = (f32[104,128]{1,0:T(8,128)}, f32[104,128]{1,0:T(8,128)}, f32[104,32]{1,0:T(8,128)}, f32[104,32]{1,0:T(8,128)}) custom-call(f32[512,128]{1,0:T(8,128)} %copy.29.state_ref.refs_0_), custom_call_target="tpu_custom_call" | custom-call | tf_op jit(solution)/shard_map/pallas_call | solution.py:348
  35.5 4.2 %shard_map.105 = (f32[3,8,32,256]{3,2,1,0:T(8,128)}, f32[296,128]{1,0:T(8,128)}, f32[296,128]{1,0:T(8,128)}, f32[152,128]{1,0:T(8,128)}, f32[152,128]{1,0:T(8,128)}) custom-call(f32[3,8,32,256]{3,2,1,0:T(8,128)} %refs_0_.1, f32[8,32,256]{2,1,0:T(8,128)} %refs_1_.3, f32[4,32,256]{2,1,0:T(8,128)} %copy-done.2, f32[4,32,256]{2,1,0:T(8,128)} %copy-done.3, ...), custom_call_target="tpu_custom_call" | custom-call | tf_op jit(solution)/shard_map/pallas_call | solution.py:229
  39.7 2.6 %collective-permute-start.4 = (f32[296,128]{1,0:T(8,128)}, f32[296,128]{1,0:T(8,128)S(1)}, u32[]{:S(2)}, u32[]{:S(2)}) collective-permute-start(f32[296,128]{1,0:T(8,128)} %get-tuple-element.23), channel_id=1, source_target_pairs={{0,4},{4,8},{8,12},{12,16},{16,20},{20,24},{24,28},{28,32},{32,36}... | collective-permute-start | bytes 454664 | tf_op jit(solution)/shard_map/ppermute | solution.py:381
  42.3 1.9 %collective-permute-start.5 = (f32[296,128]{1,0:T(8,128)}, f32[296,128]{1,0:T(8,128)S(1)}, u32[]{:S(2)}, u32[]{:S(2)}) collective-permute-start(f32[296,128]{1,0:T(8,128)} %get-tuple-element.24), channel_id=1, source_target_pairs={{4,0},{8,4},{12,8},{16,12},{20,16},{24,20},{28,24},{32,28},{36,32}... | collective-permute-start | bytes 454664 | tf_op jit(solution)/shard_map/ppermute | solution.py:382
  44.2 2.2 %collective-permute-start.6 = (f32[152,128]{1,0:T(8,128)}, f32[152,128]{1,0:T(8,128)S(1)}, u32[]{:S(2)}, u32[]{:S(2)}) collective-permute-start(f32[152,128]{1,0:T(8,128)} %get-tuple-element.25), channel_id=1, source_target_pairs={{0,1},{1,2},{2,3},{4,5},{5,6},{6,7},{8,9},{9,10},{10,11},{12,13},{... | collective-permute-start | bytes 233480 | tf_op jit(solution)/shard_map/ppermute | solution.py:383
  46.4 1.3 %collective-permute-start.7 = (f32[152,128]{1,0:T(8,128)}, f32[152,128]{1,0:T(8,128)S(1)}, u32[]{:S(2)}, u32[]{:S(2)}) collective-permute-start(f32[152,128]{1,0:T(8,128)} %get-tuple-element.26), channel_id=1, source_target_pairs={{1,0},{2,1},{3,2},{5,4},{6,5},{7,6},{9,8},{10,9},{11,10},{13,12},{... | collective-permute-start | bytes 233480 | tf_op jit(solution)/shard_map/ppermute | solution.py:384
  48.5 4.2 %collective-permute-done.7.refs_5_ = f32[152,128]{1,0:T(8,128)S(1)} collective-permute-done((f32[152,128]{1,0:T(8,128)}, f32[152,128]{1,0:T(8,128)S(1)}, u32[]{:S(2)}, u32[]{:S(2)}) %collective-permute-start.7) | collective-permute-done | bytes 77856 | tf_op jit(solution)/shard_map/ppermute | solution.py:384
  53.6 4.0 %shard_map.106 = (f32[3,8,32,256]{3,2,1,0:T(8,128)}, bf16[3,8,32,256]{3,2,1,0:T(8,128)(2,1)}) custom-call(f32[3,8,32,256]{3,2,1,0:T(8,128)} %get-tuple-element.22.refs_0_, f32[8,32,256]{2,1,0:T(8,128)} %refs_1_.3, f32[296,128]{1,0:T(8,128)} %copy-done.4, f32[296,128]{1,0:T(8,128)} %copy-done.5, f32[152,128]{1,0:T(8,128)} %copy-done.6, f32[152,128]{1,0:T(8,128)} %copy-done.7, ...), custom_call_target="tpu_custom_call" | custom-call | tf_op jit(solution)/shard_map/pallas_call | solution.py:236
  57.6 1.2 %convolution_convert_fusion = bf16[768,256]{1,0:T(8,128)(2,1)S(1)} fusion(bf16[768,256]{1,0:T(8,128)(2,1)} %bitcast.60, bf16[256,256]{1,0:T(8,128)(2,1)S(1)} %copy-done.10), kind=kOutput, calls=%fused_computation.5 | convolution fusion | flops 100859904 | bytes 917504 | tf_op jit(solution)/shard_map/dot_general | solution.py:265
  59.5 2.0 %copy.38 = bf16[3,1,8,4,8,8,32]{6,3,0,5,4,2,1:T(4,128)(2,1)S(1)} copy(bf16[3,1,8,4,8,8,32]{6,5,4,3,2,0,1:T(8,128)(2,1)S(1)} %reshape.129) | data formatting | bytes 786432 | tf_op jit(solution)/shard_map/reshape | solution.py:267
  62.6 1.0 fusion.4
  63.6 5.2 %shard_map.107 = (f32[512,128]{1,0:T(8,128)}, f32[104,128]{1,0:T(8,128)}, f32[104,128]{1,0:T(8,128)}, f32[104,32]{1,0:T(8,128)}, f32[104,32]{1,0:T(8,128)}) custom-call(f32[512,128]{1,0:T(8,128)} %copy.29.state_ref.refs_0_, f32[384,128]{1,0:T(8,128)} %bitcast.53, f32[296,128]{1,0:T(8,128)} %copy-done.4, f32[296,128]{1,0:T(8,128)} %copy-done.5, ...), custom_call_target="tpu_custom_call" | custom-call | tf_op jit(solution)/shard_map/pallas_call | solution.py:360
  68.8 4.0 %collective-permute-start.8 = (f32[104,128]{1,0:T(8,128)}, f32[104,128]{1,0:T(8,128)S(1)}, u32[]{:S(2)}, u32[]{:S(2)}) collective-permute-start(f32[104,128]{1,0:T(8,128)} %get-tuple-element.30), channel_id=1, source_target_pairs={{0,4},{4,8},{8,12},{12,16},{16,20},{20,24},{24,28},{28,32},{32,36}... | collective-permute-start | bytes 159752 | tf_op jit(solution)/shard_map/ppermute | solution.py:381
  72.9 1.9 %collective-permute-start.9 = (f32[104,128]{1,0:T(8,128)}, f32[104,128]{1,0:T(8,128)S(1)}, u32[]{:S(2)}, u32[]{:S(2)}) collective-permute-start(f32[104,128]{1,0:T(8,128)} %get-tuple-element.31), channel_id=1, source_target_pairs={{4,0},{8,4},{12,8},{16,12},{20,16},{24,20},{28,24},{32,28},{36,32}... | collective-permute-start | bytes 159752 | tf_op jit(solution)/shard_map/ppermute | solution.py:382
  74.8 2.8 %collective-permute-start.10 = (f32[104,32]{1,0:T(8,128)}, f32[104,32]{1,0:T(8,128)S(1)}, u32[]{:S(2)}, u32[]{:S(2)}) collective-permute-start(f32[104,32]{1,0:T(8,128)} %get-tuple-element.32), channel_id=1, source_target_pairs={{0,1},{1,2},{2,3},{4,5},{5,6},{6,7},{8,9},{9,10},{10,11},{12,13},{... | collective-permute-start | bytes 39944 | tf_op jit(solution)/shard_map/ppermute | solution.py:383
  77.6 1.5 %collective-permute-start.11 = (f32[104,32]{1,0:T(8,128)}, f32[104,32]{1,0:T(8,128)S(1)}, u32[]{:S(2)}, u32[]{:S(2)}) collective-permute-start(f32[104,32]{1,0:T(8,128)} %get-tuple-element.33), channel_id=1, source_target_pairs={{1,0},{2,1},{3,2},{5,4},{6,5},{7,6},{9,8},{10,9},{11,10},{13,12},{... | collective-permute-start | bytes 39944 | tf_op jit(solution)/shard_map/ppermute | solution.py:384
  79.2 3.4 %collective-permute-done.11.refs_5_ = f32[104,32]{1,0:T(8,128)S(1)} collective-permute-done((f32[104,32]{1,0:T(8,128)}, f32[104,32]{1,0:T(8,128)S(1)}, u32[]{:S(2)}, u32[]{:S(2)}) %collective-permute-start.11) | collective-permute-done | bytes 13344 | tf_op jit(solution)/shard_map/ppermute | solution.py:384
  83.3 5.0 %shard_map.108 = f32[512,128]{1,0:T(8,128)} custom-call(f32[512,128]{1,0:T(8,128)} %get-tuple-element.29.refs_0_, f32[384,128]{1,0:T(8,128)} %bitcast.54, f32[104,128]{1,0:T(8,128)} %copy-done.12, f32[104,128]{1,0:T(8,128)} %copy-done.13, f32[104,32]{1,0:T(8,128)} %copy-done.14, f32[104,32]{1,0:T(8,128)} %copy-done.15, f32[512,512]{1,0:T(8,128)} %constant.6.clone.refs_6_, ...), custom_call_target="tpu_custom_call" | custom-call | tf_op jit(solution)/shard_map/pallas_call | solution.py:360
  88.3 1.1 copy.34
  89.4 1.0 gather_fusion
  90.7 1.1 broadcast_select_fusion
  91.8 12.8 %all-to-all-start.1 = ((f32[512,128,2]{0,2,1:T(2,128)}), f32[512,128,2]{0,2,1:T(2,128)S(1)}, u32[]{:S(2)}, u32[]{:S(2)}) async-start(f32[512,128,2]{0,2,1:T(2,128)} %broadcast_select_fusion), calls=%async_computation.1 | async-start | bytes 1048576 | tf_op jit(solution)/shard_map/all_to_all | solution.py:421
  104.6 14.1 %all-to-all-done.1 = f32[512,128,2]{0,2,1:T(2,128)S(1)} async-done(((f32[512,128,2]{0,2,1:T(2,128)}), f32[512,128,2]{0,2,1:T(2,128)S(1)}, u32[]{:S(2)}, u32[]{:S(2)}) %all-to-all-start.1) | async-done | bytes 524320 | tf_op jit(solution)/shard_map/all_to_all | solution.py:421
  (67 shorter events, 10.5 us)
Async XLA Ops:
  2.3 13.9 %copy-start = (f32[3,8,32,256]{3,2,1,0:T(8,128)S(1)}, f32[3,8,32,256]{3,2,1,0:T(8,128)}, u32[]{:S(2)}) copy-start(f32[3,8,32,256]{3,2,1,0:T(8,128)} %refs_0_.1) | copy-start | bytes 2359300
  2.3 13.9 %copy-start.1 = (f32[8,32,256]{2,1,0:T(8,128)S(1)}, f32[8,32,256]{2,1,0:T(8,128)}, u32[]{:S(2)}) copy-start(f32[8,32,256]{2,1,0:T(8,128)} %refs_1_.3) | copy-start | bytes 786436
  4.7 21.6 %copy-start.16 = (s32[1,128,2]{1,2,0:T(2,128)S(1)}, s32[1,128,2]{1,2,0:T(2,128)}, u32[]{:S(2)}) copy-start(s32[1,128,2]{1,2,0:T(2,128)} %param.13) | copy-start | bytes 3076
  4.7 25.6 %all-to-all-start = ((f32[512,128,2]{0,2,1:T(2,128)}), f32[512,128,2]{0,2,1:T(2,128)S(1)}, u32[]{:S(2)}, u32[]{:S(2)}) async-start(f32[512,128,2]{0,2,1:T(2,128)} %all_to_all.14), calls=%async_computation | async-start | bytes 1048576 | tf_op jit(solution)/shard_map/all_to_all | solution.py:398
  16.2 18.5 %collective-permute-start = (f32[4,32,256]{2,1,0:T(8,128)S(1)}, f32[4,32,256]{2,1,0:T(8,128)S(1)}, u32[]{:S(2)}, u32[]{:S(2)}) collective-permute-start(f32[4,32,256]{2,1,0:T(8,128)S(1)} %get-tuple-element.37), channel_id=1, source_target_pairs={{0,4},{4,8},{8,12},{12,16},{16,20},{20,24},{24,28},{28,32},{32,36}... | collective-permute-start | bytes 393224 | tf_op jit(solution)/shard_map/ppermute | solution.py:250
  19.9 14.9 %collective-permute-start.1 = (f32[4,32,256]{2,1,0:T(8,128)S(1)}, f32[4,32,256]{2,1,0:T(8,128)S(1)}, u32[]{:S(2)}, u32[]{:S(2)}) collective-permute-start(f32[4,32,256]{2,1,0:T(8,128)S(1)} %get-tuple-element.36), channel_id=1, source_target_pairs={{4,0},{8,4},{12,8},{16,12},{20,16},{24,20},{28,24},{32,28},{36,32}... | collective-permute-start | bytes 393224 | tf_op jit(solution)/shard_map/ppermute | solution.py:251
  21.9 12.9 %collective-permute-start.2 = (f32[4,8,1,256]{3,2,1,0:T(1,128)S(1)}, f32[4,8,1,256]{3,2,1,0:T(1,128)S(1)}, u32[]{:S(2)}, u32[]{:S(2)}) collective-permute-start(f32[4,8,1,256]{3,2,1,0:T(1,128)S(1)} %get-tuple-element.35), channel_id=1, source_target_pairs={{0,1},{1,2},{2,3},{4,5},{5,6},{6,7},{8,9},{9,10},{10,11},{12,13},{... | collective-permute-start | bytes 98312 | tf_op jit(solution)/shard_map/ppermute | solution.py:252
  25.0 9.8 %collective-permute-start.3 = (f32[4,8,1,256]{3,2,1,0:T(1,128)S(1)}, f32[4,8,1,256]{3,2,1,0:T(1,128)S(1)}, u32[]{:S(2)}, u32[]{:S(2)}) collective-permute-start(f32[4,8,1,256]{3,2,1,0:T(1,128)S(1)} %get-tuple-element.34), channel_id=1, source_target_pairs={{1,0},{2,1},{3,2},{5,4},{6,5},{7,6},{9,8},{10,9},{11,10},{13,12},{... | collective-permute-start | bytes 98312 | tf_op jit(solution)/shard_map/ppermute | solution.py:253
  34.8 0.6 copy-start.8
  34.8 0.6 copy-start.9
  34.8 0.7 copy-start.2
  34.8 0.7 copy-start.3
  35.5 22.1 %copy-start.10 = (bf16[256,256]{1,0:T(8,128)(2,1)S(1)}, bf16[256,256]{1,0:T(8,128)(2,1)}, u32[]{:S(2)}) copy-start(bf16[256,256]{1,0:T(8,128)(2,1)} %constant.24.clone) | copy-start | bytes 393220
  39.7 13.1 %collective-permute-start.4 = (f32[296,128]{1,0:T(8,128)}, f32[296,128]{1,0:T(8,128)S(1)}, u32[]{:S(2)}, u32[]{:S(2)}) collective-permute-start(f32[296,128]{1,0:T(8,128)} %get-tuple-element.23), channel_id=1, source_target_pairs={{0,4},{4,8},{8,12},{12,16},{16,20},{20,24},{24,28},{28,32},{32,36}... | collective-permute-start | bytes 454664 | tf_op jit(solution)/shard_map/ppermute | solution.py:381
  42.3 10.5 %collective-permute-start.5 = (f32[296,128]{1,0:T(8,128)}, f32[296,128]{1,0:T(8,128)S(1)}, u32[]{:S(2)}, u32[]{:S(2)}) collective-permute-start(f32[296,128]{1,0:T(8,128)} %get-tuple-element.24), channel_id=1, source_target_pairs={{4,0},{8,4},{12,8},{16,12},{20,16},{24,20},{28,24},{32,28},{36,32}... | collective-permute-start | bytes 454664 | tf_op jit(solution)/shard_map/ppermute | solution.py:382
  44.2 4.4 %collective-permute-start.6 = (f32[152,128]{1,0:T(8,128)}, f32[152,128]{1,0:T(8,128)S(1)}, u32[]{:S(2)}, u32[]{:S(2)}) collective-permute-start(f32[152,128]{1,0:T(8,128)} %get-tuple-element.25), channel_id=1, source_target_pairs={{0,1},{1,2},{2,3},{4,5},{5,6},{6,7},{8,9},{9,10},{10,11},{12,13},{... | collective-permute-start | bytes 233480 | tf_op jit(solution)/shard_map/ppermute | solution.py:383
  46.4 6.4 %collective-permute-start.7 = (f32[152,128]{1,0:T(8,128)}, f32[152,128]{1,0:T(8,128)S(1)}, u32[]{:S(2)}, u32[]{:S(2)}) collective-permute-start(f32[152,128]{1,0:T(8,128)} %get-tuple-element.26), channel_id=1, source_target_pairs={{1,0},{2,1},{3,2},{5,4},{6,5},{7,6},{9,8},{10,9},{11,10},{13,12},{... | collective-permute-start | bytes 233480 | tf_op jit(solution)/shard_map/ppermute | solution.py:384
  48.5 4.3 %copy-start.6 = (f32[152,128]{1,0:T(8,128)}, f32[152,128]{1,0:T(8,128)S(1)}, u32[]{:S(2)}) copy-start(f32[152,128]{1,0:T(8,128)S(1)} %collective-permute-done.6.refs_4_) | copy-start | bytes 233476
  52.8 0.6 copy-start.7
  52.8 0.7 copy-start.4
  52.8 0.8 copy-start.5
  61.5 1.1 copy-start.11
  68.8 13.9 %collective-permute-start.8 = (f32[104,128]{1,0:T(8,128)}, f32[104,128]{1,0:T(8,128)S(1)}, u32[]{:S(2)}, u32[]{:S(2)}) collective-permute-start(f32[104,128]{1,0:T(8,128)} %get-tuple-element.30), channel_id=1, source_target_pairs={{0,4},{4,8},{8,12},{12,16},{16,20},{20,24},{24,28},{28,32},{32,36}... | collective-permute-start | bytes 159752 | tf_op jit(solution)/shard_map/ppermute | solution.py:381
  72.9 9.8 %collective-permute-start.9 = (f32[104,128]{1,0:T(8,128)}, f32[104,128]{1,0:T(8,128)S(1)}, u32[]{:S(2)}, u32[]{:S(2)}) collective-permute-start(f32[104,128]{1,0:T(8,128)} %get-tuple-element.31), channel_id=1, source_target_pairs={{4,0},{8,4},{12,8},{16,12},{20,16},{24,20},{28,24},{32,28},{36,32}... | collective-permute-start | bytes 159752 | tf_op jit(solution)/shard_map/ppermute | solution.py:382
  74.8 4.4 %collective-permute-start.10 = (f32[104,32]{1,0:T(8,128)}, f32[104,32]{1,0:T(8,128)S(1)}, u32[]{:S(2)}, u32[]{:S(2)}) collective-permute-start(f32[104,32]{1,0:T(8,128)} %get-tuple-element.32), channel_id=1, source_target_pairs={{0,1},{1,2},{2,3},{4,5},{5,6},{6,7},{8,9},{9,10},{10,11},{12,13},{... | collective-permute-start | bytes 39944 | tf_op jit(solution)/shard_map/ppermute | solution.py:383
  77.6 5.1 %collective-permute-start.11 = (f32[104,32]{1,0:T(8,128)}, f32[104,32]{1,0:T(8,128)S(1)}, u32[]{:S(2)}, u32[]{:S(2)}) collective-permute-start(f32[104,32]{1,0:T(8,128)} %get-tuple-element.33), channel_id=1, source_target_pairs={{1,0},{2,1},{3,2},{5,4},{6,5},{7,6},{9,8},{10,9},{11,10},{13,12},{... | collective-permute-start | bytes 39944 | tf_op jit(solution)/shard_map/ppermute | solution.py:384
  79.2 3.5 %copy-start.14 = (f32[104,32]{1,0:T(8,128)}, f32[104,32]{1,0:T(8,128)S(1)}, u32[]{:S(2)}) copy-start(f32[104,32]{1,0:T(8,128)S(1)} %collective-permute-done.10.refs_4_) | copy-start | bytes 39940
  82.7 0.6 copy-start.15
  82.7 0.6 copy-start.12
  82.7 0.6 copy-start.13
  91.8 26.9 %all-to-all-start.1 = ((f32[512,128,2]{0,2,1:T(2,128)}), f32[512,128,2]{0,2,1:T(2,128)S(1)}, u32[]{:S(2)}, u32[]{:S(2)}) async-start(f32[512,128,2]{0,2,1:T(2,128)} %broadcast_select_fusion), calls=%async_computation.1 | async-start | bytes 1048576 | tf_op jit(solution)/shard_map/all_to_all | solution.py:421

commit v5 on v4

--- a/solution.py
+++ b/solution.py
@@ -114,7 +114,7 @@
     row = lax.broadcasted_iota(jnp.int32, (size_y, size_z), 0)
     lane = lax.broadcasted_iota(jnp.int32, (size_y, size_z), 1)
     if mode == 0:
-        sx0_ref, sx4_ref, sy0_ref, sy4_ref, out_ref, mxup_ref, mxdn_ref, myup_ref, mydn_ref = rest
+        (out_ref,) = rest
 
         def xlo(c):
             return vxlo_ref[c]
@@ -202,34 +202,13 @@
         return carry
 
     lax.fori_loop(0, size_x, step, 0)
-    if mode == 0:
-        for c in range(3):
-            for h in range(2):
-                mxup_ref[pl.ds(c * 2 * size_y + h * size_y, size_y), :] = out_ref[c, size_x - 1, :, pl.ds(h * half, half)]
-                mxdn_ref[pl.ds(c * 2 * size_y + h * size_y, size_y), :] = out_ref[c, 0, :, pl.ds(h * half, half)]
-                for x in range(size_x):
-                    at = c * 2 * size_x + h * size_x + x
-                    myup_ref[pl.ds(at, 1), :] = out_ref[c, x, pl.ds(size_y - 1, 1), pl.ds(h * half, half)]
-                    mydn_ref[pl.ds(at, 1), :] = out_ref[c, x, pl.ds(0, 1), pl.ds(h * half, half)]
-        xrows = 3 * 2 * size_y
-        yrows = 3 * 2 * size_x
-        mxup_ref[pl.ds(xrows, FACE_ROWS), :] = sx4_ref[...]
-        mxdn_ref[pl.ds(xrows, FACE_ROWS), :] = sx0_ref[...]
-        zeros = jnp.zeros((FACE_ROWS, half), jnp.float32)
-        myup_ref[pl.ds(yrows, FACE_ROWS), :] = zeros
-        mydn_ref[pl.ds(yrows, FACE_ROWS), :] = zeros
-        myup_ref[pl.ds(yrows, FACE_ROWS), pl.ds(0, sy4_ref.shape[1])] = sy4_ref[...]
-        mydn_ref[pl.ds(yrows, FACE_ROWS), pl.ds(0, sy0_ref.shape[1])] = sy0_ref[...]
-
-
-def les_section_first(vel, nu, joint, faces):
-    size_x, size_y, size_z = vel.shape[1], vel.shape[2], vel.shape[3]
-    xbuf = jax.ShapeDtypeStruct((3 * 2 * size_y + FACE_ROWS, size_z // 2), jnp.float32)
-    ybuf = jax.ShapeDtypeStruct((3 * 2 * size_x + FACE_ROWS, size_z // 2), jnp.float32)
+
+
+def les_section_first(vel, nu, joint):
     return pl.pallas_call(
         lambda *refs: les_kernel(0, *refs),
-        out_shape=(jax.ShapeDtypeStruct(vel.shape, jnp.float32), xbuf, xbuf, ybuf, ybuf),
-    )(vel, nu, *joint, *joint, *faces)
+        out_shape=(jax.ShapeDtypeStruct(vel.shape, jnp.float32),),
+    )(vel, nu, *joint, *joint)[0]
 
 
 def les_section_last(vel, nu, merged, joint):
@@ -297,18 +276,63 @@
     sy4_ref[...] = last[:, :row_len]
 
 
-def dg_faces_kernel(state_ref, sx0_ref, sx4_ref, sy0_ref, sy4_ref, face_ref):
+def one_hot(shape, ids, axis):
+    return jnp.where(lax.broadcasted_iota(jnp.int32, shape, axis) == ids, 1.0, 0.0).astype(jnp.float32)
+
+
+def route_out_kernel(acoustic_ref, place_ref, out_ref, pad_ref):
+    comps, nodes, elems = acoustic_ref.shape
+    pad_ref[...] = jnp.zeros(pad_ref.shape, jnp.float32)
+    for comp in range(comps):
+        pad_ref[pl.ds(comp * 128, nodes), :] = acoustic_ref[comp]
+    slots = out_ref.shape[0]
+    place_hot = one_hot((slots, elems), place_ref[...], 0)
+    out_ref[...] = lax.dot_general(place_hot, pad_ref[...], (((1,), (1,)), ((), ())),
+                                   precision=HIGH, preferred_element_type=jnp.float32)
+
+
+def route_in_kernel(arrived_ref, place_ref, out_ref):
+    slots, rows = arrived_ref.shape
+    comps, nodes, elems = out_ref.shape
+    place_hot = one_hot((slots, elems), place_ref[...], 0)
+    back = jnp.dot(arrived_ref[...].T, place_hot, precision=HIGH, preferred_element_type=jnp.float32)
+    for comp in range(comps):
+        out_ref[comp] = back[comp * 128:comp * 128 + nodes]
+
+
+def dg_faces_kernel(arrived_ref, send_ref, vel_ref, state_ref, mxup_ref, mxdn_ref, myup_ref, mydn_ref, face_ref):
+    slots, rows = arrived_ref.shape
+    elems = state_ref.shape[1]
+    home_hot = one_hot((slots, elems), send_ref[...], 1)
+    state_ref[...] = jnp.dot(arrived_ref[...].T, home_hot, precision=HIGH, preferred_element_type=jnp.float32)
     face_ref[...] = jnp.zeros(face_ref.shape, jnp.float32)
     extract_faces(state_ref, face_ref)
-    send_faces(face_ref, sx0_ref, sx4_ref, sy0_ref, sy4_ref, sy0_ref.shape[1])
+    size_x, size_y, size_z = vel_ref.shape[1], vel_ref.shape[2], vel_ref.shape[3]
+    half = size_z // 2
+    row_len = size_z // 8
+    for c in range(3):
+        for h in range(2):
+            mxup_ref[pl.ds(c * 2 * size_y + h * size_y, size_y), :] = vel_ref[c, size_x - 1, :, pl.ds(h * half, half)]
+            mxdn_ref[pl.ds(c * 2 * size_y + h * size_y, size_y), :] = vel_ref[c, 0, :, pl.ds(h * half, half)]
+            for x in range(size_x):
+                at = c * 2 * size_x + h * size_x + x
+                myup_ref[pl.ds(at, 1), :] = vel_ref[c, x, pl.ds(size_y - 1, 1), pl.ds(h * half, half)]
+                mydn_ref[pl.ds(at, 1), :] = vel_ref[c, x, pl.ds(0, 1), pl.ds(h * half, half)]
+    xrows = 3 * 2 * size_y
+    yrows = 3 * 2 * size_x
+    mxup_ref[pl.ds(xrows, FACE_ROWS), :] = face_ref[1]
+    mxdn_ref[pl.ds(xrows, FACE_ROWS), :] = face_ref[0]
+    lane = lax.broadcasted_iota(jnp.int32, (FACE_ROWS, elems), 1)
+    myup_ref[pl.ds(yrows, FACE_ROWS), :] = jnp.where(lane < row_len, pltpu.roll(face_ref[3], row_len, 1), 0.0)
+    mydn_ref[pl.ds(yrows, FACE_ROWS), :] = jnp.where(lane < row_len, face_ref[2], 0.0)
 
 
 def dg_step_kernel(want_faces, xoff, yoff, row_len, state_ref, src_ref, xlo_ref, xhi_ref, ylo_ref, yhi_ref, own_ref, other_ref,
-                   out_ref, *rest):
+                   send_ref, out_ref, *rest):
     if want_faces:
         sx0_ref, sx4_ref, sy0_ref, sy4_ref, face_ref, oth_ref, pad_ref = rest
     else:
-        face_ref, oth_ref, pad_ref = rest
+        leave_ref, face_ref, oth_ref, pad_ref = rest
     elems = state_ref.shape[1]
     lane = lax.broadcasted_iota(jnp.int32, (FACE_ROWS, elems), 1)
     ez = lane % row_len
@@ -335,6 +359,11 @@
     if want_faces:
         extract_faces(out_ref, face_ref)
         send_faces(face_ref, sx0_ref, sx4_ref, sy0_ref, sy4_ref, row_len)
+    else:
+        slots = leave_ref.shape[0]
+        home_hot = one_hot((slots, elems), send_ref[...], 1)
+        leave_ref[...] = lax.dot_general(home_hot, out_ref[...], (((1,), (1,)), ((), ())),
+                                         precision=HIGH, preferred_element_type=jnp.float32)
 
 
 def face_shapes(elems, row_len):
@@ -343,20 +372,42 @@
     return [big, big, small, small]
 
 
-def dg_faces(state, row_len):
-    elems = state.shape[1]
+def dg_faces(arrived, sending, vel):
+    elems = vel.shape[2] // 8 * (vel.shape[3] // 8) * (vel.shape[1] // 8)
+    size_x, size_y, size_z = vel.shape[1], vel.shape[2], vel.shape[3]
+    xbuf = jax.ShapeDtypeStruct((3 * 2 * size_y + FACE_ROWS, size_z // 2), jnp.float32)
+    ybuf = jax.ShapeDtypeStruct((3 * 2 * size_x + FACE_ROWS, size_z // 2), jnp.float32)
     return pl.pallas_call(
         dg_faces_kernel,
-        out_shape=tuple(face_shapes(elems, row_len)),
+        out_shape=(jax.ShapeDtypeStruct((arrived.shape[1], elems), jnp.float32), xbuf, xbuf, ybuf, ybuf),
         scratch_shapes=[pltpu.VMEM((6, FACE_ROWS, elems), jnp.float32)],
-    )(state)
-
-
-def dg_step(state, src, recv, own_mat, other_mat, want_faces, row_len, xoff=0, yoff=0):
+    )(arrived, sending, vel)
+
+
+def route_out(acoustic, placing, slots):
+    return pl.pallas_call(
+        route_out_kernel,
+        out_shape=jax.ShapeDtypeStruct((slots, 512), jnp.float32),
+        scratch_shapes=[pltpu.VMEM((512, acoustic.shape[2]), jnp.float32)],
+    )(acoustic, placing)
+
+
+def route_in(returned, placing, nodes):
+    elems = placing.shape[1]
+    return pl.pallas_call(
+        route_in_kernel,
+        out_shape=jax.ShapeDtypeStruct((4, nodes, elems), jnp.float32),
+    )(returned, placing)
+
+
+def dg_step(state, src, recv, own_mat, other_mat, want_faces, row_len, xoff=0, yoff=0, sending=None):
     elems = state.shape[1]
     out_shape = [jax.ShapeDtypeStruct(state.shape, jnp.float32)]
+    extra = [sending]
     if want_faces:
         out_shape += face_shapes(elems, row_len)
+    else:
+        out_shape.append(jax.ShapeDtypeStruct((sending.shape[0], state.shape[0]), jnp.float32))
     res = pl.pallas_call(
         lambda *refs: dg_step_kernel(want_faces, xoff, yoff, row_len, *refs),
         out_shape=tuple(out_shape),
@@ -365,7 +416,7 @@
             pltpu.VMEM((768, elems), jnp.float32),
             pltpu.VMEM((FACE_ROWS, elems), jnp.float32),
         ],
-    )(state, src, *recv, own_mat, other_mat)
+    )(state, src, *recv, own_mat, other_mat, *extra)
     return res
 
 
@@ -390,36 +441,28 @@
     flow_size = lax.axis_size("flow")
     grp_size = lax.axis_size("grp")
     slot_cap = route_send.shape[2]
-    elem_count = acoustic_state.shape[2]
     total_slots = flow_size * grp_size * slot_cap
-    placing = route_place.reshape(-1)
-    padded_state = jnp.pad(acoustic_state, ((0, 0), (0, 3), (0, 0))).reshape(512, elem_count)
-    outgoing = jnp.zeros((512, total_slots), jnp.float32).at[:, placing].set(padded_state)
-    arrived = lax.all_to_all(outgoing, ("flow", "grp"), split_axis=1, concat_axis=1, tiled=True)
-    sending = route_send.reshape(-1)
-    filled = sending >= 0
-    target = jnp.where(filled, sending, elem_count)
-    state = jnp.zeros((512, elem_count), jnp.float32).at[:, target].set(arrived, mode="drop")
+    sending = route_send.reshape(total_slots, 1)
+    outgoing = route_out(acoustic_state, route_place, total_slots)
+    arrived = lax.all_to_all(outgoing, ("flow", "grp"), split_axis=0, concat_axis=0, tiled=True)
+    vel = les_section_first(velocity, eddy_visc, joint)
 
     row_len = velocity.shape[3] // 8
     own_np, other_np = dg_matrices()
     own_mat = jnp.asarray(own_np)
     other_mat = jnp.asarray(other_np)
-    sent = dg_faces(state, row_len)
-    vel, mxup, mxdn, myup, mydn = les_section_first(velocity, eddy_visc, joint, sent)
+    state, mxup, mxdn, myup, mydn = dg_faces(arrived, sending, vel)
     merged = exchange_faces((mxdn, mxup, mydn, myup))
     vel, lamb = les_section_last(vel, eddy_visc, merged, joint)
     source = project(lamb, projection)
     xoff = 3 * 2 * velocity.shape[2]
     yoff = 3 * 2 * velocity.shape[1]
-    res = dg_step(state, source, merged, own_mat, other_mat, True, row_len, xoff, yoff)
+    res = dg_step(state, source, merged, own_mat, other_mat, True, row_len, xoff, yoff, sending=sending)
     state = res[0]
     recv = exchange_faces(res[1:])
-    state = dg_step(state, source, recv, own_mat, other_mat, False, row_len)[0]
-    flat_state = state
-    leaving = jnp.where(filled[None, :], flat_state[:, jnp.where(filled, sending, 0)], 0.0)
-    returned = lax.all_to_all(leaving, ("flow", "grp"), split_axis=1, concat_axis=1, tiled=True)
-    acoustic_out = returned[:, placing].reshape(4, 128, elem_count)[:, :125]
+    leaving = dg_step(state, source, recv, own_mat, other_mat, False, row_len, sending=sending)[1]
+    returned = lax.all_to_all(leaving, ("flow", "grp"), split_axis=0, concat_axis=0, tiled=True)
+    acoustic_out = route_in(returned, route_place, acoustic_state.shape[1])
     return (vel, acoustic_out)
 
 

time: 122 us -> 129 us (1.057)
  blocking collectives: 0 us -> 27.4 us
  waiting for transfers between devices: 26.4 us -> 7.81 us
  starting transfers between devices: 52.5 us -> 44.8 us
  Pallas kernels: 20.1 us -> 27.2 us
  other arithmetic: 1.87 us -> 0.07 us
    all_to_all x0 -> x1, blocking collectives: none -> 27.4 us  [body(): lax.all_to_all(leaving, ('flow', 'grp'), split_axis=0, concat_axis=0, til...]
    all_to_all x2 -> x1, waiting for transfers between devices: 17.9 us -> 0.01 us  [body(): lax.all_to_all(outgoing, ('flow', 'grp'), split_axis=0, concat_axis=0, ti...]
    all_to_all x2 -> x1, starting transfers between devices: 24.3 us -> 11.5 us  [body(): lax.all_to_all(outgoing, ('flow', 'grp'), split_axis=0, concat_axis=0, ti...]
    pallas_call x1 -> x3, Pallas kernels: 1.68 us -> 7.62 us  [the longest x1 2.93 us: dg_faces(): pl.pallas_call(dg_faces_kernel, out_shape=(jax.ShapeDtypeStruct((arrived....]
    all_to_all x3 -> x4, local copies, waits for them, and re-layouts: 1.82 us -> 5.81 us  [the longest x2 3.31 us: body(): lax.all_to_all(outgoing, ('flow', 'grp'), split_axis=0, concat_axis=0, ti...]
    scatter x3 -> x0, local copies, waits for them, and re-layouts: 3.51 us -> none  [the longest x2 2.37 us: body(): jnp.zeros((512, elem_count), jnp.float32).at[:, target]]
    unnamed x37, local copies, waits for them, and re-layouts: 4.04 us -> 7.01 us
    ppermute x2, starting transfers between devices: 4.99 us -> 7.21 us  [exchange_faces(): lax.ppermute(sy4, 'grp', up_g)]
  transfers between devices with their start and end apart: 14 -> 13, of which waited for: 5 -> 4; matrix products, arithmetic and copies ran while one was open for 3% -> 1% of each run, Pallas kernels for 1% -> 3%
where the time goes in v5:
time: 129 us; the launch traced here: 128 us
  starting transfers between devices  44.8 us (35%)
  blocking collectives  27.4 us (21%)
  Pallas kernels  27.2 us (21%)
  local copies, waits for them, and re-layouts  17.3 us (13%)
  waiting for transfers between devices  7.81 us (6%)
  matrix products  2.23 us (2%)
    all_to_all x1, blocking collectives, body(): lax.all_to_all(leaving, ('flow', 'grp'), split_axis=0, concat_axis=0, til...  27.4 us
    pallas_call x2, Pallas kernels, dg_step(): pl.pallas_call(lambda *refs: dg_step_kernel(want_faces, xoff, yoff, row_l...  11.6 us
    all_to_all x1, starting transfers between devices, body(): lax.all_to_all(outgoing, ('flow', 'grp'), split_axis=0, concat_axis=0, ti...  11.5 us
    ppermute x2, starting transfers between devices, exchange_faces(): lax.ppermute(sx4, 'flow', up_f)  8.62 us
    ppermute x2, starting transfers between devices, exchange_faces(): lax.ppermute(sy4, 'grp', up_g)  7.21 us
    ppermute x2, waiting for transfers between devices, exchange_faces(): lax.ppermute(sy0, 'grp', down_g)  7.18 us
    unnamed x37, local copies, waits for them, and re-layouts  7.01 us
    pallas_call x1, Pallas kernels, les_section_last(): pl.pallas_call(lambda *refs: les_kernel(1, *refs), out_shape=(jax.ShapeDt...  4.03 us
  transfers between devices with their start and end apart: 13, of which 4 were waited for; matrix products, arithmetic and copies ran while one was open for 1% of the time, Pallas kernels for 3%

profile of v5, /device:TPU:1, one launch (start us, length us, event | category | flops | bytes accessed | tf_op | source)
XLA Modules:
  0.0 127.7 jit_solution(2239538641643745573)
XLA Ops:
  0.7 1.7 %copy.22.acoustic_ref = f32[4,125,128]{2,1,0:T(8,128)} copy(f32[4,125,128]{2,0,1:T(4,128)} %param.12) | data formatting | bytes 512000 | tf_op args[3]
  2.4 2.3 %shard_map.105 = f32[256,512]{1,0:T(8,128)} custom-call(f32[4,125,128]{2,1,0:T(8,128)} %copy.22.acoustic_ref, s32[1,128]{1,0:T(1,128)} %place_ref.3), custom_call_target="tpu_custom_call" | custom-call | tf_op jit(solution)/shard_map/pallas_call | solution.py:388
  4.7 2.2 %all_to_all.14 = f32[128,2,512]{2,1,0:T(2,128)} reshape(f32[256,512]{1,0:T(8,128)} %shard_map.105) | data formatting | bytes 1048576 | tf_op jit(solution)/shard_map/all_to_all | solution.py:447
  6.9 11.5 %all-to-all-start = ((f32[128,2,512]{2,1,0:T(2,128)}), f32[128,2,512]{2,1,0:T(2,128)S(1)}, u32[]{:S(2)}, u32[]{:S(2)}) async-start(f32[128,2,512]{2,1,0:T(2,128)} %all_to_all.14), calls=%async_computation | async-start | bytes 1048576 | tf_op jit(solution)/shard_map/all_to_all | solution.py:447
  18.4 3.0 %collective-permute-start.1 = (f32[4,32,256]{2,1,0:T(8,128)S(1)}, f32[4,32,256]{2,1,0:T(8,128)S(1)}, u32[]{:S(2)}, u32[]{:S(2)}) collective-permute-start(f32[4,32,256]{2,1,0:T(8,128)S(1)} %get-tuple-element.36), channel_id=1, source_target_pairs={{4,0},{8,4},{12,8},{16,12},{20,16},{24,20},{28,24},{32,28},{36,32}... | collective-permute-start | bytes 393224 | tf_op jit(solution)/shard_map/ppermute | solution.py:230
  21.4 2.6 %collective-permute-start = (f32[4,32,256]{2,1,0:T(8,128)S(1)}, f32[4,32,256]{2,1,0:T(8,128)S(1)}, u32[]{:S(2)}, u32[]{:S(2)}) collective-permute-start(f32[4,32,256]{2,1,0:T(8,128)S(1)} %get-tuple-element.37), channel_id=1, source_target_pairs={{0,4},{4,8},{8,12},{12,16},{16,20},{20,24},{24,28},{28,32},{32,36}... | collective-permute-start | bytes 393224 | tf_op jit(solution)/shard_map/ppermute | solution.py:229
  24.1 1.3 %collective-permute-start.3 = (f32[4,8,1,256]{3,2,1,0:T(1,128)S(1)}, f32[4,8,1,256]{3,2,1,0:T(1,128)S(1)}, u32[]{:S(2)}, u32[]{:S(2)}) collective-permute-start(f32[4,8,1,256]{3,2,1,0:T(1,128)S(1)} %get-tuple-element.34), channel_id=1, source_target_pairs={{1,0},{2,1},{3,2},{5,4},{6,5},{7,6},{9,8},{10,9},{11,10},{13,12},{... | collective-permute-start | bytes 98312 | tf_op jit(solution)/shard_map/ppermute | solution.py:232
  25.4 4.0 %collective-permute-start.2 = (f32[4,8,1,256]{3,2,1,0:T(1,128)S(1)}, f32[4,8,1,256]{3,2,1,0:T(1,128)S(1)}, u32[]{:S(2)}, u32[]{:S(2)}) collective-permute-start(f32[4,8,1,256]{3,2,1,0:T(1,128)S(1)} %get-tuple-element.35), channel_id=1, source_target_pairs={{0,1},{1,2},{2,3},{4,5},{5,6},{6,7},{8,9},{9,10},{10,11},{12,13},{... | collective-permute-start | bytes 98312 | tf_op jit(solution)/shard_map/ppermute | solution.py:231
  31.7 4.0 %shard_map.104.vel_ref.refs_0_ = f32[3,8,32,256]{3,2,1,0:T(8,128)} custom-call(f32[3,8,32,256]{3,2,1,0:T(8,128)} %refs_0_.1, f32[8,32,256]{2,1,0:T(8,128)} %refs_1_.3, f32[4,32,256]{2,1,0:T(8,128)} %copy-done.3, f32[4,32,256]{2,1,0:T(8,128)} %copy-done.2, f32[4,8,1,256]{3,2,1,0:T(1,128)} %copy-done.9, f32[4,8,1,256]{3,2,1,0:T(1,128)} %copy-done.8, ...), custom_call_target="tpu_custom_call" | custom-call | tf_op jit(solution)/shard_map/pallas_call | solution.py:208
  35.7 1.2 all_to_all.16.arrived_ref
  36.9 2.9 %shard_map.106 = (f32[512,128]{1,0:T(8,128)}, f32[296,128]{1,0:T(8,128)}, f32[296,128]{1,0:T(8,128)}, f32[152,128]{1,0:T(8,128)}, f32[152,128]{1,0:T(8,128)}) custom-call(f32[256,512]{1,0:T(8,128)} %all_to_all.16.arrived_ref, s32[256,1]{1,0:T(8,128)} %reshape.31.send_ref.refs_8_, f32[3,8,32,256]{3,2,1,0:T(8,128)} %shard_map.104.vel_ref.refs_0_), custom_call_target="tpu_custom_call" | custom-call | tf_op jit(solution)/shard_map/pallas_call | solution.py:380
  39.8 3.6 %collective-permute-start.4 = (f32[296,128]{1,0:T(8,128)}, f32[296,128]{1,0:T(8,128)S(1)}, u32[]{:S(2)}, u32[]{:S(2)}) collective-permute-start(f32[296,128]{1,0:T(8,128)} %get-tuple-element.15), channel_id=1, source_target_pairs={{0,4},{4,8},{8,12},{12,16},{16,20},{20,24},{24,28},{28,32},{32,36}... | collective-permute-start | bytes 454664 | tf_op jit(solution)/shard_map/ppermute | solution.py:432
  43.4 1.9 %collective-permute-start.5 = (f32[296,128]{1,0:T(8,128)}, f32[296,128]{1,0:T(8,128)S(1)}, u32[]{:S(2)}, u32[]{:S(2)}) collective-permute-start(f32[296,128]{1,0:T(8,128)} %get-tuple-element.16), channel_id=1, source_target_pairs={{4,0},{8,4},{12,8},{16,12},{20,16},{24,20},{28,24},{32,28},{36,32}... | collective-permute-start | bytes 454664 | tf_op jit(solution)/shard_map/ppermute | solution.py:433
  45.3 4.1 %collective-permute-start.6 = (f32[152,128]{1,0:T(8,128)}, f32[152,128]{1,0:T(8,128)S(1)}, u32[]{:S(2)}, u32[]{:S(2)}) collective-permute-start(f32[152,128]{1,0:T(8,128)} %get-tuple-element.17), channel_id=1, source_target_pairs={{0,1},{1,2},{2,3},{4,5},{5,6},{6,7},{8,9},{9,10},{10,11},{12,13},{... | collective-permute-start | bytes 233480 | tf_op jit(solution)/shard_map/ppermute | solution.py:434
  49.4 1.3 %collective-permute-start.7 = (f32[152,128]{1,0:T(8,128)}, f32[152,128]{1,0:T(8,128)S(1)}, u32[]{:S(2)}, u32[]{:S(2)}) collective-permute-start(f32[152,128]{1,0:T(8,128)} %get-tuple-element.18), channel_id=1, source_target_pairs={{1,0},{2,1},{3,2},{5,4},{6,5},{7,6},{9,8},{10,9},{11,10},{13,12},{... | collective-permute-start | bytes 233480 | tf_op jit(solution)/shard_map/ppermute | solution.py:435
  51.2 3.6 %collective-permute-done.7.refs_5_ = f32[152,128]{1,0:T(8,128)S(1)} collective-permute-done((f32[152,128]{1,0:T(8,128)}, f32[152,128]{1,0:T(8,128)S(1)}, u32[]{:S(2)}, u32[]{:S(2)}) %collective-permute-start.7) | collective-permute-done | bytes 77856 | tf_op jit(solution)/shard_map/ppermute | solution.py:435
  56.1 4.0 %shard_map.107 = (f32[3,8,32,256]{3,2,1,0:T(8,128)}, bf16[3,8,32,256]{3,2,1,0:T(8,128)(2,1)}) custom-call(f32[3,8,32,256]{3,2,1,0:T(8,128)} %shard_map.104.vel_ref.refs_0_, f32[8,32,256]{2,1,0:T(8,128)} %refs_1_.3, f32[296,128]{1,0:T(8,128)} %copy-done.4, f32[296,128]{1,0:T(8,128)} %copy-done.5, f32[152,128]{1,0:T(8,128)} %copy-done.6, ...), custom_call_target="tpu_custom_call" | custom-call | tf_op jit(solution)/shard_map/pallas_call | solution.py:215
  60.2 1.3 convolution_convert_fusion
  62.1 2.0 %copy.31 = bf16[3,1,8,4,8,8,32]{6,3,0,5,4,2,1:T(4,128)(2,1)S(1)} copy(bf16[3,1,8,4,8,8,32]{6,5,4,3,2,0,1:T(8,128)(2,1)S(1)} %reshape.27) | data formatting | bytes 786432 | tf_op jit(solution)/shard_map/reshape | solution.py:246
  65.2 1.0 fusion
  66.1 5.2 %shard_map.108 = (f32[512,128]{1,0:T(8,128)}, f32[104,128]{1,0:T(8,128)}, f32[104,128]{1,0:T(8,128)}, f32[104,32]{1,0:T(8,128)}, f32[104,32]{1,0:T(8,128)}) custom-call(f32[512,128]{1,0:T(8,128)} %get-tuple-element.20.refs_0_, f32[384,128]{1,0:T(8,128)} %bitcast.25, f32[296,128]{1,0:T(8,128)} %copy-done.4, f32[296,128]{1,0:T(8,128)} %copy-done.5, ...), custom_call_target="tpu_custom_call" | custom-call | tf_op jit(solution)/shard_map/pallas_call | solution.py:411
  71.3 5.1 %collective-permute-start.8 = (f32[104,128]{1,0:T(8,128)}, f32[104,128]{1,0:T(8,128)S(1)}, u32[]{:S(2)}, u32[]{:S(2)}) collective-permute-start(f32[104,128]{1,0:T(8,128)} %get-tuple-element.23), channel_id=1, source_target_pairs={{0,4},{4,8},{8,12},{12,16},{16,20},{20,24},{24,28},{28,32},{32,36}... | collective-permute-start | bytes 159752 | tf_op jit(solution)/shard_map/ppermute | solution.py:432
  76.4 1.9 %collective-permute-start.9 = (f32[104,128]{1,0:T(8,128)}, f32[104,128]{1,0:T(8,128)S(1)}, u32[]{:S(2)}, u32[]{:S(2)}) collective-permute-start(f32[104,128]{1,0:T(8,128)} %get-tuple-element.24), channel_id=1, source_target_pairs={{4,0},{8,4},{12,8},{16,12},{20,16},{24,20},{28,24},{32,28},{36,32}... | collective-permute-start | bytes 159752 | tf_op jit(solution)/shard_map/ppermute | solution.py:433
  78.3 3.1 %collective-permute-start.10 = (f32[104,32]{1,0:T(8,128)}, f32[104,32]{1,0:T(8,128)S(1)}, u32[]{:S(2)}, u32[]{:S(2)}) collective-permute-start(f32[104,32]{1,0:T(8,128)} %get-tuple-element.25), channel_id=1, source_target_pairs={{0,1},{1,2},{2,3},{4,5},{5,6},{6,7},{8,9},{9,10},{10,11},{12,13},{... | collective-permute-start | bytes 39944 | tf_op jit(solution)/shard_map/ppermute | solution.py:434
  81.4 1.5 %collective-permute-start.11 = (f32[104,32]{1,0:T(8,128)}, f32[104,32]{1,0:T(8,128)S(1)}, u32[]{:S(2)}, u32[]{:S(2)}) collective-permute-start(f32[104,32]{1,0:T(8,128)} %get-tuple-element.26), channel_id=1, source_target_pairs={{1,0},{2,1},{3,2},{5,4},{6,5},{7,6},{9,8},{10,9},{11,10},{13,12},{... | collective-permute-start | bytes 39944 | tf_op jit(solution)/shard_map/ppermute | solution.py:435
  83.0 3.6 %collective-permute-done.11.refs_5_ = f32[104,32]{1,0:T(8,128)S(1)} collective-permute-done((f32[104,32]{1,0:T(8,128)}, f32[104,32]{1,0:T(8,128)S(1)}, u32[]{:S(2)}, u32[]{:S(2)}) %collective-permute-start.11) | collective-permute-done | bytes 13344 | tf_op jit(solution)/shard_map/ppermute | solution.py:435
  87.2 6.4 %shard_map.109 = (f32[512,128]{1,0:T(8,128)}, f32[256,512]{1,0:T(8,128)}) custom-call(f32[512,128]{1,0:T(8,128)} %get-tuple-element.22.refs_0_, f32[384,128]{1,0:T(8,128)} %bitcast.26, f32[104,128]{1,0:T(8,128)} %copy-done.12, f32[104,128]{1,0:T(8,128)} %copy-done.13, f32[104,32]{1,0:T(8,128)} %copy-done.14, f32[104,32]{1,0:T(8,128)} %copy-done.15, ...), custom_call_target="tpu_custom_call" | custom-call | tf_op jit(solution)/shard_map/pallas_call | solution.py:411
  93.6 1.3 %all_to_all.17 = f32[128,2,512]{2,1,0:T(2,128)S(1)} reshape(f32[256,512]{1,0:T(8,128)} %get-tuple-element.27) | data formatting | bytes 1048576 | tf_op jit(solution)/shard_map/all_to_all | solution.py:464
  94.9 27.4 %all_to_all.22 = f32[128,2,512]{2,1,0:T(2,128)S(1)} all-to-all(f32[128,2,512]{2,1,0:T(2,128)S(1)} %all_to_all.17), channel_id=1, replica_groups=mesh['flow'=32,'grp'=4] {'flow','grp'}, dimensions={0} | all-to-all | bytes 1048576 | tf_op jit(solution)/shard_map/all_to_all | solution.py:464
  122.4 1.2 all_to_all.19.arrived_ref
  123.5 2.4 %shard_map.110 = f32[4,125,128]{2,1,0:T(8,128)} custom-call(f32[256,512]{1,0:T(8,128)} %all_to_all.19.arrived_ref, s32[1,128]{1,0:T(1,128)} %place_ref.3), custom_call_target="tpu_custom_call" | custom-call | tf_op jit(solution)/shard_map/pallas_call | solution.py:397
  125.9 1.8 %copy.29 = f32[4,125,128]{2,0,1:T(4,128)} copy(f32[4,125,128]{2,1,0:T(8,128)} %shard_map.110) | data formatting | bytes 512000
  (52 shorter events, 6.6 us)
Async XLA Ops:
  0.6 17.8 %copy-start = (f32[3,8,32,256]{3,2,1,0:T(8,128)S(1)}, f32[3,8,32,256]{3,2,1,0:T(8,128)}, u32[]{:S(2)}) copy-start(f32[3,8,32,256]{3,2,1,0:T(8,128)} %refs_0_.1) | copy-start | bytes 2359300
  0.6 17.8 %copy-start.1 = (f32[8,32,256]{2,1,0:T(8,128)S(1)}, f32[8,32,256]{2,1,0:T(8,128)}, u32[]{:S(2)}) copy-start(f32[8,32,256]{2,1,0:T(8,128)} %refs_1_.3) | copy-start | bytes 786436
  6.9 22.5 %copy-start.16 = (s32[1,128,2]{1,2,0:T(2,128)S(1)}, s32[1,128,2]{1,2,0:T(2,128)}, u32[]{:S(2)}) copy-start(s32[1,128,2]{1,2,0:T(2,128)} %param.13) | copy-start | bytes 3076
  6.9 28.8 %all-to-all-start = ((f32[128,2,512]{2,1,0:T(2,128)}), f32[128,2,512]{2,1,0:T(2,128)S(1)}, u32[]{:S(2)}, u32[]{:S(2)}) async-start(f32[128,2,512]{2,1,0:T(2,128)} %all_to_all.14), calls=%async_computation | async-start | bytes 1048576 | tf_op jit(solution)/shard_map/all_to_all | solution.py:447
  18.4 12.0 %collective-permute-start.1 = (f32[4,32,256]{2,1,0:T(8,128)S(1)}, f32[4,32,256]{2,1,0:T(8,128)S(1)}, u32[]{:S(2)}, u32[]{:S(2)}) collective-permute-start(f32[4,32,256]{2,1,0:T(8,128)S(1)} %get-tuple-element.36), channel_id=1, source_target_pairs={{4,0},{8,4},{12,8},{16,12},{20,16},{24,20},{28,24},{32,28},{36,32}... | collective-permute-start | bytes 393224 | tf_op jit(solution)/shard_map/ppermute | solution.py:230
  21.4 9.0 %collective-permute-start = (f32[4,32,256]{2,1,0:T(8,128)S(1)}, f32[4,32,256]{2,1,0:T(8,128)S(1)}, u32[]{:S(2)}, u32[]{:S(2)}) collective-permute-start(f32[4,32,256]{2,1,0:T(8,128)S(1)} %get-tuple-element.37), channel_id=1, source_target_pairs={{0,4},{4,8},{8,12},{12,16},{16,20},{20,24},{24,28},{28,32},{32,36}... | collective-permute-start | bytes 393224 | tf_op jit(solution)/shard_map/ppermute | solution.py:229
  24.1 6.2 %collective-permute-start.3 = (f32[4,8,1,256]{3,2,1,0:T(1,128)S(1)}, f32[4,8,1,256]{3,2,1,0:T(1,128)S(1)}, u32[]{:S(2)}, u32[]{:S(2)}) collective-permute-start(f32[4,8,1,256]{3,2,1,0:T(1,128)S(1)} %get-tuple-element.34), channel_id=1, source_target_pairs={{1,0},{2,1},{3,2},{5,4},{6,5},{7,6},{9,8},{10,9},{11,10},{13,12},{... | collective-permute-start | bytes 98312 | tf_op jit(solution)/shard_map/ppermute | solution.py:232
  25.4 5.0 %collective-permute-start.2 = (f32[4,8,1,256]{3,2,1,0:T(1,128)S(1)}, f32[4,8,1,256]{3,2,1,0:T(1,128)S(1)}, u32[]{:S(2)}, u32[]{:S(2)}) collective-permute-start(f32[4,8,1,256]{3,2,1,0:T(1,128)S(1)} %get-tuple-element.35), channel_id=1, source_target_pairs={{0,1},{1,2},{2,3},{4,5},{5,6},{6,7},{8,9},{9,10},{10,11},{12,13},{... | collective-permute-start | bytes 98312 | tf_op jit(solution)/shard_map/ppermute | solution.py:231
  30.3 0.6 copy-start.8
  30.4 0.6 copy-start.9
  30.4 0.7 copy-start.2
  31.1 0.7 copy-start.3
  36.9 23.3 %copy-start.10 = (bf16[256,256]{1,0:T(8,128)(2,1)S(1)}, bf16[256,256]{1,0:T(8,128)(2,1)}, u32[]{:S(2)}) copy-start(bf16[256,256]{1,0:T(8,128)(2,1)} %constant.11.clone) | copy-start | bytes 393220
  39.8 15.0 %collective-permute-start.4 = (f32[296,128]{1,0:T(8,128)}, f32[296,128]{1,0:T(8,128)S(1)}, u32[]{:S(2)}, u32[]{:S(2)}) collective-permute-start(f32[296,128]{1,0:T(8,128)} %get-tuple-element.15), channel_id=1, source_target_pairs={{0,4},{4,8},{8,12},{12,16},{16,20},{20,24},{24,28},{28,32},{32,36}... | collective-permute-start | bytes 454664 | tf_op jit(solution)/shard_map/ppermute | solution.py:432
  43.4 11.4 %collective-permute-start.5 = (f32[296,128]{1,0:T(8,128)}, f32[296,128]{1,0:T(8,128)S(1)}, u32[]{:S(2)}, u32[]{:S(2)}) collective-permute-start(f32[296,128]{1,0:T(8,128)} %get-tuple-element.16), channel_id=1, source_target_pairs={{4,0},{8,4},{12,8},{16,12},{20,16},{24,20},{28,24},{32,28},{36,32}... | collective-permute-start | bytes 454664 | tf_op jit(solution)/shard_map/ppermute | solution.py:433
  45.3 5.9 %collective-permute-start.6 = (f32[152,128]{1,0:T(8,128)}, f32[152,128]{1,0:T(8,128)S(1)}, u32[]{:S(2)}, u32[]{:S(2)}) collective-permute-start(f32[152,128]{1,0:T(8,128)} %get-tuple-element.17), channel_id=1, source_target_pairs={{0,1},{1,2},{2,3},{4,5},{5,6},{6,7},{8,9},{9,10},{10,11},{12,13},{... | collective-permute-start | bytes 233480 | tf_op jit(solution)/shard_map/ppermute | solution.py:434
  49.4 5.4 %collective-permute-start.7 = (f32[152,128]{1,0:T(8,128)}, f32[152,128]{1,0:T(8,128)S(1)}, u32[]{:S(2)}, u32[]{:S(2)}) collective-permute-start(f32[152,128]{1,0:T(8,128)} %get-tuple-element.18), channel_id=1, source_target_pairs={{1,0},{2,1},{3,2},{5,4},{6,5},{7,6},{9,8},{10,9},{11,10},{13,12},{... | collective-permute-start | bytes 233480 | tf_op jit(solution)/shard_map/ppermute | solution.py:435
  51.2 3.6 %copy-start.6 = (f32[152,128]{1,0:T(8,128)}, f32[152,128]{1,0:T(8,128)S(1)}, u32[]{:S(2)}) copy-start(f32[152,128]{1,0:T(8,128)S(1)} %collective-permute-done.6.refs_4_) | copy-start | bytes 233476
  54.8 0.6 copy-start.7
  54.8 0.7 copy-start.4
  55.5 0.7 copy-start.5
  64.1 1.1 copy-start.11
  71.3 15.2 %collective-permute-start.8 = (f32[104,128]{1,0:T(8,128)}, f32[104,128]{1,0:T(8,128)S(1)}, u32[]{:S(2)}, u32[]{:S(2)}) collective-permute-start(f32[104,128]{1,0:T(8,128)} %get-tuple-element.23), channel_id=1, source_target_pairs={{0,4},{4,8},{8,12},{12,16},{16,20},{20,24},{24,28},{28,32},{32,36}... | collective-permute-start | bytes 159752 | tf_op jit(solution)/shard_map/ppermute | solution.py:432
  76.4 10.1 %collective-permute-start.9 = (f32[104,128]{1,0:T(8,128)}, f32[104,128]{1,0:T(8,128)S(1)}, u32[]{:S(2)}, u32[]{:S(2)}) collective-permute-start(f32[104,128]{1,0:T(8,128)} %get-tuple-element.24), channel_id=1, source_target_pairs={{4,0},{8,4},{12,8},{16,12},{20,16},{24,20},{28,24},{32,28},{36,32}... | collective-permute-start | bytes 159752 | tf_op jit(solution)/shard_map/ppermute | solution.py:433
  78.3 4.6 %collective-permute-start.10 = (f32[104,32]{1,0:T(8,128)}, f32[104,32]{1,0:T(8,128)S(1)}, u32[]{:S(2)}, u32[]{:S(2)}) collective-permute-start(f32[104,32]{1,0:T(8,128)} %get-tuple-element.25), channel_id=1, source_target_pairs={{0,1},{1,2},{2,3},{4,5},{5,6},{6,7},{8,9},{9,10},{10,11},{12,13},{... | collective-permute-start | bytes 39944 | tf_op jit(solution)/shard_map/ppermute | solution.py:434
  81.4 5.1 %collective-permute-start.11 = (f32[104,32]{1,0:T(8,128)}, f32[104,32]{1,0:T(8,128)S(1)}, u32[]{:S(2)}, u32[]{:S(2)}) collective-permute-start(f32[104,32]{1,0:T(8,128)} %get-tuple-element.26), channel_id=1, source_target_pairs={{1,0},{2,1},{3,2},{5,4},{6,5},{7,6},{9,8},{10,9},{11,10},{13,12},{... | collective-permute-start | bytes 39944 | tf_op jit(solution)/shard_map/ppermute | solution.py:435
  83.0 3.6 %copy-start.14 = (f32[104,32]{1,0:T(8,128)}, f32[104,32]{1,0:T(8,128)S(1)}, u32[]{:S(2)}) copy-start(f32[104,32]{1,0:T(8,128)S(1)} %collective-permute-done.10.refs_4_) | copy-start | bytes 39940
  86.5 0.6 copy-start.15
  86.5 0.6 copy-start.12
  86.5 0.7 copy-start.13

commit v6 on v5

--- a/solution.py
+++ b/solution.py
@@ -280,31 +280,8 @@
     return jnp.where(lax.broadcasted_iota(jnp.int32, shape, axis) == ids, 1.0, 0.0).astype(jnp.float32)
 
 
-def route_out_kernel(acoustic_ref, place_ref, out_ref, pad_ref):
-    comps, nodes, elems = acoustic_ref.shape
-    pad_ref[...] = jnp.zeros(pad_ref.shape, jnp.float32)
-    for comp in range(comps):
-        pad_ref[pl.ds(comp * 128, nodes), :] = acoustic_ref[comp]
-    slots = out_ref.shape[0]
-    place_hot = one_hot((slots, elems), place_ref[...], 0)
-    out_ref[...] = lax.dot_general(place_hot, pad_ref[...], (((1,), (1,)), ((), ())),
-                                   precision=HIGH, preferred_element_type=jnp.float32)
-
-
-def route_in_kernel(arrived_ref, place_ref, out_ref):
-    slots, rows = arrived_ref.shape
-    comps, nodes, elems = out_ref.shape
-    place_hot = one_hot((slots, elems), place_ref[...], 0)
-    back = jnp.dot(arrived_ref[...].T, place_hot, precision=HIGH, preferred_element_type=jnp.float32)
-    for comp in range(comps):
-        out_ref[comp] = back[comp * 128:comp * 128 + nodes]
-
-
-def dg_faces_kernel(arrived_ref, send_ref, vel_ref, state_ref, mxup_ref, mxdn_ref, myup_ref, mydn_ref, face_ref):
-    slots, rows = arrived_ref.shape
+def dg_faces_kernel(state_ref, vel_ref, mxup_ref, mxdn_ref, myup_ref, mydn_ref, face_ref):
     elems = state_ref.shape[1]
-    home_hot = one_hot((slots, elems), send_ref[...], 1)
-    state_ref[...] = jnp.dot(arrived_ref[...].T, home_hot, precision=HIGH, preferred_element_type=jnp.float32)
     face_ref[...] = jnp.zeros(face_ref.shape, jnp.float32)
     extract_faces(state_ref, face_ref)
     size_x, size_y, size_z = vel_ref.shape[1], vel_ref.shape[2], vel_ref.shape[3]
@@ -332,7 +309,7 @@
     if want_faces:
         sx0_ref, sx4_ref, sy0_ref, sy4_ref, face_ref, oth_ref, pad_ref = rest
     else:
-        leave_ref, face_ref, oth_ref, pad_ref = rest
+        face_ref, oth_ref, pad_ref = rest
     elems = state_ref.shape[1]
     lane = lax.broadcasted_iota(jnp.int32, (FACE_ROWS, elems), 1)
     ez = lane % row_len
@@ -359,11 +336,6 @@
     if want_faces:
         extract_faces(out_ref, face_ref)
         send_faces(face_ref, sx0_ref, sx4_ref, sy0_ref, sy4_ref, row_len)
-    else:
-        slots = leave_ref.shape[0]
-        home_hot = one_hot((slots, elems), send_ref[...], 1)
-        leave_ref[...] = lax.dot_general(home_hot, out_ref[...], (((1,), (1,)), ((), ())),
-                                         precision=HIGH, preferred_element_type=jnp.float32)
 
 
 def face_shapes(elems, row_len):
@@ -372,32 +344,16 @@
     return [big, big, small, small]
 
 
-def dg_faces(arrived, sending, vel):
-    elems = vel.shape[2] // 8 * (vel.shape[3] // 8) * (vel.shape[1] // 8)
+def dg_faces(state, vel):
+    elems = state.shape[1]
     size_x, size_y, size_z = vel.shape[1], vel.shape[2], vel.shape[3]
     xbuf = jax.ShapeDtypeStruct((3 * 2 * size_y + FACE_ROWS, size_z // 2), jnp.float32)
     ybuf = jax.ShapeDtypeStruct((3 * 2 * size_x + FACE_ROWS, size_z // 2), jnp.float32)
     return pl.pallas_call(
         dg_faces_kernel,
-        out_shape=(jax.ShapeDtypeStruct((arrived.shape[1], elems), jnp.float32), xbuf, xbuf, ybuf, ybuf),
+        out_shape=(xbuf, xbuf, ybuf, ybuf),
         scratch_shapes=[pltpu.VMEM((6, FACE_ROWS, elems), jnp.float32)],
-    )(arrived, sending, vel)
-
-
-def route_out(acoustic, placing, slots):
-    return pl.pallas_call(
-        route_out_kernel,
-        out_shape=jax.ShapeDtypeStruct((slots, 512), jnp.float32),
-        scratch_shapes=[pltpu.VMEM((512, acoustic.shape[2]), jnp.float32)],
-    )(acoustic, placing)
-
-
-def route_in(returned, placing, nodes):
-    elems = placing.shape[1]
-    return pl.pallas_call(
-        route_in_kernel,
-        out_shape=jax.ShapeDtypeStruct((4, nodes, elems), jnp.float32),
-    )(returned, placing)
+    )(state, vel)
 
 
 def dg_step(state, src, recv, own_mat, other_mat, want_faces, row_len, xoff=0, yoff=0, sending=None):
@@ -406,8 +362,6 @@
     extra = [sending]
     if want_faces:
         out_shape += face_shapes(elems, row_len)
-    else:
-        out_shape.append(jax.ShapeDtypeStruct((sending.shape[0], state.shape[0]), jnp.float32))
     res = pl.pallas_call(
         lambda *refs: dg_step_kernel(want_faces, xoff, yoff, row_len, *refs),
         out_shape=tuple(out_shape),
@@ -441,28 +395,36 @@
     flow_size = lax.axis_size("flow")
     grp_size = lax.axis_size("grp")
     slot_cap = route_send.shape[2]
+    elem_count = acoustic_state.shape[2]
     total_slots = flow_size * grp_size * slot_cap
-    sending = route_send.reshape(total_slots, 1)
-    outgoing = route_out(acoustic_state, route_place, total_slots)
-    arrived = lax.all_to_all(outgoing, ("flow", "grp"), split_axis=0, concat_axis=0, tiled=True)
+    placing = route_place.reshape(-1)
+    padded_state = jnp.pad(acoustic_state, ((0, 0), (0, 3), (0, 0))).reshape(512, elem_count)
+    outgoing = jnp.zeros((512, total_slots), jnp.float32).at[:, placing].set(padded_state)
+    arrived = lax.all_to_all(outgoing, ("flow", "grp"), split_axis=1, concat_axis=1, tiled=True)
+    sending = route_send.reshape(-1)
+    filled = sending >= 0
+    target = jnp.where(filled, sending, elem_count)
     vel = les_section_first(velocity, eddy_visc, joint)
+    state = jnp.zeros((512, elem_count), jnp.float32).at[:, target].set(arrived, mode="drop")
 
     row_len = velocity.shape[3] // 8
     own_np, other_np = dg_matrices()
     own_mat = jnp.asarray(own_np)
     other_mat = jnp.asarray(other_np)
-    state, mxup, mxdn, myup, mydn = dg_faces(arrived, sending, vel)
+    mxup, mxdn, myup, mydn = dg_faces(state, vel)
     merged = exchange_faces((mxdn, mxup, mydn, myup))
     vel, lamb = les_section_last(vel, eddy_visc, merged, joint)
     source = project(lamb, projection)
     xoff = 3 * 2 * velocity.shape[2]
     yoff = 3 * 2 * velocity.shape[1]
-    res = dg_step(state, source, merged, own_mat, other_mat, True, row_len, xoff, yoff, sending=sending)
+    slot_col = sending.reshape(-1, 1)
+    res = dg_step(state, source, merged, own_mat, other_mat, True, row_len, xoff, yoff, sending=slot_col)
     state = res[0]
     recv = exchange_faces(res[1:])
-    leaving = dg_step(state, source, recv, own_mat, other_mat, False, row_len, sending=sending)[1]
-    returned = lax.all_to_all(leaving, ("flow", "grp"), split_axis=0, concat_axis=0, tiled=True)
-    acoustic_out = route_in(returned, route_place, acoustic_state.shape[1])
+    state = dg_step(state, source, recv, own_mat, other_mat, False, row_len, sending=slot_col)[0]
+    leaving = jnp.where(filled[None, :], state[:, jnp.where(filled, sending, 0)], 0.0)
+    returned = lax.all_to_all(leaving, ("flow", "grp"), split_axis=1, concat_axis=1, tiled=True)
+    acoustic_out = returned[:, placing].reshape(4, 128, elem_count)[:, :125]
     return (vel, acoustic_out)
 
 

time: 129 us -> 125 us (0.969)
  blocking collectives: 27.4 us -> 0 us
  waiting for transfers between devices: 7.81 us -> 24.2 us
  starting transfers between devices: 44.8 us -> 55.9 us
  Pallas kernels: 27.2 us -> 20.2 us
  other arithmetic: 0.07 us -> 1.85 us
  local copies, waits for them, and re-layouts: 17.3 us -> 18.6 us
    all_to_all x1 -> x0, blocking collectives: 27.4 us -> none  [body(): lax.all_to_all(leaving, ('flow', 'grp'), split_axis=0, concat_axis=0, til...]
    all_to_all x1 -> x2, waiting for transfers between devices: 0.01 us -> 14.1 us  [the longest x1 14.1 us: body(): lax.all_to_all(leaving, ('flow', 'grp'), split_axis=1, concat_axis=1, til...]
    all_to_all x1 -> x2, starting transfers between devices: 11.5 us -> 23.6 us  [the longest x1 12.1 us: body(): lax.all_to_all(leaving, ('flow', 'grp'), split_axis=1, concat_axis=1, til...]
    pallas_call x3 -> x1, Pallas kernels: 7.62 us -> 2.05 us  [dg_faces(): pl.pallas_call(dg_faces_kernel, out_shape=(xbuf, xbuf, ybuf, ybuf), scrat...]
    all_to_all x4 -> x3, local copies, waits for them, and re-layouts: 5.81 us -> 1.82 us  [the longest x2 1.46 us: body(): lax.all_to_all(outgoing, ('flow', 'grp'), split_axis=1, concat_axis=1, ti...]
    scatter x0 -> x3, local copies, waits for them, and re-layouts: none -> 3.49 us  [the longest x2 2.36 us: body(): jnp.zeros((512, elem_count), jnp.float32).at[:, target]]
    ppermute x1, waiting for transfers between devices: 0.01 us -> 3.35 us  [halos(): lax.ppermute(lax.slice_in_dim(field, 0, 1, axis=lead + 1), 'grp', down_g)]
    gather x0 -> x3, local copies, waits for them, and re-layouts: none -> 2.03 us  [the longest x2 1.28 us: body(): state[:, jnp.where(filled, sending, 0)]]
  transfers between devices with their start and end apart: 13 -> 14, of which waited for: 4 -> 4; matrix products, arithmetic and copies ran while one was open for 1% -> 1% of each run, Pallas kernels for 3% -> 3%
where the time goes in v6:
time: 125 us; the launch traced here: 124 us
  starting transfers between devices  55.9 us (45%)
  waiting for transfers between devices  24.2 us (19%)
  Pallas kernels  20.2 us (16%)
  local copies, waits for them, and re-layouts  18.6 us (15%)
  matrix products  2.23 us (2%)
  other arithmetic  1.85 us (1%)
    all_to_all x1, waiting for transfers between devices, body(): lax.all_to_all(leaving, ('flow', 'grp'), split_axis=1, concat_axis=1, til...  14.1 us
    all_to_all x1, starting transfers between devices, body(): lax.all_to_all(leaving, ('flow', 'grp'), split_axis=1, concat_axis=1, til...  12.1 us
    all_to_all x1, starting transfers between devices, body(): lax.all_to_all(outgoing, ('flow', 'grp'), split_axis=1, concat_axis=1, ti...  11.5 us
    pallas_call x2, Pallas kernels, dg_step(): pl.pallas_call(lambda *refs: dg_step_kernel(want_faces, xoff, yoff, row_l...  10.2 us
    ppermute x2, starting transfers between devices, exchange_faces(): lax.ppermute(sx4, 'flow', up_f)  9.82 us
    ppermute x2, waiting for transfers between devices, exchange_faces(): lax.ppermute(sy0, 'grp', down_g)  6.68 us
    ppermute x2, starting transfers between devices, exchange_faces(): lax.ppermute(sy4, 'grp', up_g)  5.92 us
    unnamed x37, local copies, waits for them, and re-layouts  5.22 us
  transfers between devices with their start and end apart: 14, of which 4 were waited for; matrix products, arithmetic and copies ran while one was open for 1% of the time, Pallas kernels for 3%

profile of v6, /device:TPU:1, one launch (start us, length us, event | category | flops | bytes accessed | tf_op | source)
XLA Modules:
  0.0 124.1 jit_solution(5896480968910020201)
XLA Ops:
  2.4 1.1 scatter_custom_fusion
  3.6 1.1 all_to_all.14
  4.7 11.5 %all-to-all-start = ((f32[512,128,2]{0,2,1:T(2,128)}), f32[512,128,2]{0,2,1:T(2,128)S(1)}, u32[]{:S(2)}, u32[]{:S(2)}) async-start(f32[512,128,2]{0,2,1:T(2,128)} %all_to_all.14), calls=%async_computation | async-start | bytes 1048576 | tf_op jit(solution)/shard_map/all_to_all | solution.py:403
  16.2 3.7 %collective-permute-start = (f32[4,32,256]{2,1,0:T(8,128)S(1)}, f32[4,32,256]{2,1,0:T(8,128)S(1)}, u32[]{:S(2)}, u32[]{:S(2)}) collective-permute-start(f32[4,32,256]{2,1,0:T(8,128)S(1)} %get-tuple-element.27), channel_id=1, source_target_pairs={{0,4},{4,8},{8,12},{12,16},{16,20},{20,24},{24,28},{28,32},{32,36}... | collective-permute-start | bytes 393224 | tf_op jit(solution)/shard_map/ppermute | solution.py:229
  19.9 1.9 %collective-permute-start.1 = (f32[4,32,256]{2,1,0:T(8,128)S(1)}, f32[4,32,256]{2,1,0:T(8,128)S(1)}, u32[]{:S(2)}, u32[]{:S(2)}) collective-permute-start(f32[4,32,256]{2,1,0:T(8,128)S(1)} %get-tuple-element.26), channel_id=1, source_target_pairs={{4,0},{8,4},{12,8},{16,12},{20,16},{24,20},{28,24},{32,28},{36,32}... | collective-permute-start | bytes 393224 | tf_op jit(solution)/shard_map/ppermute | solution.py:230
  21.9 3.1 %collective-permute-start.2 = (f32[4,8,1,256]{3,2,1,0:T(1,128)S(1)}, f32[4,8,1,256]{3,2,1,0:T(1,128)S(1)}, u32[]{:S(2)}, u32[]{:S(2)}) collective-permute-start(f32[4,8,1,256]{3,2,1,0:T(1,128)S(1)} %get-tuple-element.25), channel_id=1, source_target_pairs={{0,1},{1,2},{2,3},{4,5},{5,6},{6,7},{8,9},{9,10},{10,11},{12,13},{... | collective-permute-start | bytes 98312 | tf_op jit(solution)/shard_map/ppermute | solution.py:231
  25.0 1.3 %collective-permute-start.3 = (f32[4,8,1,256]{3,2,1,0:T(1,128)S(1)}, f32[4,8,1,256]{3,2,1,0:T(1,128)S(1)}, u32[]{:S(2)}, u32[]{:S(2)}) collective-permute-start(f32[4,8,1,256]{3,2,1,0:T(1,128)S(1)} %get-tuple-element.24), channel_id=1, source_target_pairs={{1,0},{2,1},{3,2},{5,4},{6,5},{7,6},{9,8},{10,9},{11,10},{13,12},{... | collective-permute-start | bytes 98312 | tf_op jit(solution)/shard_map/ppermute | solution.py:232
  26.6 3.4 %collective-permute-done.3.refs_5_.refs_9_ = f32[4,8,1,256]{3,2,1,0:T(1,128)S(1)} collective-permute-done((f32[4,8,1,256]{3,2,1,0:T(1,128)S(1)}, f32[4,8,1,256]{3,2,1,0:T(1,128)S(1)}, u32[]{:S(2)}, u32[]{:S(2)}) %collective-permute-start.3) | collective-permute-done | bytes 32800 | tf_op jit(solution)/shard_map/ppermute | solution.py:232
  31.3 4.0 %shard_map.104.vel_ref.refs_0_ = f32[3,8,32,256]{3,2,1,0:T(8,128)} custom-call(f32[3,8,32,256]{3,2,1,0:T(8,128)} %refs_0_.1, f32[8,32,256]{2,1,0:T(8,128)} %refs_1_.3, f32[4,32,256]{2,1,0:T(8,128)} %copy-done.2, f32[4,32,256]{2,1,0:T(8,128)} %copy-done.3, f32[4,8,1,256]{3,2,1,0:T(1,128)} %copy-done.8, f32[4,8,1,256]{3,2,1,0:T(1,128)} %copy-done.9, ...), custom_call_target="tpu_custom_call" | custom-call | tf_op jit(solution)/shard_map/pallas_call | solution.py:208
  35.6 1.5 %scatter_custom_fusion.1 = f32[512,128]{0,1:T(8,128)S(1)} fusion(s32[256]{0:T(256)S(1)} %bitcast.62, f32[512,256]{0,1:T(8,128)S(1)} %reshape.158, f32[]{:T(128)} %constant.8.clone.1), kind=kCustom, calls=%fused_computation.6 | custom fusion | bytes 786436 | tf_op jit(solution)/shard_map/scatter | solution.py:408
  38.0 2.0 %shard_map.105 = (f32[296,128]{1,0:T(8,128)}, f32[296,128]{1,0:T(8,128)}, f32[152,128]{1,0:T(8,128)}, f32[152,128]{1,0:T(8,128)}) custom-call(f32[512,128]{1,0:T(8,128)} %copy.32.state_ref.refs_0_, f32[3,8,32,256]{3,2,1,0:T(8,128)} %shard_map.104.vel_ref.refs_0_), custom_call_target="tpu_custom_call" | custom-call | tf_op jit(solution)/shard_map/pallas_call | solution.py:352
  40.0 4.8 %collective-permute-start.4 = (f32[296,128]{1,0:T(8,128)}, f32[296,128]{1,0:T(8,128)S(1)}, u32[]{:S(2)}, u32[]{:S(2)}) collective-permute-start(f32[296,128]{1,0:T(8,128)} %get-tuple-element.13), channel_id=1, source_target_pairs={{0,4},{4,8},{8,12},{12,16},{16,20},{20,24},{24,28},{28,32},{32,36}... | collective-permute-start | bytes 454664 | tf_op jit(solution)/shard_map/ppermute | solution.py:386
  44.8 1.9 %collective-permute-start.5 = (f32[296,128]{1,0:T(8,128)}, f32[296,128]{1,0:T(8,128)S(1)}, u32[]{:S(2)}, u32[]{:S(2)}) collective-permute-start(f32[296,128]{1,0:T(8,128)} %get-tuple-element.14), channel_id=1, source_target_pairs={{4,0},{8,4},{12,8},{16,12},{20,16},{24,20},{28,24},{32,28},{36,32}... | collective-permute-start | bytes 454664 | tf_op jit(solution)/shard_map/ppermute | solution.py:387
  46.7 3.1 %collective-permute-start.6 = (f32[152,128]{1,0:T(8,128)}, f32[152,128]{1,0:T(8,128)S(1)}, u32[]{:S(2)}, u32[]{:S(2)}) collective-permute-start(f32[152,128]{1,0:T(8,128)} %get-tuple-element.15), channel_id=1, source_target_pairs={{0,1},{1,2},{2,3},{4,5},{5,6},{6,7},{8,9},{9,10},{10,11},{12,13},{... | collective-permute-start | bytes 233480 | tf_op jit(solution)/shard_map/ppermute | solution.py:388
  49.8 1.3 %collective-permute-start.7 = (f32[152,128]{1,0:T(8,128)}, f32[152,128]{1,0:T(8,128)S(1)}, u32[]{:S(2)}, u32[]{:S(2)}) collective-permute-start(f32[152,128]{1,0:T(8,128)} %get-tuple-element.16), channel_id=1, source_target_pairs={{1,0},{2,1},{3,2},{5,4},{6,5},{7,6},{9,8},{10,9},{11,10},{13,12},{... | collective-permute-start | bytes 233480 | tf_op jit(solution)/shard_map/ppermute | solution.py:389
  51.9 3.2 %collective-permute-done.7.refs_5_ = f32[152,128]{1,0:T(8,128)S(1)} collective-permute-done((f32[152,128]{1,0:T(8,128)}, f32[152,128]{1,0:T(8,128)S(1)}, u32[]{:S(2)}, u32[]{:S(2)}) %collective-permute-start.7) | collective-permute-done | bytes 77856 | tf_op jit(solution)/shard_map/ppermute | solution.py:389
  56.5 4.0 %shard_map.106 = (f32[3,8,32,256]{3,2,1,0:T(8,128)}, bf16[3,8,32,256]{3,2,1,0:T(8,128)(2,1)}) custom-call(f32[3,8,32,256]{3,2,1,0:T(8,128)} %shard_map.104.vel_ref.refs_0_, f32[8,32,256]{2,1,0:T(8,128)} %refs_1_.3, f32[296,128]{1,0:T(8,128)} %copy-done.4, f32[296,128]{1,0:T(8,128)} %copy-done.5, f32[152,128]{1,0:T(8,128)} %copy-done.6, ...), custom_call_target="tpu_custom_call" | custom-call | tf_op jit(solution)/shard_map/pallas_call | solution.py:215
  60.6 1.3 %convolution_convert_fusion = bf16[768,256]{1,0:T(8,128)(2,1)S(1)} fusion(bf16[768,256]{1,0:T(8,128)(2,1)} %bitcast.60, bf16[256,256]{1,0:T(8,128)(2,1)S(1)} %copy-done.10), kind=kOutput, calls=%fused_computation.5 | convolution fusion | flops 100859904 | bytes 917504 | tf_op jit(solution)/shard_map/dot_general | solution.py:244
  62.5 2.0 %copy.43 = bf16[3,1,8,4,8,8,32]{6,3,0,5,4,2,1:T(4,128)(2,1)S(1)} copy(bf16[3,1,8,4,8,8,32]{6,5,4,3,2,0,1:T(8,128)(2,1)S(1)} %reshape.129) | data formatting | bytes 786432 | tf_op jit(solution)/shard_map/reshape | solution.py:246
  65.6 1.0 fusion.4
  66.5 5.2 %shard_map.107 = (f32[512,128]{1,0:T(8,128)}, f32[104,128]{1,0:T(8,128)}, f32[104,128]{1,0:T(8,128)}, f32[104,32]{1,0:T(8,128)}, f32[104,32]{1,0:T(8,128)}) custom-call(f32[512,128]{1,0:T(8,128)} %copy.32.state_ref.refs_0_, f32[384,128]{1,0:T(8,128)} %bitcast.53, f32[296,128]{1,0:T(8,128)} %copy-done.4, f32[296,128]{1,0:T(8,128)} %copy-done.5, ...), custom_call_target="tpu_custom_call" | custom-call | tf_op jit(solution)/shard_map/pallas_call | solution.py:365
  71.7 5.1 %collective-permute-start.8 = (f32[104,128]{1,0:T(8,128)}, f32[104,128]{1,0:T(8,128)S(1)}, u32[]{:S(2)}, u32[]{:S(2)}) collective-permute-start(f32[104,128]{1,0:T(8,128)} %get-tuple-element.20), channel_id=1, source_target_pairs={{0,4},{4,8},{8,12},{12,16},{16,20},{20,24},{24,28},{28,32},{32,36}... | collective-permute-start | bytes 159752 | tf_op jit(solution)/shard_map/ppermute | solution.py:386
  76.8 1.9 %collective-permute-start.9 = (f32[104,128]{1,0:T(8,128)}, f32[104,128]{1,0:T(8,128)S(1)}, u32[]{:S(2)}, u32[]{:S(2)}) collective-permute-start(f32[104,128]{1,0:T(8,128)} %get-tuple-element.21), channel_id=1, source_target_pairs={{4,0},{8,4},{12,8},{16,12},{20,16},{24,20},{28,24},{32,28},{36,32}... | collective-permute-start | bytes 159752 | tf_op jit(solution)/shard_map/ppermute | solution.py:387
  78.7 2.8 %collective-permute-start.10 = (f32[104,32]{1,0:T(8,128)}, f32[104,32]{1,0:T(8,128)S(1)}, u32[]{:S(2)}, u32[]{:S(2)}) collective-permute-start(f32[104,32]{1,0:T(8,128)} %get-tuple-element.22), channel_id=1, source_target_pairs={{0,1},{1,2},{2,3},{4,5},{5,6},{6,7},{8,9},{9,10},{10,11},{12,13},{... | collective-permute-start | bytes 39944 | tf_op jit(solution)/shard_map/ppermute | solution.py:388
  81.6 1.5 %collective-permute-start.11 = (f32[104,32]{1,0:T(8,128)}, f32[104,32]{1,0:T(8,128)S(1)}, u32[]{:S(2)}, u32[]{:S(2)}) collective-permute-start(f32[104,32]{1,0:T(8,128)} %get-tuple-element.23), channel_id=1, source_target_pairs={{1,0},{2,1},{3,2},{5,4},{6,5},{7,6},{9,8},{10,9},{11,10},{13,12},{... | collective-permute-start | bytes 39944 | tf_op jit(solution)/shard_map/ppermute | solution.py:389
  83.2 3.4 %collective-permute-done.11.refs_5_ = f32[104,32]{1,0:T(8,128)S(1)} collective-permute-done((f32[104,32]{1,0:T(8,128)}, f32[104,32]{1,0:T(8,128)S(1)}, u32[]{:S(2)}, u32[]{:S(2)}) %collective-permute-start.11) | collective-permute-done | bytes 13344 | tf_op jit(solution)/shard_map/ppermute | solution.py:389
  87.3 5.0 %shard_map.108 = f32[512,128]{1,0:T(8,128)} custom-call(f32[512,128]{1,0:T(8,128)} %get-tuple-element.19.refs_0_, f32[384,128]{1,0:T(8,128)} %bitcast.54, f32[104,128]{1,0:T(8,128)} %copy-done.12, f32[104,128]{1,0:T(8,128)} %copy-done.13, f32[104,32]{1,0:T(8,128)} %copy-done.14, f32[104,32]{1,0:T(8,128)} %copy-done.15, f32[512,512]{1,0:T(8,128)} %constant.6.clone.refs_6_, ...), custom_call_target="tpu_custom_call" | custom-call | tf_op jit(solution)/shard_map/pallas_call | solution.py:365
  92.3 1.1 copy.39
  93.4 1.0 gather_fusion
  94.7 1.1 broadcast_select_fusion
  95.8 12.1 %all-to-all-start.1 = ((f32[512,128,2]{0,2,1:T(2,128)}), f32[512,128,2]{0,2,1:T(2,128)S(1)}, u32[]{:S(2)}, u32[]{:S(2)}) async-start(f32[512,128,2]{0,2,1:T(2,128)} %broadcast_select_fusion), calls=%async_computation.1 | async-start | bytes 1048576 | tf_op jit(solution)/shard_map/all_to_all | solution.py:426
  107.9 14.1 %all-to-all-done.1 = f32[512,128,2]{0,2,1:T(2,128)S(1)} async-done(((f32[512,128,2]{0,2,1:T(2,128)}), f32[512,128,2]{0,2,1:T(2,128)S(1)}, u32[]{:S(2)}, u32[]{:S(2)}) %all-to-all-start.1) | async-done | bytes 524320 | tf_op jit(solution)/shard_map/all_to_all | solution.py:426
  (68 shorter events, 11.6 us)
Async XLA Ops:
  2.3 13.9 %copy-start = (f32[3,8,32,256]{3,2,1,0:T(8,128)S(1)}, f32[3,8,32,256]{3,2,1,0:T(8,128)}, u32[]{:S(2)}) copy-start(f32[3,8,32,256]{3,2,1,0:T(8,128)} %refs_0_.1) | copy-start | bytes 2359300
  2.3 13.9 %copy-start.1 = (f32[8,32,256]{2,1,0:T(8,128)S(1)}, f32[8,32,256]{2,1,0:T(8,128)}, u32[]{:S(2)}) copy-start(f32[8,32,256]{2,1,0:T(8,128)} %refs_1_.3) | copy-start | bytes 786436
  4.7 21.6 %copy-start.16 = (s32[1,128,2]{1,2,0:T(2,128)S(1)}, s32[1,128,2]{1,2,0:T(2,128)}, u32[]{:S(2)}) copy-start(s32[1,128,2]{1,2,0:T(2,128)} %param.13) | copy-start | bytes 3076
  4.7 30.5 %all-to-all-start = ((f32[512,128,2]{0,2,1:T(2,128)}), f32[512,128,2]{0,2,1:T(2,128)S(1)}, u32[]{:S(2)}, u32[]{:S(2)}) async-start(f32[512,128,2]{0,2,1:T(2,128)} %all_to_all.14), calls=%async_computation | async-start | bytes 1048576 | tf_op jit(solution)/shard_map/all_to_all | solution.py:403
  16.2 13.7 %collective-permute-start = (f32[4,32,256]{2,1,0:T(8,128)S(1)}, f32[4,32,256]{2,1,0:T(8,128)S(1)}, u32[]{:S(2)}, u32[]{:S(2)}) collective-permute-start(f32[4,32,256]{2,1,0:T(8,128)S(1)} %get-tuple-element.27), channel_id=1, source_target_pairs={{0,4},{4,8},{8,12},{12,16},{16,20},{20,24},{24,28},{28,32},{32,36}... | collective-permute-start | bytes 393224 | tf_op jit(solution)/shard_map/ppermute | solution.py:229
  19.9 10.1 %collective-permute-start.1 = (f32[4,32,256]{2,1,0:T(8,128)S(1)}, f32[4,32,256]{2,1,0:T(8,128)S(1)}, u32[]{:S(2)}, u32[]{:S(2)}) collective-permute-start(f32[4,32,256]{2,1,0:T(8,128)S(1)} %get-tuple-element.26), channel_id=1, source_target_pairs={{4,0},{8,4},{12,8},{16,12},{20,16},{24,20},{28,24},{32,28},{36,32}... | collective-permute-start | bytes 393224 | tf_op jit(solution)/shard_map/ppermute | solution.py:230
  21.9 4.7 %collective-permute-start.2 = (f32[4,8,1,256]{3,2,1,0:T(1,128)S(1)}, f32[4,8,1,256]{3,2,1,0:T(1,128)S(1)}, u32[]{:S(2)}, u32[]{:S(2)}) collective-permute-start(f32[4,8,1,256]{3,2,1,0:T(1,128)S(1)} %get-tuple-element.25), channel_id=1, source_target_pairs={{0,1},{1,2},{2,3},{4,5},{5,6},{6,7},{8,9},{9,10},{10,11},{12,13},{... | collective-permute-start | bytes 98312 | tf_op jit(solution)/shard_map/ppermute | solution.py:231
  25.0 5.0 %collective-permute-start.3 = (f32[4,8,1,256]{3,2,1,0:T(1,128)S(1)}, f32[4,8,1,256]{3,2,1,0:T(1,128)S(1)}, u32[]{:S(2)}, u32[]{:S(2)}) collective-permute-start(f32[4,8,1,256]{3,2,1,0:T(1,128)S(1)} %get-tuple-element.24), channel_id=1, source_target_pairs={{1,0},{2,1},{3,2},{5,4},{6,5},{7,6},{9,8},{10,9},{11,10},{13,12},{... | collective-permute-start | bytes 98312 | tf_op jit(solution)/shard_map/ppermute | solution.py:232
  26.6 3.4 %copy-start.8 = (f32[4,8,1,256]{3,2,1,0:T(1,128)}, f32[4,8,1,256]{3,2,1,0:T(1,128)S(1)}, u32[]{:S(2)}) copy-start(f32[4,8,1,256]{3,2,1,0:T(1,128)S(1)} %collective-permute-done.2.refs_4_.refs_8_) | copy-start | bytes 98308
  30.0 0.6 copy-start.9
  30.0 0.7 copy-start.2
  30.6 0.6 copy-start.3
  38.0 22.6 %copy-start.10 = (bf16[256,256]{1,0:T(8,128)(2,1)S(1)}, bf16[256,256]{1,0:T(8,128)(2,1)}, u32[]{:S(2)}) copy-start(bf16[256,256]{1,0:T(8,128)(2,1)} %constant.24.clone) | copy-start | bytes 393220
  40.0 15.2 %collective-permute-start.4 = (f32[296,128]{1,0:T(8,128)}, f32[296,128]{1,0:T(8,128)S(1)}, u32[]{:S(2)}, u32[]{:S(2)}) collective-permute-start(f32[296,128]{1,0:T(8,128)} %get-tuple-element.13), channel_id=1, source_target_pairs={{0,4},{4,8},{8,12},{12,16},{16,20},{20,24},{24,28},{28,32},{32,36}... | collective-permute-start | bytes 454664 | tf_op jit(solution)/shard_map/ppermute | solution.py:386
  44.8 10.4 %collective-permute-start.5 = (f32[296,128]{1,0:T(8,128)}, f32[296,128]{1,0:T(8,128)S(1)}, u32[]{:S(2)}, u32[]{:S(2)}) collective-permute-start(f32[296,128]{1,0:T(8,128)} %get-tuple-element.14), channel_id=1, source_target_pairs={{4,0},{8,4},{12,8},{16,12},{20,16},{24,20},{28,24},{32,28},{36,32}... | collective-permute-start | bytes 454664 | tf_op jit(solution)/shard_map/ppermute | solution.py:387
  46.7 5.2 %collective-permute-start.6 = (f32[152,128]{1,0:T(8,128)}, f32[152,128]{1,0:T(8,128)S(1)}, u32[]{:S(2)}, u32[]{:S(2)}) collective-permute-start(f32[152,128]{1,0:T(8,128)} %get-tuple-element.15), channel_id=1, source_target_pairs={{0,1},{1,2},{2,3},{4,5},{5,6},{6,7},{8,9},{9,10},{10,11},{12,13},{... | collective-permute-start | bytes 233480 | tf_op jit(solution)/shard_map/ppermute | solution.py:388
  49.8 5.4 %collective-permute-start.7 = (f32[152,128]{1,0:T(8,128)}, f32[152,128]{1,0:T(8,128)S(1)}, u32[]{:S(2)}, u32[]{:S(2)}) collective-permute-start(f32[152,128]{1,0:T(8,128)} %get-tuple-element.16), channel_id=1, source_target_pairs={{1,0},{2,1},{3,2},{5,4},{6,5},{7,6},{9,8},{10,9},{11,10},{13,12},{... | collective-permute-start | bytes 233480 | tf_op jit(solution)/shard_map/ppermute | solution.py:389
  51.9 3.3 %copy-start.6 = (f32[152,128]{1,0:T(8,128)}, f32[152,128]{1,0:T(8,128)S(1)}, u32[]{:S(2)}) copy-start(f32[152,128]{1,0:T(8,128)S(1)} %collective-permute-done.6.refs_4_) | copy-start | bytes 233476
  55.2 0.6 copy-start.7
  55.2 0.7 copy-start.4
  55.9 0.7 copy-start.5
  64.5 1.1 copy-start.11
  71.7 14.9 %collective-permute-start.8 = (f32[104,128]{1,0:T(8,128)}, f32[104,128]{1,0:T(8,128)S(1)}, u32[]{:S(2)}, u32[]{:S(2)}) collective-permute-start(f32[104,128]{1,0:T(8,128)} %get-tuple-element.20), channel_id=1, source_target_pairs={{0,4},{4,8},{8,12},{12,16},{16,20},{20,24},{24,28},{28,32},{32,36}... | collective-permute-start | bytes 159752 | tf_op jit(solution)/shard_map/ppermute | solution.py:386
  76.8 9.8 %collective-permute-start.9 = (f32[104,128]{1,0:T(8,128)}, f32[104,128]{1,0:T(8,128)S(1)}, u32[]{:S(2)}, u32[]{:S(2)}) collective-permute-start(f32[104,128]{1,0:T(8,128)} %get-tuple-element.21), channel_id=1, source_target_pairs={{4,0},{8,4},{12,8},{16,12},{20,16},{24,20},{28,24},{32,28},{36,32}... | collective-permute-start | bytes 159752 | tf_op jit(solution)/shard_map/ppermute | solution.py:387
  78.7 4.5 %collective-permute-start.10 = (f32[104,32]{1,0:T(8,128)}, f32[104,32]{1,0:T(8,128)S(1)}, u32[]{:S(2)}, u32[]{:S(2)}) collective-permute-start(f32[104,32]{1,0:T(8,128)} %get-tuple-element.22), channel_id=1, source_target_pairs={{0,1},{1,2},{2,3},{4,5},{5,6},{6,7},{8,9},{9,10},{10,11},{12,13},{... | collective-permute-start | bytes 39944 | tf_op jit(solution)/shard_map/ppermute | solution.py:388
  81.6 5.1 %collective-permute-start.11 = (f32[104,32]{1,0:T(8,128)}, f32[104,32]{1,0:T(8,128)S(1)}, u32[]{:S(2)}, u32[]{:S(2)}) collective-permute-start(f32[104,32]{1,0:T(8,128)} %get-tuple-element.23), channel_id=1, source_target_pairs={{1,0},{2,1},{3,2},{5,4},{6,5},{7,6},{9,8},{10,9},{11,10},{13,12},{... | collective-permute-start | bytes 39944 | tf_op jit(solution)/shard_map/ppermute | solution.py:389
  83.2 3.5 %copy-start.14 = (f32[104,32]{1,0:T(8,128)}, f32[104,32]{1,0:T(8,128)S(1)}, u32[]{:S(2)}) copy-start(f32[104,32]{1,0:T(8,128)S(1)} %collective-permute-done.10.refs_4_) | copy-start | bytes 39940
  86.6 0.6 copy-start.15
  86.6 0.6 copy-start.12
  86.7 0.7 copy-start.13
  95.8 26.3 %all-to-all-start.1 = ((f32[512,128,2]{0,2,1:T(2,128)}), f32[512,128,2]{0,2,1:T(2,128)S(1)}, u32[]{:S(2)}, u32[]{:S(2)}) async-start(f32[512,128,2]{0,2,1:T(2,128)} %broadcast_select_fusion), calls=%async_computation.1 | async-start | bytes 1048576 | tf_op jit(solution)/shard_map/all_to_all | solution.py:426

commit v7 on v4

--- a/solution.py
+++ b/solution.py
@@ -17,6 +17,7 @@
 GEOMETRY = 2.0
 LIFT_FACTOR = 20.0
 HIGH = lax.Precision.HIGHEST
+THREE_PASS = lax.Precision.HIGH
 
 
 def gll_derivative():
@@ -328,8 +329,8 @@
     oth_ref[pl.ds(640, FACE_ROWS), :] = jnp.where(
         ez == row_len - 1, 0.0, pltpu.roll(face_ref[4], elems - 1, 1))
     state = state_ref[...]
-    rate = jnp.dot(own_ref[...], state, precision=HIGH, preferred_element_type=jnp.float32)
-    rate = rate + jnp.dot(other_ref[...], oth_ref[...], precision=HIGH, preferred_element_type=jnp.float32)
+    rate = jnp.dot(own_ref[...], state, precision=THREE_PASS, preferred_element_type=jnp.float32)
+    rate = rate + jnp.dot(other_ref[...], oth_ref[...], precision=THREE_PASS, preferred_element_type=jnp.float32)
     out_ref[pl.ds(0, 128), :] = state[:128] + TIME_STEP_ACOUSTIC * rate[:128]
     out_ref[pl.ds(128, 384), :] = state[128:] + TIME_STEP_ACOUSTIC * (rate[128:] - src_ref[...])
     if want_faces:

time: 122 us -> 120 us (0.984)
  Pallas kernels: 20.1 us -> 18.1 us
    pallas_call x2, Pallas kernels: 10.3 us -> 8.21 us  [dg_step(): pl.pallas_call(lambda *refs: dg_step_kernel(want_faces, xoff, yoff, row_l...]
where the time goes in v7:
time: 120 us; the launch traced here: 119 us
  starting transfers between devices  52.5 us (44%)
  waiting for transfers between devices  26.4 us (22%)
  Pallas kernels  18.1 us (15%)
  local copies, waits for them, and re-layouts  16.7 us (14%)
  matrix products  2.22 us (2%)
  other arithmetic  1.87 us (2%)
    all_to_all x1, waiting for transfers between devices, body(): lax.all_to_all(leaving, ('flow', 'grp'), split_axis=1, concat_axis=1, til...  14.1 us
    all_to_all x1, starting transfers between devices, body(): lax.all_to_all(leaving, ('flow', 'grp'), split_axis=1, concat_axis=1, til...  12.8 us
    all_to_all x1, starting transfers between devices, body(): lax.all_to_all(outgoing, ('flow', 'grp'), split_axis=1, concat_axis=1, ti...  11.5 us
    pallas_call x2, Pallas kernels, dg_step(): pl.pallas_call(lambda *refs: dg_step_kernel(want_faces, xoff, yoff, row_l...  8.21 us
    ppermute x2, waiting for transfers between devices, exchange_faces(): lax.ppermute(sy0, 'grp', down_g)  7.67 us
    ppermute x2, starting transfers between devices, exchange_faces(): lax.ppermute(sx4, 'flow', up_f)  6.61 us
    ppermute x2, starting transfers between devices, exchange_faces(): lax.ppermute(sy4, 'grp', up_g)  4.99 us
    pallas_call x1, Pallas kernels, les_section_first(): pl.pallas_call(lambda *refs: les_kernel(0, *refs), out_shape=(jax.ShapeDt...  4.16 us
  transfers between devices with their start and end apart: 14, of which 5 were waited for; matrix products, arithmetic and copies ran while one was open for 3% of the time, Pallas kernels for 1%

profile of v7, /device:TPU:1, one launch (start us, length us, event | category | flops | bytes accessed | tf_op | source)
XLA Modules:
  0.0 118.8 jit_solution(3896484091517824889)
XLA Ops:
  2.4 1.1 scatter_custom_fusion
  3.6 1.1 all_to_all.14
  4.7 11.5 %all-to-all-start = ((f32[512,128,2]{0,2,1:T(2,128)}), f32[512,128,2]{0,2,1:T(2,128)S(1)}, u32[]{:S(2)}, u32[]{:S(2)}) async-start(f32[512,128,2]{0,2,1:T(2,128)} %all_to_all.14), calls=%async_computation | async-start | bytes 1048576 | tf_op jit(solution)/shard_map/all_to_all | solution.py:399
  16.2 3.7 %collective-permute-start = (f32[4,32,256]{2,1,0:T(8,128)S(1)}, f32[4,32,256]{2,1,0:T(8,128)S(1)}, u32[]{:S(2)}, u32[]{:S(2)}) collective-permute-start(f32[4,32,256]{2,1,0:T(8,128)S(1)} %get-tuple-element.37), channel_id=1, source_target_pairs={{0,4},{4,8},{8,12},{12,16},{16,20},{20,24},{24,28},{28,32},{32,36}... | collective-permute-start | bytes 393224 | tf_op jit(solution)/shard_map/ppermute | solution.py:251
  19.9 1.9 %collective-permute-start.1 = (f32[4,32,256]{2,1,0:T(8,128)S(1)}, f32[4,32,256]{2,1,0:T(8,128)S(1)}, u32[]{:S(2)}, u32[]{:S(2)}) collective-permute-start(f32[4,32,256]{2,1,0:T(8,128)S(1)} %get-tuple-element.36), channel_id=1, source_target_pairs={{4,0},{8,4},{12,8},{16,12},{20,16},{24,20},{28,24},{32,28},{36,32}... | collective-permute-start | bytes 393224 | tf_op jit(solution)/shard_map/ppermute | solution.py:252
  21.9 3.1 %collective-permute-start.2 = (f32[4,8,1,256]{3,2,1,0:T(1,128)S(1)}, f32[4,8,1,256]{3,2,1,0:T(1,128)S(1)}, u32[]{:S(2)}, u32[]{:S(2)}) collective-permute-start(f32[4,8,1,256]{3,2,1,0:T(1,128)S(1)} %get-tuple-element.35), channel_id=1, source_target_pairs={{0,1},{1,2},{2,3},{4,5},{5,6},{6,7},{8,9},{9,10},{10,11},{12,13},{... | collective-permute-start | bytes 98312 | tf_op jit(solution)/shard_map/ppermute | solution.py:253
  25.0 1.3 %collective-permute-start.3 = (f32[4,8,1,256]{3,2,1,0:T(1,128)S(1)}, f32[4,8,1,256]{3,2,1,0:T(1,128)S(1)}, u32[]{:S(2)}, u32[]{:S(2)}) collective-permute-start(f32[4,8,1,256]{3,2,1,0:T(1,128)S(1)} %get-tuple-element.34), channel_id=1, source_target_pairs={{1,0},{2,1},{3,2},{5,4},{6,5},{7,6},{9,8},{10,9},{11,10},{13,12},{... | collective-permute-start | bytes 98312 | tf_op jit(solution)/shard_map/ppermute | solution.py:254
  26.6 3.7 %all-to-all-done = f32[512,128,2]{0,2,1:T(2,128)S(1)} async-done(((f32[512,128,2]{0,2,1:T(2,128)}), f32[512,128,2]{0,2,1:T(2,128)S(1)}, u32[]{:S(2)}, u32[]{:S(2)}) %all-to-all-start) | async-done | bytes 524320 | tf_op jit(solution)/shard_map/all_to_all | solution.py:399
  30.7 1.5 %scatter_custom_fusion.1 = f32[512,128]{0,1:T(8,128)S(1)} fusion(s32[256]{0:T(256)S(1)} %bitcast.62, f32[512,256]{0,1:T(8,128)S(1)} %reshape.158, f32[]{:T(128)} %constant.8.clone.1), kind=kCustom, calls=%fused_computation.6 | custom fusion | bytes 786436 | tf_op jit(solution)/shard_map/scatter | solution.py:403
  33.1 1.7 %shard_map.104 = (f32[104,128]{1,0:T(8,128)}, f32[104,128]{1,0:T(8,128)}, f32[104,32]{1,0:T(8,128)}, f32[104,32]{1,0:T(8,128)}) custom-call(f32[512,128]{1,0:T(8,128)} %copy.29.state_ref.refs_0_), custom_call_target="tpu_custom_call" | custom-call | tf_op jit(solution)/shard_map/pallas_call | solution.py:349
  35.5 4.2 %shard_map.105 = (f32[3,8,32,256]{3,2,1,0:T(8,128)}, f32[296,128]{1,0:T(8,128)}, f32[296,128]{1,0:T(8,128)}, f32[152,128]{1,0:T(8,128)}, f32[152,128]{1,0:T(8,128)}) custom-call(f32[3,8,32,256]{3,2,1,0:T(8,128)} %refs_0_.1, f32[8,32,256]{2,1,0:T(8,128)} %refs_1_.3, f32[4,32,256]{2,1,0:T(8,128)} %copy-done.2, f32[4,32,256]{2,1,0:T(8,128)} %copy-done.3, ...), custom_call_target="tpu_custom_call" | custom-call | tf_op jit(solution)/shard_map/pallas_call | solution.py:230
  39.7 2.6 %collective-permute-start.4 = (f32[296,128]{1,0:T(8,128)}, f32[296,128]{1,0:T(8,128)S(1)}, u32[]{:S(2)}, u32[]{:S(2)}) collective-permute-start(f32[296,128]{1,0:T(8,128)} %get-tuple-element.23), channel_id=1, source_target_pairs={{0,4},{4,8},{8,12},{12,16},{16,20},{20,24},{24,28},{28,32},{32,36}... | collective-permute-start | bytes 454664 | tf_op jit(solution)/shard_map/ppermute | solution.py:382
  42.3 1.9 %collective-permute-start.5 = (f32[296,128]{1,0:T(8,128)}, f32[296,128]{1,0:T(8,128)S(1)}, u32[]{:S(2)}, u32[]{:S(2)}) collective-permute-start(f32[296,128]{1,0:T(8,128)} %get-tuple-element.24), channel_id=1, source_target_pairs={{4,0},{8,4},{12,8},{16,12},{20,16},{24,20},{28,24},{32,28},{36,32}... | collective-permute-start | bytes 454664 | tf_op jit(solution)/shard_map/ppermute | solution.py:383
  44.2 2.2 %collective-permute-start.6 = (f32[152,128]{1,0:T(8,128)}, f32[152,128]{1,0:T(8,128)S(1)}, u32[]{:S(2)}, u32[]{:S(2)}) collective-permute-start(f32[152,128]{1,0:T(8,128)} %get-tuple-element.25), channel_id=1, source_target_pairs={{0,1},{1,2},{2,3},{4,5},{5,6},{6,7},{8,9},{9,10},{10,11},{12,13},{... | collective-permute-start | bytes 233480 | tf_op jit(solution)/shard_map/ppermute | solution.py:384
  46.4 1.3 %collective-permute-start.7 = (f32[152,128]{1,0:T(8,128)}, f32[152,128]{1,0:T(8,128)S(1)}, u32[]{:S(2)}, u32[]{:S(2)}) collective-permute-start(f32[152,128]{1,0:T(8,128)} %get-tuple-element.26), channel_id=1, source_target_pairs={{1,0},{2,1},{3,2},{5,4},{6,5},{7,6},{9,8},{10,9},{11,10},{13,12},{... | collective-permute-start | bytes 233480 | tf_op jit(solution)/shard_map/ppermute | solution.py:385
  48.5 4.2 %collective-permute-done.7.refs_5_ = f32[152,128]{1,0:T(8,128)S(1)} collective-permute-done((f32[152,128]{1,0:T(8,128)}, f32[152,128]{1,0:T(8,128)S(1)}, u32[]{:S(2)}, u32[]{:S(2)}) %collective-permute-start.7) | collective-permute-done | bytes 77856 | tf_op jit(solution)/shard_map/ppermute | solution.py:385
  53.6 4.0 %shard_map.106 = (f32[3,8,32,256]{3,2,1,0:T(8,128)}, bf16[3,8,32,256]{3,2,1,0:T(8,128)(2,1)}) custom-call(f32[3,8,32,256]{3,2,1,0:T(8,128)} %get-tuple-element.22.refs_0_, f32[8,32,256]{2,1,0:T(8,128)} %refs_1_.3, f32[296,128]{1,0:T(8,128)} %copy-done.4, f32[296,128]{1,0:T(8,128)} %copy-done.5, f32[152,128]{1,0:T(8,128)} %copy-done.6, f32[152,128]{1,0:T(8,128)} %copy-done.7, ...), custom_call_target="tpu_custom_call" | custom-call | tf_op jit(solution)/shard_map/pallas_call | solution.py:237
  57.6 1.2 %convolution_convert_fusion = bf16[768,256]{1,0:T(8,128)(2,1)S(1)} fusion(bf16[768,256]{1,0:T(8,128)(2,1)} %bitcast.60, bf16[256,256]{1,0:T(8,128)(2,1)S(1)} %copy-done.10), kind=kOutput, calls=%fused_computation.5 | convolution fusion | flops 100859904 | bytes 917504 | tf_op jit(solution)/shard_map/dot_general | solution.py:266
  59.5 2.0 %copy.38 = bf16[3,1,8,4,8,8,32]{6,3,0,5,4,2,1:T(4,128)(2,1)S(1)} copy(bf16[3,1,8,4,8,8,32]{6,5,4,3,2,0,1:T(8,128)(2,1)S(1)} %reshape.129) | data formatting | bytes 786432 | tf_op jit(solution)/shard_map/reshape | solution.py:268
  62.6 1.0 fusion.4
  63.6 4.2 %shard_map.107 = (f32[512,128]{1,0:T(8,128)}, f32[104,128]{1,0:T(8,128)}, f32[104,128]{1,0:T(8,128)}, f32[104,32]{1,0:T(8,128)}, f32[104,32]{1,0:T(8,128)}) custom-call(f32[512,128]{1,0:T(8,128)} %copy.29.state_ref.refs_0_, f32[384,128]{1,0:T(8,128)} %bitcast.53, f32[296,128]{1,0:T(8,128)} %copy-done.4, f32[296,128]{1,0:T(8,128)} %copy-done.5, ...), custom_call_target="tpu_custom_call" | custom-call | tf_op jit(solution)/shard_map/pallas_call | solution.py:361
  67.8 4.0 %collective-permute-start.8 = (f32[104,128]{1,0:T(8,128)}, f32[104,128]{1,0:T(8,128)S(1)}, u32[]{:S(2)}, u32[]{:S(2)}) collective-permute-start(f32[104,128]{1,0:T(8,128)} %get-tuple-element.30), channel_id=1, source_target_pairs={{0,4},{4,8},{8,12},{12,16},{16,20},{20,24},{24,28},{28,32},{32,36}... | collective-permute-start | bytes 159752 | tf_op jit(solution)/shard_map/ppermute | solution.py:382
  71.8 1.9 %collective-permute-start.9 = (f32[104,128]{1,0:T(8,128)}, f32[104,128]{1,0:T(8,128)S(1)}, u32[]{:S(2)}, u32[]{:S(2)}) collective-permute-start(f32[104,128]{1,0:T(8,128)} %get-tuple-element.31), channel_id=1, source_target_pairs={{4,0},{8,4},{12,8},{16,12},{20,16},{24,20},{28,24},{32,28},{36,32}... | collective-permute-start | bytes 159752 | tf_op jit(solution)/shard_map/ppermute | solution.py:383
  73.8 2.8 %collective-permute-start.10 = (f32[104,32]{1,0:T(8,128)}, f32[104,32]{1,0:T(8,128)S(1)}, u32[]{:S(2)}, u32[]{:S(2)}) collective-permute-start(f32[104,32]{1,0:T(8,128)} %get-tuple-element.32), channel_id=1, source_target_pairs={{0,1},{1,2},{2,3},{4,5},{5,6},{6,7},{8,9},{9,10},{10,11},{12,13},{... | collective-permute-start | bytes 39944 | tf_op jit(solution)/shard_map/ppermute | solution.py:384
  76.5 1.5 %collective-permute-start.11 = (f32[104,32]{1,0:T(8,128)}, f32[104,32]{1,0:T(8,128)S(1)}, u32[]{:S(2)}, u32[]{:S(2)}) collective-permute-start(f32[104,32]{1,0:T(8,128)} %get-tuple-element.33), channel_id=1, source_target_pairs={{1,0},{2,1},{3,2},{5,4},{6,5},{7,6},{9,8},{10,9},{11,10},{13,12},{... | collective-permute-start | bytes 39944 | tf_op jit(solution)/shard_map/ppermute | solution.py:385
  78.2 3.4 %collective-permute-done.11.refs_5_ = f32[104,32]{1,0:T(8,128)S(1)} collective-permute-done((f32[104,32]{1,0:T(8,128)}, f32[104,32]{1,0:T(8,128)S(1)}, u32[]{:S(2)}, u32[]{:S(2)}) %collective-permute-start.11) | collective-permute-done | bytes 13344 | tf_op jit(solution)/shard_map/ppermute | solution.py:385
  82.3 4.0 %shard_map.108 = f32[512,128]{1,0:T(8,128)} custom-call(f32[512,128]{1,0:T(8,128)} %get-tuple-element.29.refs_0_, f32[384,128]{1,0:T(8,128)} %bitcast.54, f32[104,128]{1,0:T(8,128)} %copy-done.12, f32[104,128]{1,0:T(8,128)} %copy-done.13, f32[104,32]{1,0:T(8,128)} %copy-done.14, f32[104,32]{1,0:T(8,128)} %copy-done.15, f32[512,512]{1,0:T(8,128)} %constant.6.clone.refs_6_, ...), custom_call_target="tpu_custom_call" | custom-call | tf_op jit(solution)/shard_map/pallas_call | solution.py:361
  86.3 1.1 copy.34
  87.4 1.0 gather_fusion
  88.7 1.1 broadcast_select_fusion
  89.8 12.8 %all-to-all-start.1 = ((f32[512,128,2]{0,2,1:T(2,128)}), f32[512,128,2]{0,2,1:T(2,128)S(1)}, u32[]{:S(2)}, u32[]{:S(2)}) async-start(f32[512,128,2]{0,2,1:T(2,128)} %broadcast_select_fusion), calls=%async_computation.1 | async-start | bytes 1048576 | tf_op jit(solution)/shard_map/all_to_all | solution.py:422
  102.6 14.1 %all-to-all-done.1 = f32[512,128,2]{0,2,1:T(2,128)S(1)} async-done(((f32[512,128,2]{0,2,1:T(2,128)}), f32[512,128,2]{0,2,1:T(2,128)S(1)}, u32[]{:S(2)}, u32[]{:S(2)}) %all-to-all-start.1) | async-done | bytes 524320 | tf_op jit(solution)/shard_map/all_to_all | solution.py:422
  (67 shorter events, 10.5 us)
Async XLA Ops:
  2.3 13.9 %copy-start = (f32[3,8,32,256]{3,2,1,0:T(8,128)S(1)}, f32[3,8,32,256]{3,2,1,0:T(8,128)}, u32[]{:S(2)}) copy-start(f32[3,8,32,256]{3,2,1,0:T(8,128)} %refs_0_.1) | copy-start | bytes 2359300
  2.3 13.9 %copy-start.1 = (f32[8,32,256]{2,1,0:T(8,128)S(1)}, f32[8,32,256]{2,1,0:T(8,128)}, u32[]{:S(2)}) copy-start(f32[8,32,256]{2,1,0:T(8,128)} %refs_1_.3) | copy-start | bytes 786436
  4.7 21.6 %copy-start.16 = (s32[1,128,2]{1,2,0:T(2,128)S(1)}, s32[1,128,2]{1,2,0:T(2,128)}, u32[]{:S(2)}) copy-start(s32[1,128,2]{1,2,0:T(2,128)} %param.13) | copy-start | bytes 3076
  4.7 25.6 %all-to-all-start = ((f32[512,128,2]{0,2,1:T(2,128)}), f32[512,128,2]{0,2,1:T(2,128)S(1)}, u32[]{:S(2)}, u32[]{:S(2)}) async-start(f32[512,128,2]{0,2,1:T(2,128)} %all_to_all.14), calls=%async_computation | async-start | bytes 1048576 | tf_op jit(solution)/shard_map/all_to_all | solution.py:399
  16.2 18.5 %collective-permute-start = (f32[4,32,256]{2,1,0:T(8,128)S(1)}, f32[4,32,256]{2,1,0:T(8,128)S(1)}, u32[]{:S(2)}, u32[]{:S(2)}) collective-permute-start(f32[4,32,256]{2,1,0:T(8,128)S(1)} %get-tuple-element.37), channel_id=1, source_target_pairs={{0,4},{4,8},{8,12},{12,16},{16,20},{20,24},{24,28},{28,32},{32,36}... | collective-permute-start | bytes 393224 | tf_op jit(solution)/shard_map/ppermute | solution.py:251
  19.9 14.9 %collective-permute-start.1 = (f32[4,32,256]{2,1,0:T(8,128)S(1)}, f32[4,32,256]{2,1,0:T(8,128)S(1)}, u32[]{:S(2)}, u32[]{:S(2)}) collective-permute-start(f32[4,32,256]{2,1,0:T(8,128)S(1)} %get-tuple-element.36), channel_id=1, source_target_pairs={{4,0},{8,4},{12,8},{16,12},{20,16},{24,20},{28,24},{32,28},{36,32}... | collective-permute-start | bytes 393224 | tf_op jit(solution)/shard_map/ppermute | solution.py:252
  21.9 12.9 %collective-permute-start.2 = (f32[4,8,1,256]{3,2,1,0:T(1,128)S(1)}, f32[4,8,1,256]{3,2,1,0:T(1,128)S(1)}, u32[]{:S(2)}, u32[]{:S(2)}) collective-permute-start(f32[4,8,1,256]{3,2,1,0:T(1,128)S(1)} %get-tuple-element.35), channel_id=1, source_target_pairs={{0,1},{1,2},{2,3},{4,5},{5,6},{6,7},{8,9},{9,10},{10,11},{12,13},{... | collective-permute-start | bytes 98312 | tf_op jit(solution)/shard_map/ppermute | solution.py:253
  25.0 9.8 %collective-permute-start.3 = (f32[4,8,1,256]{3,2,1,0:T(1,128)S(1)}, f32[4,8,1,256]{3,2,1,0:T(1,128)S(1)}, u32[]{:S(2)}, u32[]{:S(2)}) collective-permute-start(f32[4,8,1,256]{3,2,1,0:T(1,128)S(1)} %get-tuple-element.34), channel_id=1, source_target_pairs={{1,0},{2,1},{3,2},{5,4},{6,5},{7,6},{9,8},{10,9},{11,10},{13,12},{... | collective-permute-start | bytes 98312 | tf_op jit(solution)/shard_map/ppermute | solution.py:254
  34.8 0.6 copy-start.8
  34.8 0.6 copy-start.9
  34.8 0.7 copy-start.2
  34.8 0.7 copy-start.3
  35.5 22.1 %copy-start.10 = (bf16[256,256]{1,0:T(8,128)(2,1)S(1)}, bf16[256,256]{1,0:T(8,128)(2,1)}, u32[]{:S(2)}) copy-start(bf16[256,256]{1,0:T(8,128)(2,1)} %constant.24.clone) | copy-start | bytes 393220
  39.7 13.1 %collective-permute-start.4 = (f32[296,128]{1,0:T(8,128)}, f32[296,128]{1,0:T(8,128)S(1)}, u32[]{:S(2)}, u32[]{:S(2)}) collective-permute-start(f32[296,128]{1,0:T(8,128)} %get-tuple-element.23), channel_id=1, source_target_pairs={{0,4},{4,8},{8,12},{12,16},{16,20},{20,24},{24,28},{28,32},{32,36}... | collective-permute-start | bytes 454664 | tf_op jit(solution)/shard_map/ppermute | solution.py:382
  42.3 10.5 %collective-permute-start.5 = (f32[296,128]{1,0:T(8,128)}, f32[296,128]{1,0:T(8,128)S(1)}, u32[]{:S(2)}, u32[]{:S(2)}) collective-permute-start(f32[296,128]{1,0:T(8,128)} %get-tuple-element.24), channel_id=1, source_target_pairs={{4,0},{8,4},{12,8},{16,12},{20,16},{24,20},{28,24},{32,28},{36,32}... | collective-permute-start | bytes 454664 | tf_op jit(solution)/shard_map/ppermute | solution.py:383
  44.2 4.4 %collective-permute-start.6 = (f32[152,128]{1,0:T(8,128)}, f32[152,128]{1,0:T(8,128)S(1)}, u32[]{:S(2)}, u32[]{:S(2)}) collective-permute-start(f32[152,128]{1,0:T(8,128)} %get-tuple-element.25), channel_id=1, source_target_pairs={{0,1},{1,2},{2,3},{4,5},{5,6},{6,7},{8,9},{9,10},{10,11},{12,13},{... | collective-permute-start | bytes 233480 | tf_op jit(solution)/shard_map/ppermute | solution.py:384
  46.4 6.4 %collective-permute-start.7 = (f32[152,128]{1,0:T(8,128)}, f32[152,128]{1,0:T(8,128)S(1)}, u32[]{:S(2)}, u32[]{:S(2)}) collective-permute-start(f32[152,128]{1,0:T(8,128)} %get-tuple-element.26), channel_id=1, source_target_pairs={{1,0},{2,1},{3,2},{5,4},{6,5},{7,6},{9,8},{10,9},{11,10},{13,12},{... | collective-permute-start | bytes 233480 | tf_op jit(solution)/shard_map/ppermute | solution.py:385
  48.5 4.3 %copy-start.6 = (f32[152,128]{1,0:T(8,128)}, f32[152,128]{1,0:T(8,128)S(1)}, u32[]{:S(2)}) copy-start(f32[152,128]{1,0:T(8,128)S(1)} %collective-permute-done.6.refs_4_) | copy-start | bytes 233476
  52.8 0.6 copy-start.7
  52.8 0.7 copy-start.4
  52.8 0.8 copy-start.5
  61.5 1.1 copy-start.11
  67.8 13.9 %collective-permute-start.8 = (f32[104,128]{1,0:T(8,128)}, f32[104,128]{1,0:T(8,128)S(1)}, u32[]{:S(2)}, u32[]{:S(2)}) collective-permute-start(f32[104,128]{1,0:T(8,128)} %get-tuple-element.30), channel_id=1, source_target_pairs={{0,4},{4,8},{8,12},{12,16},{16,20},{20,24},{24,28},{28,32},{32,36}... | collective-permute-start | bytes 159752 | tf_op jit(solution)/shard_map/ppermute | solution.py:382
  71.8 9.8 %collective-permute-start.9 = (f32[104,128]{1,0:T(8,128)}, f32[104,128]{1,0:T(8,128)S(1)}, u32[]{:S(2)}, u32[]{:S(2)}) collective-permute-start(f32[104,128]{1,0:T(8,128)} %get-tuple-element.31), channel_id=1, source_target_pairs={{4,0},{8,4},{12,8},{16,12},{20,16},{24,20},{28,24},{32,28},{36,32}... | collective-permute-start | bytes 159752 | tf_op jit(solution)/shard_map/ppermute | solution.py:383
  73.8 4.4 %collective-permute-start.10 = (f32[104,32]{1,0:T(8,128)}, f32[104,32]{1,0:T(8,128)S(1)}, u32[]{:S(2)}, u32[]{:S(2)}) collective-permute-start(f32[104,32]{1,0:T(8,128)} %get-tuple-element.32), channel_id=1, source_target_pairs={{0,1},{1,2},{2,3},{4,5},{5,6},{6,7},{8,9},{9,10},{10,11},{12,13},{... | collective-permute-start | bytes 39944 | tf_op jit(solution)/shard_map/ppermute | solution.py:384
  76.5 5.1 %collective-permute-start.11 = (f32[104,32]{1,0:T(8,128)}, f32[104,32]{1,0:T(8,128)S(1)}, u32[]{:S(2)}, u32[]{:S(2)}) collective-permute-start(f32[104,32]{1,0:T(8,128)} %get-tuple-element.33), channel_id=1, source_target_pairs={{1,0},{2,1},{3,2},{5,4},{6,5},{7,6},{9,8},{10,9},{11,10},{13,12},{... | collective-permute-start | bytes 39944 | tf_op jit(solution)/shard_map/ppermute | solution.py:385
  78.2 3.5 %copy-start.14 = (f32[104,32]{1,0:T(8,128)}, f32[104,32]{1,0:T(8,128)S(1)}, u32[]{:S(2)}) copy-start(f32[104,32]{1,0:T(8,128)S(1)} %collective-permute-done.10.refs_4_) | copy-start | bytes 39940
  81.6 0.6 copy-start.15
  81.6 0.6 copy-start.12
  81.7 0.6 copy-start.13
  89.8 26.9 %all-to-all-start.1 = ((f32[512,128,2]{0,2,1:T(2,128)}), f32[512,128,2]{0,2,1:T(2,128)S(1)}, u32[]{:S(2)}, u32[]{:S(2)}) async-start(f32[512,128,2]{0,2,1:T(2,128)} %broadcast_select_fusion), calls=%async_computation.1 | async-start | bytes 1048576 | tf_op jit(solution)/shard_map/all_to_all | solution.py:422

commit v8 on v7

--- a/solution.py
+++ b/solution.py
@@ -59,46 +59,34 @@
 
 def dg_matrices():
     dmat = gll_derivative()
-    own = np.zeros((500, 500))
+    half = LIFT_FACTOR * 0.5
+    apu = np.zeros((128, 384))
+    aup = np.zeros((384, 128))
+    diag = np.zeros((512, 1))
+    lift = np.zeros((128, 152))
     for a in range(5):
         for b in range(5):
             for c in range(5):
-                row = node_id((a, b, c))
                 pos = (a, b, c)
+                row = node_id(pos)
                 for dim in range(3):
                     for k in range(5):
                         col_pos = list(pos)
                         col_pos[dim] = k
                         col = node_id(col_pos)
                         weight = -GEOMETRY * dmat[pos[dim], k]
-                        own[row, (1 + dim) * 125 + col] += weight
-                        own[(1 + dim) * 125 + row, col] += weight
-    half = LIFT_FACTOR * 0.5
-    other = np.zeros((500, 600))
-    face_order = []
+                        apu[row, dim * 128 + col] += weight
+                        aup[dim * 128 + row, col] += weight
     for dim in range(3):
-        for sign, at in ((-1.0, 0), (1.0, 4)):
-            face_order.append((dim, sign, at))
-    for slot, (dim, sign, at) in enumerate(face_order):
-        for t, node in enumerate(face_nodes(dim, at)):
-            col = lambda comp: slot * 100 + comp * 25 + t
-            own[node, (1 + dim) * 125 + node] += half * sign
-            own[node, node] += -half
-            other[node, col(1 + dim)] += -half * sign
-            other[node, col(0)] += half
-            for k in range(3):
-                own[(1 + k) * 125 + node, (1 + k) * 125 + node] += -half
-                other[(1 + k) * 125 + node, col(1 + k)] += half
-            own[(1 + dim) * 125 + node, node] += half * sign
-            other[(1 + dim) * 125 + node, col(0)] += -half * sign
-    own_pad = np.zeros((512, 512), np.float32)
-    other_pad = np.zeros((512, 768), np.float32)
-    for ci in range(4):
-        for cj in range(4):
-            own_pad[ci * 128:ci * 128 + 125, cj * 128:cj * 128 + 125] = own[ci * 125:(ci + 1) * 125, cj * 125:(cj + 1) * 125]
-        for slot in range(6):
-            other_pad[ci * 128:ci * 128 + 125, slot * 128:slot * 128 + 100] = other[ci * 125:(ci + 1) * 125, slot * 100:(slot + 1) * 100]
-    return own_pad, other_pad
+        for side, (sign, at) in enumerate(((-1.0, 0), (1.0, 4))):
+            f = 2 * dim + side
+            for t, node in enumerate(face_nodes(dim, at)):
+                apu[node, dim * 128 + node] += half * sign
+                aup[dim * 128 + node, node] += half * sign
+                for comp in range(4):
+                    diag[comp * 128 + node, 0] += -half
+                lift[node, f * 25 + t] = 1.0
+    return (apu.astype(np.float32), aup.astype(np.float32), diag.astype(np.float32), lift.astype(np.float32))
 
 
 def face_rows(state, dim, at):
@@ -304,12 +292,12 @@
     send_faces(face_ref, sx0_ref, sx4_ref, sy0_ref, sy4_ref, sy0_ref.shape[1])
 
 
-def dg_step_kernel(want_faces, xoff, yoff, row_len, state_ref, src_ref, xlo_ref, xhi_ref, ylo_ref, yhi_ref, own_ref, other_ref,
-                   out_ref, *rest):
+def dg_step_kernel(want_faces, xoff, yoff, row_len, state_ref, src_ref, xlo_ref, xhi_ref, ylo_ref, yhi_ref,
+                   apu_ref, aup_ref, diag_ref, lift_ref, out_ref, *rest):
     if want_faces:
-        sx0_ref, sx4_ref, sy0_ref, sy4_ref, face_ref, oth_ref, pad_ref = rest
+        sx0_ref, sx4_ref, sy0_ref, sy4_ref, face_ref, oth_ref, pad_ref, g_ref = rest
     else:
-        face_ref, oth_ref, pad_ref = rest
+        face_ref, oth_ref, pad_ref, g_ref = rest
     elems = state_ref.shape[1]
     lane = lax.broadcasted_iota(jnp.int32, (FACE_ROWS, elems), 1)
     ez = lane % row_len
@@ -328,11 +316,32 @@
     oth_ref[pl.ds(512, FACE_ROWS), :] = jnp.where(ez == 0, 0.0, pltpu.roll(face_ref[5], 1, 1))
     oth_ref[pl.ds(640, FACE_ROWS), :] = jnp.where(
         ez == row_len - 1, 0.0, pltpu.roll(face_ref[4], elems - 1, 1))
+    g_ref[pl.ds(144, 8), :] = jnp.zeros((8, 4 * elems), jnp.float32)
+    half = LIFT_FACTOR * 0.5
+    for dim in range(3):
+        for side, sign in ((0, -1.0), (1, 1.0)):
+            f = 2 * dim + side
+            o_p = oth_ref[pl.ds(f * 128, 25), :]
+            o_u = [oth_ref[pl.ds(f * 128 + (1 + k) * 25, 25), :] for k in range(3)]
+            g_ref[pl.ds(f * 25, 25), pl.ds(0, elems)] = half * (o_p - sign * o_u[dim])
+            for k in range(3):
+                value = half * o_u[k]
+                if k == dim:
+                    value = value - half * sign * o_p
+                g_ref[pl.ds(f * 25, 25), pl.ds((1 + k) * elems, elems)] = value
+    faces = jnp.dot(lift_ref[...], g_ref[...], precision=THREE_PASS, preferred_element_type=jnp.float32)
     state = state_ref[...]
-    rate = jnp.dot(own_ref[...], state, precision=THREE_PASS, preferred_element_type=jnp.float32)
-    rate = rate + jnp.dot(other_ref[...], oth_ref[...], precision=THREE_PASS, preferred_element_type=jnp.float32)
-    out_ref[pl.ds(0, 128), :] = state[:128] + TIME_STEP_ACOUSTIC * rate[:128]
-    out_ref[pl.ds(128, 384), :] = state[128:] + TIME_STEP_ACOUSTIC * (rate[128:] - src_ref[...])
+    pres = state[:128]
+    vel = state[128:]
+    rate_p = jnp.dot(apu_ref[...], vel, precision=THREE_PASS, preferred_element_type=jnp.float32)
+    rate_p = rate_p + diag_ref[pl.ds(0, 128), :] * pres + faces[:, :elems]
+    out_ref[pl.ds(0, 128), :] = pres + TIME_STEP_ACOUSTIC * rate_p
+    rate_u = jnp.dot(aup_ref[...], pres, precision=THREE_PASS, preferred_element_type=jnp.float32)
+    for k in range(3):
+        rows = pl.ds(128 + k * 128, 128)
+        rate_k = rate_u[k * 128:(k + 1) * 128] + diag_ref[rows, :] * state_ref[rows, :]
+        rate_k = rate_k + faces[:, (1 + k) * elems:(2 + k) * elems]
+        out_ref[rows, :] = state_ref[rows, :] + TIME_STEP_ACOUSTIC * (rate_k - src_ref[pl.ds(k * 128, 128), :])
     if want_faces:
         extract_faces(out_ref, face_ref)
         send_faces(face_ref, sx0_ref, sx4_ref, sy0_ref, sy4_ref, row_len)
@@ -353,7 +362,7 @@
     )(state)
 
 
-def dg_step(state, src, recv, own_mat, other_mat, want_faces, row_len, xoff=0, yoff=0):
+def dg_step(state, src, recv, mats, want_faces, row_len, xoff=0, yoff=0):
     elems = state.shape[1]
     out_shape = [jax.ShapeDtypeStruct(state.shape, jnp.float32)]
     if want_faces:
@@ -365,8 +374,9 @@
             pltpu.VMEM((6, FACE_ROWS, elems), jnp.float32),
             pltpu.VMEM((768, elems), jnp.float32),
             pltpu.VMEM((FACE_ROWS, elems), jnp.float32),
+            pltpu.VMEM((152, 4 * elems), jnp.float32),
         ],
-    )(state, src, *recv, own_mat, other_mat)
+    )(state, src, *recv, *mats)
     return res
 
 
@@ -403,9 +413,7 @@
     state = jnp.zeros((512, elem_count), jnp.float32).at[:, target].set(arrived, mode="drop")
 
     row_len = velocity.shape[3] // 8
-    own_np, other_np = dg_matrices()
-    own_mat = jnp.asarray(own_np)
-    other_mat = jnp.asarray(other_np)
+    mats = [jnp.asarray(m) for m in dg_matrices()]
     sent = dg_faces(state, row_len)
     vel, mxup, mxdn, myup, mydn = les_section_first(velocity, eddy_visc, joint, sent)
     merged = exchange_faces((mxdn, mxup, mydn, myup))
@@ -413,10 +421,10 @@
     source = project(lamb, projection)
     xoff = 3 * 2 * velocity.shape[2]
     yoff = 3 * 2 * velocity.shape[1]
-    res = dg_step(state, source, merged, own_mat, other_mat, True, row_len, xoff, yoff)
+    res = dg_step(state, source, merged, mats, True, row_len, xoff, yoff)
     state = res[0]
     recv = exchange_faces(res[1:])
-    state = dg_step(state, source, recv, own_mat, other_mat, False, row_len)[0]
+    state = dg_step(state, source, recv, mats, False, row_len)[0]
     flat_state = state
     leaving = jnp.where(filled[None, :], flat_state[:, jnp.where(filled, sending, 0)], 0.0)
     returned = lax.all_to_all(leaving, ("flow", "grp"), split_axis=1, concat_axis=1, tiled=True)

time: 120 us -> 117 us (0.975)
  Pallas kernels: 18.1 us -> 15.5 us
    pallas_call x2, Pallas kernels: 8.21 us -> 5.66 us  [dg_step(): pl.pallas_call(lambda *refs: dg_step_kernel(want_faces, xoff, yoff, row_l...]
  transfers between devices with their start and end apart: 14 -> 14, of which waited for: 5 -> 6; matrix products, arithmetic and copies ran while one was open for 3% -> 3% of each run, Pallas kernels for 1% -> 1%
where the time goes in v8:
time: 117 us; the launch traced here: 116 us
  starting transfers between devices  52.3 us (45%)
  waiting for transfers between devices  26.6 us (23%)
  local copies, waits for them, and re-layouts  16.7 us (14%)
  Pallas kernels  15.5 us (13%)
  matrix products  2.23 us (2%)
  other arithmetic  1.87 us (2%)
    all_to_all x1, waiting for transfers between devices, body(): lax.all_to_all(leaving, ('flow', 'grp'), split_axis=1, concat_axis=1, til...  14.1 us
    all_to_all x1, starting transfers between devices, body(): lax.all_to_all(leaving, ('flow', 'grp'), split_axis=1, concat_axis=1, til...  12.8 us
    all_to_all x1, starting transfers between devices, body(): lax.all_to_all(outgoing, ('flow', 'grp'), split_axis=1, concat_axis=1, ti...  11.5 us
    ppermute x2, waiting for transfers between devices, exchange_faces(): lax.ppermute(sy0, 'grp', down_g)  7.81 us
    ppermute x2, starting transfers between devices, exchange_faces(): lax.ppermute(sx4, 'flow', up_f)  6.6 us
    pallas_call x2, Pallas kernels, dg_step(): pl.pallas_call(lambda *refs: dg_step_kernel(want_faces, xoff, yoff, row_l...  5.66 us
    ppermute x2, starting transfers between devices, exchange_faces(): lax.ppermute(sy4, 'grp', up_g)  4.99 us
    pallas_call x1, Pallas kernels, les_section_first(): pl.pallas_call(lambda *refs: les_kernel(0, *refs), out_shape=(jax.ShapeDt...  4.16 us
  transfers between devices with their start and end apart: 14, of which 6 were waited for; matrix products, arithmetic and copies ran while one was open for 3% of the time, Pallas kernels for 1%

profile of v8, /device:TPU:1, one launch (start us, length us, event | category | flops | bytes accessed | tf_op | source)
XLA Modules:
  0.0 116.2 jit_solution(2166152434343214629)
XLA Ops:
  2.4 1.1 scatter_custom_fusion
  3.6 1.1 all_to_all.14
  4.7 11.5 %all-to-all-start = ((f32[512,128,2]{0,2,1:T(2,128)}), f32[512,128,2]{0,2,1:T(2,128)S(1)}, u32[]{:S(2)}, u32[]{:S(2)}) async-start(f32[512,128,2]{0,2,1:T(2,128)} %all_to_all.14), calls=%async_computation | async-start | bytes 1048576 | tf_op jit(solution)/shard_map/all_to_all | solution.py:409
  16.2 3.7 %collective-permute-start = (f32[4,32,256]{2,1,0:T(8,128)S(1)}, f32[4,32,256]{2,1,0:T(8,128)S(1)}, u32[]{:S(2)}, u32[]{:S(2)}) collective-permute-start(f32[4,32,256]{2,1,0:T(8,128)S(1)} %get-tuple-element.37), channel_id=1, source_target_pairs={{0,4},{4,8},{8,12},{12,16},{16,20},{20,24},{24,28},{28,32},{32,36}... | collective-permute-start | bytes 393224 | tf_op jit(solution)/shard_map/ppermute | solution.py:239
  19.9 1.9 %collective-permute-start.1 = (f32[4,32,256]{2,1,0:T(8,128)S(1)}, f32[4,32,256]{2,1,0:T(8,128)S(1)}, u32[]{:S(2)}, u32[]{:S(2)}) collective-permute-start(f32[4,32,256]{2,1,0:T(8,128)S(1)} %get-tuple-element.36), channel_id=1, source_target_pairs={{4,0},{8,4},{12,8},{16,12},{20,16},{24,20},{28,24},{32,28},{36,32}... | collective-permute-start | bytes 393224 | tf_op jit(solution)/shard_map/ppermute | solution.py:240
  21.9 3.1 %collective-permute-start.2 = (f32[4,8,1,256]{3,2,1,0:T(1,128)S(1)}, f32[4,8,1,256]{3,2,1,0:T(1,128)S(1)}, u32[]{:S(2)}, u32[]{:S(2)}) collective-permute-start(f32[4,8,1,256]{3,2,1,0:T(1,128)S(1)} %get-tuple-element.35), channel_id=1, source_target_pairs={{0,1},{1,2},{2,3},{4,5},{5,6},{6,7},{8,9},{9,10},{10,11},{12,13},{... | collective-permute-start | bytes 98312 | tf_op jit(solution)/shard_map/ppermute | solution.py:241
  25.0 1.3 %collective-permute-start.3 = (f32[4,8,1,256]{3,2,1,0:T(1,128)S(1)}, f32[4,8,1,256]{3,2,1,0:T(1,128)S(1)}, u32[]{:S(2)}, u32[]{:S(2)}) collective-permute-start(f32[4,8,1,256]{3,2,1,0:T(1,128)S(1)} %get-tuple-element.34), channel_id=1, source_target_pairs={{1,0},{2,1},{3,2},{5,4},{6,5},{7,6},{9,8},{10,9},{11,10},{13,12},{... | collective-permute-start | bytes 98312 | tf_op jit(solution)/shard_map/ppermute | solution.py:242
  26.6 3.7 %all-to-all-done = f32[512,128,2]{0,2,1:T(2,128)S(1)} async-done(((f32[512,128,2]{0,2,1:T(2,128)}), f32[512,128,2]{0,2,1:T(2,128)S(1)}, u32[]{:S(2)}, u32[]{:S(2)}) %all-to-all-start) | async-done | bytes 524320 | tf_op jit(solution)/shard_map/all_to_all | solution.py:409
  30.7 1.5 %scatter_custom_fusion.1 = f32[512,128]{0,1:T(8,128)S(1)} fusion(s32[256]{0:T(256)S(1)} %bitcast.62, f32[512,256]{0,1:T(8,128)S(1)} %reshape.158, f32[]{:T(128)} %constant.10.clone.1), kind=kCustom, calls=%fused_computation.6 | custom fusion | bytes 786436 | tf_op jit(solution)/shard_map/scatter | solution.py:413
  33.1 1.7 %shard_map.122 = (f32[104,128]{1,0:T(8,128)}, f32[104,128]{1,0:T(8,128)}, f32[104,32]{1,0:T(8,128)}, f32[104,32]{1,0:T(8,128)}) custom-call(f32[512,128]{1,0:T(8,128)} %copy.31.state_ref.refs_0_), custom_call_target="tpu_custom_call" | custom-call | tf_op jit(solution)/shard_map/pallas_call | solution.py:358
  35.5 4.2 %shard_map.123 = (f32[3,8,32,256]{3,2,1,0:T(8,128)}, f32[296,128]{1,0:T(8,128)}, f32[296,128]{1,0:T(8,128)}, f32[152,128]{1,0:T(8,128)}, f32[152,128]{1,0:T(8,128)}) custom-call(f32[3,8,32,256]{3,2,1,0:T(8,128)} %refs_0_.1, f32[8,32,256]{2,1,0:T(8,128)} %refs_1_.3, f32[4,32,256]{2,1,0:T(8,128)} %copy-done.2, f32[4,32,256]{2,1,0:T(8,128)} %copy-done.3, ...), custom_call_target="tpu_custom_call" | custom-call | tf_op jit(solution)/shard_map/pallas_call | solution.py:218
  39.7 2.6 %collective-permute-start.4 = (f32[296,128]{1,0:T(8,128)}, f32[296,128]{1,0:T(8,128)S(1)}, u32[]{:S(2)}, u32[]{:S(2)}) collective-permute-start(f32[296,128]{1,0:T(8,128)} %get-tuple-element.23), channel_id=1, source_target_pairs={{0,4},{4,8},{8,12},{12,16},{16,20},{20,24},{24,28},{28,32},{32,36}... | collective-permute-start | bytes 454664 | tf_op jit(solution)/shard_map/ppermute | solution.py:392
  42.3 1.9 %collective-permute-start.5 = (f32[296,128]{1,0:T(8,128)}, f32[296,128]{1,0:T(8,128)S(1)}, u32[]{:S(2)}, u32[]{:S(2)}) collective-permute-start(f32[296,128]{1,0:T(8,128)} %get-tuple-element.24), channel_id=1, source_target_pairs={{4,0},{8,4},{12,8},{16,12},{20,16},{24,20},{28,24},{32,28},{36,32}... | collective-permute-start | bytes 454664 | tf_op jit(solution)/shard_map/ppermute | solution.py:393
  44.2 2.2 %collective-permute-start.6 = (f32[152,128]{1,0:T(8,128)}, f32[152,128]{1,0:T(8,128)S(1)}, u32[]{:S(2)}, u32[]{:S(2)}) collective-permute-start(f32[152,128]{1,0:T(8,128)} %get-tuple-element.25), channel_id=1, source_target_pairs={{0,1},{1,2},{2,3},{4,5},{5,6},{6,7},{8,9},{9,10},{10,11},{12,13},{... | collective-permute-start | bytes 233480 | tf_op jit(solution)/shard_map/ppermute | solution.py:394
  46.4 1.3 %collective-permute-start.7 = (f32[152,128]{1,0:T(8,128)}, f32[152,128]{1,0:T(8,128)S(1)}, u32[]{:S(2)}, u32[]{:S(2)}) collective-permute-start(f32[152,128]{1,0:T(8,128)} %get-tuple-element.26), channel_id=1, source_target_pairs={{1,0},{2,1},{3,2},{5,4},{6,5},{7,6},{9,8},{10,9},{11,10},{13,12},{... | collective-permute-start | bytes 233480 | tf_op jit(solution)/shard_map/ppermute | solution.py:395
  48.5 4.2 %collective-permute-done.7.refs_5_ = f32[152,128]{1,0:T(8,128)S(1)} collective-permute-done((f32[152,128]{1,0:T(8,128)}, f32[152,128]{1,0:T(8,128)S(1)}, u32[]{:S(2)}, u32[]{:S(2)}) %collective-permute-start.7) | collective-permute-done | bytes 77856 | tf_op jit(solution)/shard_map/ppermute | solution.py:395
  53.6 4.0 %shard_map.124 = (f32[3,8,32,256]{3,2,1,0:T(8,128)}, bf16[3,8,32,256]{3,2,1,0:T(8,128)(2,1)}) custom-call(f32[3,8,32,256]{3,2,1,0:T(8,128)} %get-tuple-element.22.refs_0_, f32[8,32,256]{2,1,0:T(8,128)} %refs_1_.3, f32[296,128]{1,0:T(8,128)} %copy-done.4, f32[296,128]{1,0:T(8,128)} %copy-done.5, f32[152,128]{1,0:T(8,128)} %copy-done.6, f32[152,128]{1,0:T(8,128)} %copy-done.7, ...), custom_call_target="tpu_custom_call" | custom-call | tf_op jit(solution)/shard_map/pallas_call | solution.py:225
  57.6 1.3 %convolution_convert_fusion = bf16[768,256]{1,0:T(8,128)(2,1)S(1)} fusion(bf16[768,256]{1,0:T(8,128)(2,1)} %bitcast.60, bf16[256,256]{1,0:T(8,128)(2,1)S(1)} %copy-done.10), kind=kOutput, calls=%fused_computation.5 | convolution fusion | flops 100859904 | bytes 917504 | tf_op jit(solution)/shard_map/dot_general | solution.py:254
  59.5 2.0 %copy.40 = bf16[3,1,8,4,8,8,32]{6,3,0,5,4,2,1:T(4,128)(2,1)S(1)} copy(bf16[3,1,8,4,8,8,32]{6,5,4,3,2,0,1:T(8,128)(2,1)S(1)} %reshape.129) | data formatting | bytes 786432 | tf_op jit(solution)/shard_map/reshape | solution.py:256
  62.6 1.0 fusion.4
  63.6 2.9 %shard_map.125 = (f32[512,128]{1,0:T(8,128)}, f32[104,128]{1,0:T(8,128)}, f32[104,128]{1,0:T(8,128)}, f32[104,32]{1,0:T(8,128)}, f32[104,32]{1,0:T(8,128)}) custom-call(f32[512,128]{1,0:T(8,128)} %copy.31.state_ref.refs_0_, f32[384,128]{1,0:T(8,128)} %bitcast.53, f32[296,128]{1,0:T(8,128)} %copy-done.4, f32[296,128]{1,0:T(8,128)} %copy-done.5, ...), custom_call_target="tpu_custom_call" | custom-call | tf_op jit(solution)/shard_map/pallas_call | solution.py:370
  66.5 4.0 %collective-permute-start.8 = (f32[104,128]{1,0:T(8,128)}, f32[104,128]{1,0:T(8,128)S(1)}, u32[]{:S(2)}, u32[]{:S(2)}) collective-permute-start(f32[104,128]{1,0:T(8,128)} %get-tuple-element.30), channel_id=1, source_target_pairs={{0,4},{4,8},{8,12},{12,16},{16,20},{20,24},{24,28},{28,32},{32,36}... | collective-permute-start | bytes 159752 | tf_op jit(solution)/shard_map/ppermute | solution.py:392
  70.6 1.9 %collective-permute-start.9 = (f32[104,128]{1,0:T(8,128)}, f32[104,128]{1,0:T(8,128)S(1)}, u32[]{:S(2)}, u32[]{:S(2)}) collective-permute-start(f32[104,128]{1,0:T(8,128)} %get-tuple-element.31), channel_id=1, source_target_pairs={{4,0},{8,4},{12,8},{16,12},{20,16},{24,20},{28,24},{32,28},{36,32}... | collective-permute-start | bytes 159752 | tf_op jit(solution)/shard_map/ppermute | solution.py:393
  72.5 2.8 %collective-permute-start.10 = (f32[104,32]{1,0:T(8,128)}, f32[104,32]{1,0:T(8,128)S(1)}, u32[]{:S(2)}, u32[]{:S(2)}) collective-permute-start(f32[104,32]{1,0:T(8,128)} %get-tuple-element.32), channel_id=1, source_target_pairs={{0,1},{1,2},{2,3},{4,5},{5,6},{6,7},{8,9},{9,10},{10,11},{12,13},{... | collective-permute-start | bytes 39944 | tf_op jit(solution)/shard_map/ppermute | solution.py:394
  75.3 1.3 %collective-permute-start.11 = (f32[104,32]{1,0:T(8,128)}, f32[104,32]{1,0:T(8,128)S(1)}, u32[]{:S(2)}, u32[]{:S(2)}) collective-permute-start(f32[104,32]{1,0:T(8,128)} %get-tuple-element.33), channel_id=1, source_target_pairs={{1,0},{2,1},{3,2},{5,4},{6,5},{7,6},{9,8},{10,9},{11,10},{13,12},{... | collective-permute-start | bytes 39944 | tf_op jit(solution)/shard_map/ppermute | solution.py:395
  76.8 3.6 %collective-permute-done.11.refs_5_ = f32[104,32]{1,0:T(8,128)S(1)} collective-permute-done((f32[104,32]{1,0:T(8,128)}, f32[104,32]{1,0:T(8,128)S(1)}, u32[]{:S(2)}, u32[]{:S(2)}) %collective-permute-start.11) | collective-permute-done | bytes 13344 | tf_op jit(solution)/shard_map/ppermute | solution.py:395
  81.0 2.7 %shard_map.126 = f32[512,128]{1,0:T(8,128)} custom-call(f32[512,128]{1,0:T(8,128)} %get-tuple-element.29.refs_0_, f32[384,128]{1,0:T(8,128)} %bitcast.54, f32[104,128]{1,0:T(8,128)} %copy-done.12, f32[104,128]{1,0:T(8,128)} %copy-done.13, f32[104,32]{1,0:T(8,128)} %copy-done.14, f32[104,32]{1,0:T(8,128)} %copy-done.15, f32[128,384]{1,0:T(8,128)} %constant.8.clone.refs_6_, ...), custom_call_target="tpu_custom_call" | custom-call | tf_op jit(solution)/shard_map/pallas_call | solution.py:370
  83.7 1.1 copy.36
  84.8 1.0 gather_fusion
  86.1 1.1 broadcast_select_fusion
  87.2 12.8 %all-to-all-start.1 = ((f32[512,128,2]{0,2,1:T(2,128)}), f32[512,128,2]{0,2,1:T(2,128)S(1)}, u32[]{:S(2)}, u32[]{:S(2)}) async-start(f32[512,128,2]{0,2,1:T(2,128)} %broadcast_select_fusion), calls=%async_computation.1 | async-start | bytes 1048576 | tf_op jit(solution)/shard_map/all_to_all | solution.py:430
  100.0 14.1 %all-to-all-done.1 = f32[512,128,2]{0,2,1:T(2,128)S(1)} async-done(((f32[512,128,2]{0,2,1:T(2,128)}), f32[512,128,2]{0,2,1:T(2,128)S(1)}, u32[]{:S(2)}, u32[]{:S(2)}) %all-to-all-start.1) | async-done | bytes 524320 | tf_op jit(solution)/shard_map/all_to_all | solution.py:430
  (67 shorter events, 10.5 us)
Async XLA Ops:
  2.3 13.9 %copy-start = (f32[3,8,32,256]{3,2,1,0:T(8,128)S(1)}, f32[3,8,32,256]{3,2,1,0:T(8,128)}, u32[]{:S(2)}) copy-start(f32[3,8,32,256]{3,2,1,0:T(8,128)} %refs_0_.1) | copy-start | bytes 2359300
  2.3 13.9 %copy-start.1 = (f32[8,32,256]{2,1,0:T(8,128)S(1)}, f32[8,32,256]{2,1,0:T(8,128)}, u32[]{:S(2)}) copy-start(f32[8,32,256]{2,1,0:T(8,128)} %refs_1_.3) | copy-start | bytes 786436
  4.7 21.6 %copy-start.16 = (s32[1,128,2]{1,2,0:T(2,128)S(1)}, s32[1,128,2]{1,2,0:T(2,128)}, u32[]{:S(2)}) copy-start(s32[1,128,2]{1,2,0:T(2,128)} %param.15) | copy-start | bytes 3076
  4.7 25.6 %all-to-all-start = ((f32[512,128,2]{0,2,1:T(2,128)}), f32[512,128,2]{0,2,1:T(2,128)S(1)}, u32[]{:S(2)}, u32[]{:S(2)}) async-start(f32[512,128,2]{0,2,1:T(2,128)} %all_to_all.14), calls=%async_computation | async-start | bytes 1048576 | tf_op jit(solution)/shard_map/all_to_all | solution.py:409
  16.2 18.5 %collective-permute-start = (f32[4,32,256]{2,1,0:T(8,128)S(1)}, f32[4,32,256]{2,1,0:T(8,128)S(1)}, u32[]{:S(2)}, u32[]{:S(2)}) collective-permute-start(f32[4,32,256]{2,1,0:T(8,128)S(1)} %get-tuple-element.37), channel_id=1, source_target_pairs={{0,4},{4,8},{8,12},{12,16},{16,20},{20,24},{24,28},{28,32},{32,36}... | collective-permute-start | bytes 393224 | tf_op jit(solution)/shard_map/ppermute | solution.py:239
  19.9 14.9 %collective-permute-start.1 = (f32[4,32,256]{2,1,0:T(8,128)S(1)}, f32[4,32,256]{2,1,0:T(8,128)S(1)}, u32[]{:S(2)}, u32[]{:S(2)}) collective-permute-start(f32[4,32,256]{2,1,0:T(8,128)S(1)} %get-tuple-element.36), channel_id=1, source_target_pairs={{4,0},{8,4},{12,8},{16,12},{20,16},{24,20},{28,24},{32,28},{36,32}... | collective-permute-start | bytes 393224 | tf_op jit(solution)/shard_map/ppermute | solution.py:240
  21.9 12.9 %collective-permute-start.2 = (f32[4,8,1,256]{3,2,1,0:T(1,128)S(1)}, f32[4,8,1,256]{3,2,1,0:T(1,128)S(1)}, u32[]{:S(2)}, u32[]{:S(2)}) collective-permute-start(f32[4,8,1,256]{3,2,1,0:T(1,128)S(1)} %get-tuple-element.35), channel_id=1, source_target_pairs={{0,1},{1,2},{2,3},{4,5},{5,6},{6,7},{8,9},{9,10},{10,11},{12,13},{... | collective-permute-start | bytes 98312 | tf_op jit(solution)/shard_map/ppermute | solution.py:241
  25.0 9.8 %collective-permute-start.3 = (f32[4,8,1,256]{3,2,1,0:T(1,128)S(1)}, f32[4,8,1,256]{3,2,1,0:T(1,128)S(1)}, u32[]{:S(2)}, u32[]{:S(2)}) collective-permute-start(f32[4,8,1,256]{3,2,1,0:T(1,128)S(1)} %get-tuple-element.34), channel_id=1, source_target_pairs={{1,0},{2,1},{3,2},{5,4},{6,5},{7,6},{9,8},{10,9},{11,10},{13,12},{... | collective-permute-start | bytes 98312 | tf_op jit(solution)/shard_map/ppermute | solution.py:242
  34.8 0.6 copy-start.8
  34.8 0.6 copy-start.9
  34.8 0.7 copy-start.2
  34.8 0.7 copy-start.3
  35.5 22.1 %copy-start.10 = (bf16[256,256]{1,0:T(8,128)(2,1)S(1)}, bf16[256,256]{1,0:T(8,128)(2,1)}, u32[]{:S(2)}) copy-start(bf16[256,256]{1,0:T(8,128)(2,1)} %constant.30.clone) | copy-start | bytes 393220
  39.7 13.1 %collective-permute-start.4 = (f32[296,128]{1,0:T(8,128)}, f32[296,128]{1,0:T(8,128)S(1)}, u32[]{:S(2)}, u32[]{:S(2)}) collective-permute-start(f32[296,128]{1,0:T(8,128)} %get-tuple-element.23), channel_id=1, source_target_pairs={{0,4},{4,8},{8,12},{12,16},{16,20},{20,24},{24,28},{28,32},{32,36}... | collective-permute-start | bytes 454664 | tf_op jit(solution)/shard_map/ppermute | solution.py:392
  42.3 10.5 %collective-permute-start.5 = (f32[296,128]{1,0:T(8,128)}, f32[296,128]{1,0:T(8,128)S(1)}, u32[]{:S(2)}, u32[]{:S(2)}) collective-permute-start(f32[296,128]{1,0:T(8,128)} %get-tuple-element.24), channel_id=1, source_target_pairs={{4,0},{8,4},{12,8},{16,12},{20,16},{24,20},{28,24},{32,28},{36,32}... | collective-permute-start | bytes 454664 | tf_op jit(solution)/shard_map/ppermute | solution.py:393
  44.2 4.4 %collective-permute-start.6 = (f32[152,128]{1,0:T(8,128)}, f32[152,128]{1,0:T(8,128)S(1)}, u32[]{:S(2)}, u32[]{:S(2)}) collective-permute-start(f32[152,128]{1,0:T(8,128)} %get-tuple-element.25), channel_id=1, source_target_pairs={{0,1},{1,2},{2,3},{4,5},{5,6},{6,7},{8,9},{9,10},{10,11},{12,13},{... | collective-permute-start | bytes 233480 | tf_op jit(solution)/shard_map/ppermute | solution.py:394
  46.4 6.4 %collective-permute-start.7 = (f32[152,128]{1,0:T(8,128)}, f32[152,128]{1,0:T(8,128)S(1)}, u32[]{:S(2)}, u32[]{:S(2)}) collective-permute-start(f32[152,128]{1,0:T(8,128)} %get-tuple-element.26), channel_id=1, source_target_pairs={{1,0},{2,1},{3,2},{5,4},{6,5},{7,6},{9,8},{10,9},{11,10},{13,12},{... | collective-permute-start | bytes 233480 | tf_op jit(solution)/shard_map/ppermute | solution.py:395
  48.5 4.3 %copy-start.6 = (f32[152,128]{1,0:T(8,128)}, f32[152,128]{1,0:T(8,128)S(1)}, u32[]{:S(2)}) copy-start(f32[152,128]{1,0:T(8,128)S(1)} %collective-permute-done.6.refs_4_) | copy-start | bytes 233476
  52.8 0.6 copy-start.7
  52.8 0.7 copy-start.4
  52.8 0.8 copy-start.5
  61.5 1.1 copy-start.11
  66.5 13.8 %collective-permute-start.8 = (f32[104,128]{1,0:T(8,128)}, f32[104,128]{1,0:T(8,128)S(1)}, u32[]{:S(2)}, u32[]{:S(2)}) collective-permute-start(f32[104,128]{1,0:T(8,128)} %get-tuple-element.30), channel_id=1, source_target_pairs={{0,4},{4,8},{8,12},{12,16},{16,20},{20,24},{24,28},{28,32},{32,36}... | collective-permute-start | bytes 159752 | tf_op jit(solution)/shard_map/ppermute | solution.py:392
  70.6 9.8 %collective-permute-start.9 = (f32[104,128]{1,0:T(8,128)}, f32[104,128]{1,0:T(8,128)S(1)}, u32[]{:S(2)}, u32[]{:S(2)}) collective-permute-start(f32[104,128]{1,0:T(8,128)} %get-tuple-element.31), channel_id=1, source_target_pairs={{4,0},{8,4},{12,8},{16,12},{20,16},{24,20},{28,24},{32,28},{36,32}... | collective-permute-start | bytes 159752 | tf_op jit(solution)/shard_map/ppermute | solution.py:393
  72.5 4.3 %collective-permute-start.10 = (f32[104,32]{1,0:T(8,128)}, f32[104,32]{1,0:T(8,128)S(1)}, u32[]{:S(2)}, u32[]{:S(2)}) collective-permute-start(f32[104,32]{1,0:T(8,128)} %get-tuple-element.32), channel_id=1, source_target_pairs={{0,1},{1,2},{2,3},{4,5},{5,6},{6,7},{8,9},{9,10},{10,11},{12,13},{... | collective-permute-start | bytes 39944 | tf_op jit(solution)/shard_map/ppermute | solution.py:394
  75.3 5.1 %collective-permute-start.11 = (f32[104,32]{1,0:T(8,128)}, f32[104,32]{1,0:T(8,128)S(1)}, u32[]{:S(2)}, u32[]{:S(2)}) collective-permute-start(f32[104,32]{1,0:T(8,128)} %get-tuple-element.33), channel_id=1, source_target_pairs={{1,0},{2,1},{3,2},{5,4},{6,5},{7,6},{9,8},{10,9},{11,10},{13,12},{... | collective-permute-start | bytes 39944 | tf_op jit(solution)/shard_map/ppermute | solution.py:395
  76.8 3.6 %copy-start.14 = (f32[104,32]{1,0:T(8,128)}, f32[104,32]{1,0:T(8,128)S(1)}, u32[]{:S(2)}) copy-start(f32[104,32]{1,0:T(8,128)S(1)} %collective-permute-done.10.refs_4_) | copy-start | bytes 39940
  80.4 0.6 copy-start.15
  80.4 0.6 copy-start.12
  80.4 0.6 copy-start.13
  87.2 26.9 %all-to-all-start.1 = ((f32[512,128,2]{0,2,1:T(2,128)}), f32[512,128,2]{0,2,1:T(2,128)S(1)}, u32[]{:S(2)}, u32[]{:S(2)}) async-start(f32[512,128,2]{0,2,1:T(2,128)} %broadcast_select_fusion), calls=%async_computation.1 | async-start | bytes 1048576 | tf_op jit(solution)/shard_map/all_to_all | solution.py:430

commit v9 on v8

--- a/solution.py
+++ b/solution.py
@@ -404,13 +404,13 @@
     elem_count = acoustic_state.shape[2]
     total_slots = flow_size * grp_size * slot_cap
     placing = route_place.reshape(-1)
+    sending = route_send.reshape(-1)
+    place_hot = (placing[:, None] == jnp.arange(total_slots, dtype=jnp.int32)[None, :]).astype(jnp.float32)
+    home_hot = (sending[:, None] == jnp.arange(elem_count, dtype=jnp.int32)[None, :]).astype(jnp.float32)
     padded_state = jnp.pad(acoustic_state, ((0, 0), (0, 3), (0, 0))).reshape(512, elem_count)
-    outgoing = jnp.zeros((512, total_slots), jnp.float32).at[:, placing].set(padded_state)
+    outgoing = jnp.dot(padded_state, place_hot, precision=HIGH)
     arrived = lax.all_to_all(outgoing, ("flow", "grp"), split_axis=1, concat_axis=1, tiled=True)
-    sending = route_send.reshape(-1)
-    filled = sending >= 0
-    target = jnp.where(filled, sending, elem_count)
-    state = jnp.zeros((512, elem_count), jnp.float32).at[:, target].set(arrived, mode="drop")
+    state = jnp.dot(arrived, home_hot, precision=HIGH)
 
     row_len = velocity.shape[3] // 8
     mats = [jnp.asarray(m) for m in dg_matrices()]
@@ -425,10 +425,10 @@
     state = res[0]
     recv = exchange_faces(res[1:])
     state = dg_step(state, source, recv, mats, False, row_len)[0]
-    flat_state = state
-    leaving = jnp.where(filled[None, :], flat_state[:, jnp.where(filled, sending, 0)], 0.0)
+    leaving = lax.dot_general(state, home_hot, (((1,), (1,)), ((), ())), precision=HIGH)
     returned = lax.all_to_all(leaving, ("flow", "grp"), split_axis=1, concat_axis=1, tiled=True)
-    acoustic_out = returned[:, placing].reshape(4, 128, elem_count)[:, :125]
+    acoustic_out = lax.dot_general(returned, place_hot, (((1,), (1,)), ((), ())), precision=HIGH)
+    acoustic_out = acoustic_out.reshape(4, 128, elem_count)[:, :125]
     return (vel, acoustic_out)
 
 

time: 117 us -> 114 us (0.974)
  blocking collectives: 0 us -> 28.1 us
  waiting for transfers between devices: 26.6 us -> 11.2 us
  starting transfers between devices: 52.3 us -> 40.5 us
  local copies, waits for them, and re-layouts: 16.7 us -> 10.1 us
  matrix products: 2.23 us -> 6.77 us
  other arithmetic: 1.87 us -> 0.07 us
    all_to_all x0 -> x1, blocking collectives: none -> 28.1 us  [body(): lax.all_to_all(leaving, ('flow', 'grp'), split_axis=1, concat_axis=1, til...]
    all_to_all x1 -> x0, waiting for transfers between devices: 14.1 us -> none  [body(): lax.all_to_all(leaving, ('flow', 'grp'), split_axis=1, concat_axis=1, til...]
    all_to_all x1 -> x0, starting transfers between devices: 12.8 us -> none  [body(): lax.all_to_all(leaving, ('flow', 'grp'), split_axis=1, concat_axis=1, til...]
    dot_general x0 -> x4, matrix products: none -> 4.55 us  [the longest x1 1.36 us: body(): lax.dot_general(state, home_hot, (((1,), (1,)), ((), ())), precision=HIGH)]
    scatter x3 -> x0, local copies, waits for them, and re-layouts: 3.51 us -> none  [the longest x2 2.37 us: body(): jnp.zeros((512, elem_count), jnp.float32).at[:, target]]
    gather x3 -> x0, local copies, waits for them, and re-layouts: 2.03 us -> none  [the longest x2 1.28 us: body(): flat_state[:, jnp.where(filled, sending, 0)]]
    select_n x3 -> x0, other arithmetic: 1.78 us -> none  [the longest x1 1.11 us: body(): jnp.where(filled[None, :], flat_state[:, jnp.where(filled, sending, 0)],...]
    ppermute x1, starting transfers between devices: 1.92 us -> 3.54 us  [halos(): lax.ppermute(lax.index_in_dim(field, 0, lead, keepdims=False), 'flow', do...]
  transfers between devices with their start and end apart: 14 -> 13, of which waited for: 6 -> 5; matrix products, arithmetic and copies ran while one was open for 3% -> 1% of each run, Pallas kernels for 1% -> 1%
where the time goes in v9:
time: 114 us; the launch traced here: 113 us
  starting transfers between devices  40.5 us (36%)
  blocking collectives  28.1 us (25%)
  Pallas kernels  15.5 us (14%)
  waiting for transfers between devices  11.2 us (10%)
  local copies, waits for them, and re-layouts  10.1 us (9%)
  matrix products  6.77 us (6%)
    all_to_all x1, blocking collectives, body(): lax.all_to_all(leaving, ('flow', 'grp'), split_axis=1, concat_axis=1, til...  28.1 us
    all_to_all x1, starting transfers between devices, body(): lax.all_to_all(outgoing, ('flow', 'grp'), split_axis=1, concat_axis=1, ti...  11.5 us
    ppermute x2, waiting for transfers between devices, exchange_faces(): lax.ppermute(sy0, 'grp', down_g)  7.61 us
    ppermute x2, starting transfers between devices, exchange_faces(): lax.ppermute(sx4, 'flow', up_f)  6.46 us
    pallas_call x2, Pallas kernels, dg_step(): pl.pallas_call(lambda *refs: dg_step_kernel(want_faces, xoff, yoff, row_l...  5.65 us
    ppermute x2, starting transfers between devices, exchange_faces(): lax.ppermute(sy4, 'grp', up_g)  4.67 us
    pallas_call x1, Pallas kernels, les_section_first(): pl.pallas_call(lambda *refs: les_kernel(0, *refs), out_shape=(jax.ShapeDt...  4.16 us
    unnamed x39, local copies, waits for them, and re-layouts  4.08 us
  transfers between devices with their start and end apart: 13, of which 5 were waited for; matrix products, arithmetic and copies ran while one was open for 1% of the time, Pallas kernels for 1%

profile of v9, /device:TPU:1, one launch (start us, length us, event | category | flops | bytes accessed | tf_op | source)
XLA Modules:
  0.0 113.2 jit_solution(4288710441966325013)
XLA Ops:
  0.6 1.0 copy.37
  1.7 1.2 %fusion.9 = f32[512,128,2]{1,0,2:T(8,128)S(1)} fusion(f32[512,128,1]{1,0,2:T(8,128)S(1)} %bitcast.47, s32[128,2]{0,1:T(2,128)S(1)} %multiply_add_fusion, s32[128]{0:T(128)} %bitcast.49), kind=kOutput, calls=%fused_computation.14 | convolution fusion | flops 201359360 | bytes 787968 | tf_op jit(solution)/shard_map/dot_general | solution.py:411
  2.9 1.0 copy.31
  3.9 11.5 %all-to-all-start = ((f32[512,128,2]{0,2,1:T(2,128)}), f32[512,128,2]{0,2,1:T(2,128)S(1)}, u32[]{:S(2)}, u32[]{:S(2)}) async-start(f32[512,128,2]{0,2,1:T(2,128)} %copy.31), calls=%async_computation | async-start | bytes 1048576 | tf_op jit(solution)/shard_map/all_to_all | solution.py:412
  15.4 1.3 %collective-permute-start.3 = (f32[4,8,1,256]{3,2,1,0:T(1,128)S(1)}, f32[4,8,1,256]{3,2,1,0:T(1,128)S(1)}, u32[]{:S(2)}, u32[]{:S(2)}) collective-permute-start(f32[4,8,1,256]{3,2,1,0:T(1,128)S(1)} %get-tuple-element.42), channel_id=1, source_target_pairs={{1,0},{2,1},{3,2},{5,4},{6,5},{7,6},{9,8},{10,9},{11,10},{13,12},{... | collective-permute-start | bytes 98312 | tf_op jit(solution)/shard_map/ppermute | solution.py:242
  16.7 4.0 %collective-permute-start.2 = (f32[4,8,1,256]{3,2,1,0:T(1,128)S(1)}, f32[4,8,1,256]{3,2,1,0:T(1,128)S(1)}, u32[]{:S(2)}, u32[]{:S(2)}) collective-permute-start(f32[4,8,1,256]{3,2,1,0:T(1,128)S(1)} %get-tuple-element.43), channel_id=1, source_target_pairs={{0,1},{1,2},{2,3},{4,5},{5,6},{6,7},{8,9},{9,10},{10,11},{12,13},{... | collective-permute-start | bytes 98312 | tf_op jit(solution)/shard_map/ppermute | solution.py:241
  20.8 3.5 %collective-permute-start.1 = (f32[4,32,256]{2,1,0:T(8,128)S(1)}, f32[4,32,256]{2,1,0:T(8,128)S(1)}, u32[]{:S(2)}, u32[]{:S(2)}) collective-permute-start(f32[4,32,256]{2,1,0:T(8,128)S(1)} %get-tuple-element.44), channel_id=1, source_target_pairs={{4,0},{8,4},{12,8},{16,12},{20,16},{24,20},{28,24},{32,28},{36,32}... | collective-permute-start | bytes 393224 | tf_op jit(solution)/shard_map/ppermute | solution.py:240
  24.3 2.6 %collective-permute-start = (f32[4,32,256]{2,1,0:T(8,128)S(1)}, f32[4,32,256]{2,1,0:T(8,128)S(1)}, u32[]{:S(2)}, u32[]{:S(2)}) collective-permute-start(f32[4,32,256]{2,1,0:T(8,128)S(1)} %get-tuple-element.45), channel_id=1, source_target_pairs={{0,4},{4,8},{8,12},{12,16},{16,20},{20,24},{24,28},{28,32},{32,36}... | collective-permute-start | bytes 393224 | tf_op jit(solution)/shard_map/ppermute | solution.py:239
  27.2 2.3 %all-to-all-done = f32[512,128,2]{0,2,1:T(2,128)S(1)} async-done(((f32[512,128,2]{0,2,1:T(2,128)}), f32[512,128,2]{0,2,1:T(2,128)S(1)}, u32[]{:S(2)}, u32[]{:S(2)}) %all-to-all-start) | async-done | bytes 524320 | tf_op jit(solution)/shard_map/all_to_all | solution.py:412
  29.9 1.4 %fusion.6.state_ref.refs_0_ = f32[512,128]{1,0:T(8,128)} fusion(f32[512,256]{0,1:T(8,128)S(1)} %all_to_all.13, s32[256]{0:T(256)S(1)} %eq.61), kind=kOutput, calls=%fused_computation.12 | convolution fusion | flops 201359360 | bytes 787456 | tf_op jit(solution)/shard_map/dot_general | solution.py:413
  31.2 1.7 %shard_map.122 = (f32[104,128]{1,0:T(8,128)}, f32[104,128]{1,0:T(8,128)}, f32[104,32]{1,0:T(8,128)}, f32[104,32]{1,0:T(8,128)}) custom-call(f32[512,128]{1,0:T(8,128)} %fusion.6.state_ref.refs_0_), custom_call_target="tpu_custom_call" | custom-call | tf_op jit(solution)/shard_map/pallas_call | solution.py:358
  33.7 4.2 %shard_map.123 = (f32[3,8,32,256]{3,2,1,0:T(8,128)}, f32[296,128]{1,0:T(8,128)}, f32[296,128]{1,0:T(8,128)}, f32[152,128]{1,0:T(8,128)}, f32[152,128]{1,0:T(8,128)}) custom-call(f32[3,8,32,256]{3,2,1,0:T(8,128)} %refs_0_.1, f32[8,32,256]{2,1,0:T(8,128)} %refs_1_.3, f32[4,32,256]{2,1,0:T(8,128)} %copy-done.3, f32[4,32,256]{2,1,0:T(8,128)} %copy-done.2, ...), custom_call_target="tpu_custom_call" | custom-call | tf_op jit(solution)/shard_map/pallas_call | solution.py:218
  37.8 2.6 %collective-permute-start.4 = (f32[296,128]{1,0:T(8,128)}, f32[296,128]{1,0:T(8,128)S(1)}, u32[]{:S(2)}, u32[]{:S(2)}) collective-permute-start(f32[296,128]{1,0:T(8,128)} %get-tuple-element.23), channel_id=1, source_target_pairs={{0,4},{4,8},{8,12},{12,16},{16,20},{20,24},{24,28},{28,32},{32,36}... | collective-permute-start | bytes 454664 | tf_op jit(solution)/shard_map/ppermute | solution.py:392
  40.4 1.9 %collective-permute-start.5 = (f32[296,128]{1,0:T(8,128)}, f32[296,128]{1,0:T(8,128)S(1)}, u32[]{:S(2)}, u32[]{:S(2)}) collective-permute-start(f32[296,128]{1,0:T(8,128)} %get-tuple-element.24), channel_id=1, source_target_pairs={{4,0},{8,4},{12,8},{16,12},{20,16},{24,20},{28,24},{32,28},{36,32}... | collective-permute-start | bytes 454664 | tf_op jit(solution)/shard_map/ppermute | solution.py:393
  42.3 2.4 %collective-permute-start.6 = (f32[152,128]{1,0:T(8,128)}, f32[152,128]{1,0:T(8,128)S(1)}, u32[]{:S(2)}, u32[]{:S(2)}) collective-permute-start(f32[152,128]{1,0:T(8,128)} %get-tuple-element.25), channel_id=1, source_target_pairs={{0,1},{1,2},{2,3},{4,5},{5,6},{6,7},{8,9},{9,10},{10,11},{12,13},{... | collective-permute-start | bytes 233480 | tf_op jit(solution)/shard_map/ppermute | solution.py:394
  44.7 1.3 %collective-permute-start.7 = (f32[152,128]{1,0:T(8,128)}, f32[152,128]{1,0:T(8,128)S(1)}, u32[]{:S(2)}, u32[]{:S(2)}) collective-permute-start(f32[152,128]{1,0:T(8,128)} %get-tuple-element.26), channel_id=1, source_target_pairs={{1,0},{2,1},{3,2},{5,4},{6,5},{7,6},{9,8},{10,9},{11,10},{13,12},{... | collective-permute-start | bytes 233480 | tf_op jit(solution)/shard_map/ppermute | solution.py:395
  46.0 1.0 collective-permute-done.6.refs_4_
  47.0 4.0 %collective-permute-done.7.refs_5_ = f32[152,128]{1,0:T(8,128)S(1)} collective-permute-done((f32[152,128]{1,0:T(8,128)}, f32[152,128]{1,0:T(8,128)S(1)}, u32[]{:S(2)}, u32[]{:S(2)}) %collective-permute-start.7) | collective-permute-done | bytes 77856 | tf_op jit(solution)/shard_map/ppermute | solution.py:395
  51.9 4.0 %shard_map.124 = (f32[3,8,32,256]{3,2,1,0:T(8,128)}, bf16[3,8,32,256]{3,2,1,0:T(8,128)(2,1)}) custom-call(f32[3,8,32,256]{3,2,1,0:T(8,128)} %get-tuple-element.22.refs_0_, f32[8,32,256]{2,1,0:T(8,128)} %refs_1_.3, f32[296,128]{1,0:T(8,128)} %copy-done.4, f32[296,128]{1,0:T(8,128)} %copy-done.5, f32[152,128]{1,0:T(8,128)} %copy-done.6, f32[152,128]{1,0:T(8,128)} %copy-done.7, ...), custom_call_target="tpu_custom_call" | custom-call | tf_op jit(solution)/shard_map/pallas_call | solution.py:225
  55.9 1.3 %convolution_convert_fusion = bf16[768,256]{1,0:T(8,128)(2,1)S(1)} fusion(bf16[768,256]{1,0:T(8,128)(2,1)} %bitcast.48, bf16[256,256]{1,0:T(8,128)(2,1)S(1)} %copy-done.10), kind=kOutput, calls=%fused_computation.1 | convolution fusion | flops 100859904 | bytes 917504 | tf_op jit(solution)/shard_map/dot_general | solution.py:254
  57.8 2.0 %copy.42 = bf16[3,1,8,4,8,8,32]{6,3,0,5,4,2,1:T(4,128)(2,1)S(1)} copy(bf16[3,1,8,4,8,8,32]{6,5,4,3,2,0,1:T(8,128)(2,1)S(1)} %reshape.50) | data formatting | bytes 786432 | tf_op jit(solution)/shard_map/reshape | solution.py:256
  60.9 1.0 fusion.2
  61.9 2.9 %shard_map.125 = (f32[512,128]{1,0:T(8,128)}, f32[104,128]{1,0:T(8,128)}, f32[104,128]{1,0:T(8,128)}, f32[104,32]{1,0:T(8,128)}, f32[104,32]{1,0:T(8,128)}) custom-call(f32[512,128]{1,0:T(8,128)} %fusion.6.state_ref.refs_0_, f32[384,128]{1,0:T(8,128)} %bitcast.43, f32[296,128]{1,0:T(8,128)} %copy-done.4, f32[296,128]{1,0:T(8,128)} %copy-done.5, ...), custom_call_target="tpu_custom_call" | custom-call | tf_op jit(solution)/shard_map/pallas_call | solution.py:370
  64.8 3.9 %collective-permute-start.8 = (f32[104,128]{1,0:T(8,128)}, f32[104,128]{1,0:T(8,128)S(1)}, u32[]{:S(2)}, u32[]{:S(2)}) collective-permute-start(f32[104,128]{1,0:T(8,128)} %get-tuple-element.30), channel_id=1, source_target_pairs={{0,4},{4,8},{8,12},{12,16},{16,20},{20,24},{24,28},{28,32},{32,36}... | collective-permute-start | bytes 159752 | tf_op jit(solution)/shard_map/ppermute | solution.py:392
  68.7 1.9 %collective-permute-start.9 = (f32[104,128]{1,0:T(8,128)}, f32[104,128]{1,0:T(8,128)S(1)}, u32[]{:S(2)}, u32[]{:S(2)}) collective-permute-start(f32[104,128]{1,0:T(8,128)} %get-tuple-element.31), channel_id=1, source_target_pairs={{4,0},{8,4},{12,8},{16,12},{20,16},{24,20},{28,24},{32,28},{36,32}... | collective-permute-start | bytes 159752 | tf_op jit(solution)/shard_map/ppermute | solution.py:393
  70.6 2.3 %collective-permute-start.10 = (f32[104,32]{1,0:T(8,128)}, f32[104,32]{1,0:T(8,128)S(1)}, u32[]{:S(2)}, u32[]{:S(2)}) collective-permute-start(f32[104,32]{1,0:T(8,128)} %get-tuple-element.32), channel_id=1, source_target_pairs={{0,1},{1,2},{2,3},{4,5},{5,6},{6,7},{8,9},{9,10},{10,11},{12,13},{... | collective-permute-start | bytes 39944 | tf_op jit(solution)/shard_map/ppermute | solution.py:394
  72.9 1.3 %collective-permute-start.11 = (f32[104,32]{1,0:T(8,128)}, f32[104,32]{1,0:T(8,128)S(1)}, u32[]{:S(2)}, u32[]{:S(2)}) collective-permute-start(f32[104,32]{1,0:T(8,128)} %get-tuple-element.33), channel_id=1, source_target_pairs={{1,0},{2,1},{3,2},{5,4},{6,5},{7,6},{9,8},{10,9},{11,10},{13,12},{... | collective-permute-start | bytes 39944 | tf_op jit(solution)/shard_map/ppermute | solution.py:395
  74.4 3.6 %collective-permute-done.11.refs_5_ = f32[104,32]{1,0:T(8,128)S(1)} collective-permute-done((f32[104,32]{1,0:T(8,128)}, f32[104,32]{1,0:T(8,128)S(1)}, u32[]{:S(2)}, u32[]{:S(2)}) %collective-permute-start.11) | collective-permute-done | bytes 13344 | tf_op jit(solution)/shard_map/ppermute | solution.py:395
  78.7 2.7 %shard_map.126 = f32[512,128]{1,0:T(8,128)} custom-call(f32[512,128]{1,0:T(8,128)} %get-tuple-element.29.refs_0_, f32[384,128]{1,0:T(8,128)} %bitcast.44, f32[104,128]{1,0:T(8,128)} %copy-done.12, f32[104,128]{1,0:T(8,128)} %copy-done.13, f32[104,32]{1,0:T(8,128)} %copy-done.14, f32[104,32]{1,0:T(8,128)} %copy-done.15, f32[128,384]{1,0:T(8,128)} %constant.17.clone.refs_6_, ...), custom_call_target="tpu_custom_call" | custom-call | tf_op jit(solution)/shard_map/pallas_call | solution.py:370
  81.4 1.4 %fusion.5 = f32[512,256]{0,1:T(8,128)S(1)} fusion(f32[512,128]{1,0:T(8,128)} %shard_map.126, s32[256]{0:T(256)S(1)} %eq.61), kind=kOutput, calls=%fused_computation.11 | convolution fusion | flops 201359360 | bytes 787456 | tf_op jit(solution)/shard_map/dot_general | solution.py:428
  83.1 28.1 %all_to_all.18 = f32[512,128,2]{0,2,1:T(2,128)S(1)} all-to-all(f32[512,128,2]{0,2,1:T(2,128)S(1)} %all_to_all.14), channel_id=1, replica_groups=mesh['flow'=32,'grp'=4] {'flow','grp'}, dimensions={1} | all-to-all | bytes 1048576 | tf_op jit(solution)/shard_map/all_to_all | solution.py:429
  112.3 0.9 copy.36
  (58 shorter events, 6.2 us)
Async XLA Ops:
  1.6 13.7 %copy-start = (f32[3,8,32,256]{3,2,1,0:T(8,128)S(1)}, f32[3,8,32,256]{3,2,1,0:T(8,128)}, u32[]{:S(2)}) copy-start(f32[3,8,32,256]{3,2,1,0:T(8,128)} %refs_0_.1) | copy-start | bytes 2359300
  1.7 13.7 %copy-start.1 = (f32[8,32,256]{2,1,0:T(8,128)S(1)}, f32[8,32,256]{2,1,0:T(8,128)}, u32[]{:S(2)}) copy-start(f32[8,32,256]{2,1,0:T(8,128)} %refs_1_.3) | copy-start | bytes 786436
  3.9 23.1 %copy-start.17 = (s32[1,128,2]{1,2,0:T(2,128)S(1)}, s32[1,128,2]{1,2,0:T(2,128)}, u32[]{:S(2)}) copy-start(s32[1,128,2]{1,2,0:T(2,128)} %param.15) | copy-start | bytes 3076
  3.9 25.6 %all-to-all-start = ((f32[512,128,2]{0,2,1:T(2,128)}), f32[512,128,2]{0,2,1:T(2,128)S(1)}, u32[]{:S(2)}, u32[]{:S(2)}) async-start(f32[512,128,2]{0,2,1:T(2,128)} %copy.31), calls=%async_computation | async-start | bytes 1048576 | tf_op jit(solution)/shard_map/all_to_all | solution.py:412
  15.4 17.5 %collective-permute-start.3 = (f32[4,8,1,256]{3,2,1,0:T(1,128)S(1)}, f32[4,8,1,256]{3,2,1,0:T(1,128)S(1)}, u32[]{:S(2)}, u32[]{:S(2)}) collective-permute-start(f32[4,8,1,256]{3,2,1,0:T(1,128)S(1)} %get-tuple-element.42), channel_id=1, source_target_pairs={{1,0},{2,1},{3,2},{5,4},{6,5},{7,6},{9,8},{10,9},{11,10},{13,12},{... | collective-permute-start | bytes 98312 | tf_op jit(solution)/shard_map/ppermute | solution.py:242
  16.7 16.2 %collective-permute-start.2 = (f32[4,8,1,256]{3,2,1,0:T(1,128)S(1)}, f32[4,8,1,256]{3,2,1,0:T(1,128)S(1)}, u32[]{:S(2)}, u32[]{:S(2)}) collective-permute-start(f32[4,8,1,256]{3,2,1,0:T(1,128)S(1)} %get-tuple-element.43), channel_id=1, source_target_pairs={{0,1},{1,2},{2,3},{4,5},{5,6},{6,7},{8,9},{9,10},{10,11},{12,13},{... | collective-permute-start | bytes 98312 | tf_op jit(solution)/shard_map/ppermute | solution.py:241
  20.8 12.2 %collective-permute-start.1 = (f32[4,32,256]{2,1,0:T(8,128)S(1)}, f32[4,32,256]{2,1,0:T(8,128)S(1)}, u32[]{:S(2)}, u32[]{:S(2)}) collective-permute-start(f32[4,32,256]{2,1,0:T(8,128)S(1)} %get-tuple-element.44), channel_id=1, source_target_pairs={{4,0},{8,4},{12,8},{16,12},{20,16},{24,20},{28,24},{32,28},{36,32}... | collective-permute-start | bytes 393224 | tf_op jit(solution)/shard_map/ppermute | solution.py:240
  24.3 8.6 %collective-permute-start = (f32[4,32,256]{2,1,0:T(8,128)S(1)}, f32[4,32,256]{2,1,0:T(8,128)S(1)}, u32[]{:S(2)}, u32[]{:S(2)}) collective-permute-start(f32[4,32,256]{2,1,0:T(8,128)S(1)} %get-tuple-element.45), channel_id=1, source_target_pairs={{0,4},{4,8},{8,12},{12,16},{16,20},{20,24},{24,28},{28,32},{32,36}... | collective-permute-start | bytes 393224 | tf_op jit(solution)/shard_map/ppermute | solution.py:239
  32.9 0.6 copy-start.8
  32.9 0.6 copy-start.9
  32.9 0.7 copy-start.2
  33.0 0.7 copy-start.3
  33.6 22.2 %copy-start.10 = (bf16[256,256]{1,0:T(8,128)(2,1)S(1)}, bf16[256,256]{1,0:T(8,128)(2,1)}, u32[]{:S(2)}) copy-start(bf16[256,256]{1,0:T(8,128)(2,1)} %constant.21.clone) | copy-start | bytes 393220
  37.8 13.3 %collective-permute-start.4 = (f32[296,128]{1,0:T(8,128)}, f32[296,128]{1,0:T(8,128)S(1)}, u32[]{:S(2)}, u32[]{:S(2)}) collective-permute-start(f32[296,128]{1,0:T(8,128)} %get-tuple-element.23), channel_id=1, source_target_pairs={{0,4},{4,8},{8,12},{12,16},{16,20},{20,24},{24,28},{28,32},{32,36}... | collective-permute-start | bytes 454664 | tf_op jit(solution)/shard_map/ppermute | solution.py:392
  40.4 10.7 %collective-permute-start.5 = (f32[296,128]{1,0:T(8,128)}, f32[296,128]{1,0:T(8,128)S(1)}, u32[]{:S(2)}, u32[]{:S(2)}) collective-permute-start(f32[296,128]{1,0:T(8,128)} %get-tuple-element.24), channel_id=1, source_target_pairs={{4,0},{8,4},{12,8},{16,12},{20,16},{24,20},{28,24},{32,28},{36,32}... | collective-permute-start | bytes 454664 | tf_op jit(solution)/shard_map/ppermute | solution.py:393
  42.3 4.7 %collective-permute-start.6 = (f32[152,128]{1,0:T(8,128)}, f32[152,128]{1,0:T(8,128)S(1)}, u32[]{:S(2)}, u32[]{:S(2)}) collective-permute-start(f32[152,128]{1,0:T(8,128)} %get-tuple-element.25), channel_id=1, source_target_pairs={{0,1},{1,2},{2,3},{4,5},{5,6},{6,7},{8,9},{9,10},{10,11},{12,13},{... | collective-permute-start | bytes 233480 | tf_op jit(solution)/shard_map/ppermute | solution.py:394
  44.7 6.4 %collective-permute-start.7 = (f32[152,128]{1,0:T(8,128)}, f32[152,128]{1,0:T(8,128)S(1)}, u32[]{:S(2)}, u32[]{:S(2)}) collective-permute-start(f32[152,128]{1,0:T(8,128)} %get-tuple-element.26), channel_id=1, source_target_pairs={{1,0},{2,1},{3,2},{5,4},{6,5},{7,6},{9,8},{10,9},{11,10},{13,12},{... | collective-permute-start | bytes 233480 | tf_op jit(solution)/shard_map/ppermute | solution.py:395
  47.0 4.1 %copy-start.6 = (f32[152,128]{1,0:T(8,128)}, f32[152,128]{1,0:T(8,128)S(1)}, u32[]{:S(2)}) copy-start(f32[152,128]{1,0:T(8,128)S(1)} %collective-permute-done.6.refs_4_) | copy-start | bytes 233476
  51.1 0.6 copy-start.7
  51.1 0.7 copy-start.4
  51.1 0.8 copy-start.5
  59.8 1.1 copy-start.11
  64.8 13.2 %collective-permute-start.8 = (f32[104,128]{1,0:T(8,128)}, f32[104,128]{1,0:T(8,128)S(1)}, u32[]{:S(2)}, u32[]{:S(2)}) collective-permute-start(f32[104,128]{1,0:T(8,128)} %get-tuple-element.30), channel_id=1, source_target_pairs={{0,4},{4,8},{8,12},{12,16},{16,20},{20,24},{24,28},{28,32},{32,36}... | collective-permute-start | bytes 159752 | tf_op jit(solution)/shard_map/ppermute | solution.py:392
  68.7 9.3 %collective-permute-start.9 = (f32[104,128]{1,0:T(8,128)}, f32[104,128]{1,0:T(8,128)S(1)}, u32[]{:S(2)}, u32[]{:S(2)}) collective-permute-start(f32[104,128]{1,0:T(8,128)} %get-tuple-element.31), channel_id=1, source_target_pairs={{4,0},{8,4},{12,8},{16,12},{20,16},{24,20},{28,24},{32,28},{36,32}... | collective-permute-start | bytes 159752 | tf_op jit(solution)/shard_map/ppermute | solution.py:393
  70.6 3.8 %collective-permute-start.10 = (f32[104,32]{1,0:T(8,128)}, f32[104,32]{1,0:T(8,128)S(1)}, u32[]{:S(2)}, u32[]{:S(2)}) collective-permute-start(f32[104,32]{1,0:T(8,128)} %get-tuple-element.32), channel_id=1, source_target_pairs={{0,1},{1,2},{2,3},{4,5},{5,6},{6,7},{8,9},{9,10},{10,11},{12,13},{... | collective-permute-start | bytes 39944 | tf_op jit(solution)/shard_map/ppermute | solution.py:394
  72.9 5.1 %collective-permute-start.11 = (f32[104,32]{1,0:T(8,128)}, f32[104,32]{1,0:T(8,128)S(1)}, u32[]{:S(2)}, u32[]{:S(2)}) collective-permute-start(f32[104,32]{1,0:T(8,128)} %get-tuple-element.33), channel_id=1, source_target_pairs={{1,0},{2,1},{3,2},{5,4},{6,5},{7,6},{9,8},{10,9},{11,10},{13,12},{... | collective-permute-start | bytes 39944 | tf_op jit(solution)/shard_map/ppermute | solution.py:395
  74.4 3.6 %copy-start.14 = (f32[104,32]{1,0:T(8,128)}, f32[104,32]{1,0:T(8,128)S(1)}, u32[]{:S(2)}) copy-start(f32[104,32]{1,0:T(8,128)S(1)} %collective-permute-done.10.refs_4_) | copy-start | bytes 39940
  78.0 0.6 copy-start.15
  78.0 0.7 copy-start.12
  78.0 0.7 copy-start.13
  82.8 28.9 %copy-start.16 = (s32[1,128]{1,0:T(1,128)S(1)}, s32[1,128]{1,0:T(1,128)}, u32[]{:S(2)}) copy-start(s32[1,128]{1,0:T(1,128)} %param.16) | copy-start | bytes 1540

commit v10 on v9

--- a/solution.py
+++ b/solution.py
@@ -117,7 +117,7 @@
         def yhi(c, x):
             return vyhi_ref[c, x]
     else:
-        out_ref, lamb_ref = rest
+        perm_ref, out_ref, lamb_ref = rest
 
         def plane(ref, c):
             return jnp.concatenate(
@@ -187,7 +187,9 @@
                 total = term if total is None else total + term
             out_ref[c, x] = u[c] + TIME_STEP_LES * (total - lamb[c])
             if mode == 1:
-                lamb_ref[c, x] = lamb[c].astype(lamb_ref.dtype)
+                rounded = lamb[c].astype(jnp.bfloat16)
+                moved = jnp.dot(rounded, perm_ref[...], preferred_element_type=jnp.float32)
+                lamb_ref[c, x] = moved.astype(lamb_ref.dtype)
         return carry
 
     lax.fori_loop(0, size_x, step, 0)
@@ -221,11 +223,20 @@
     )(vel, nu, *joint, *joint, *faces)
 
 
+def lane_perm(size_z):
+    bz = size_z // 8
+    perm = np.zeros((size_z, size_z), np.float32)
+    for ez in range(bz):
+        for cz in range(8):
+            perm[ez * 8 + cz, cz * bz + ez] = 1.0
+    return jnp.asarray(perm, jnp.bfloat16)
+
+
 def les_section_last(vel, nu, merged, joint):
     return pl.pallas_call(
         lambda *refs: les_kernel(1, *refs),
         out_shape=(jax.ShapeDtypeStruct(vel.shape, jnp.float32), jax.ShapeDtypeStruct(vel.shape, jnp.bfloat16)),
-    )(vel, nu, *merged, *joint)
+    )(vel, nu, *merged, *joint, lane_perm(vel.shape[3]))
 
 
 def halos(field, lead):
@@ -243,16 +254,9 @@
     return xlo, xhi, ylo, yhi
 
 
-def project(lamb, projection):
-    size_x, size_y, size_z = (lamb.shape[1], lamb.shape[2], lamb.shape[3])
+def project(moved, projection):
+    size_x, size_y, size_z = (moved.shape[1], moved.shape[2], moved.shape[3])
     bx, by, bz = size_x // 8, size_y // 8, size_z // 8
-    perm = np.zeros((size_z, size_z), np.float32)
-    for ez in range(bz):
-        for cz in range(8):
-            perm[ez * 8 + cz, cz * bz + ez] = 1.0
-    rows = lamb.reshape(-1, size_z)
-    moved = jnp.dot(rows, jnp.asarray(perm, jnp.bfloat16), preferred_element_type=jnp.float32)
-    moved = moved.astype(jnp.bfloat16)
     blocks = moved.reshape(3, bx, 8, by, 8, 8, bz).transpose(2, 4, 5, 0, 1, 3, 6).reshape(512, -1)
     padded_proj = jnp.pad(projection, ((0, 3), (0, 0)))
     source = jnp.dot(padded_proj, blocks, preferred_element_type=jnp.float32)
@@ -292,8 +296,29 @@
     send_faces(face_ref, sx0_ref, sx4_ref, sy0_ref, sy4_ref, sy0_ref.shape[1])
 
 
-def dg_step_kernel(want_faces, xoff, yoff, row_len, state_ref, src_ref, xlo_ref, xhi_ref, ylo_ref, yhi_ref,
-                   apu_ref, aup_ref, diag_ref, lift_ref, out_ref, *rest):
+def dg_volume_kernel(state_ref, apu_ref, aup_ref, diag_ref, out_ref):
+    state = state_ref[...]
+    pres = state[:128]
+    vel = state[128:]
+    rate_p = jnp.dot(apu_ref[...], vel, precision=THREE_PASS, preferred_element_type=jnp.float32)
+    rate_p = rate_p + diag_ref[pl.ds(0, 128), :] * pres
+    out_ref[pl.ds(0, 128), :] = pres + TIME_STEP_ACOUSTIC * rate_p
+    rate_u = jnp.dot(aup_ref[...], pres, precision=THREE_PASS, preferred_element_type=jnp.float32)
+    for k in range(3):
+        rows = pl.ds(128 + k * 128, 128)
+        rate_k = rate_u[k * 128:(k + 1) * 128] + diag_ref[rows, :] * state_ref[rows, :]
+        out_ref[rows, :] = state_ref[rows, :] + TIME_STEP_ACOUSTIC * rate_k
+
+
+def dg_volume(state, mats):
+    return pl.pallas_call(
+        dg_volume_kernel,
+        out_shape=jax.ShapeDtypeStruct(state.shape, jnp.float32),
+    )(state, *mats[:3])
+
+
+def dg_step_kernel(want_faces, xoff, yoff, row_len, state_ref, part_ref, src_ref, xlo_ref, xhi_ref, ylo_ref, yhi_ref,
+                   lift_ref, out_ref, *rest):
     if want_faces:
         sx0_ref, sx4_ref, sy0_ref, sy4_ref, face_ref, oth_ref, pad_ref, g_ref = rest
     else:
@@ -330,18 +355,11 @@
                     value = value - half * sign * o_p
                 g_ref[pl.ds(f * 25, 25), pl.ds((1 + k) * elems, elems)] = value
     faces = jnp.dot(lift_ref[...], g_ref[...], precision=THREE_PASS, preferred_element_type=jnp.float32)
-    state = state_ref[...]
-    pres = state[:128]
-    vel = state[128:]
-    rate_p = jnp.dot(apu_ref[...], vel, precision=THREE_PASS, preferred_element_type=jnp.float32)
-    rate_p = rate_p + diag_ref[pl.ds(0, 128), :] * pres + faces[:, :elems]
-    out_ref[pl.ds(0, 128), :] = pres + TIME_STEP_ACOUSTIC * rate_p
-    rate_u = jnp.dot(aup_ref[...], pres, precision=THREE_PASS, preferred_element_type=jnp.float32)
+    out_ref[pl.ds(0, 128), :] = part_ref[pl.ds(0, 128), :] + TIME_STEP_ACOUSTIC * faces[:, :elems]
     for k in range(3):
         rows = pl.ds(128 + k * 128, 128)
-        rate_k = rate_u[k * 128:(k + 1) * 128] + diag_ref[rows, :] * state_ref[rows, :]
-        rate_k = rate_k + faces[:, (1 + k) * elems:(2 + k) * elems]
-        out_ref[rows, :] = state_ref[rows, :] + TIME_STEP_ACOUSTIC * (rate_k - src_ref[pl.ds(k * 128, 128), :])
+        rate_k = faces[:, (1 + k) * elems:(2 + k) * elems] - src_ref[pl.ds(k * 128, 128), :]
+        out_ref[rows, :] = part_ref[rows, :] + TIME_STEP_ACOUSTIC * rate_k
     if want_faces:
         extract_faces(out_ref, face_ref)
         send_faces(face_ref, sx0_ref, sx4_ref, sy0_ref, sy4_ref, row_len)
@@ -376,7 +394,7 @@
             pltpu.VMEM((FACE_ROWS, elems), jnp.float32),
             pltpu.VMEM((152, 4 * elems), jnp.float32),
         ],
-    )(state, src, *recv, *mats)
+    )(state, dg_volume(state, mats), src, *recv, mats[3])
     return res
 
 

time: 114 us -> 114 us (level)
  Pallas kernels: 15.5 us -> 20.1 us
  waiting for transfers between devices: 11.2 us -> 8.1 us
  local copies, waits for them, and re-layouts: 10.1 us -> 12 us
  blocking collectives: 28.1 us -> 26.7 us
  matrix products: 6.77 us -> 5.53 us
    pallas_call x0 -> x2, Pallas kernels: none -> 4.53 us  [dg_volume(): pl.pallas_call(dg_volume_kernel, out_shape=jax.ShapeDtypeStruct(state.sha...]
    ppermute x2, waiting for transfers between devices: 7.61 us -> 4.32 us  [exchange_faces(): lax.ppermute(sy0, 'grp', down_g)]
    ppermute x1, starting transfers between devices: 3.54 us -> 1.92 us  [halos(): lax.ppermute(lax.index_in_dim(field, 0, lead, keepdims=False), 'flow', do...]
    all_to_all x1, waiting for transfers between devices: 2.31 us -> 3.76 us  [body(): lax.all_to_all(outgoing, ('flow', 'grp'), split_axis=1, concat_axis=1, ti...]
    all_to_all x1, blocking collectives: 28.1 us -> 26.7 us  [body(): lax.all_to_all(leaving, ('flow', 'grp'), split_axis=1, concat_axis=1, til...]
    reshape x3, local copies, waits for them, and re-layouts: 3.51 us -> 4.82 us  [project(): moved.reshape(3, bx, 8, by, 8, 8, bz).transpose(2, 4, 5, 0, 1, 3, 6)]
    dot_general x1 -> x0, matrix products: 1.25 us -> none  [project(): jnp.dot(rows, jnp.asarray(perm, jnp.bfloat16), preferred_element_type=jnp...]
    ppermute x2, waiting for transfers between devices: 1.23 us -> 0.01 us  [exchange_faces(): lax.ppermute(sy4, 'grp', up_g)]
  transfers between devices with their start and end apart: 13 -> 13, of which waited for: 5 -> 3; matrix products, arithmetic and copies ran while one was open for 1% -> 1% of each run, Pallas kernels for 1% -> 6%
where the time goes in v10:
time: 114 us; the launch traced here: 113 us
  starting transfers between devices  39.5 us (35%)
  blocking collectives  26.7 us (23%)
  Pallas kernels  20.1 us (18%)
  local copies, waits for them, and re-layouts  12 us (11%)
  waiting for transfers between devices  8.1 us (7%)
  matrix products  5.53 us (5%)
    all_to_all x1, blocking collectives, body(): lax.all_to_all(leaving, ('flow', 'grp'), split_axis=1, concat_axis=1, til...  26.7 us
    all_to_all x1, starting transfers between devices, body(): lax.all_to_all(outgoing, ('flow', 'grp'), split_axis=1, concat_axis=1, ti...  11.5 us
    ppermute x2, starting transfers between devices, exchange_faces(): lax.ppermute(sx4, 'flow', up_f)  6.61 us
    ppermute x2, starting transfers between devices, exchange_faces(): lax.ppermute(sy4, 'grp', up_g)  4.98 us
    pallas_call x2, Pallas kernels, dg_step(): pl.pallas_call(lambda *refs: dg_step_kernel(want_faces, xoff, yoff, row_l...  4.91 us
    reshape x3, local copies, waits for them, and re-layouts, project(): moved.reshape(3, bx, 8, by, 8, 8, bz).transpose(2, 4, 5, 0, 1, 3, 6)  4.82 us
    pallas_call x1, Pallas kernels, les_section_last(): pl.pallas_call(lambda *refs: les_kernel(1, *refs), out_shape=(jax.ShapeDt...  4.79 us
    unnamed x37, local copies, waits for them, and re-layouts  4.64 us
  transfers between devices with their start and end apart: 13, of which 3 were waited for; matrix products, arithmetic and copies ran while one was open for 1% of the time, Pallas kernels for 6%

profile of v10, /device:TPU:1, one launch (start us, length us, event | category | flops | bytes accessed | tf_op | source)
XLA Modules:
  0.0 113.0 jit_solution(16720545402268883995)
XLA Ops:
  0.6 1.0 copy.37
  1.7 1.2 %fusion.9 = f32[512,128,2]{1,0,2:T(8,128)S(1)} fusion(f32[512,128,1]{1,0,2:T(8,128)S(1)} %bitcast.46, s32[128,2]{0,1:T(2,128)S(1)} %multiply_add_fusion, s32[128]{0:T(128)} %bitcast.47), kind=kOutput, calls=%fused_computation.13 | convolution fusion | flops 201359360 | bytes 787968 | tf_op jit(solution)/shard_map/dot_general | solution.py:429
  2.9 1.0 copy.31
  3.9 11.5 %all-to-all-start = ((f32[512,128,2]{0,2,1:T(2,128)}), f32[512,128,2]{0,2,1:T(2,128)S(1)}, u32[]{:S(2)}, u32[]{:S(2)}) async-start(f32[512,128,2]{0,2,1:T(2,128)} %copy.31), calls=%async_computation | async-start | bytes 1048576 | tf_op jit(solution)/shard_map/all_to_all | solution.py:430
  15.4 3.7 %collective-permute-start = (f32[4,32,256]{2,1,0:T(8,128)S(1)}, f32[4,32,256]{2,1,0:T(8,128)S(1)}, u32[]{:S(2)}, u32[]{:S(2)}) collective-permute-start(f32[4,32,256]{2,1,0:T(8,128)S(1)} %get-tuple-element.45), channel_id=1, source_target_pairs={{0,4},{4,8},{8,12},{12,16},{16,20},{20,24},{24,28},{28,32},{32,36}... | collective-permute-start | bytes 393224 | tf_op jit(solution)/shard_map/ppermute | solution.py:250
  19.1 1.9 %collective-permute-start.1 = (f32[4,32,256]{2,1,0:T(8,128)S(1)}, f32[4,32,256]{2,1,0:T(8,128)S(1)}, u32[]{:S(2)}, u32[]{:S(2)}) collective-permute-start(f32[4,32,256]{2,1,0:T(8,128)S(1)} %get-tuple-element.44), channel_id=1, source_target_pairs={{4,0},{8,4},{12,8},{16,12},{20,16},{24,20},{28,24},{32,28},{36,32}... | collective-permute-start | bytes 393224 | tf_op jit(solution)/shard_map/ppermute | solution.py:251
  21.1 3.1 %collective-permute-start.2 = (f32[4,8,1,256]{3,2,1,0:T(1,128)S(1)}, f32[4,8,1,256]{3,2,1,0:T(1,128)S(1)}, u32[]{:S(2)}, u32[]{:S(2)}) collective-permute-start(f32[4,8,1,256]{3,2,1,0:T(1,128)S(1)} %get-tuple-element.43), channel_id=1, source_target_pairs={{0,1},{1,2},{2,3},{4,5},{5,6},{6,7},{8,9},{9,10},{10,11},{12,13},{... | collective-permute-start | bytes 98312 | tf_op jit(solution)/shard_map/ppermute | solution.py:252
  24.2 1.3 %collective-permute-start.3 = (f32[4,8,1,256]{3,2,1,0:T(1,128)S(1)}, f32[4,8,1,256]{3,2,1,0:T(1,128)S(1)}, u32[]{:S(2)}, u32[]{:S(2)}) collective-permute-start(f32[4,8,1,256]{3,2,1,0:T(1,128)S(1)} %get-tuple-element.42), channel_id=1, source_target_pairs={{1,0},{2,1},{3,2},{5,4},{6,5},{7,6},{9,8},{10,9},{11,10},{13,12},{... | collective-permute-start | bytes 98312 | tf_op jit(solution)/shard_map/ppermute | solution.py:253
  25.7 3.8 %all-to-all-done = f32[512,128,2]{0,2,1:T(2,128)S(1)} async-done(((f32[512,128,2]{0,2,1:T(2,128)}), f32[512,128,2]{0,2,1:T(2,128)S(1)}, u32[]{:S(2)}, u32[]{:S(2)}) %all-to-all-start) | async-done | bytes 524320 | tf_op jit(solution)/shard_map/all_to_all | solution.py:430
  29.9 1.4 %fusion.6.state_ref.refs_0_ = f32[512,128]{1,0:T(8,128)} fusion(f32[512,256]{0,1:T(8,128)S(1)} %all_to_all.13, s32[256]{0:T(256)S(1)} %eq.61), kind=kOutput, calls=%fused_computation.11 | convolution fusion | flops 201359360 | bytes 787456 | tf_op jit(solution)/shard_map/dot_general | solution.py:431
  31.2 1.7 %shard_map.122 = (f32[104,128]{1,0:T(8,128)}, f32[104,128]{1,0:T(8,128)}, f32[104,32]{1,0:T(8,128)}, f32[104,32]{1,0:T(8,128)}) custom-call(f32[512,128]{1,0:T(8,128)} %fusion.6.state_ref.refs_0_), custom_call_target="tpu_custom_call" | custom-call | tf_op jit(solution)/shard_map/pallas_call | solution.py:376
  33.7 4.1 %shard_map.123 = (f32[3,8,32,256]{3,2,1,0:T(8,128)}, f32[296,128]{1,0:T(8,128)}, f32[296,128]{1,0:T(8,128)}, f32[152,128]{1,0:T(8,128)}, f32[152,128]{1,0:T(8,128)}) custom-call(f32[3,8,32,256]{3,2,1,0:T(8,128)} %refs_0_.1, f32[8,32,256]{2,1,0:T(8,128)} %refs_1_.3, f32[4,32,256]{2,1,0:T(8,128)} %copy-done.2, f32[4,32,256]{2,1,0:T(8,128)} %copy-done.3, ...), custom_call_target="tpu_custom_call" | custom-call | tf_op jit(solution)/shard_map/pallas_call | solution.py:220
  37.8 2.6 %collective-permute-start.4 = (f32[296,128]{1,0:T(8,128)}, f32[296,128]{1,0:T(8,128)S(1)}, u32[]{:S(2)}, u32[]{:S(2)}) collective-permute-start(f32[296,128]{1,0:T(8,128)} %get-tuple-element.23), channel_id=1, source_target_pairs={{0,4},{4,8},{8,12},{12,16},{16,20},{20,24},{24,28},{28,32},{32,36}... | collective-permute-start | bytes 454664 | tf_op jit(solution)/shard_map/ppermute | solution.py:410
  40.4 1.9 %collective-permute-start.5 = (f32[296,128]{1,0:T(8,128)}, f32[296,128]{1,0:T(8,128)S(1)}, u32[]{:S(2)}, u32[]{:S(2)}) collective-permute-start(f32[296,128]{1,0:T(8,128)} %get-tuple-element.24), channel_id=1, source_target_pairs={{4,0},{8,4},{12,8},{16,12},{20,16},{24,20},{28,24},{32,28},{36,32}... | collective-permute-start | bytes 454664 | tf_op jit(solution)/shard_map/ppermute | solution.py:411
  42.3 2.2 %collective-permute-start.6 = (f32[152,128]{1,0:T(8,128)}, f32[152,128]{1,0:T(8,128)S(1)}, u32[]{:S(2)}, u32[]{:S(2)}) collective-permute-start(f32[152,128]{1,0:T(8,128)} %get-tuple-element.25), channel_id=1, source_target_pairs={{0,1},{1,2},{2,3},{4,5},{5,6},{6,7},{8,9},{9,10},{10,11},{12,13},{... | collective-permute-start | bytes 233480 | tf_op jit(solution)/shard_map/ppermute | solution.py:412
  44.5 1.3 %collective-permute-start.7 = (f32[152,128]{1,0:T(8,128)}, f32[152,128]{1,0:T(8,128)S(1)}, u32[]{:S(2)}, u32[]{:S(2)}) collective-permute-start(f32[152,128]{1,0:T(8,128)} %get-tuple-element.26), channel_id=1, source_target_pairs={{1,0},{2,1},{3,2},{5,4},{6,5},{7,6},{9,8},{10,9},{11,10},{13,12},{... | collective-permute-start | bytes 233480 | tf_op jit(solution)/shard_map/ppermute | solution.py:413
  45.8 2.3 %shard_map.125.refs_1_ = f32[512,128]{1,0:T(8,128)} custom-call(f32[512,128]{1,0:T(8,128)} %fusion.6.state_ref.refs_0_, f32[128,384]{1,0:T(8,128)} %constant.17.clone.apu_ref, f32[384,128]{1,0:T(8,128)} %constant.18.clone.aup_ref, f32[512,1]{1,0:T(8,128)} %constant.19.clone.diag_ref), custom_call_target="tpu_custom_call" | custom-call | tf_op jit(solution)/shard_map/pallas_call | solution.py:314
  48.1 2.8 %collective-permute-done.7.refs_5_.refs_6_ = f32[152,128]{1,0:T(8,128)S(1)} collective-permute-done((f32[152,128]{1,0:T(8,128)}, f32[152,128]{1,0:T(8,128)S(1)}, u32[]{:S(2)}, u32[]{:S(2)}) %collective-permute-start.7) | collective-permute-done | bytes 77856 | tf_op jit(solution)/shard_map/ppermute | solution.py:413
  51.7 4.8 %shard_map.124 = (f32[3,8,32,256]{3,2,1,0:T(8,128)}, bf16[3,8,32,256]{3,2,1,0:T(8,128)(2,1)}) custom-call(f32[3,8,32,256]{3,2,1,0:T(8,128)} %get-tuple-element.22.refs_0_, f32[8,32,256]{2,1,0:T(8,128)} %refs_1_.3, f32[296,128]{1,0:T(8,128)} %copy-done.4, f32[296,128]{1,0:T(8,128)} %copy-done.5, f32[152,128]{1,0:T(8,128)} %copy-done.6, f32[152,128]{1,0:T(8,128)} %copy-done.7, ...), custom_call_target="tpu_custom_call" | custom-call | tf_op jit(solution)/shard_map/pallas_call | solution.py:236
  56.4 1.9 %reshape.46 = bf16[3,1,8,4,8,8,32]{6,5,4,3,2,0,1:T(8,128)(2,1)S(1)} reshape(bf16[3,8,32,256]{3,2,1,0:T(8,128)(2,1)} %get-tuple-element.28) | data formatting | bytes 786432 | tf_op jit(solution)/shard_map/reshape | solution.py:260
  58.4 2.0 %copy.42 = bf16[3,1,8,4,8,8,32]{6,3,0,5,4,2,1:T(4,128)(2,1)S(1)} copy(bf16[3,1,8,4,8,8,32]{6,5,4,3,2,0,1:T(8,128)(2,1)S(1)} %reshape.46) | data formatting | bytes 786432 | tf_op jit(solution)/shard_map/reshape | solution.py:260
  61.5 1.0 fusion.2
  62.5 2.6 %shard_map.126 = (f32[512,128]{1,0:T(8,128)}, f32[104,128]{1,0:T(8,128)}, f32[104,128]{1,0:T(8,128)}, f32[104,32]{1,0:T(8,128)}, f32[104,32]{1,0:T(8,128)}) custom-call(f32[512,128]{1,0:T(8,128)} %fusion.6.state_ref.refs_0_, f32[512,128]{1,0:T(8,128)} %shard_map.125.refs_1_, f32[384,128]{1,0:T(8,128)} %bitcast.42, f32[296,128]{1,0:T(8,128)} %copy-done.4, ...), custom_call_target="tpu_custom_call" | custom-call | tf_op jit(solution)/shard_map/pallas_call | solution.py:388
  65.0 4.0 %collective-permute-start.8 = (f32[104,128]{1,0:T(8,128)}, f32[104,128]{1,0:T(8,128)S(1)}, u32[]{:S(2)}, u32[]{:S(2)}) collective-permute-start(f32[104,128]{1,0:T(8,128)} %get-tuple-element.30), channel_id=1, source_target_pairs={{0,4},{4,8},{8,12},{12,16},{16,20},{20,24},{24,28},{28,32},{32,36}... | collective-permute-start | bytes 159752 | tf_op jit(solution)/shard_map/ppermute | solution.py:410
  69.1 1.9 %collective-permute-start.9 = (f32[104,128]{1,0:T(8,128)}, f32[104,128]{1,0:T(8,128)S(1)}, u32[]{:S(2)}, u32[]{:S(2)}) collective-permute-start(f32[104,128]{1,0:T(8,128)} %get-tuple-element.31), channel_id=1, source_target_pairs={{4,0},{8,4},{12,8},{16,12},{20,16},{24,20},{28,24},{32,28},{36,32}... | collective-permute-start | bytes 159752 | tf_op jit(solution)/shard_map/ppermute | solution.py:411
  71.0 2.8 %collective-permute-start.10 = (f32[104,32]{1,0:T(8,128)}, f32[104,32]{1,0:T(8,128)S(1)}, u32[]{:S(2)}, u32[]{:S(2)}) collective-permute-start(f32[104,32]{1,0:T(8,128)} %get-tuple-element.32), channel_id=1, source_target_pairs={{0,1},{1,2},{2,3},{4,5},{5,6},{6,7},{8,9},{9,10},{10,11},{12,13},{... | collective-permute-start | bytes 39944 | tf_op jit(solution)/shard_map/ppermute | solution.py:412
  73.8 1.3 %collective-permute-start.11 = (f32[104,32]{1,0:T(8,128)}, f32[104,32]{1,0:T(8,128)S(1)}, u32[]{:S(2)}, u32[]{:S(2)}) collective-permute-start(f32[104,32]{1,0:T(8,128)} %get-tuple-element.33), channel_id=1, source_target_pairs={{1,0},{2,1},{3,2},{5,4},{6,5},{7,6},{9,8},{10,9},{11,10},{13,12},{... | collective-permute-start | bytes 39944 | tf_op jit(solution)/shard_map/ppermute | solution.py:413
  75.1 2.2 %shard_map.127.refs_1_ = f32[512,128]{1,0:T(8,128)} custom-call(f32[512,128]{1,0:T(8,128)} %get-tuple-element.29.state_ref.refs_0_, f32[128,384]{1,0:T(8,128)} %constant.17.clone.apu_ref, f32[384,128]{1,0:T(8,128)} %constant.18.clone.aup_ref, f32[512,1]{1,0:T(8,128)} %constant.19.clone.diag_ref), custom_call_target="tpu_custom_call" | custom-call | tf_op jit(solution)/shard_map/pallas_call | solution.py:314
  77.3 1.5 %collective-permute-done.11.refs_6_ = f32[104,32]{1,0:T(8,128)S(1)} collective-permute-done((f32[104,32]{1,0:T(8,128)}, f32[104,32]{1,0:T(8,128)S(1)}, u32[]{:S(2)}, u32[]{:S(2)}) %collective-permute-start.11) | collective-permute-done | bytes 13344 | tf_op jit(solution)/shard_map/ppermute | solution.py:413
  80.1 2.4 %shard_map.128 = f32[512,128]{1,0:T(8,128)} custom-call(f32[512,128]{1,0:T(8,128)} %get-tuple-element.29.state_ref.refs_0_, f32[512,128]{1,0:T(8,128)} %shard_map.127.refs_1_, f32[384,128]{1,0:T(8,128)} %bitcast.43, f32[104,128]{1,0:T(8,128)} %copy-done.11, f32[104,128]{1,0:T(8,128)} %copy-done.12, f32[104,32]{1,0:T(8,128)} %copy-done.13, ...), custom_call_target="tpu_custom_call" | custom-call | tf_op jit(solution)/shard_map/pallas_call | solution.py:388
  82.5 1.4 %fusion.5 = f32[512,256]{0,1:T(8,128)S(1)} fusion(f32[512,128]{1,0:T(8,128)} %shard_map.128, s32[256]{0:T(256)S(1)} %eq.61), kind=kOutput, calls=%fused_computation.10 | convolution fusion | flops 201359360 | bytes 787456 | tf_op jit(solution)/shard_map/dot_general | solution.py:446
  84.2 26.7 %all_to_all.18 = f32[512,128,2]{0,2,1:T(2,128)S(1)} all-to-all(f32[512,128,2]{0,2,1:T(2,128)S(1)} %all_to_all.14), channel_id=1, replica_groups=mesh['flow'=32,'grp'=4] {'flow','grp'}, dimensions={1} | all-to-all | bytes 1048576 | tf_op jit(solution)/shard_map/all_to_all | solution.py:447
  (57 shorter events, 6.8 us)
Async XLA Ops:
  1.6 13.7 %copy-start = (f32[3,8,32,256]{3,2,1,0:T(8,128)S(1)}, f32[3,8,32,256]{3,2,1,0:T(8,128)}, u32[]{:S(2)}) copy-start(f32[3,8,32,256]{3,2,1,0:T(8,128)} %refs_0_.1) | copy-start | bytes 2359300
  1.7 13.7 %copy-start.1 = (f32[8,32,256]{2,1,0:T(8,128)S(1)}, f32[8,32,256]{2,1,0:T(8,128)}, u32[]{:S(2)}) copy-start(f32[8,32,256]{2,1,0:T(8,128)} %refs_1_.3) | copy-start | bytes 786436
  3.9 21.6 %copy-start.16 = (s32[1,128,2]{1,2,0:T(2,128)S(1)}, s32[1,128,2]{1,2,0:T(2,128)}, u32[]{:S(2)}) copy-start(s32[1,128,2]{1,2,0:T(2,128)} %param.15) | copy-start | bytes 3076
  3.9 25.6 %all-to-all-start = ((f32[512,128,2]{0,2,1:T(2,128)}), f32[512,128,2]{0,2,1:T(2,128)S(1)}, u32[]{:S(2)}, u32[]{:S(2)}) async-start(f32[512,128,2]{0,2,1:T(2,128)} %copy.31), calls=%async_computation | async-start | bytes 1048576 | tf_op jit(solution)/shard_map/all_to_all | solution.py:430
  15.4 17.5 %collective-permute-start = (f32[4,32,256]{2,1,0:T(8,128)S(1)}, f32[4,32,256]{2,1,0:T(8,128)S(1)}, u32[]{:S(2)}, u32[]{:S(2)}) collective-permute-start(f32[4,32,256]{2,1,0:T(8,128)S(1)} %get-tuple-element.45), channel_id=1, source_target_pairs={{0,4},{4,8},{8,12},{12,16},{16,20},{20,24},{24,28},{28,32},{32,36}... | collective-permute-start | bytes 393224 | tf_op jit(solution)/shard_map/ppermute | solution.py:250
  19.1 13.9 %collective-permute-start.1 = (f32[4,32,256]{2,1,0:T(8,128)S(1)}, f32[4,32,256]{2,1,0:T(8,128)S(1)}, u32[]{:S(2)}, u32[]{:S(2)}) collective-permute-start(f32[4,32,256]{2,1,0:T(8,128)S(1)} %get-tuple-element.44), channel_id=1, source_target_pairs={{4,0},{8,4},{12,8},{16,12},{20,16},{24,20},{28,24},{32,28},{36,32}... | collective-permute-start | bytes 393224 | tf_op jit(solution)/shard_map/ppermute | solution.py:251
  21.1 11.9 %collective-permute-start.2 = (f32[4,8,1,256]{3,2,1,0:T(1,128)S(1)}, f32[4,8,1,256]{3,2,1,0:T(1,128)S(1)}, u32[]{:S(2)}, u32[]{:S(2)}) collective-permute-start(f32[4,8,1,256]{3,2,1,0:T(1,128)S(1)} %get-tuple-element.43), channel_id=1, source_target_pairs={{0,1},{1,2},{2,3},{4,5},{5,6},{6,7},{8,9},{9,10},{10,11},{12,13},{... | collective-permute-start | bytes 98312 | tf_op jit(solution)/shard_map/ppermute | solution.py:252
  24.2 8.7 %collective-permute-start.3 = (f32[4,8,1,256]{3,2,1,0:T(1,128)S(1)}, f32[4,8,1,256]{3,2,1,0:T(1,128)S(1)}, u32[]{:S(2)}, u32[]{:S(2)}) collective-permute-start(f32[4,8,1,256]{3,2,1,0:T(1,128)S(1)} %get-tuple-element.42), channel_id=1, source_target_pairs={{1,0},{2,1},{3,2},{5,4},{6,5},{7,6},{9,8},{10,9},{11,10},{13,12},{... | collective-permute-start | bytes 98312 | tf_op jit(solution)/shard_map/ppermute | solution.py:253
  32.9 0.6 copy-start.8
  32.9 0.6 copy-start.9
  33.0 0.7 copy-start.2
  33.0 0.7 copy-start.3
  37.8 13.1 %collective-permute-start.4 = (f32[296,128]{1,0:T(8,128)}, f32[296,128]{1,0:T(8,128)S(1)}, u32[]{:S(2)}, u32[]{:S(2)}) collective-permute-start(f32[296,128]{1,0:T(8,128)} %get-tuple-element.23), channel_id=1, source_target_pairs={{0,4},{4,8},{8,12},{12,16},{16,20},{20,24},{24,28},{28,32},{32,36}... | collective-permute-start | bytes 454664 | tf_op jit(solution)/shard_map/ppermute | solution.py:410
  40.4 10.5 %collective-permute-start.5 = (f32[296,128]{1,0:T(8,128)}, f32[296,128]{1,0:T(8,128)S(1)}, u32[]{:S(2)}, u32[]{:S(2)}) collective-permute-start(f32[296,128]{1,0:T(8,128)} %get-tuple-element.24), channel_id=1, source_target_pairs={{4,0},{8,4},{12,8},{16,12},{20,16},{24,20},{28,24},{32,28},{36,32}... | collective-permute-start | bytes 454664 | tf_op jit(solution)/shard_map/ppermute | solution.py:411
  42.3 5.8 %collective-permute-start.6 = (f32[152,128]{1,0:T(8,128)}, f32[152,128]{1,0:T(8,128)S(1)}, u32[]{:S(2)}, u32[]{:S(2)}) collective-permute-start(f32[152,128]{1,0:T(8,128)} %get-tuple-element.25), channel_id=1, source_target_pairs={{0,1},{1,2},{2,3},{4,5},{5,6},{6,7},{8,9},{9,10},{10,11},{12,13},{... | collective-permute-start | bytes 233480 | tf_op jit(solution)/shard_map/ppermute | solution.py:412
  44.5 6.4 %collective-permute-start.7 = (f32[152,128]{1,0:T(8,128)}, f32[152,128]{1,0:T(8,128)S(1)}, u32[]{:S(2)}, u32[]{:S(2)}) collective-permute-start(f32[152,128]{1,0:T(8,128)} %get-tuple-element.26), channel_id=1, source_target_pairs={{1,0},{2,1},{3,2},{5,4},{6,5},{7,6},{9,8},{10,9},{11,10},{13,12},{... | collective-permute-start | bytes 233480 | tf_op jit(solution)/shard_map/ppermute | solution.py:413
  48.1 2.8 %copy-start.6 = (f32[152,128]{1,0:T(8,128)}, f32[152,128]{1,0:T(8,128)S(1)}, u32[]{:S(2)}) copy-start(f32[152,128]{1,0:T(8,128)S(1)} %collective-permute-done.6.refs_4_.refs_5_) | copy-start | bytes 233476
  50.9 0.6 copy-start.7
  50.9 0.7 copy-start.4
  50.9 0.7 copy-start.5
  60.4 1.1 copy-start.10
  65.0 13.8 %collective-permute-start.8 = (f32[104,128]{1,0:T(8,128)}, f32[104,128]{1,0:T(8,128)S(1)}, u32[]{:S(2)}, u32[]{:S(2)}) collective-permute-start(f32[104,128]{1,0:T(8,128)} %get-tuple-element.30), channel_id=1, source_target_pairs={{0,4},{4,8},{8,12},{12,16},{16,20},{20,24},{24,28},{28,32},{32,36}... | collective-permute-start | bytes 159752 | tf_op jit(solution)/shard_map/ppermute | solution.py:410
  69.1 9.8 %collective-permute-start.9 = (f32[104,128]{1,0:T(8,128)}, f32[104,128]{1,0:T(8,128)S(1)}, u32[]{:S(2)}, u32[]{:S(2)}) collective-permute-start(f32[104,128]{1,0:T(8,128)} %get-tuple-element.31), channel_id=1, source_target_pairs={{4,0},{8,4},{12,8},{16,12},{20,16},{24,20},{28,24},{32,28},{36,32}... | collective-permute-start | bytes 159752 | tf_op jit(solution)/shard_map/ppermute | solution.py:411
  71.0 6.3 %collective-permute-start.10 = (f32[104,32]{1,0:T(8,128)}, f32[104,32]{1,0:T(8,128)S(1)}, u32[]{:S(2)}, u32[]{:S(2)}) collective-permute-start(f32[104,32]{1,0:T(8,128)} %get-tuple-element.32), channel_id=1, source_target_pairs={{0,1},{1,2},{2,3},{4,5},{5,6},{6,7},{8,9},{9,10},{10,11},{12,13},{... | collective-permute-start | bytes 39944 | tf_op jit(solution)/shard_map/ppermute | solution.py:412
  73.8 5.1 %collective-permute-start.11 = (f32[104,32]{1,0:T(8,128)}, f32[104,32]{1,0:T(8,128)S(1)}, u32[]{:S(2)}, u32[]{:S(2)}) collective-permute-start(f32[104,32]{1,0:T(8,128)} %get-tuple-element.33), channel_id=1, source_target_pairs={{1,0},{2,1},{3,2},{5,4},{6,5},{7,6},{9,8},{10,9},{11,10},{13,12},{... | collective-permute-start | bytes 39944 | tf_op jit(solution)/shard_map/ppermute | solution.py:413
  77.3 1.6 %copy-start.13 = (f32[104,32]{1,0:T(8,128)}, f32[104,32]{1,0:T(8,128)S(1)}, u32[]{:S(2)}) copy-start(f32[104,32]{1,0:T(8,128)S(1)} %collective-permute-done.10.refs_5_) | copy-start | bytes 39940
  78.9 0.6 copy-start.14
  78.9 0.6 copy-start.11
  79.5 0.6 copy-start.12
  83.9 27.6 %copy-start.15 = (s32[1,128]{1,0:T(1,128)S(1)}, s32[1,128]{1,0:T(1,128)}, u32[]{:S(2)}) copy-start(s32[1,128]{1,0:T(1,128)} %param.16) | copy-start | bytes 1540

commit v11 on v9

--- a/solution.py
+++ b/solution.py
@@ -96,26 +96,32 @@
     return face.reshape(100, elems)
 
 
-def les_kernel(mode, vel_ref, nu_ref, vxlo_ref, vxhi_ref, vylo_ref, vyhi_ref,
+def les_kernel(mode, flow_n, grp_n, vel_ref, nu_ref, vxlo_ref, vxhi_ref, vylo_ref, vyhi_ref,
                nxlo_ref, nxhi_ref, nylo_ref, nyhi_ref, *rest):
     size_x, size_y, size_z = vel_ref.shape[1], vel_ref.shape[2], vel_ref.shape[3]
     half = size_z // 2
+    flow_i = lax.axis_index("flow")
+    grp_i = lax.axis_index("grp")
+    at_lo_f = flow_i == 0
+    at_hi_f = flow_i == flow_n - 1
+    at_lo_g = grp_i == 0
+    at_hi_g = grp_i == grp_n - 1
     row = lax.broadcasted_iota(jnp.int32, (size_y, size_z), 0)
     lane = lax.broadcasted_iota(jnp.int32, (size_y, size_z), 1)
     if mode == 0:
         sx0_ref, sx4_ref, sy0_ref, sy4_ref, out_ref, mxup_ref, mxdn_ref, myup_ref, mydn_ref = rest
 
         def xlo(c):
-            return vxlo_ref[c]
+            return jnp.where(at_lo_f, 0.0, vxlo_ref[c])
 
         def xhi(c):
-            return vxhi_ref[c]
+            return jnp.where(at_hi_f, 0.0, vxhi_ref[c])
 
         def ylo(c, x):
-            return vylo_ref[c, x]
+            return jnp.where(at_lo_g, 0.0, vylo_ref[c, x])
 
         def yhi(c, x):
-            return vyhi_ref[c, x]
+            return jnp.where(at_hi_g, 0.0, vyhi_ref[c, x])
     else:
         out_ref, lamb_ref = rest
 
@@ -128,16 +134,16 @@
                 [ref[pl.ds(c * 2 * size_x + x, 1), :], ref[pl.ds(c * 2 * size_x + size_x + x, 1), :]], axis=1)
 
         def xlo(c):
-            return plane(vxlo_ref, c)
+            return jnp.where(at_lo_f, 0.0, plane(vxlo_ref, c))
 
         def xhi(c):
-            return plane(vxhi_ref, c)
+            return jnp.where(at_hi_f, 0.0, plane(vxhi_ref, c))
 
         def ylo(c, x):
-            return line(vylo_ref, c, x)
+            return jnp.where(at_lo_g, 0.0, line(vylo_ref, c, x))
 
         def yhi(c, x):
-            return line(vyhi_ref, c, x)
+            return jnp.where(at_hi_g, 0.0, line(vyhi_ref, c, x))
 
     def yp(f, halo):
         return jnp.where(row == size_y - 1, halo, pltpu.roll(f, size_y - 1, 0))
@@ -162,10 +168,10 @@
         uzm = [zm(u[c]) for c in range(3)]
         uzp = [zp(u[c]) for c in range(3)]
         nu = nu_ref[x]
-        nxm = jnp.where(x == 0, nxlo_ref[3], nu_ref[lo])
-        nxp = jnp.where(x == size_x - 1, nxhi_ref[3], nu_ref[hi])
-        nym = ym(nu, nylo_ref[3, x])
-        nyp = yp(nu, nyhi_ref[3, x])
+        nxm = jnp.where(x == 0, jnp.where(at_lo_f, 0.0, nxlo_ref[3]), nu_ref[lo])
+        nxp = jnp.where(x == size_x - 1, jnp.where(at_hi_f, 0.0, nxhi_ref[3]), nu_ref[hi])
+        nym = ym(nu, jnp.where(at_lo_g, 0.0, nylo_ref[3, x]))
+        nyp = yp(nu, jnp.where(at_hi_g, 0.0, nyhi_ref[3, x]))
         nzm = zm(nu)
         nzp = zp(nu)
         plus = (uxp, uyp, uzp)
@@ -216,14 +222,14 @@
     xbuf = jax.ShapeDtypeStruct((3 * 2 * size_y + FACE_ROWS, size_z // 2), jnp.float32)
     ybuf = jax.ShapeDtypeStruct((3 * 2 * size_x + FACE_ROWS, size_z // 2), jnp.float32)
     return pl.pallas_call(
-        lambda *refs: les_kernel(0, *refs),
+        lambda *refs: les_kernel(0, lax.axis_size("flow"), lax.axis_size("grp"), *refs),
         out_shape=(jax.ShapeDtypeStruct(vel.shape, jnp.float32), xbuf, xbuf, ybuf, ybuf),
     )(vel, nu, *joint, *joint, *faces)
 
 
 def les_section_last(vel, nu, merged, joint):
     return pl.pallas_call(
-        lambda *refs: les_kernel(1, *refs),
+        lambda *refs: les_kernel(1, lax.axis_size("flow"), lax.axis_size("grp"), *refs),
         out_shape=(jax.ShapeDtypeStruct(vel.shape, jnp.float32), jax.ShapeDtypeStruct(vel.shape, jnp.bfloat16)),
     )(vel, nu, *merged, *joint)
 
@@ -231,10 +237,10 @@
 def halos(field, lead):
     flow_n = lax.axis_size("flow")
     grp_n = lax.axis_size("grp")
-    up_f = [(i, i + 1) for i in range(flow_n - 1)]
-    down_f = [(i + 1, i) for i in range(flow_n - 1)]
-    up_g = [(i, i + 1) for i in range(grp_n - 1)]
-    down_g = [(i + 1, i) for i in range(grp_n - 1)]
+    up_f = [(i, (i + 1) % flow_n) for i in range(flow_n)]
+    down_f = [((i + 1) % flow_n, i) for i in range(flow_n)]
+    up_g = [(i, (i + 1) % grp_n) for i in range(grp_n)]
+    down_g = [((i + 1) % grp_n, i) for i in range(grp_n)]
     size_x, size_y = field.shape[lead], field.shape[lead + 1]
     xlo = lax.ppermute(lax.index_in_dim(field, size_x - 1, lead, keepdims=False), "flow", up_f)
     xhi = lax.ppermute(lax.index_in_dim(field, 0, lead, keepdims=False), "flow", down_f)
@@ -292,7 +298,7 @@
     send_faces(face_ref, sx0_ref, sx4_ref, sy0_ref, sy4_ref, sy0_ref.shape[1])
 
 
-def dg_step_kernel(want_faces, xoff, yoff, row_len, state_ref, src_ref, xlo_ref, xhi_ref, ylo_ref, yhi_ref,
+def dg_step_kernel(want_faces, xoff, yoff, row_len, flow_n, grp_n, state_ref, src_ref, xlo_ref, xhi_ref, ylo_ref, yhi_ref,
                    apu_ref, aup_ref, diag_ref, lift_ref, out_ref, *rest):
     if want_faces:
         sx0_ref, sx4_ref, sy0_ref, sy4_ref, face_ref, oth_ref, pad_ref, g_ref = rest
@@ -304,12 +310,16 @@
     face_ref[...] = jnp.zeros(face_ref.shape, jnp.float32)
     oth_ref[...] = jnp.zeros(oth_ref.shape, jnp.float32)
     extract_faces(state_ref, face_ref)
-    oth_ref[pl.ds(0, FACE_ROWS), :] = xlo_ref[pl.ds(xoff, FACE_ROWS), :]
-    oth_ref[pl.ds(128, FACE_ROWS), :] = xhi_ref[pl.ds(xoff, FACE_ROWS), :]
-    pad_ref[:, pl.ds(0, row_len)] = ylo_ref[pl.ds(yoff, FACE_ROWS), pl.ds(0, row_len)]
+    flow_i = lax.axis_index("flow")
+    grp_i = lax.axis_index("grp")
+    oth_ref[pl.ds(0, FACE_ROWS), :] = jnp.where(flow_i == 0, 0.0, xlo_ref[pl.ds(xoff, FACE_ROWS), :])
+    oth_ref[pl.ds(128, FACE_ROWS), :] = jnp.where(flow_i == flow_n - 1, 0.0, xhi_ref[pl.ds(xoff, FACE_ROWS), :])
+    pad_ref[:, pl.ds(0, row_len)] = jnp.where(
+        grp_i == 0, 0.0, ylo_ref[pl.ds(yoff, FACE_ROWS), pl.ds(0, row_len)])
     oth_ref[pl.ds(256, FACE_ROWS), :] = jnp.where(
         lane < row_len, pad_ref[...], pltpu.roll(face_ref[3], row_len, 1))
-    pad_ref[:, pl.ds(0, row_len)] = yhi_ref[pl.ds(yoff, FACE_ROWS), pl.ds(0, row_len)]
+    pad_ref[:, pl.ds(0, row_len)] = jnp.where(
+        grp_i == grp_n - 1, 0.0, yhi_ref[pl.ds(yoff, FACE_ROWS), pl.ds(0, row_len)])
     oth_ref[pl.ds(384, FACE_ROWS), :] = jnp.where(
         lane >= elems - row_len, pltpu.roll(pad_ref[...], elems - row_len, 1),
         pltpu.roll(face_ref[2], elems - row_len, 1))
@@ -368,7 +378,7 @@
     if want_faces:
         out_shape += face_shapes(elems, row_len)
     res = pl.pallas_call(
-        lambda *refs: dg_step_kernel(want_faces, xoff, yoff, row_len, *refs),
+        lambda *refs: dg_step_kernel(want_faces, xoff, yoff, row_len, lax.axis_size("flow"), lax.axis_size("grp"), *refs),
         out_shape=tuple(out_shape),
         scratch_shapes=[
             pltpu.VMEM((6, FACE_ROWS, elems), jnp.float32),
@@ -384,10 +394,10 @@
     sx0, sx4, sy0, sy4 = sent
     flow_n = lax.axis_size("flow")
     grp_n = lax.axis_size("grp")
-    up_f = [(i, i + 1) for i in range(flow_n - 1)]
-    down_f = [(i + 1, i) for i in range(flow_n - 1)]
-    up_g = [(i, i + 1) for i in range(grp_n - 1)]
-    down_g = [(i + 1, i) for i in range(grp_n - 1)]
+    up_f = [(i, (i + 1) % flow_n) for i in range(flow_n)]
+    down_f = [((i + 1) % flow_n, i) for i in range(flow_n)]
+    up_g = [(i, (i + 1) % grp_n) for i in range(grp_n)]
+    down_g = [((i + 1) % grp_n, i) for i in range(grp_n)]
     return (
         lax.ppermute(sx4, "flow", up_f),
         lax.ppermute(sx0, "flow", down_f),

time: 114 us -> 100 us (0.88)
  starting transfers between devices: 40.5 us -> 28 us
  blocking collectives: 28.1 us -> 24.8 us
  waiting for transfers between devices: 11.2 us -> 13.2 us
    ppermute x2, waiting for transfers between devices: 7.61 us -> 0.01 us  [exchange_faces(): lax.ppermute(sy0, 'grp', down_g)]
    all_to_all x1, waiting for transfers between devices: 2.31 us -> 9.44 us  [body(): lax.all_to_all(outgoing, ('flow', 'grp'), split_axis=1, concat_axis=1, ti...]
    ppermute x2, starting transfers between devices: 4.67 us -> 0.3 us  [exchange_faces(): lax.ppermute(sy4, 'grp', up_g)]
    ppermute x1, starting transfers between devices: 3.99 us -> 0.01 us  [halos(): lax.ppermute(lax.slice_in_dim(field, size_y - 1, size_y, axis=lead + 1),...]
    ppermute x2, starting transfers between devices: 6.46 us -> 3.01 us  [exchange_faces(): lax.ppermute(sx4, 'flow', up_f)]
    all_to_all x1, blocking collectives: 28.1 us -> 24.8 us  [body(): lax.all_to_all(leaving, ('flow', 'grp'), split_axis=1, concat_axis=1, til...]
    ppermute x1, starting transfers between devices: 3.54 us -> 0.71 us  [halos(): lax.ppermute(lax.index_in_dim(field, 0, lead, keepdims=False), 'flow', do...]
    ppermute x2, starting transfers between devices: 2.58 us -> 5.31 us  [exchange_faces(): lax.ppermute(sy0, 'grp', down_g)]
  transfers between devices with their start and end apart: 13 -> 13, of which waited for: 5 -> 3; matrix products, arithmetic and copies ran while one was open for 1% -> 2% of each run, Pallas kernels for 1% -> 2%
where the time goes in v11:
time: 100 us; the launch traced here: 99.5 us
  starting transfers between devices  28 us (28%)
  blocking collectives  24.8 us (25%)
  Pallas kernels  15.7 us (16%)
  waiting for transfers between devices  13.2 us (13%)
  local copies, waits for them, and re-layouts  10.1 us (10%)
  matrix products  6.78 us (7%)
    all_to_all x1, blocking collectives, body(): lax.all_to_all(leaving, ('flow', 'grp'), split_axis=1, concat_axis=1, til...  24.8 us
    all_to_all x1, starting transfers between devices, body(): lax.all_to_all(outgoing, ('flow', 'grp'), split_axis=1, concat_axis=1, ti...  11.5 us
    all_to_all x1, waiting for transfers between devices, body(): lax.all_to_all(outgoing, ('flow', 'grp'), split_axis=1, concat_axis=1, ti...  9.44 us
    pallas_call x2, Pallas kernels, dg_step(): pl.pallas_call(lambda *refs: dg_step_kernel(want_faces, xoff, yoff, row_l...  5.67 us
    ppermute x2, starting transfers between devices, exchange_faces(): lax.ppermute(sy0, 'grp', down_g)  5.31 us
    pallas_call x1, Pallas kernels, les_section_first(): pl.pallas_call(lambda *refs: les_kernel(0, lax.axis_size('flow'), lax.axi...  4.21 us
    pallas_call x1, Pallas kernels, les_section_last(): pl.pallas_call(lambda *refs: les_kernel(1, lax.axis_size('flow'), lax.axi...  4.13 us
    unnamed x39, local copies, waits for them, and re-layouts  4.09 us
  transfers between devices with their start and end apart: 13, of which 3 were waited for; matrix products, arithmetic and copies ran while one was open for 2% of the time, Pallas kernels for 2%

profile of v11, /device:TPU:1, one launch (start us, length us, event | category | flops | bytes accessed | tf_op | source)
XLA Modules:
  0.0 99.5 jit_solution(4731987557314665591)
XLA Ops:
  0.6 1.0 copy.37
  1.7 1.2 %fusion.9 = f32[512,128,2]{1,0,2:T(8,128)S(1)} fusion(f32[512,128,1]{1,0,2:T(8,128)S(1)} %bitcast.47, s32[128,2]{0,1:T(2,128)S(1)} %multiply_add_fusion, s32[128]{0:T(128)} %bitcast.49), kind=kOutput, calls=%fused_computation.14 | convolution fusion | flops 201359360 | bytes 787968 | tf_op jit(solution)/shard_map/dot_general | solution.py:421
  2.9 1.0 %copy.31 = f32[512,128,2]{0,2,1:T(2,128)} copy(f32[512,128,2]{1,0,2:T(8,128)S(1)} %fusion.9) | data formatting | bytes 1048576 | tf_op jit(solution)/shard_map/dot_general | solution.py:421
  3.9 11.5 %all-to-all-start = ((f32[512,128,2]{0,2,1:T(2,128)}), f32[512,128,2]{0,2,1:T(2,128)S(1)}, u32[]{:S(2)}, u32[]{:S(2)}) async-start(f32[512,128,2]{0,2,1:T(2,128)} %copy.31), calls=%async_computation | async-start | bytes 1048576 | tf_op jit(solution)/shard_map/all_to_all | solution.py:422
  15.4 2.7 %collective-permute-start.3 = (f32[4,8,1,256]{3,2,1,0:T(1,128)S(1)}, f32[4,8,1,256]{3,2,1,0:T(1,128)S(1)}, u32[]{:S(2)}, u32[]{:S(2)}) collective-permute-start(f32[4,8,1,256]{3,2,1,0:T(1,128)S(1)} %get-tuple-element.42), channel_id=1, source_target_pairs={{1,0},{2,1},{3,2},{0,3},{5,4},{6,5},{7,6},{4,7},{9,8},{10,9},{11,1... | collective-permute-start | bytes 98312 | tf_op jit(solution)/shard_map/ppermute | solution.py:248
  18.1 0.7 collective-permute-start.1
  18.8 1.3 %collective-permute-start = (f32[4,32,256]{2,1,0:T(8,128)S(1)}, f32[4,32,256]{2,1,0:T(8,128)S(1)}, u32[]{:S(2)}, u32[]{:S(2)}) collective-permute-start(f32[4,32,256]{2,1,0:T(8,128)S(1)} %get-tuple-element.45), channel_id=1, source_target_pairs={{0,4},{4,8},{8,12},{12,16},{16,20},{20,24},{24,28},{28,32},{32,36}... | collective-permute-start | bytes 393224 | tf_op jit(solution)/shard_map/ppermute | solution.py:245
  20.4 9.4 %all-to-all-done = f32[512,128,2]{0,2,1:T(2,128)S(1)} async-done(((f32[512,128,2]{0,2,1:T(2,128)}), f32[512,128,2]{0,2,1:T(2,128)S(1)}, u32[]{:S(2)}, u32[]{:S(2)}) %all-to-all-start) | async-done | bytes 524320 | tf_op jit(solution)/shard_map/all_to_all | solution.py:422
  30.2 1.4 %fusion.6.state_ref.refs_0_ = f32[512,128]{1,0:T(8,128)} fusion(f32[512,256]{0,1:T(8,128)S(1)} %all_to_all.13, s32[256]{0:T(256)S(1)} %eq.61), kind=kOutput, calls=%fused_computation.12 | convolution fusion | flops 201359360 | bytes 787456 | tf_op jit(solution)/shard_map/dot_general | solution.py:423
  31.6 1.7 %shard_map.122 = (f32[104,128]{1,0:T(8,128)}, f32[104,128]{1,0:T(8,128)}, f32[104,32]{1,0:T(8,128)}, f32[104,32]{1,0:T(8,128)}) custom-call(f32[512,128]{1,0:T(8,128)} %fusion.6.state_ref.refs_0_), custom_call_target="tpu_custom_call" | custom-call | tf_op jit(solution)/shard_map/pallas_call | solution.py:368
  33.3 0.5 copy-done.8
  34.0 4.2 %shard_map.123 = (f32[3,8,32,256]{3,2,1,0:T(8,128)}, f32[296,128]{1,0:T(8,128)}, f32[296,128]{1,0:T(8,128)}, f32[152,128]{1,0:T(8,128)}, f32[152,128]{1,0:T(8,128)}) custom-call(f32[3,8,32,256]{3,2,1,0:T(8,128)} %refs_0_.1, f32[8,32,256]{2,1,0:T(8,128)} %refs_1_.3, f32[4,32,256]{2,1,0:T(8,128)} %copy-done.3, f32[4,32,256]{2,1,0:T(8,128)} %copy-done.2, ...), custom_call_target="tpu_custom_call" | custom-call | tf_op jit(solution)/shard_map/pallas_call | solution.py:224
  39.0 2.4 %collective-permute-start.7 = (f32[152,128]{1,0:T(8,128)}, f32[152,128]{1,0:T(8,128)S(1)}, u32[]{:S(2)}, u32[]{:S(2)}) collective-permute-start(f32[152,128]{1,0:T(8,128)} %get-tuple-element.26), channel_id=1, source_target_pairs={{1,0},{2,1},{3,2},{0,3},{5,4},{6,5},{7,6},{4,7},{9,8},{10,9},{11,1... | collective-permute-start | bytes 233480 | tf_op jit(solution)/shard_map/ppermute | solution.py:405
  41.4 2.0 %collective-permute-done.6.refs_4_ = f32[152,128]{1,0:T(8,128)S(1)} collective-permute-done((f32[152,128]{1,0:T(8,128)}, f32[152,128]{1,0:T(8,128)S(1)}, u32[]{:S(2)}, u32[]{:S(2)}) %collective-permute-start.6) | collective-permute-done | bytes 77856 | tf_op jit(solution)/shard_map/ppermute | solution.py:404
  43.5 0.6 copy-done.6
  44.2 4.1 %shard_map.124 = (f32[3,8,32,256]{3,2,1,0:T(8,128)}, bf16[3,8,32,256]{3,2,1,0:T(8,128)(2,1)}) custom-call(f32[3,8,32,256]{3,2,1,0:T(8,128)} %get-tuple-element.22.refs_0_, f32[8,32,256]{2,1,0:T(8,128)} %refs_1_.3, f32[296,128]{1,0:T(8,128)} %copy-done.4, f32[296,128]{1,0:T(8,128)} %copy-done.5, f32[152,128]{1,0:T(8,128)} %copy-done.6, f32[152,128]{1,0:T(8,128)} %copy-done.7, ...), custom_call_target="tpu_custom_call" | custom-call | tf_op jit(solution)/shard_map/pallas_call | solution.py:231
  48.4 1.3 %convolution_convert_fusion = bf16[768,256]{1,0:T(8,128)(2,1)S(1)} fusion(bf16[768,256]{1,0:T(8,128)(2,1)} %bitcast.48, bf16[256,256]{1,0:T(8,128)(2,1)S(1)} %copy-done.10), kind=kOutput, calls=%fused_computation.1 | convolution fusion | flops 100859904 | bytes 917504 | tf_op jit(solution)/shard_map/dot_general | solution.py:260
  49.6 0.6 reshape.50
  50.3 2.0 %copy.42 = bf16[3,1,8,4,8,8,32]{6,3,0,5,4,2,1:T(4,128)(2,1)S(1)} copy(bf16[3,1,8,4,8,8,32]{6,5,4,3,2,0,1:T(8,128)(2,1)S(1)} %reshape.50) | data formatting | bytes 786432 | tf_op jit(solution)/shard_map/reshape | solution.py:262
  52.3 0.9 reshape.51
  53.4 1.0 fusion.2
  54.3 2.9 %shard_map.125 = (f32[512,128]{1,0:T(8,128)}, f32[104,128]{1,0:T(8,128)}, f32[104,128]{1,0:T(8,128)}, f32[104,32]{1,0:T(8,128)}, f32[104,32]{1,0:T(8,128)}) custom-call(f32[512,128]{1,0:T(8,128)} %fusion.6.state_ref.refs_0_, f32[384,128]{1,0:T(8,128)} %bitcast.43, f32[296,128]{1,0:T(8,128)} %copy-done.4, f32[296,128]{1,0:T(8,128)} %copy-done.5, ...), custom_call_target="tpu_custom_call" | custom-call | tf_op jit(solution)/shard_map/pallas_call | solution.py:380
  57.3 2.7 %collective-permute-start.8 = (f32[104,128]{1,0:T(8,128)}, f32[104,128]{1,0:T(8,128)S(1)}, u32[]{:S(2)}, u32[]{:S(2)}) collective-permute-start(f32[104,128]{1,0:T(8,128)} %get-tuple-element.30), channel_id=1, source_target_pairs={{0,4},{4,8},{8,12},{12,16},{16,20},{20,24},{24,28},{28,32},{32,36}... | collective-permute-start | bytes 159752 | tf_op jit(solution)/shard_map/ppermute | solution.py:402
  60.0 2.9 %collective-permute-start.9 = (f32[104,128]{1,0:T(8,128)}, f32[104,128]{1,0:T(8,128)S(1)}, u32[]{:S(2)}, u32[]{:S(2)}) collective-permute-start(f32[104,128]{1,0:T(8,128)} %get-tuple-element.31), channel_id=1, source_target_pairs={{4,0},{8,4},{12,8},{16,12},{20,16},{24,20},{28,24},{32,28},{36,32}... | collective-permute-start | bytes 159752 | tf_op jit(solution)/shard_map/ppermute | solution.py:403
  62.9 2.9 %collective-permute-start.11 = (f32[104,32]{1,0:T(8,128)}, f32[104,32]{1,0:T(8,128)S(1)}, u32[]{:S(2)}, u32[]{:S(2)}) collective-permute-start(f32[104,32]{1,0:T(8,128)} %get-tuple-element.33), channel_id=1, source_target_pairs={{1,0},{2,1},{3,2},{0,3},{5,4},{6,5},{7,6},{4,7},{9,8},{10,9},{11,1... | collective-permute-start | bytes 39944 | tf_op jit(solution)/shard_map/ppermute | solution.py:405
  65.9 1.7 %collective-permute-done.10.refs_4_ = f32[104,32]{1,0:T(8,128)S(1)} collective-permute-done((f32[104,32]{1,0:T(8,128)}, f32[104,32]{1,0:T(8,128)S(1)}, u32[]{:S(2)}, u32[]{:S(2)}) %collective-permute-start.10) | collective-permute-done | bytes 13344 | tf_op jit(solution)/shard_map/ppermute | solution.py:404
  67.6 0.6 copy-done.14
  68.3 2.7 %shard_map.126 = f32[512,128]{1,0:T(8,128)} custom-call(f32[512,128]{1,0:T(8,128)} %get-tuple-element.29.refs_0_, f32[384,128]{1,0:T(8,128)} %bitcast.44, f32[104,128]{1,0:T(8,128)} %copy-done.12, f32[104,128]{1,0:T(8,128)} %copy-done.13, f32[104,32]{1,0:T(8,128)} %copy-done.14, f32[104,32]{1,0:T(8,128)} %copy-done.15, f32[128,384]{1,0:T(8,128)} %constant.17.clone.refs_6_, ...), custom_call_target="tpu_custom_call" | custom-call | tf_op jit(solution)/shard_map/pallas_call | solution.py:380
  71.0 1.4 %fusion.5 = f32[512,256]{0,1:T(8,128)S(1)} fusion(f32[512,128]{1,0:T(8,128)} %shard_map.126, s32[256]{0:T(256)S(1)} %eq.61), kind=kOutput, calls=%fused_computation.11 | convolution fusion | flops 201359360 | bytes 787456 | tf_op jit(solution)/shard_map/dot_general | solution.py:438
  72.7 24.8 %all_to_all.18 = f32[512,128,2]{0,2,1:T(2,128)S(1)} all-to-all(f32[512,128,2]{0,2,1:T(2,128)S(1)} %all_to_all.14), channel_id=1, replica_groups=mesh['flow'=32,'grp'=4] {'flow','grp'}, dimensions={1} | all-to-all | bytes 1048576 | tf_op jit(solution)/shard_map/all_to_all | solution.py:439
  98.0 0.6 fusion
  98.7 0.9 copy.36
  (58 shorter events, 3.0 us)
Async XLA Ops:
  1.6 13.7 %copy-start = (f32[3,8,32,256]{3,2,1,0:T(8,128)S(1)}, f32[3,8,32,256]{3,2,1,0:T(8,128)}, u32[]{:S(2)}) copy-start(f32[3,8,32,256]{3,2,1,0:T(8,128)} %refs_0_.1) | copy-start | bytes 2359300
  1.7 13.7 %copy-start.1 = (f32[8,32,256]{2,1,0:T(8,128)S(1)}, f32[8,32,256]{2,1,0:T(8,128)}, u32[]{:S(2)}) copy-start(f32[8,32,256]{2,1,0:T(8,128)} %refs_1_.3) | copy-start | bytes 786436
  3.9 16.3 %copy-start.17 = (s32[1,128,2]{1,2,0:T(2,128)S(1)}, s32[1,128,2]{1,2,0:T(2,128)}, u32[]{:S(2)}) copy-start(s32[1,128,2]{1,2,0:T(2,128)} %param.15) | copy-start | bytes 3076
  3.9 26.0 %all-to-all-start = ((f32[512,128,2]{0,2,1:T(2,128)}), f32[512,128,2]{0,2,1:T(2,128)S(1)}, u32[]{:S(2)}, u32[]{:S(2)}) async-start(f32[512,128,2]{0,2,1:T(2,128)} %copy.31), calls=%async_computation | async-start | bytes 1048576 | tf_op jit(solution)/shard_map/all_to_all | solution.py:422
  15.4 17.8 %collective-permute-start.3 = (f32[4,8,1,256]{3,2,1,0:T(1,128)S(1)}, f32[4,8,1,256]{3,2,1,0:T(1,128)S(1)}, u32[]{:S(2)}, u32[]{:S(2)}) collective-permute-start(f32[4,8,1,256]{3,2,1,0:T(1,128)S(1)} %get-tuple-element.42), channel_id=1, source_target_pairs={{1,0},{2,1},{3,2},{0,3},{5,4},{6,5},{7,6},{4,7},{9,8},{10,9},{11,1... | collective-permute-start | bytes 98312 | tf_op jit(solution)/shard_map/ppermute | solution.py:248
  18.1 15.2 %collective-permute-start.2 = (f32[4,8,1,256]{3,2,1,0:T(1,128)S(1)}, f32[4,8,1,256]{3,2,1,0:T(1,128)S(1)}, u32[]{:S(2)}, u32[]{:S(2)}) collective-permute-start(f32[4,8,1,256]{3,2,1,0:T(1,128)S(1)} %get-tuple-element.43), channel_id=1, source_target_pairs={{0,1},{1,2},{2,3},{3,0},{4,5},{5,6},{6,7},{7,4},{8,9},{9,10},{10,1... | collective-permute-start | bytes 98312 | tf_op jit(solution)/shard_map/ppermute | solution.py:247
  18.1 15.2 %collective-permute-start.1 = (f32[4,32,256]{2,1,0:T(8,128)S(1)}, f32[4,32,256]{2,1,0:T(8,128)S(1)}, u32[]{:S(2)}, u32[]{:S(2)}) collective-permute-start(f32[4,32,256]{2,1,0:T(8,128)S(1)} %get-tuple-element.44), channel_id=1, source_target_pairs={{4,0},{8,4},{12,8},{16,12},{20,16},{24,20},{28,24},{32,28},{36,32}... | collective-permute-start | bytes 393224 | tf_op jit(solution)/shard_map/ppermute | solution.py:246
  18.8 14.5 %collective-permute-start = (f32[4,32,256]{2,1,0:T(8,128)S(1)}, f32[4,32,256]{2,1,0:T(8,128)S(1)}, u32[]{:S(2)}, u32[]{:S(2)}) collective-permute-start(f32[4,32,256]{2,1,0:T(8,128)S(1)} %get-tuple-element.45), channel_id=1, source_target_pairs={{0,4},{4,8},{8,12},{12,16},{16,20},{20,24},{24,28},{28,32},{32,36}... | collective-permute-start | bytes 393224 | tf_op jit(solution)/shard_map/ppermute | solution.py:245
  33.3 0.6 copy-start.8
  33.3 0.6 copy-start.9
  33.3 0.7 copy-start.2
  33.3 0.7 copy-start.3
  34.0 14.3 %copy-start.10 = (bf16[256,256]{1,0:T(8,128)(2,1)S(1)}, bf16[256,256]{1,0:T(8,128)(2,1)}, u32[]{:S(2)}) copy-start(bf16[256,256]{1,0:T(8,128)(2,1)} %constant.21.clone) | copy-start | bytes 393220
  38.2 5.2 %collective-permute-start.4 = (f32[296,128]{1,0:T(8,128)}, f32[296,128]{1,0:T(8,128)S(1)}, u32[]{:S(2)}, u32[]{:S(2)}) collective-permute-start(f32[296,128]{1,0:T(8,128)} %get-tuple-element.23), channel_id=1, source_target_pairs={{0,4},{4,8},{8,12},{12,16},{16,20},{20,24},{24,28},{28,32},{32,36}... | collective-permute-start | bytes 454664 | tf_op jit(solution)/shard_map/ppermute | solution.py:402
  38.5 4.9 %collective-permute-start.5 = (f32[296,128]{1,0:T(8,128)}, f32[296,128]{1,0:T(8,128)S(1)}, u32[]{:S(2)}, u32[]{:S(2)}) collective-permute-start(f32[296,128]{1,0:T(8,128)} %get-tuple-element.24), channel_id=1, source_target_pairs={{4,0},{8,4},{12,8},{16,12},{20,16},{24,20},{28,24},{32,28},{36,32}... | collective-permute-start | bytes 454664 | tf_op jit(solution)/shard_map/ppermute | solution.py:403
  38.7 4.7 %collective-permute-start.6 = (f32[152,128]{1,0:T(8,128)}, f32[152,128]{1,0:T(8,128)S(1)}, u32[]{:S(2)}, u32[]{:S(2)}) collective-permute-start(f32[152,128]{1,0:T(8,128)} %get-tuple-element.25), channel_id=1, source_target_pairs={{0,1},{1,2},{2,3},{3,0},{4,5},{5,6},{6,7},{7,4},{8,9},{9,10},{10,1... | collective-permute-start | bytes 233480 | tf_op jit(solution)/shard_map/ppermute | solution.py:404
  39.0 4.4 %collective-permute-start.7 = (f32[152,128]{1,0:T(8,128)}, f32[152,128]{1,0:T(8,128)S(1)}, u32[]{:S(2)}, u32[]{:S(2)}) collective-permute-start(f32[152,128]{1,0:T(8,128)} %get-tuple-element.26), channel_id=1, source_target_pairs={{1,0},{2,1},{3,2},{0,3},{5,4},{6,5},{7,6},{4,7},{9,8},{10,9},{11,1... | collective-permute-start | bytes 233480 | tf_op jit(solution)/shard_map/ppermute | solution.py:405
  43.4 0.6 copy-start.6
  43.4 0.7 copy-start.7
  43.4 0.7 copy-start.4
  43.4 0.8 copy-start.5
  52.3 1.1 %copy-start.11 = (bf16[125,512]{1,0:T(8,128)(2,1)S(1)}, bf16[125,512]{1,0:T(8,128)(2,1)}, u32[]{:S(2)}) copy-start(bf16[125,512]{1,0:T(8,128)(2,1)} %param.13) | copy-start | bytes 384004
  57.3 10.3 %collective-permute-start.8 = (f32[104,128]{1,0:T(8,128)}, f32[104,128]{1,0:T(8,128)S(1)}, u32[]{:S(2)}, u32[]{:S(2)}) collective-permute-start(f32[104,128]{1,0:T(8,128)} %get-tuple-element.30), channel_id=1, source_target_pairs={{0,4},{4,8},{8,12},{12,16},{16,20},{20,24},{24,28},{28,32},{32,36}... | collective-permute-start | bytes 159752 | tf_op jit(solution)/shard_map/ppermute | solution.py:402
  60.0 7.6 %collective-permute-start.9 = (f32[104,128]{1,0:T(8,128)}, f32[104,128]{1,0:T(8,128)S(1)}, u32[]{:S(2)}, u32[]{:S(2)}) collective-permute-start(f32[104,128]{1,0:T(8,128)} %get-tuple-element.31), channel_id=1, source_target_pairs={{4,0},{8,4},{12,8},{16,12},{20,16},{24,20},{28,24},{32,28},{36,32}... | collective-permute-start | bytes 159752 | tf_op jit(solution)/shard_map/ppermute | solution.py:403
  62.9 4.7 %collective-permute-start.10 = (f32[104,32]{1,0:T(8,128)}, f32[104,32]{1,0:T(8,128)S(1)}, u32[]{:S(2)}, u32[]{:S(2)}) collective-permute-start(f32[104,32]{1,0:T(8,128)} %get-tuple-element.32), channel_id=1, source_target_pairs={{0,1},{1,2},{2,3},{3,0},{4,5},{5,6},{6,7},{7,4},{8,9},{9,10},{10,1... | collective-permute-start | bytes 39944 | tf_op jit(solution)/shard_map/ppermute | solution.py:404
  62.9 4.7 %collective-permute-start.11 = (f32[104,32]{1,0:T(8,128)}, f32[104,32]{1,0:T(8,128)S(1)}, u32[]{:S(2)}, u32[]{:S(2)}) collective-permute-start(f32[104,32]{1,0:T(8,128)} %get-tuple-element.33), channel_id=1, source_target_pairs={{1,0},{2,1},{3,2},{0,3},{5,4},{6,5},{7,6},{4,7},{9,8},{10,9},{11,1... | collective-permute-start | bytes 39944 | tf_op jit(solution)/shard_map/ppermute | solution.py:405
  67.6 0.6 copy-start.14
  67.6 0.6 copy-start.15
  67.6 0.7 copy-start.12
  67.6 0.7 copy-start.13
  72.4 25.6 %copy-start.16 = (s32[1,128]{1,0:T(1,128)S(1)}, s32[1,128]{1,0:T(1,128)}, u32[]{:S(2)}) copy-start(s32[1,128]{1,0:T(1,128)} %param.16) | copy-start | bytes 1540

commit v12 on v11

--- a/solution.py
+++ b/solution.py
@@ -109,7 +109,7 @@
     row = lax.broadcasted_iota(jnp.int32, (size_y, size_z), 0)
     lane = lax.broadcasted_iota(jnp.int32, (size_y, size_z), 1)
     if mode == 0:
-        sx0_ref, sx4_ref, sy0_ref, sy4_ref, out_ref, mxup_ref, mxdn_ref, myup_ref, mydn_ref = rest
+        (out_ref,) = rest
 
         def xlo(c):
             return jnp.where(at_lo_f, 0.0, vxlo_ref[c])
@@ -197,34 +197,13 @@
         return carry
 
     lax.fori_loop(0, size_x, step, 0)
-    if mode == 0:
-        for c in range(3):
-            for h in range(2):
-                mxup_ref[pl.ds(c * 2 * size_y + h * size_y, size_y), :] = out_ref[c, size_x - 1, :, pl.ds(h * half, half)]
-                mxdn_ref[pl.ds(c * 2 * size_y + h * size_y, size_y), :] = out_ref[c, 0, :, pl.ds(h * half, half)]
-                for x in range(size_x):
-                    at = c * 2 * size_x + h * size_x + x
-                    myup_ref[pl.ds(at, 1), :] = out_ref[c, x, pl.ds(size_y - 1, 1), pl.ds(h * half, half)]
-                    mydn_ref[pl.ds(at, 1), :] = out_ref[c, x, pl.ds(0, 1), pl.ds(h * half, half)]
-        xrows = 3 * 2 * size_y
-        yrows = 3 * 2 * size_x
-        mxup_ref[pl.ds(xrows, FACE_ROWS), :] = sx4_ref[...]
-        mxdn_ref[pl.ds(xrows, FACE_ROWS), :] = sx0_ref[...]
-        zeros = jnp.zeros((FACE_ROWS, half), jnp.float32)
-        myup_ref[pl.ds(yrows, FACE_ROWS), :] = zeros
-        mydn_ref[pl.ds(yrows, FACE_ROWS), :] = zeros
-        myup_ref[pl.ds(yrows, FACE_ROWS), pl.ds(0, sy4_ref.shape[1])] = sy4_ref[...]
-        mydn_ref[pl.ds(yrows, FACE_ROWS), pl.ds(0, sy0_ref.shape[1])] = sy0_ref[...]
-
-
-def les_section_first(vel, nu, joint, faces):
-    size_x, size_y, size_z = vel.shape[1], vel.shape[2], vel.shape[3]
-    xbuf = jax.ShapeDtypeStruct((3 * 2 * size_y + FACE_ROWS, size_z // 2), jnp.float32)
-    ybuf = jax.ShapeDtypeStruct((3 * 2 * size_x + FACE_ROWS, size_z // 2), jnp.float32)
+
+
+def les_section_first(vel, nu, joint):
     return pl.pallas_call(
         lambda *refs: les_kernel(0, lax.axis_size("flow"), lax.axis_size("grp"), *refs),
-        out_shape=(jax.ShapeDtypeStruct(vel.shape, jnp.float32), xbuf, xbuf, ybuf, ybuf),
-    )(vel, nu, *joint, *joint, *faces)
+        out_shape=(jax.ShapeDtypeStruct(vel.shape, jnp.float32),),
+    )(vel, nu, *joint, *joint)[0]
 
 
 def les_section_last(vel, nu, merged, joint):
@@ -292,10 +271,28 @@
     sy4_ref[...] = last[:, :row_len]
 
 
-def dg_faces_kernel(state_ref, sx0_ref, sx4_ref, sy0_ref, sy4_ref, face_ref):
+def dg_faces_kernel(state_ref, vel_ref, mxup_ref, mxdn_ref, myup_ref, mydn_ref, face_ref):
+    elems = state_ref.shape[1]
     face_ref[...] = jnp.zeros(face_ref.shape, jnp.float32)
     extract_faces(state_ref, face_ref)
-    send_faces(face_ref, sx0_ref, sx4_ref, sy0_ref, sy4_ref, sy0_ref.shape[1])
+    size_x, size_y, size_z = vel_ref.shape[1], vel_ref.shape[2], vel_ref.shape[3]
+    half = size_z // 2
+    row_len = size_z // 8
+    for c in range(3):
+        for h in range(2):
+            mxup_ref[pl.ds(c * 2 * size_y + h * size_y, size_y), :] = vel_ref[c, size_x - 1, :, pl.ds(h * half, half)]
+            mxdn_ref[pl.ds(c * 2 * size_y + h * size_y, size_y), :] = vel_ref[c, 0, :, pl.ds(h * half, half)]
+            for x in range(size_x):
+                at = c * 2 * size_x + h * size_x + x
+                myup_ref[pl.ds(at, 1), :] = vel_ref[c, x, pl.ds(size_y - 1, 1), pl.ds(h * half, half)]
+                mydn_ref[pl.ds(at, 1), :] = vel_ref[c, x, pl.ds(0, 1), pl.ds(h * half, half)]
+    xrows = 3 * 2 * size_y
+    yrows = 3 * 2 * size_x
+    mxup_ref[pl.ds(xrows, FACE_ROWS), :] = face_ref[1]
+    mxdn_ref[pl.ds(xrows, FACE_ROWS), :] = face_ref[0]
+    lane = lax.broadcasted_iota(jnp.int32, (FACE_ROWS, elems), 1)
+    myup_ref[pl.ds(yrows, FACE_ROWS), :] = jnp.where(lane < row_len, pltpu.roll(face_ref[3], row_len, 1), 0.0)
+    mydn_ref[pl.ds(yrows, FACE_ROWS), :] = jnp.where(lane < row_len, face_ref[2], 0.0)
 
 
 def dg_step_kernel(want_faces, xoff, yoff, row_len, flow_n, grp_n, state_ref, src_ref, xlo_ref, xhi_ref, ylo_ref, yhi_ref,
@@ -363,13 +360,16 @@
     return [big, big, small, small]
 
 
-def dg_faces(state, row_len):
+def dg_faces(state, vel):
     elems = state.shape[1]
+    size_x, size_y, size_z = vel.shape[1], vel.shape[2], vel.shape[3]
+    xbuf = jax.ShapeDtypeStruct((3 * 2 * size_y + FACE_ROWS, size_z // 2), jnp.float32)
+    ybuf = jax.ShapeDtypeStruct((3 * 2 * size_x + FACE_ROWS, size_z // 2), jnp.float32)
     return pl.pallas_call(
         dg_faces_kernel,
-        out_shape=tuple(face_shapes(elems, row_len)),
+        out_shape=(xbuf, xbuf, ybuf, ybuf),
         scratch_shapes=[pltpu.VMEM((6, FACE_ROWS, elems), jnp.float32)],
-    )(state)
+    )(state, vel)
 
 
 def dg_step(state, src, recv, mats, want_faces, row_len, xoff=0, yoff=0):
@@ -424,8 +424,8 @@
 
     row_len = velocity.shape[3] // 8
     mats = [jnp.asarray(m) for m in dg_matrices()]
-    sent = dg_faces(state, row_len)
-    vel, mxup, mxdn, myup, mydn = les_section_first(velocity, eddy_visc, joint, sent)
+    vel = les_section_first(velocity, eddy_visc, joint)
+    mxup, mxdn, myup, mydn = dg_faces(state, vel)
     merged = exchange_faces((mxdn, mxup, mydn, myup))
     vel, lamb = les_section_last(vel, eddy_visc, merged, joint)
     source = project(lamb, projection)

time: 100 us -> 101 us (1.010)
  waiting for transfers between devices: 13.2 us -> 7.95 us
  starting transfers between devices: 28 us -> 33.2 us
  local copies, waits for them, and re-layouts: 10.1 us -> 11.3 us
    all_to_all x1, waiting for transfers between devices: 9.44 us -> 0.01 us  [body(): lax.all_to_all(outgoing, ('flow', 'grp'), split_axis=1, concat_axis=1, ti...]
    ppermute x2, starting transfers between devices: 3.14 us -> 9.73 us  [exchange_faces(): lax.ppermute(sx0, 'flow', down_f)]
    ppermute x1, waiting for transfers between devices: 0.01 us -> 2.97 us  [halos(): lax.ppermute(lax.slice_in_dim(field, 0, 1, axis=lead + 1), 'grp', down_g)]
    ppermute x1, waiting for transfers between devices: 0.01 us -> 1.23 us  [halos(): lax.ppermute(lax.slice_in_dim(field, size_y - 1, size_y, axis=lead + 1),...]
    unnamed x39, local copies, waits for them, and re-layouts: 4.09 us -> 5.28 us
    ppermute x2, starting transfers between devices: 3.01 us -> 1.9 us  [exchange_faces(): lax.ppermute(sx4, 'flow', up_f)]
  transfers between devices with their start and end apart: 13 -> 13, of which waited for: 3 -> 4; matrix products, arithmetic and copies ran while one was open for 2% -> 0% of each run, Pallas kernels for 2% -> 4%
where the time goes in v12:
time: 101 us
  starting transfers between devices  33.2 us (33%)
  blocking collectives  24.8 us (25%)
  Pallas kernels  15.8 us (16%)
  local copies, waits for them, and re-layouts  11.3 us (11%)
  waiting for transfers between devices  7.95 us (8%)
  matrix products  6.78 us (7%)
    all_to_all x1, blocking collectives, body(): lax.all_to_all(leaving, ('flow', 'grp'), split_axis=1, concat_axis=1, til...  24.8 us
    all_to_all x1, starting transfers between devices, body(): lax.all_to_all(outgoing, ('flow', 'grp'), split_axis=1, concat_axis=1, ti...  11.5 us
    ppermute x2, starting transfers between devices, exchange_faces(): lax.ppermute(sx0, 'flow', down_f)  9.73 us
    pallas_call x2, Pallas kernels, dg_step(): pl.pallas_call(lambda *refs: dg_step_kernel(want_faces, xoff, yoff, row_l...  5.67 us
    unnamed x39, local copies, waits for them, and re-layouts  5.28 us
    ppermute x2, starting transfers between devices, exchange_faces(): lax.ppermute(sy0, 'grp', down_g)  4.98 us
    pallas_call x1, Pallas kernels, les_section_last(): pl.pallas_call(lambda *refs: les_kernel(1, lax.axis_size('flow'), lax.axi...  4.13 us
    pallas_call x1, Pallas kernels, les_section_first(): pl.pallas_call(lambda *refs: les_kernel(0, lax.axis_size('flow'), lax.axi...  4 us
  transfers between devices with their start and end apart: 13, of which 4 were waited for; matrix products, arithmetic and copies ran while one was open for 0% of the time, Pallas kernels for 4%

profile of v12, /device:TPU:1, one launch (start us, length us, event | category | flops | bytes accessed | tf_op | source)
XLA Modules:
  0.0 100.9 jit_solution(10838137824020524865)
XLA Ops:
  0.6 1.0 copy.37
  1.7 1.2 %fusion.9 = f32[512,128,2]{1,0,2:T(8,128)S(1)} fusion(f32[512,128,1]{1,0,2:T(8,128)S(1)} %bitcast.47, s32[128,2]{0,1:T(2,128)S(1)} %multiply_add_fusion, s32[128]{0:T(128)} %bitcast.49), kind=kOutput, calls=%fused_computation.14 | convolution fusion | flops 201359360 | bytes 787968 | tf_op jit(solution)/shard_map/dot_general | solution.py:421
  2.9 1.0 copy.31
  3.9 11.5 %all-to-all-start = ((f32[512,128,2]{0,2,1:T(2,128)}), f32[512,128,2]{0,2,1:T(2,128)S(1)}, u32[]{:S(2)}, u32[]{:S(2)}) async-start(f32[512,128,2]{0,2,1:T(2,128)} %copy.31), calls=%async_computation | async-start | bytes 1048576 | tf_op jit(solution)/shard_map/all_to_all | solution.py:422
  15.4 1.1 %collective-permute-start.1 = (f32[4,32,256]{2,1,0:T(8,128)S(1)}, f32[4,32,256]{2,1,0:T(8,128)S(1)}, u32[]{:S(2)}, u32[]{:S(2)}) collective-permute-start(f32[4,32,256]{2,1,0:T(8,128)S(1)} %get-tuple-element.34), channel_id=1, source_target_pairs={{4,0},{8,4},{12,8},{16,12},{20,16},{24,20},{28,24},{32,28},{36,32}... | collective-permute-start | bytes 393224 | tf_op jit(solution)/shard_map/ppermute | solution.py:225
  16.6 0.8 collective-permute-start
  17.4 2.6 %collective-permute-start.3 = (f32[4,8,1,256]{3,2,1,0:T(1,128)S(1)}, f32[4,8,1,256]{3,2,1,0:T(1,128)S(1)}, u32[]{:S(2)}, u32[]{:S(2)}) collective-permute-start(f32[4,8,1,256]{3,2,1,0:T(1,128)S(1)} %get-tuple-element.32), channel_id=1, source_target_pairs={{1,0},{2,1},{3,2},{0,3},{5,4},{6,5},{7,6},{4,7},{9,8},{10,9},{11,1... | collective-permute-start | bytes 98312 | tf_op jit(solution)/shard_map/ppermute | solution.py:227
  20.2 3.0 %collective-permute-done.3.refs_5_.refs_9_ = f32[4,8,1,256]{3,2,1,0:T(1,128)S(1)} collective-permute-done((f32[4,8,1,256]{3,2,1,0:T(1,128)S(1)}, f32[4,8,1,256]{3,2,1,0:T(1,128)S(1)}, u32[]{:S(2)}, u32[]{:S(2)}) %collective-permute-start.3) | collective-permute-done | bytes 32800 | tf_op jit(solution)/shard_map/ppermute | solution.py:227
  23.2 1.2 %collective-permute-done.2.refs_4_.refs_8_ = f32[4,8,1,256]{3,2,1,0:T(1,128)S(1)} collective-permute-done((f32[4,8,1,256]{3,2,1,0:T(1,128)S(1)}, f32[4,8,1,256]{3,2,1,0:T(1,128)S(1)}, u32[]{:S(2)}, u32[]{:S(2)}) %collective-permute-start.2) | collective-permute-done | bytes 32800 | tf_op jit(solution)/shard_map/ppermute | solution.py:226
  25.1 0.6 copy-done.3
  25.7 4.0 %shard_map.122.vel_ref.refs_0_ = f32[3,8,32,256]{3,2,1,0:T(8,128)} custom-call(f32[3,8,32,256]{3,2,1,0:T(8,128)} %refs_0_.1, f32[8,32,256]{2,1,0:T(8,128)} %refs_1_.3, f32[4,32,256]{2,1,0:T(8,128)} %copy-done.3, f32[4,32,256]{2,1,0:T(8,128)} %copy-done.2, f32[4,8,1,256]{3,2,1,0:T(1,128)} %copy-done.9, f32[4,8,1,256]{3,2,1,0:T(1,128)} %copy-done.8, ...), custom_call_target="tpu_custom_call" | custom-call | tf_op jit(solution)/shard_map/pallas_call | solution.py:203
  30.1 1.4 %fusion.6.state_ref.refs_0_ = f32[512,128]{1,0:T(8,128)} fusion(f32[512,256]{0,1:T(8,128)S(1)} %all_to_all.13, s32[256]{0:T(256)S(1)} %eq.61), kind=kOutput, calls=%fused_computation.12 | convolution fusion | flops 201359360 | bytes 787456 | tf_op jit(solution)/shard_map/dot_general | solution.py:423
  31.5 2.0 %shard_map.123 = (f32[296,128]{1,0:T(8,128)}, f32[296,128]{1,0:T(8,128)}, f32[152,128]{1,0:T(8,128)}, f32[152,128]{1,0:T(8,128)}) custom-call(f32[512,128]{1,0:T(8,128)} %fusion.6.state_ref.refs_0_, f32[3,8,32,256]{3,2,1,0:T(8,128)} %shard_map.122.vel_ref.refs_0_), custom_call_target="tpu_custom_call" | custom-call | tf_op jit(solution)/shard_map/pallas_call | solution.py:368
  33.5 1.9 %collective-permute-start.4 = (f32[296,128]{1,0:T(8,128)}, f32[296,128]{1,0:T(8,128)S(1)}, u32[]{:S(2)}, u32[]{:S(2)}) collective-permute-start(f32[296,128]{1,0:T(8,128)} %get-tuple-element.13), channel_id=1, source_target_pairs={{0,4},{4,8},{8,12},{12,16},{16,20},{20,24},{24,28},{28,32},{32,36}... | collective-permute-start | bytes 454664 | tf_op jit(solution)/shard_map/ppermute | solution.py:402
  35.4 3.5 %collective-permute-start.5 = (f32[296,128]{1,0:T(8,128)}, f32[296,128]{1,0:T(8,128)S(1)}, u32[]{:S(2)}, u32[]{:S(2)}) collective-permute-start(f32[296,128]{1,0:T(8,128)} %get-tuple-element.14), channel_id=1, source_target_pairs={{4,0},{8,4},{12,8},{16,12},{20,16},{24,20},{28,24},{32,28},{36,32}... | collective-permute-start | bytes 454664 | tf_op jit(solution)/shard_map/ppermute | solution.py:403
  39.2 2.3 %collective-permute-start.7 = (f32[152,128]{1,0:T(8,128)}, f32[152,128]{1,0:T(8,128)S(1)}, u32[]{:S(2)}, u32[]{:S(2)}) collective-permute-start(f32[152,128]{1,0:T(8,128)} %get-tuple-element.16), channel_id=1, source_target_pairs={{1,0},{2,1},{3,2},{0,3},{5,4},{6,5},{7,6},{4,7},{9,8},{10,9},{11,1... | collective-permute-start | bytes 233480 | tf_op jit(solution)/shard_map/ppermute | solution.py:405
  41.6 2.0 %collective-permute-done.6.refs_4_ = f32[152,128]{1,0:T(8,128)S(1)} collective-permute-done((f32[152,128]{1,0:T(8,128)}, f32[152,128]{1,0:T(8,128)S(1)}, u32[]{:S(2)}, u32[]{:S(2)}) %collective-permute-start.6) | collective-permute-done | bytes 77856 | tf_op jit(solution)/shard_map/ppermute | solution.py:404
  44.3 0.7 copy-done.5
  44.9 4.1 %shard_map.124 = (f32[3,8,32,256]{3,2,1,0:T(8,128)}, bf16[3,8,32,256]{3,2,1,0:T(8,128)(2,1)}) custom-call(f32[3,8,32,256]{3,2,1,0:T(8,128)} %shard_map.122.vel_ref.refs_0_, f32[8,32,256]{2,1,0:T(8,128)} %refs_1_.3, f32[296,128]{1,0:T(8,128)} %copy-done.4, f32[296,128]{1,0:T(8,128)} %copy-done.5, f32[152,128]{1,0:T(8,128)} %copy-done.6, ...), custom_call_target="tpu_custom_call" | custom-call | tf_op jit(solution)/shard_map/pallas_call | solution.py:210
  49.1 1.2 %convolution_convert_fusion = bf16[768,256]{1,0:T(8,128)(2,1)S(1)} fusion(bf16[768,256]{1,0:T(8,128)(2,1)} %bitcast.48, bf16[256,256]{1,0:T(8,128)(2,1)S(1)} %copy-done.10), kind=kOutput, calls=%fused_computation.1 | convolution fusion | flops 100859904 | bytes 917504 | tf_op jit(solution)/shard_map/dot_general | solution.py:239
  51.0 2.0 %copy.42 = bf16[3,1,8,4,8,8,32]{6,3,0,5,4,2,1:T(4,128)(2,1)S(1)} copy(bf16[3,1,8,4,8,8,32]{6,5,4,3,2,0,1:T(8,128)(2,1)S(1)} %reshape.50) | data formatting | bytes 786432 | tf_op jit(solution)/shard_map/reshape | solution.py:241
  53.0 0.9 reshape.51
  54.1 1.0 fusion.2
  55.0 3.0 %shard_map.125 = (f32[512,128]{1,0:T(8,128)}, f32[104,128]{1,0:T(8,128)}, f32[104,128]{1,0:T(8,128)}, f32[104,32]{1,0:T(8,128)}, f32[104,32]{1,0:T(8,128)}) custom-call(f32[512,128]{1,0:T(8,128)} %fusion.6.state_ref.refs_0_, f32[384,128]{1,0:T(8,128)} %bitcast.43, f32[296,128]{1,0:T(8,128)} %copy-done.4, f32[296,128]{1,0:T(8,128)} %copy-done.5, ...), custom_call_target="tpu_custom_call" | custom-call | tf_op jit(solution)/shard_map/pallas_call | solution.py:380
  58.0 6.3 %collective-permute-start.9 = (f32[104,128]{1,0:T(8,128)}, f32[104,128]{1,0:T(8,128)S(1)}, u32[]{:S(2)}, u32[]{:S(2)}) collective-permute-start(f32[104,128]{1,0:T(8,128)} %get-tuple-element.21), channel_id=1, source_target_pairs={{4,0},{8,4},{12,8},{16,12},{20,16},{24,20},{28,24},{32,28},{36,32}... | collective-permute-start | bytes 159752 | tf_op jit(solution)/shard_map/ppermute | solution.py:403
  64.5 2.7 %collective-permute-start.11 = (f32[104,32]{1,0:T(8,128)}, f32[104,32]{1,0:T(8,128)S(1)}, u32[]{:S(2)}, u32[]{:S(2)}) collective-permute-start(f32[104,32]{1,0:T(8,128)} %get-tuple-element.23), channel_id=1, source_target_pairs={{1,0},{2,1},{3,2},{0,3},{5,4},{6,5},{7,6},{4,7},{9,8},{10,9},{11,1... | collective-permute-start | bytes 39944 | tf_op jit(solution)/shard_map/ppermute | solution.py:405
  67.2 1.7 %collective-permute-done.10.refs_4_ = f32[104,32]{1,0:T(8,128)S(1)} collective-permute-done((f32[104,32]{1,0:T(8,128)}, f32[104,32]{1,0:T(8,128)S(1)}, u32[]{:S(2)}, u32[]{:S(2)}) %collective-permute-start.10) | collective-permute-done | bytes 13344 | tf_op jit(solution)/shard_map/ppermute | solution.py:404
  69.6 2.7 %shard_map.126 = f32[512,128]{1,0:T(8,128)} custom-call(f32[512,128]{1,0:T(8,128)} %get-tuple-element.19.refs_0_, f32[384,128]{1,0:T(8,128)} %bitcast.44, f32[104,128]{1,0:T(8,128)} %copy-done.12, f32[104,128]{1,0:T(8,128)} %copy-done.13, f32[104,32]{1,0:T(8,128)} %copy-done.14, f32[104,32]{1,0:T(8,128)} %copy-done.15, f32[128,384]{1,0:T(8,128)} %constant.17.clone.refs_6_, ...), custom_call_target="tpu_custom_call" | custom-call | tf_op jit(solution)/shard_map/pallas_call | solution.py:380
  72.3 1.4 %fusion.5 = f32[512,256]{0,1:T(8,128)S(1)} fusion(f32[512,128]{1,0:T(8,128)} %shard_map.126, s32[256]{0:T(256)S(1)} %eq.61), kind=kOutput, calls=%fused_computation.11 | convolution fusion | flops 201359360 | bytes 787456 | tf_op jit(solution)/shard_map/dot_general | solution.py:438
  74.0 24.8 %all_to_all.18 = f32[512,128,2]{0,2,1:T(2,128)S(1)} all-to-all(f32[512,128,2]{0,2,1:T(2,128)S(1)} %all_to_all.14), channel_id=1, replica_groups=mesh['flow'=32,'grp'=4] {'flow','grp'}, dimensions={1} | all-to-all | bytes 1048576 | tf_op jit(solution)/shard_map/all_to_all | solution.py:439
  99.4 0.6 fusion
  100.0 0.9 copy.36
  (58 shorter events, 5.0 us)
Async XLA Ops:
  1.6 13.7 %copy-start = (f32[3,8,32,256]{3,2,1,0:T(8,128)S(1)}, f32[3,8,32,256]{3,2,1,0:T(8,128)}, u32[]{:S(2)}) copy-start(f32[3,8,32,256]{3,2,1,0:T(8,128)} %refs_0_.1) | copy-start | bytes 2359300
  1.7 13.7 %copy-start.1 = (f32[8,32,256]{2,1,0:T(8,128)S(1)}, f32[8,32,256]{2,1,0:T(8,128)}, u32[]{:S(2)}) copy-start(f32[8,32,256]{2,1,0:T(8,128)} %refs_1_.3) | copy-start | bytes 786436
  3.9 16.1 %copy-start.17 = (s32[1,128,2]{1,2,0:T(2,128)S(1)}, s32[1,128,2]{1,2,0:T(2,128)}, u32[]{:S(2)}) copy-start(s32[1,128,2]{1,2,0:T(2,128)} %param.15) | copy-start | bytes 3076
  3.9 25.9 %all-to-all-start = ((f32[512,128,2]{0,2,1:T(2,128)}), f32[512,128,2]{0,2,1:T(2,128)S(1)}, u32[]{:S(2)}, u32[]{:S(2)}) async-start(f32[512,128,2]{0,2,1:T(2,128)} %copy.31), calls=%async_computation | async-start | bytes 1048576 | tf_op jit(solution)/shard_map/all_to_all | solution.py:422
  15.4 9.0 %collective-permute-start.1 = (f32[4,32,256]{2,1,0:T(8,128)S(1)}, f32[4,32,256]{2,1,0:T(8,128)S(1)}, u32[]{:S(2)}, u32[]{:S(2)}) collective-permute-start(f32[4,32,256]{2,1,0:T(8,128)S(1)} %get-tuple-element.34), channel_id=1, source_target_pairs={{4,0},{8,4},{12,8},{16,12},{20,16},{24,20},{28,24},{32,28},{36,32}... | collective-permute-start | bytes 393224 | tf_op jit(solution)/shard_map/ppermute | solution.py:225
  16.6 7.9 %collective-permute-start = (f32[4,32,256]{2,1,0:T(8,128)S(1)}, f32[4,32,256]{2,1,0:T(8,128)S(1)}, u32[]{:S(2)}, u32[]{:S(2)}) collective-permute-start(f32[4,32,256]{2,1,0:T(8,128)S(1)} %get-tuple-element.35), channel_id=1, source_target_pairs={{0,4},{4,8},{8,12},{12,16},{16,20},{20,24},{24,28},{28,32},{32,36}... | collective-permute-start | bytes 393224 | tf_op jit(solution)/shard_map/ppermute | solution.py:224
  17.4 5.8 %collective-permute-start.3 = (f32[4,8,1,256]{3,2,1,0:T(1,128)S(1)}, f32[4,8,1,256]{3,2,1,0:T(1,128)S(1)}, u32[]{:S(2)}, u32[]{:S(2)}) collective-permute-start(f32[4,8,1,256]{3,2,1,0:T(1,128)S(1)} %get-tuple-element.32), channel_id=1, source_target_pairs={{1,0},{2,1},{3,2},{0,3},{5,4},{6,5},{7,6},{4,7},{9,8},{10,9},{11,1... | collective-permute-start | bytes 98312 | tf_op jit(solution)/shard_map/ppermute | solution.py:227
  19.9 4.5 %collective-permute-start.2 = (f32[4,8,1,256]{3,2,1,0:T(1,128)S(1)}, f32[4,8,1,256]{3,2,1,0:T(1,128)S(1)}, u32[]{:S(2)}, u32[]{:S(2)}) collective-permute-start(f32[4,8,1,256]{3,2,1,0:T(1,128)S(1)} %get-tuple-element.33), channel_id=1, source_target_pairs={{0,1},{1,2},{2,3},{3,0},{4,5},{5,6},{6,7},{7,4},{8,9},{9,10},{10,1... | collective-permute-start | bytes 98312 | tf_op jit(solution)/shard_map/ppermute | solution.py:226
  23.2 1.3 %copy-start.8 = (f32[4,8,1,256]{3,2,1,0:T(1,128)}, f32[4,8,1,256]{3,2,1,0:T(1,128)S(1)}, u32[]{:S(2)}) copy-start(f32[4,8,1,256]{3,2,1,0:T(1,128)S(1)} %collective-permute-done.3.refs_5_.refs_9_) | copy-start | bytes 98308
  24.4 0.6 copy-start.9
  24.4 0.7 copy-start.2
  25.1 0.7 copy-start.3
  31.5 17.6 %copy-start.10 = (bf16[256,256]{1,0:T(8,128)(2,1)S(1)}, bf16[256,256]{1,0:T(8,128)(2,1)}, u32[]{:S(2)}) copy-start(bf16[256,256]{1,0:T(8,128)(2,1)} %constant.21.clone) | copy-start | bytes 393220
  33.5 10.0 %collective-permute-start.4 = (f32[296,128]{1,0:T(8,128)}, f32[296,128]{1,0:T(8,128)S(1)}, u32[]{:S(2)}, u32[]{:S(2)}) collective-permute-start(f32[296,128]{1,0:T(8,128)} %get-tuple-element.13), channel_id=1, source_target_pairs={{0,4},{4,8},{8,12},{12,16},{16,20},{20,24},{24,28},{28,32},{32,36}... | collective-permute-start | bytes 454664 | tf_op jit(solution)/shard_map/ppermute | solution.py:402
  35.4 8.1 %collective-permute-start.5 = (f32[296,128]{1,0:T(8,128)}, f32[296,128]{1,0:T(8,128)S(1)}, u32[]{:S(2)}, u32[]{:S(2)}) collective-permute-start(f32[296,128]{1,0:T(8,128)} %get-tuple-element.14), channel_id=1, source_target_pairs={{4,0},{8,4},{12,8},{16,12},{20,16},{24,20},{28,24},{32,28},{36,32}... | collective-permute-start | bytes 454664 | tf_op jit(solution)/shard_map/ppermute | solution.py:403
  38.9 4.7 %collective-permute-start.6 = (f32[152,128]{1,0:T(8,128)}, f32[152,128]{1,0:T(8,128)S(1)}, u32[]{:S(2)}, u32[]{:S(2)}) collective-permute-start(f32[152,128]{1,0:T(8,128)} %get-tuple-element.15), channel_id=1, source_target_pairs={{0,1},{1,2},{2,3},{3,0},{4,5},{5,6},{6,7},{7,4},{8,9},{9,10},{10,1... | collective-permute-start | bytes 233480 | tf_op jit(solution)/shard_map/ppermute | solution.py:404
  39.2 4.3 %collective-permute-start.7 = (f32[152,128]{1,0:T(8,128)}, f32[152,128]{1,0:T(8,128)S(1)}, u32[]{:S(2)}, u32[]{:S(2)}) collective-permute-start(f32[152,128]{1,0:T(8,128)} %get-tuple-element.16), channel_id=1, source_target_pairs={{1,0},{2,1},{3,2},{0,3},{5,4},{6,5},{7,6},{4,7},{9,8},{10,9},{11,1... | collective-permute-start | bytes 233480 | tf_op jit(solution)/shard_map/ppermute | solution.py:405
  43.5 0.6 copy-start.6
  43.6 0.7 copy-start.7
  43.6 0.7 copy-start.4
  44.3 0.7 copy-start.5
  53.0 1.1 %copy-start.11 = (bf16[125,512]{1,0:T(8,128)(2,1)S(1)}, bf16[125,512]{1,0:T(8,128)(2,1)}, u32[]{:S(2)}) copy-start(bf16[125,512]{1,0:T(8,128)(2,1)} %param.13) | copy-start | bytes 384004
  58.0 10.9 %collective-permute-start.8 = (f32[104,128]{1,0:T(8,128)}, f32[104,128]{1,0:T(8,128)S(1)}, u32[]{:S(2)}, u32[]{:S(2)}) collective-permute-start(f32[104,128]{1,0:T(8,128)} %get-tuple-element.20), channel_id=1, source_target_pairs={{0,4},{4,8},{8,12},{12,16},{16,20},{20,24},{24,28},{28,32},{32,36}... | collective-permute-start | bytes 159752 | tf_op jit(solution)/shard_map/ppermute | solution.py:402
  58.0 11.0 %collective-permute-start.9 = (f32[104,128]{1,0:T(8,128)}, f32[104,128]{1,0:T(8,128)S(1)}, u32[]{:S(2)}, u32[]{:S(2)}) collective-permute-start(f32[104,128]{1,0:T(8,128)} %get-tuple-element.21), channel_id=1, source_target_pairs={{4,0},{8,4},{12,8},{16,12},{20,16},{24,20},{28,24},{32,28},{36,32}... | collective-permute-start | bytes 159752 | tf_op jit(solution)/shard_map/ppermute | solution.py:403
  64.3 4.7 %collective-permute-start.10 = (f32[104,32]{1,0:T(8,128)}, f32[104,32]{1,0:T(8,128)S(1)}, u32[]{:S(2)}, u32[]{:S(2)}) collective-permute-start(f32[104,32]{1,0:T(8,128)} %get-tuple-element.22), channel_id=1, source_target_pairs={{0,1},{1,2},{2,3},{3,0},{4,5},{5,6},{6,7},{7,4},{8,9},{9,10},{10,1... | collective-permute-start | bytes 39944 | tf_op jit(solution)/shard_map/ppermute | solution.py:404
  64.5 4.4 %collective-permute-start.11 = (f32[104,32]{1,0:T(8,128)}, f32[104,32]{1,0:T(8,128)S(1)}, u32[]{:S(2)}, u32[]{:S(2)}) collective-permute-start(f32[104,32]{1,0:T(8,128)} %get-tuple-element.23), channel_id=1, source_target_pairs={{1,0},{2,1},{3,2},{0,3},{5,4},{6,5},{7,6},{4,7},{9,8},{10,9},{11,1... | collective-permute-start | bytes 39944 | tf_op jit(solution)/shard_map/ppermute | solution.py:405
  68.9 0.6 copy-start.14
  68.9 0.6 copy-start.15
  68.9 0.6 copy-start.12
  69.0 0.6 copy-start.13
  73.7 25.7 %copy-start.16 = (s32[1,128]{1,0:T(1,128)S(1)}, s32[1,128]{1,0:T(1,128)}, u32[]{:S(2)}) copy-start(s32[1,128]{1,0:T(1,128)} %param.16) | copy-start | bytes 1540

commit v13 on v11

--- a/solution.py
+++ b/solution.py
@@ -109,7 +109,7 @@
     row = lax.broadcasted_iota(jnp.int32, (size_y, size_z), 0)
     lane = lax.broadcasted_iota(jnp.int32, (size_y, size_z), 1)
     if mode == 0:
-        sx0_ref, sx4_ref, sy0_ref, sy4_ref, out_ref, mxup_ref, mxdn_ref, myup_ref, mydn_ref = rest
+        state_ref, out_ref, mxup_ref, mxdn_ref, myup_ref, mydn_ref, face_ref = rest
 
         def xlo(c):
             return jnp.where(at_lo_f, 0.0, vxlo_ref[c])
@@ -208,23 +208,26 @@
                     mydn_ref[pl.ds(at, 1), :] = out_ref[c, x, pl.ds(0, 1), pl.ds(h * half, half)]
         xrows = 3 * 2 * size_y
         yrows = 3 * 2 * size_x
-        mxup_ref[pl.ds(xrows, FACE_ROWS), :] = sx4_ref[...]
-        mxdn_ref[pl.ds(xrows, FACE_ROWS), :] = sx0_ref[...]
-        zeros = jnp.zeros((FACE_ROWS, half), jnp.float32)
-        myup_ref[pl.ds(yrows, FACE_ROWS), :] = zeros
-        mydn_ref[pl.ds(yrows, FACE_ROWS), :] = zeros
-        myup_ref[pl.ds(yrows, FACE_ROWS), pl.ds(0, sy4_ref.shape[1])] = sy4_ref[...]
-        mydn_ref[pl.ds(yrows, FACE_ROWS), pl.ds(0, sy0_ref.shape[1])] = sy0_ref[...]
-
-
-def les_section_first(vel, nu, joint, faces):
+        elems = state_ref.shape[1]
+        row_len = size_z // 8
+        face_ref[...] = jnp.zeros(face_ref.shape, jnp.float32)
+        extract_faces(state_ref, face_ref)
+        mxup_ref[pl.ds(xrows, FACE_ROWS), :] = face_ref[1]
+        mxdn_ref[pl.ds(xrows, FACE_ROWS), :] = face_ref[0]
+        lane = lax.broadcasted_iota(jnp.int32, (FACE_ROWS, elems), 1)
+        myup_ref[pl.ds(yrows, FACE_ROWS), :] = jnp.where(lane < row_len, pltpu.roll(face_ref[3], row_len, 1), 0.0)
+        mydn_ref[pl.ds(yrows, FACE_ROWS), :] = jnp.where(lane < row_len, face_ref[2], 0.0)
+
+
+def les_section_first(vel, nu, joint, state):
     size_x, size_y, size_z = vel.shape[1], vel.shape[2], vel.shape[3]
     xbuf = jax.ShapeDtypeStruct((3 * 2 * size_y + FACE_ROWS, size_z // 2), jnp.float32)
     ybuf = jax.ShapeDtypeStruct((3 * 2 * size_x + FACE_ROWS, size_z // 2), jnp.float32)
     return pl.pallas_call(
         lambda *refs: les_kernel(0, lax.axis_size("flow"), lax.axis_size("grp"), *refs),
         out_shape=(jax.ShapeDtypeStruct(vel.shape, jnp.float32), xbuf, xbuf, ybuf, ybuf),
-    )(vel, nu, *joint, *joint, *faces)
+        scratch_shapes=[pltpu.VMEM((6, FACE_ROWS, state.shape[1]), jnp.float32)],
+    )(vel, nu, *joint, *joint, state)
 
 
 def les_section_last(vel, nu, merged, joint):
@@ -246,6 +249,25 @@
     xhi = lax.ppermute(lax.index_in_dim(field, 0, lead, keepdims=False), "flow", down_f)
     ylo = lax.ppermute(lax.slice_in_dim(field, size_y - 1, size_y, axis=lead + 1), "grp", up_g)
     yhi = lax.ppermute(lax.slice_in_dim(field, 0, 1, axis=lead + 1), "grp", down_g)
+    return xlo, xhi, ylo, yhi
+
+
+def halos_joint(vel, nu):
+    flow_n = lax.axis_size("flow")
+    grp_n = lax.axis_size("grp")
+    up_f = [(i, (i + 1) % flow_n) for i in range(flow_n)]
+    down_f = [((i + 1) % flow_n, i) for i in range(flow_n)]
+    up_g = [(i, (i + 1) % grp_n) for i in range(grp_n)]
+    down_g = [((i + 1) % grp_n, i) for i in range(grp_n)]
+    size_x, size_y = nu.shape[0], nu.shape[1]
+
+    def joined(vel_part, nu_part):
+        return jnp.concatenate([vel_part, nu_part[None]], axis=0)
+
+    xlo = lax.ppermute(joined(vel[:, size_x - 1], nu[size_x - 1]), "flow", up_f)
+    xhi = lax.ppermute(joined(vel[:, 0], nu[0]), "flow", down_f)
+    ylo = lax.ppermute(joined(vel[:, :, size_y - 1:], nu[:, size_y - 1:]), "grp", up_g)
+    yhi = lax.ppermute(joined(vel[:, :, :1], nu[:, :1]), "grp", down_g)
     return xlo, xhi, ylo, yhi
 
 
@@ -407,7 +429,7 @@
 
 
 def body(velocity, eddy_visc, projection, acoustic_state, route_send, route_place):
-    joint = halos(jnp.concatenate([velocity, eddy_visc[None]], axis=0), 1)
+    joint = halos_joint(velocity, eddy_visc)
     flow_size = lax.axis_size("flow")
     grp_size = lax.axis_size("grp")
     slot_cap = route_send.shape[2]
@@ -424,8 +446,7 @@
 
     row_len = velocity.shape[3] // 8
     mats = [jnp.asarray(m) for m in dg_matrices()]
-    sent = dg_faces(state, row_len)
-    vel, mxup, mxdn, myup, mydn = les_section_first(velocity, eddy_visc, joint, sent)
+    vel, mxup, mxdn, myup, mydn = les_section_first(velocity, eddy_visc, joint, state)
     merged = exchange_faces((mxdn, mxup, mydn, myup))
     vel, lamb = les_section_last(vel, eddy_visc, merged, joint)
     source = project(lamb, projection)
@@ -437,8 +458,8 @@
     state = dg_step(state, source, recv, mats, False, row_len)[0]
     leaving = lax.dot_general(state, home_hot, (((1,), (1,)), ((), ())), precision=HIGH)
     returned = lax.all_to_all(leaving, ("flow", "grp"), split_axis=1, concat_axis=1, tiled=True)
-    acoustic_out = lax.dot_general(returned, place_hot, (((1,), (1,)), ((), ())), precision=HIGH)
-    acoustic_out = acoustic_out.reshape(4, 128, elem_count)[:, :125]
+    returned = returned.reshape(4, 128, total_slots)[:, :acoustic_state.shape[1]]
+    acoustic_out = lax.dot_general(returned, place_hot, (((2,), (1,)), ((), ())), precision=HIGH)
     return (vel, acoustic_out)
 
 

time: 100 us -> 103 us (1.030)
  local copies, waits for them, and re-layouts: 10.1 us -> 14.3 us
  Pallas kernels: 15.7 us -> 14.2 us
    slice x0 -> x2, local copies, waits for them, and re-layouts: none -> 1.84 us  [the longest x1 1.06 us: halos_joint(): yhi = lax.ppermute(joined(vel[:, :, :1], nu[:, :1]), 'grp', down_g)]
    pallas_call x1 -> x0, Pallas kernels: 1.68 us -> none  [dg_faces(): pl.pallas_call(dg_faces_kernel, out_shape=tuple(face_shapes(elems, row_le...]
    all_to_all x1, starting transfers between devices: 11.5 us -> 10.2 us  [body(): lax.all_to_all(outgoing, ('flow', 'grp'), split_axis=1, concat_axis=1, ti...]
    unnamed x39 -> x35, local copies, waits for them, and re-layouts: 4.09 us -> 4.57 us
  transfers between devices with their start and end apart: 13 -> 13, of which waited for: 3 -> 4; matrix products, arithmetic and copies ran while one was open for 2% -> 6% of each run, Pallas kernels for 2% -> 0%
where the time goes in v13:
time: 103 us
  starting transfers between devices  27.6 us (27%)
  blocking collectives  24.8 us (24%)
  local copies, waits for them, and re-layouts  14.3 us (14%)
  Pallas kernels  14.2 us (14%)
  waiting for transfers between devices  14.1 us (14%)
  matrix products  6.69 us (6%)
    all_to_all x1, blocking collectives, body(): lax.all_to_all(leaving, ('flow', 'grp'), split_axis=1, concat_axis=1, til...  24.8 us
    all_to_all x1, starting transfers between devices, body(): lax.all_to_all(outgoing, ('flow', 'grp'), split_axis=1, concat_axis=1, ti...  10.2 us
    all_to_all x1, waiting for transfers between devices, body(): lax.all_to_all(outgoing, ('flow', 'grp'), split_axis=1, concat_axis=1, ti...  10.2 us
    pallas_call x2, Pallas kernels, dg_step(): pl.pallas_call(lambda *refs: dg_step_kernel(want_faces, xoff, yoff, row_l...  5.67 us
    ppermute x2, starting transfers between devices, exchange_faces(): lax.ppermute(sy0, 'grp', down_g)  5.3 us
    unnamed x35, local copies, waits for them, and re-layouts  4.57 us
    pallas_call x1, Pallas kernels, les_section_first(): pl.pallas_call(lambda *refs: les_kernel(0, lax.axis_size('flow'), lax.axi...  4.37 us
    pallas_call x1, Pallas kernels, les_section_last(): pl.pallas_call(lambda *refs: les_kernel(1, lax.axis_size('flow'), lax.axi...  4.13 us
  transfers between devices with their start and end apart: 13, of which 4 were waited for; matrix products, arithmetic and copies ran while one was open for 6% of the time, Pallas kernels for 0%

profile of v13, /device:TPU:1, one launch (start us, length us, event | category | flops | bytes accessed | tf_op | source)
XLA Modules:
  0.0 102.7 jit_solution(6828714821109382546)
XLA Ops:
  0.6 0.9 slice_bitcast_fusion.2
  1.5 1.1 %fusion.17 = (f32[3,8,1,256]{3,2,1,0:T(1,128)S(1)}, f32[3,8,1,256]{3,2,1,0:T(1,128)S(1)}) fusion(f32[3,8,32,256]{3,2,1,0:T(8,128)} %refs_0_.1), kind=kLoop, calls=%fused_computation.29 | loop fusion | bytes 98304 | tf_op jit(solution)/shard_map/slice | solution.py:270
  2.6 2.1 %collective-permute-start.2 = (f32[4,8,1,256]{3,2,1,0:T(1,128)S(1)}, f32[4,8,1,256]{3,2,1,0:T(1,128)S(1)}, u32[]{:S(2)}, u32[]{:S(2)}) collective-permute-start(f32[4,8,1,256]{3,2,1,0:T(1,128)S(1)} %pad_maximum_fusion.2), channel_id=1, source_target_pairs={{0,1},{1,2},{2,3},{3,0},{4,5},{5,6},{6,7},{7,4},{8,9},{9,10},{10,1... | collective-permute-start | bytes 98312 | tf_op jit(solution)/shard_map/ppermute | solution.py:269
  4.8 1.4 %collective-permute-start.3 = (f32[4,8,1,256]{3,2,1,0:T(1,128)S(1)}, f32[4,8,1,256]{3,2,1,0:T(1,128)S(1)}, u32[]{:S(2)}, u32[]{:S(2)}) collective-permute-start(f32[4,8,1,256]{3,2,1,0:T(1,128)S(1)} %pad_maximum_fusion.3), channel_id=1, source_target_pairs={{1,0},{2,1},{3,2},{0,3},{5,4},{6,5},{7,6},{4,7},{9,8},{10,9},{11,1... | collective-permute-start | bytes 98312 | tf_op jit(solution)/shard_map/ppermute | solution.py:270
  6.1 1.0 copy.48
  7.1 1.1 %fusion.9 = f32[512,128,2]{1,0,2:T(8,128)S(1)} fusion(f32[512,128,1]{1,0,2:T(8,128)S(1)} %bitcast.52, s32[128,2]{0,1:T(2,128)S(1)} %multiply_add_fusion, s32[128]{0:T(128)} %bitcast.54), kind=kOutput, calls=%fused_computation.14 | convolution fusion | flops 201359360 | bytes 787968 | tf_op jit(solution)/shard_map/dot_general | solution.py:443
  8.3 1.0 copy.39
  9.2 10.2 %all-to-all-start = ((f32[512,128,2]{0,2,1:T(2,128)}), f32[512,128,2]{0,2,1:T(2,128)S(1)}, u32[]{:S(2)}, u32[]{:S(2)}) async-start(f32[512,128,2]{0,2,1:T(2,128)} %copy.39), calls=%async_computation | async-start | bytes 1048576 | tf_op jit(solution)/shard_map/all_to_all | solution.py:444
  19.5 0.8 fusion.18
  20.2 1.0 slice_bitcast_fusion
  21.2 1.8 %collective-permute-start = (f32[4,32,256]{2,1,0:T(8,128)S(1)}, f32[4,32,256]{2,1,0:T(8,128)S(1)}, u32[]{:S(2)}, u32[]{:S(2)}) collective-permute-start(f32[4,32,256]{2,1,0:T(8,128)S(1)} %pad_maximum_fusion), channel_id=1, source_target_pairs={{0,4},{4,8},{8,12},{12,16},{16,20},{20,24},{24,28},{28,32},{32,36}... | collective-permute-start | bytes 393224 | tf_op jit(solution)/shard_map/ppermute | solution.py:267
  23.4 10.2 %all-to-all-done = f32[512,128,2]{0,2,1:T(2,128)S(1)} async-done(((f32[512,128,2]{0,2,1:T(2,128)}), f32[512,128,2]{0,2,1:T(2,128)S(1)}, u32[]{:S(2)}, u32[]{:S(2)}) %all-to-all-start) | async-done | bytes 524320 | tf_op jit(solution)/shard_map/all_to_all | solution.py:444
  34.0 1.4 %fusion.6.refs_10_.refs_0_ = f32[512,128]{1,0:T(8,128)} fusion(f32[512,256]{0,1:T(8,128)S(1)} %all_to_all.13, s32[256]{0:T(256)S(1)} %eq.61), kind=kOutput, calls=%fused_computation.12 | convolution fusion | flops 201359360 | bytes 787456 | tf_op jit(solution)/shard_map/dot_general | solution.py:445
  36.0 0.7 copy-done.1
  36.7 4.4 %shard_map.122 = (f32[3,8,32,256]{3,2,1,0:T(8,128)}, f32[296,128]{1,0:T(8,128)}, f32[296,128]{1,0:T(8,128)}, f32[152,128]{1,0:T(8,128)}, f32[152,128]{1,0:T(8,128)}) custom-call(f32[3,8,32,256]{3,2,1,0:T(8,128)} %refs_0_.1, f32[8,32,256]{2,1,0:T(8,128)} %refs_1_.3, f32[4,32,256]{2,1,0:T(8,128)} %copy-done, f32[4,32,256]{2,1,0:T(8,128)} %copy-done.1, ...), custom_call_target="tpu_custom_call" | custom-call | tf_op jit(solution)/shard_map/pallas_call | solution.py:226
  41.0 0.7 collective-permute-start.4
  42.0 2.4 %collective-permute-start.7 = (f32[152,128]{1,0:T(8,128)}, f32[152,128]{1,0:T(8,128)S(1)}, u32[]{:S(2)}, u32[]{:S(2)}) collective-permute-start(f32[152,128]{1,0:T(8,128)} %get-tuple-element.18), channel_id=1, source_target_pairs={{1,0},{2,1},{3,2},{0,3},{5,4},{6,5},{7,6},{4,7},{9,8},{10,9},{11,1... | collective-permute-start | bytes 233480 | tf_op jit(solution)/shard_map/ppermute | solution.py:427
  44.4 2.0 %collective-permute-done.6.refs_4_ = f32[152,128]{1,0:T(8,128)S(1)} collective-permute-done((f32[152,128]{1,0:T(8,128)}, f32[152,128]{1,0:T(8,128)S(1)}, u32[]{:S(2)}, u32[]{:S(2)}) %collective-permute-start.6) | collective-permute-done | bytes 77856 | tf_op jit(solution)/shard_map/ppermute | solution.py:426
  47.2 4.1 %shard_map.123 = (f32[3,8,32,256]{3,2,1,0:T(8,128)}, bf16[3,8,32,256]{3,2,1,0:T(8,128)(2,1)}) custom-call(f32[3,8,32,256]{3,2,1,0:T(8,128)} %get-tuple-element.14.refs_0_, f32[8,32,256]{2,1,0:T(8,128)} %refs_1_.3, f32[296,128]{1,0:T(8,128)} %copy-done.2, f32[296,128]{1,0:T(8,128)} %copy-done.3, f32[152,128]{1,0:T(8,128)} %copy-done.4, f32[152,128]{1,0:T(8,128)} %copy-done.5, ...), custom_call_target="tpu_custom_call" | custom-call | tf_op jit(solution)/shard_map/pallas_call | solution.py:234
  51.3 1.2 %convolution_convert_fusion = bf16[768,256]{1,0:T(8,128)(2,1)S(1)} fusion(bf16[768,256]{1,0:T(8,128)(2,1)} %bitcast.53, bf16[256,256]{1,0:T(8,128)(2,1)S(1)} %copy-done.8), kind=kOutput, calls=%fused_computation.1 | convolution fusion | flops 100859904 | bytes 917504 | tf_op jit(solution)/shard_map/dot_general | solution.py:282
  53.2 2.0 %copy.52 = bf16[3,1,8,4,8,8,32]{6,3,0,5,4,2,1:T(4,128)(2,1)S(1)} copy(bf16[3,1,8,4,8,8,32]{6,5,4,3,2,0,1:T(8,128)(2,1)S(1)} %reshape.51) | data formatting | bytes 786432 | tf_op jit(solution)/shard_map/reshape | solution.py:284
  55.3 0.9 reshape.52
  56.3 1.0 fusion.2
  57.3 3.0 %shard_map.124 = (f32[512,128]{1,0:T(8,128)}, f32[104,128]{1,0:T(8,128)}, f32[104,128]{1,0:T(8,128)}, f32[104,32]{1,0:T(8,128)}, f32[104,32]{1,0:T(8,128)}) custom-call(f32[512,128]{1,0:T(8,128)} %fusion.6.refs_10_.refs_0_, f32[384,128]{1,0:T(8,128)} %bitcast.48, f32[296,128]{1,0:T(8,128)} %copy-done.2, f32[296,128]{1,0:T(8,128)} %copy-done.3, ...), custom_call_target="tpu_custom_call" | custom-call | tf_op jit(solution)/shard_map/pallas_call | solution.py:402
  60.3 2.9 %collective-permute-start.8 = (f32[104,128]{1,0:T(8,128)}, f32[104,128]{1,0:T(8,128)S(1)}, u32[]{:S(2)}, u32[]{:S(2)}) collective-permute-start(f32[104,128]{1,0:T(8,128)} %get-tuple-element.22), channel_id=1, source_target_pairs={{0,4},{4,8},{8,12},{12,16},{16,20},{20,24},{24,28},{28,32},{32,36}... | collective-permute-start | bytes 159752 | tf_op jit(solution)/shard_map/ppermute | solution.py:424
  63.1 2.9 %collective-permute-start.9 = (f32[104,128]{1,0:T(8,128)}, f32[104,128]{1,0:T(8,128)S(1)}, u32[]{:S(2)}, u32[]{:S(2)}) collective-permute-start(f32[104,128]{1,0:T(8,128)} %get-tuple-element.23), channel_id=1, source_target_pairs={{4,0},{8,4},{12,8},{16,12},{20,16},{24,20},{28,24},{32,28},{36,32}... | collective-permute-start | bytes 159752 | tf_op jit(solution)/shard_map/ppermute | solution.py:425
  66.1 2.9 %collective-permute-start.11 = (f32[104,32]{1,0:T(8,128)}, f32[104,32]{1,0:T(8,128)S(1)}, u32[]{:S(2)}, u32[]{:S(2)}) collective-permute-start(f32[104,32]{1,0:T(8,128)} %get-tuple-element.25), channel_id=1, source_target_pairs={{1,0},{2,1},{3,2},{0,3},{5,4},{6,5},{7,6},{4,7},{9,8},{10,9},{11,1... | collective-permute-start | bytes 39944 | tf_op jit(solution)/shard_map/ppermute | solution.py:427
  69.0 1.7 %collective-permute-done.10.refs_4_ = f32[104,32]{1,0:T(8,128)S(1)} collective-permute-done((f32[104,32]{1,0:T(8,128)}, f32[104,32]{1,0:T(8,128)S(1)}, u32[]{:S(2)}, u32[]{:S(2)}) %collective-permute-start.10) | collective-permute-done | bytes 13344 | tf_op jit(solution)/shard_map/ppermute | solution.py:426
  71.4 2.7 %shard_map.125 = f32[512,128]{1,0:T(8,128)} custom-call(f32[512,128]{1,0:T(8,128)} %get-tuple-element.21.refs_0_, f32[384,128]{1,0:T(8,128)} %bitcast.49, f32[104,128]{1,0:T(8,128)} %copy-done.10, f32[104,128]{1,0:T(8,128)} %copy-done.11, f32[104,32]{1,0:T(8,128)} %copy-done.12, f32[104,32]{1,0:T(8,128)} %copy-done.13, f32[128,384]{1,0:T(8,128)} %constant.17.clone.refs_6_, ...), custom_call_target="tpu_custom_call" | custom-call | tf_op jit(solution)/shard_map/pallas_call | solution.py:402
  74.1 1.4 %fusion.5 = f32[512,256]{0,1:T(8,128)S(1)} fusion(f32[512,128]{1,0:T(8,128)} %shard_map.125, s32[256]{0:T(256)S(1)} %eq.61), kind=kOutput, calls=%fused_computation.11 | convolution fusion | flops 201359360 | bytes 787456 | tf_op jit(solution)/shard_map/dot_general | solution.py:459
  75.8 24.8 %all_to_all.18 = f32[512,128,2]{0,2,1:T(2,128)S(1)} all-to-all(f32[512,128,2]{0,2,1:T(2,128)S(1)} %all_to_all.14), channel_id=1, replica_groups=mesh['flow'=32,'grp'=4] {'flow','grp'}, dimensions={1} | all-to-all | bytes 1048576 | tf_op jit(solution)/shard_map/all_to_all | solution.py:460
  101.8 0.9 copy.44
  (59 shorter events, 5.5 us)
Async XLA Ops:
  2.6 32.7 %collective-permute-start.2 = (f32[4,8,1,256]{3,2,1,0:T(1,128)S(1)}, f32[4,8,1,256]{3,2,1,0:T(1,128)S(1)}, u32[]{:S(2)}, u32[]{:S(2)}) collective-permute-start(f32[4,8,1,256]{3,2,1,0:T(1,128)S(1)} %pad_maximum_fusion.2), channel_id=1, source_target_pairs={{0,1},{1,2},{2,3},{3,0},{4,5},{5,6},{6,7},{7,4},{8,9},{9,10},{10,1... | collective-permute-start | bytes 98312 | tf_op jit(solution)/shard_map/ppermute | solution.py:269
  4.8 30.6 %collective-permute-start.3 = (f32[4,8,1,256]{3,2,1,0:T(1,128)S(1)}, f32[4,8,1,256]{3,2,1,0:T(1,128)S(1)}, u32[]{:S(2)}, u32[]{:S(2)}) collective-permute-start(f32[4,8,1,256]{3,2,1,0:T(1,128)S(1)} %pad_maximum_fusion.3), channel_id=1, source_target_pairs={{1,0},{2,1},{3,2},{0,3},{5,4},{6,5},{7,6},{4,7},{9,8},{10,9},{11,1... | collective-permute-start | bytes 98312 | tf_op jit(solution)/shard_map/ppermute | solution.py:270
  8.2 14.9 %copy-start.15 = (s32[1,128,2]{1,2,0:T(2,128)S(1)}, s32[1,128,2]{1,2,0:T(2,128)}, u32[]{:S(2)}) copy-start(s32[1,128,2]{1,2,0:T(2,128)} %param.15) | copy-start | bytes 3076
  9.2 24.3 %all-to-all-start = ((f32[512,128,2]{0,2,1:T(2,128)}), f32[512,128,2]{0,2,1:T(2,128)S(1)}, u32[]{:S(2)}, u32[]{:S(2)}) async-start(f32[512,128,2]{0,2,1:T(2,128)} %copy.39), calls=%async_computation | async-start | bytes 1048576 | tf_op jit(solution)/shard_map/all_to_all | solution.py:444
  21.2 14.1 %collective-permute-start = (f32[4,32,256]{2,1,0:T(8,128)S(1)}, f32[4,32,256]{2,1,0:T(8,128)S(1)}, u32[]{:S(2)}, u32[]{:S(2)}) collective-permute-start(f32[4,32,256]{2,1,0:T(8,128)S(1)} %pad_maximum_fusion), channel_id=1, source_target_pairs={{0,4},{4,8},{8,12},{12,16},{16,20},{20,24},{24,28},{28,32},{32,36}... | collective-permute-start | bytes 393224 | tf_op jit(solution)/shard_map/ppermute | solution.py:267
  23.0 12.3 %collective-permute-start.1 = (f32[4,32,256]{2,1,0:T(8,128)S(1)}, f32[4,32,256]{2,1,0:T(8,128)S(1)}, u32[]{:S(2)}, u32[]{:S(2)}) collective-permute-start(f32[4,32,256]{2,1,0:T(8,128)S(1)} %pad_maximum_fusion.1), channel_id=1, source_target_pairs={{4,0},{8,4},{12,8},{16,12},{20,16},{24,20},{28,24},{32,28},{36,32}... | collective-permute-start | bytes 393224 | tf_op jit(solution)/shard_map/ppermute | solution.py:268
  35.3 16.0 %copy-start.8 = (bf16[256,256]{1,0:T(8,128)(2,1)S(1)}, bf16[256,256]{1,0:T(8,128)(2,1)}, u32[]{:S(2)}) copy-start(bf16[256,256]{1,0:T(8,128)(2,1)} %constant.21.clone) | copy-start | bytes 393220
  35.3 0.6 copy-start.6
  35.3 0.6 copy-start.7
  35.4 0.7 copy-start
  36.0 0.7 copy-start.1
  41.0 5.4 %collective-permute-start.4 = (f32[296,128]{1,0:T(8,128)}, f32[296,128]{1,0:T(8,128)S(1)}, u32[]{:S(2)}, u32[]{:S(2)}) collective-permute-start(f32[296,128]{1,0:T(8,128)} %get-tuple-element.15), channel_id=1, source_target_pairs={{0,4},{4,8},{8,12},{12,16},{16,20},{20,24},{24,28},{28,32},{32,36}... | collective-permute-start | bytes 454664 | tf_op jit(solution)/shard_map/ppermute | solution.py:424
  41.7 4.8 %collective-permute-start.5 = (f32[296,128]{1,0:T(8,128)}, f32[296,128]{1,0:T(8,128)S(1)}, u32[]{:S(2)}, u32[]{:S(2)}) collective-permute-start(f32[296,128]{1,0:T(8,128)} %get-tuple-element.16), channel_id=1, source_target_pairs={{4,0},{8,4},{12,8},{16,12},{20,16},{24,20},{28,24},{32,28},{36,32}... | collective-permute-start | bytes 454664 | tf_op jit(solution)/shard_map/ppermute | solution.py:425
  41.7 4.7 %collective-permute-start.6 = (f32[152,128]{1,0:T(8,128)}, f32[152,128]{1,0:T(8,128)S(1)}, u32[]{:S(2)}, u32[]{:S(2)}) collective-permute-start(f32[152,128]{1,0:T(8,128)} %get-tuple-element.17), channel_id=1, source_target_pairs={{0,1},{1,2},{2,3},{3,0},{4,5},{5,6},{6,7},{7,4},{8,9},{9,10},{10,1... | collective-permute-start | bytes 233480 | tf_op jit(solution)/shard_map/ppermute | solution.py:426
  42.0 4.4 %collective-permute-start.7 = (f32[152,128]{1,0:T(8,128)}, f32[152,128]{1,0:T(8,128)S(1)}, u32[]{:S(2)}, u32[]{:S(2)}) collective-permute-start(f32[152,128]{1,0:T(8,128)} %get-tuple-element.18), channel_id=1, source_target_pairs={{1,0},{2,1},{3,2},{0,3},{5,4},{6,5},{7,6},{4,7},{9,8},{10,9},{11,1... | collective-permute-start | bytes 233480 | tf_op jit(solution)/shard_map/ppermute | solution.py:427
  46.4 0.6 copy-start.4
  46.4 0.7 copy-start.5
  46.4 0.7 copy-start.2
  46.5 0.7 copy-start.3
  55.3 1.1 %copy-start.9 = (bf16[125,512]{1,0:T(8,128)(2,1)S(1)}, bf16[125,512]{1,0:T(8,128)(2,1)}, u32[]{:S(2)}) copy-start(bf16[125,512]{1,0:T(8,128)(2,1)} %param.13) | copy-start | bytes 384004
  60.3 10.5 %collective-permute-start.8 = (f32[104,128]{1,0:T(8,128)}, f32[104,128]{1,0:T(8,128)S(1)}, u32[]{:S(2)}, u32[]{:S(2)}) collective-permute-start(f32[104,128]{1,0:T(8,128)} %get-tuple-element.22), channel_id=1, source_target_pairs={{0,4},{4,8},{8,12},{12,16},{16,20},{20,24},{24,28},{28,32},{32,36}... | collective-permute-start | bytes 159752 | tf_op jit(solution)/shard_map/ppermute | solution.py:424
  63.1 7.6 %collective-permute-start.9 = (f32[104,128]{1,0:T(8,128)}, f32[104,128]{1,0:T(8,128)S(1)}, u32[]{:S(2)}, u32[]{:S(2)}) collective-permute-start(f32[104,128]{1,0:T(8,128)} %get-tuple-element.23), channel_id=1, source_target_pairs={{4,0},{8,4},{12,8},{16,12},{20,16},{24,20},{28,24},{32,28},{36,32}... | collective-permute-start | bytes 159752 | tf_op jit(solution)/shard_map/ppermute | solution.py:425
  66.1 4.7 %collective-permute-start.10 = (f32[104,32]{1,0:T(8,128)}, f32[104,32]{1,0:T(8,128)S(1)}, u32[]{:S(2)}, u32[]{:S(2)}) collective-permute-start(f32[104,32]{1,0:T(8,128)} %get-tuple-element.24), channel_id=1, source_target_pairs={{0,1},{1,2},{2,3},{3,0},{4,5},{5,6},{6,7},{7,4},{8,9},{9,10},{10,1... | collective-permute-start | bytes 39944 | tf_op jit(solution)/shard_map/ppermute | solution.py:426
  66.1 4.7 %collective-permute-start.11 = (f32[104,32]{1,0:T(8,128)}, f32[104,32]{1,0:T(8,128)S(1)}, u32[]{:S(2)}, u32[]{:S(2)}) collective-permute-start(f32[104,32]{1,0:T(8,128)} %get-tuple-element.25), channel_id=1, source_target_pairs={{1,0},{2,1},{3,2},{0,3},{5,4},{6,5},{7,6},{4,7},{9,8},{10,9},{11,1... | collective-permute-start | bytes 39944 | tf_op jit(solution)/shard_map/ppermute | solution.py:427
  70.7 0.6 copy-start.12
  70.7 0.6 copy-start.13
  70.7 0.6 copy-start.10
  70.8 0.6 copy-start.11
  75.5 25.7 %copy-start.14 = (s32[1,128]{1,0:T(1,128)S(1)}, s32[1,128]{1,0:T(1,128)}, u32[]{:S(2)}) copy-start(s32[1,128]{1,0:T(1,128)} %param.16) | copy-start | bytes 1540

commit v14 on v13

--- a/solution.py
+++ b/solution.py
@@ -249,25 +249,6 @@
     xhi = lax.ppermute(lax.index_in_dim(field, 0, lead, keepdims=False), "flow", down_f)
     ylo = lax.ppermute(lax.slice_in_dim(field, size_y - 1, size_y, axis=lead + 1), "grp", up_g)
     yhi = lax.ppermute(lax.slice_in_dim(field, 0, 1, axis=lead + 1), "grp", down_g)
-    return xlo, xhi, ylo, yhi
-
-
-def halos_joint(vel, nu):
-    flow_n = lax.axis_size("flow")
-    grp_n = lax.axis_size("grp")
-    up_f = [(i, (i + 1) % flow_n) for i in range(flow_n)]
-    down_f = [((i + 1) % flow_n, i) for i in range(flow_n)]
-    up_g = [(i, (i + 1) % grp_n) for i in range(grp_n)]
-    down_g = [((i + 1) % grp_n, i) for i in range(grp_n)]
-    size_x, size_y = nu.shape[0], nu.shape[1]
-
-    def joined(vel_part, nu_part):
-        return jnp.concatenate([vel_part, nu_part[None]], axis=0)
-
-    xlo = lax.ppermute(joined(vel[:, size_x - 1], nu[size_x - 1]), "flow", up_f)
-    xhi = lax.ppermute(joined(vel[:, 0], nu[0]), "flow", down_f)
-    ylo = lax.ppermute(joined(vel[:, :, size_y - 1:], nu[:, size_y - 1:]), "grp", up_g)
-    yhi = lax.ppermute(joined(vel[:, :, :1], nu[:, :1]), "grp", down_g)
     return xlo, xhi, ylo, yhi
 
 
@@ -429,7 +410,7 @@
 
 
 def body(velocity, eddy_visc, projection, acoustic_state, route_send, route_place):
-    joint = halos_joint(velocity, eddy_visc)
+    joint = halos(jnp.concatenate([velocity, eddy_visc[None]], axis=0), 1)
     flow_size = lax.axis_size("flow")
     grp_size = lax.axis_size("grp")
     slot_cap = route_send.shape[2]
@@ -458,8 +439,8 @@
     state = dg_step(state, source, recv, mats, False, row_len)[0]
     leaving = lax.dot_general(state, home_hot, (((1,), (1,)), ((), ())), precision=HIGH)
     returned = lax.all_to_all(leaving, ("flow", "grp"), split_axis=1, concat_axis=1, tiled=True)
-    returned = returned.reshape(4, 128, total_slots)[:, :acoustic_state.shape[1]]
-    acoustic_out = lax.dot_general(returned, place_hot, (((2,), (1,)), ((), ())), precision=HIGH)
+    acoustic_out = lax.dot_general(returned, place_hot, (((1,), (1,)), ((), ())), precision=HIGH)
+    acoustic_out = acoustic_out.reshape(4, 128, elem_count)[:, :125]
     return (vel, acoustic_out)
 
 

time: 103 us -> 99 us (0.961)
  local copies, waits for them, and re-layouts: 14.3 us -> 10.7 us
    slice x2 -> x0, local copies, waits for them, and re-layouts: 1.84 us -> none  [the longest x1 1.06 us: halos_joint(): yhi = lax.ppermute(joined(vel[:, :, :1], nu[:, :1]), 'grp', down_g)]
    all_to_all x1, starting transfers between devices: 10.2 us -> 11.5 us  [body(): lax.all_to_all(outgoing, ('flow', 'grp'), split_axis=1, concat_axis=1, ti...]
    unnamed x35 -> x39, local copies, waits for them, and re-layouts: 4.57 us -> 4.68 us
  transfers between devices with their start and end apart: 13 -> 13, of which waited for: 4 -> 3; matrix products, arithmetic and copies ran while one was open for 6% -> 2% of each run, Pallas kernels for 0% -> 0%
where the time goes in v14:
time: 99 us; the launch traced here: 98.6 us
  starting transfers between devices  27.9 us (28%)
  blocking collectives  24.8 us (25%)
  Pallas kernels  14.2 us (14%)
  waiting for transfers between devices  13.2 us (13%)
  local copies, waits for them, and re-layouts  10.7 us (11%)
  matrix products  6.78 us (7%)
    all_to_all x1, blocking collectives, body(): lax.all_to_all(leaving, ('flow', 'grp'), split_axis=1, concat_axis=1, til...  24.8 us
    all_to_all x1, starting transfers between devices, body(): lax.all_to_all(outgoing, ('flow', 'grp'), split_axis=1, concat_axis=1, ti...  11.5 us
    all_to_all x1, waiting for transfers between devices, body(): lax.all_to_all(outgoing, ('flow', 'grp'), split_axis=1, concat_axis=1, ti...  9.44 us
    pallas_call x2, Pallas kernels, dg_step(): pl.pallas_call(lambda *refs: dg_step_kernel(want_faces, xoff, yoff, row_l...  5.67 us
    ppermute x2, starting transfers between devices, exchange_faces(): lax.ppermute(sy0, 'grp', down_g)  4.92 us
    unnamed x39, local copies, waits for them, and re-layouts  4.68 us
    pallas_call x1, Pallas kernels, les_section_first(): pl.pallas_call(lambda *refs: les_kernel(0, lax.axis_size('flow'), lax.axi...  4.37 us
    pallas_call x1, Pallas kernels, les_section_last(): pl.pallas_call(lambda *refs: les_kernel(1, lax.axis_size('flow'), lax.axi...  4.13 us
  transfers between devices with their start and end apart: 13, of which 3 were waited for; matrix products, arithmetic and copies ran while one was open for 2% of the time, Pallas kernels for 0%

profile of v14, /device:TPU:1, one launch (start us, length us, event | category | flops | bytes accessed | tf_op | source)
XLA Modules:
  0.0 98.6 jit_solution(4716069145163826665)
XLA Ops:
  0.6 1.0 copy.37
  1.7 1.2 %fusion.9 = f32[512,128,2]{1,0,2:T(8,128)S(1)} fusion(f32[512,128,1]{1,0,2:T(8,128)S(1)} %bitcast.47, s32[128,2]{0,1:T(2,128)S(1)} %multiply_add_fusion, s32[128]{0:T(128)} %bitcast.49), kind=kOutput, calls=%fused_computation.14 | convolution fusion | flops 201359360 | bytes 787968 | tf_op jit(solution)/shard_map/dot_general | solution.py:424
  2.9 1.0 %copy.31 = f32[512,128,2]{0,2,1:T(2,128)} copy(f32[512,128,2]{1,0,2:T(8,128)S(1)} %fusion.9) | data formatting | bytes 1048576 | tf_op jit(solution)/shard_map/dot_general | solution.py:424
  3.9 11.5 %all-to-all-start = ((f32[512,128,2]{0,2,1:T(2,128)}), f32[512,128,2]{0,2,1:T(2,128)S(1)}, u32[]{:S(2)}, u32[]{:S(2)}) async-start(f32[512,128,2]{0,2,1:T(2,128)} %copy.31), calls=%async_computation | async-start | bytes 1048576 | tf_op jit(solution)/shard_map/all_to_all | solution.py:425
  15.4 2.7 %collective-permute-start.3 = (f32[4,8,1,256]{3,2,1,0:T(1,128)S(1)}, f32[4,8,1,256]{3,2,1,0:T(1,128)S(1)}, u32[]{:S(2)}, u32[]{:S(2)}) collective-permute-start(f32[4,8,1,256]{3,2,1,0:T(1,128)S(1)} %get-tuple-element.34), channel_id=1, source_target_pairs={{1,0},{2,1},{3,2},{0,3},{5,4},{6,5},{7,6},{4,7},{9,8},{10,9},{11,1... | collective-permute-start | bytes 98312 | tf_op jit(solution)/shard_map/ppermute | solution.py:251
  18.1 0.7 collective-permute-start.1
  18.8 1.3 %collective-permute-start = (f32[4,32,256]{2,1,0:T(8,128)S(1)}, f32[4,32,256]{2,1,0:T(8,128)S(1)}, u32[]{:S(2)}, u32[]{:S(2)}) collective-permute-start(f32[4,32,256]{2,1,0:T(8,128)S(1)} %get-tuple-element.37), channel_id=1, source_target_pairs={{0,4},{4,8},{8,12},{12,16},{16,20},{20,24},{24,28},{28,32},{32,36}... | collective-permute-start | bytes 393224 | tf_op jit(solution)/shard_map/ppermute | solution.py:248
  20.4 9.4 %all-to-all-done = f32[512,128,2]{0,2,1:T(2,128)S(1)} async-done(((f32[512,128,2]{0,2,1:T(2,128)}), f32[512,128,2]{0,2,1:T(2,128)S(1)}, u32[]{:S(2)}, u32[]{:S(2)}) %all-to-all-start) | async-done | bytes 524320 | tf_op jit(solution)/shard_map/all_to_all | solution.py:425
  30.2 1.4 %fusion.6.refs_10_.refs_0_ = f32[512,128]{1,0:T(8,128)} fusion(f32[512,256]{0,1:T(8,128)S(1)} %all_to_all.13, s32[256]{0:T(256)S(1)} %eq.61), kind=kOutput, calls=%fused_computation.12 | convolution fusion | flops 201359360 | bytes 787456 | tf_op jit(solution)/shard_map/dot_general | solution.py:426
  31.6 0.6 copy-done.8
  32.3 0.6 copy-done.3
  33.0 4.4 %shard_map.122 = (f32[3,8,32,256]{3,2,1,0:T(8,128)}, f32[296,128]{1,0:T(8,128)}, f32[296,128]{1,0:T(8,128)}, f32[152,128]{1,0:T(8,128)}, f32[152,128]{1,0:T(8,128)}) custom-call(f32[3,8,32,256]{3,2,1,0:T(8,128)} %refs_0_.1, f32[8,32,256]{2,1,0:T(8,128)} %refs_1_.3, f32[4,32,256]{2,1,0:T(8,128)} %copy-done.3, f32[4,32,256]{2,1,0:T(8,128)} %copy-done.2, ...), custom_call_target="tpu_custom_call" | custom-call | tf_op jit(solution)/shard_map/pallas_call | solution.py:226
  38.1 2.4 %collective-permute-start.7 = (f32[152,128]{1,0:T(8,128)}, f32[152,128]{1,0:T(8,128)S(1)}, u32[]{:S(2)}, u32[]{:S(2)}) collective-permute-start(f32[152,128]{1,0:T(8,128)} %get-tuple-element.18), channel_id=1, source_target_pairs={{1,0},{2,1},{3,2},{0,3},{5,4},{6,5},{7,6},{4,7},{9,8},{10,9},{11,1... | collective-permute-start | bytes 233480 | tf_op jit(solution)/shard_map/ppermute | solution.py:408
  40.5 2.0 %collective-permute-done.6.refs_4_ = f32[152,128]{1,0:T(8,128)S(1)} collective-permute-done((f32[152,128]{1,0:T(8,128)}, f32[152,128]{1,0:T(8,128)S(1)}, u32[]{:S(2)}, u32[]{:S(2)}) %collective-permute-start.6) | collective-permute-done | bytes 77856 | tf_op jit(solution)/shard_map/ppermute | solution.py:407
  42.5 0.6 copy-done.6
  43.3 4.1 %shard_map.123 = (f32[3,8,32,256]{3,2,1,0:T(8,128)}, bf16[3,8,32,256]{3,2,1,0:T(8,128)(2,1)}) custom-call(f32[3,8,32,256]{3,2,1,0:T(8,128)} %get-tuple-element.14.refs_0_, f32[8,32,256]{2,1,0:T(8,128)} %refs_1_.3, f32[296,128]{1,0:T(8,128)} %copy-done.4, f32[296,128]{1,0:T(8,128)} %copy-done.5, f32[152,128]{1,0:T(8,128)} %copy-done.6, f32[152,128]{1,0:T(8,128)} %copy-done.7, ...), custom_call_target="tpu_custom_call" | custom-call | tf_op jit(solution)/shard_map/pallas_call | solution.py:234
  47.4 1.2 %convolution_convert_fusion = bf16[768,256]{1,0:T(8,128)(2,1)S(1)} fusion(bf16[768,256]{1,0:T(8,128)(2,1)} %bitcast.48, bf16[256,256]{1,0:T(8,128)(2,1)S(1)} %copy-done.10), kind=kOutput, calls=%fused_computation.1 | convolution fusion | flops 100859904 | bytes 917504 | tf_op jit(solution)/shard_map/dot_general | solution.py:263
  48.7 0.6 reshape.50
  49.3 2.0 %copy.42 = bf16[3,1,8,4,8,8,32]{6,3,0,5,4,2,1:T(4,128)(2,1)S(1)} copy(bf16[3,1,8,4,8,8,32]{6,5,4,3,2,0,1:T(8,128)(2,1)S(1)} %reshape.50) | data formatting | bytes 786432 | tf_op jit(solution)/shard_map/reshape | solution.py:265
  51.4 0.9 reshape.51
  52.4 1.0 fusion.2
  53.4 3.0 %shard_map.124 = (f32[512,128]{1,0:T(8,128)}, f32[104,128]{1,0:T(8,128)}, f32[104,128]{1,0:T(8,128)}, f32[104,32]{1,0:T(8,128)}, f32[104,32]{1,0:T(8,128)}) custom-call(f32[512,128]{1,0:T(8,128)} %fusion.6.refs_10_.refs_0_, f32[384,128]{1,0:T(8,128)} %bitcast.43, f32[296,128]{1,0:T(8,128)} %copy-done.4, f32[296,128]{1,0:T(8,128)} %copy-done.5, ...), custom_call_target="tpu_custom_call" | custom-call | tf_op jit(solution)/shard_map/pallas_call | solution.py:383
  56.4 2.7 %collective-permute-start.8 = (f32[104,128]{1,0:T(8,128)}, f32[104,128]{1,0:T(8,128)S(1)}, u32[]{:S(2)}, u32[]{:S(2)}) collective-permute-start(f32[104,128]{1,0:T(8,128)} %get-tuple-element.22), channel_id=1, source_target_pairs={{0,4},{4,8},{8,12},{12,16},{16,20},{20,24},{24,28},{28,32},{32,36}... | collective-permute-start | bytes 159752 | tf_op jit(solution)/shard_map/ppermute | solution.py:405
  59.1 2.9 %collective-permute-start.9 = (f32[104,128]{1,0:T(8,128)}, f32[104,128]{1,0:T(8,128)S(1)}, u32[]{:S(2)}, u32[]{:S(2)}) collective-permute-start(f32[104,128]{1,0:T(8,128)} %get-tuple-element.23), channel_id=1, source_target_pairs={{4,0},{8,4},{12,8},{16,12},{20,16},{24,20},{28,24},{32,28},{36,32}... | collective-permute-start | bytes 159752 | tf_op jit(solution)/shard_map/ppermute | solution.py:406
  62.4 2.5 %collective-permute-start.11 = (f32[104,32]{1,0:T(8,128)}, f32[104,32]{1,0:T(8,128)S(1)}, u32[]{:S(2)}, u32[]{:S(2)}) collective-permute-start(f32[104,32]{1,0:T(8,128)} %get-tuple-element.25), channel_id=1, source_target_pairs={{1,0},{2,1},{3,2},{0,3},{5,4},{6,5},{7,6},{4,7},{9,8},{10,9},{11,1... | collective-permute-start | bytes 39944 | tf_op jit(solution)/shard_map/ppermute | solution.py:408
  64.9 1.7 %collective-permute-done.10.refs_4_ = f32[104,32]{1,0:T(8,128)S(1)} collective-permute-done((f32[104,32]{1,0:T(8,128)}, f32[104,32]{1,0:T(8,128)S(1)}, u32[]{:S(2)}, u32[]{:S(2)}) %collective-permute-start.10) | collective-permute-done | bytes 13344 | tf_op jit(solution)/shard_map/ppermute | solution.py:407
  66.7 0.6 copy-done.14
  67.3 2.7 %shard_map.125 = f32[512,128]{1,0:T(8,128)} custom-call(f32[512,128]{1,0:T(8,128)} %get-tuple-element.21.refs_0_, f32[384,128]{1,0:T(8,128)} %bitcast.44, f32[104,128]{1,0:T(8,128)} %copy-done.12, f32[104,128]{1,0:T(8,128)} %copy-done.13, f32[104,32]{1,0:T(8,128)} %copy-done.14, f32[104,32]{1,0:T(8,128)} %copy-done.15, f32[128,384]{1,0:T(8,128)} %constant.17.clone.refs_6_, ...), custom_call_target="tpu_custom_call" | custom-call | tf_op jit(solution)/shard_map/pallas_call | solution.py:383
  70.0 1.4 %fusion.5 = f32[512,256]{0,1:T(8,128)S(1)} fusion(f32[512,128]{1,0:T(8,128)} %shard_map.125, s32[256]{0:T(256)S(1)} %eq.61), kind=kOutput, calls=%fused_computation.11 | convolution fusion | flops 201359360 | bytes 787456 | tf_op jit(solution)/shard_map/dot_general | solution.py:440
  71.7 24.8 %all_to_all.18 = f32[512,128,2]{0,2,1:T(2,128)S(1)} all-to-all(f32[512,128,2]{0,2,1:T(2,128)S(1)} %all_to_all.14), channel_id=1, replica_groups=mesh['flow'=32,'grp'=4] {'flow','grp'}, dimensions={1} | all-to-all | bytes 1048576 | tf_op jit(solution)/shard_map/all_to_all | solution.py:441
  97.1 0.6 fusion
  97.7 0.9 copy.36
  (57 shorter events, 3.3 us)
Async XLA Ops:
  1.6 13.7 %copy-start = (f32[3,8,32,256]{3,2,1,0:T(8,128)S(1)}, f32[3,8,32,256]{3,2,1,0:T(8,128)}, u32[]{:S(2)}) copy-start(f32[3,8,32,256]{3,2,1,0:T(8,128)} %refs_0_.1) | copy-start | bytes 2359300
  1.7 13.7 %copy-start.1 = (f32[8,32,256]{2,1,0:T(8,128)S(1)}, f32[8,32,256]{2,1,0:T(8,128)}, u32[]{:S(2)}) copy-start(f32[8,32,256]{2,1,0:T(8,128)} %refs_1_.3) | copy-start | bytes 786436
  3.9 16.3 %copy-start.17 = (s32[1,128,2]{1,2,0:T(2,128)S(1)}, s32[1,128,2]{1,2,0:T(2,128)}, u32[]{:S(2)}) copy-start(s32[1,128,2]{1,2,0:T(2,128)} %param.15) | copy-start | bytes 3076
  3.9 26.0 %all-to-all-start = ((f32[512,128,2]{0,2,1:T(2,128)}), f32[512,128,2]{0,2,1:T(2,128)S(1)}, u32[]{:S(2)}, u32[]{:S(2)}) async-start(f32[512,128,2]{0,2,1:T(2,128)} %copy.31), calls=%async_computation | async-start | bytes 1048576 | tf_op jit(solution)/shard_map/all_to_all | solution.py:425
  15.4 16.2 %collective-permute-start.3 = (f32[4,8,1,256]{3,2,1,0:T(1,128)S(1)}, f32[4,8,1,256]{3,2,1,0:T(1,128)S(1)}, u32[]{:S(2)}, u32[]{:S(2)}) collective-permute-start(f32[4,8,1,256]{3,2,1,0:T(1,128)S(1)} %get-tuple-element.34), channel_id=1, source_target_pairs={{1,0},{2,1},{3,2},{0,3},{5,4},{6,5},{7,6},{4,7},{9,8},{10,9},{11,1... | collective-permute-start | bytes 98312 | tf_op jit(solution)/shard_map/ppermute | solution.py:251
  18.1 13.5 %collective-permute-start.2 = (f32[4,8,1,256]{3,2,1,0:T(1,128)S(1)}, f32[4,8,1,256]{3,2,1,0:T(1,128)S(1)}, u32[]{:S(2)}, u32[]{:S(2)}) collective-permute-start(f32[4,8,1,256]{3,2,1,0:T(1,128)S(1)} %get-tuple-element.35), channel_id=1, source_target_pairs={{0,1},{1,2},{2,3},{3,0},{4,5},{5,6},{6,7},{7,4},{8,9},{9,10},{10,1... | collective-permute-start | bytes 98312 | tf_op jit(solution)/shard_map/ppermute | solution.py:250
  18.1 13.5 %collective-permute-start.1 = (f32[4,32,256]{2,1,0:T(8,128)S(1)}, f32[4,32,256]{2,1,0:T(8,128)S(1)}, u32[]{:S(2)}, u32[]{:S(2)}) collective-permute-start(f32[4,32,256]{2,1,0:T(8,128)S(1)} %get-tuple-element.36), channel_id=1, source_target_pairs={{4,0},{8,4},{12,8},{16,12},{20,16},{24,20},{28,24},{32,28},{36,32}... | collective-permute-start | bytes 393224 | tf_op jit(solution)/shard_map/ppermute | solution.py:249
  18.8 12.8 %collective-permute-start = (f32[4,32,256]{2,1,0:T(8,128)S(1)}, f32[4,32,256]{2,1,0:T(8,128)S(1)}, u32[]{:S(2)}, u32[]{:S(2)}) collective-permute-start(f32[4,32,256]{2,1,0:T(8,128)S(1)} %get-tuple-element.37), channel_id=1, source_target_pairs={{0,4},{4,8},{8,12},{12,16},{16,20},{20,24},{24,28},{28,32},{32,36}... | collective-permute-start | bytes 393224 | tf_op jit(solution)/shard_map/ppermute | solution.py:248
  31.6 15.8 %copy-start.10 = (bf16[256,256]{1,0:T(8,128)(2,1)S(1)}, bf16[256,256]{1,0:T(8,128)(2,1)}, u32[]{:S(2)}) copy-start(bf16[256,256]{1,0:T(8,128)(2,1)} %constant.21.clone) | copy-start | bytes 393220
  31.6 0.6 copy-start.8
  31.6 0.6 copy-start.9
  31.6 0.7 copy-start.2
  32.3 0.7 copy-start.3
  37.3 5.2 %collective-permute-start.4 = (f32[296,128]{1,0:T(8,128)}, f32[296,128]{1,0:T(8,128)S(1)}, u32[]{:S(2)}, u32[]{:S(2)}) collective-permute-start(f32[296,128]{1,0:T(8,128)} %get-tuple-element.15), channel_id=1, source_target_pairs={{0,4},{4,8},{8,12},{12,16},{16,20},{20,24},{24,28},{28,32},{32,36}... | collective-permute-start | bytes 454664 | tf_op jit(solution)/shard_map/ppermute | solution.py:405
  37.6 4.9 %collective-permute-start.5 = (f32[296,128]{1,0:T(8,128)}, f32[296,128]{1,0:T(8,128)S(1)}, u32[]{:S(2)}, u32[]{:S(2)}) collective-permute-start(f32[296,128]{1,0:T(8,128)} %get-tuple-element.16), channel_id=1, source_target_pairs={{4,0},{8,4},{12,8},{16,12},{20,16},{24,20},{28,24},{32,28},{36,32}... | collective-permute-start | bytes 454664 | tf_op jit(solution)/shard_map/ppermute | solution.py:406
  37.8 4.7 %collective-permute-start.6 = (f32[152,128]{1,0:T(8,128)}, f32[152,128]{1,0:T(8,128)S(1)}, u32[]{:S(2)}, u32[]{:S(2)}) collective-permute-start(f32[152,128]{1,0:T(8,128)} %get-tuple-element.17), channel_id=1, source_target_pairs={{0,1},{1,2},{2,3},{3,0},{4,5},{5,6},{6,7},{7,4},{8,9},{9,10},{10,1... | collective-permute-start | bytes 233480 | tf_op jit(solution)/shard_map/ppermute | solution.py:407
  38.1 4.4 %collective-permute-start.7 = (f32[152,128]{1,0:T(8,128)}, f32[152,128]{1,0:T(8,128)S(1)}, u32[]{:S(2)}, u32[]{:S(2)}) collective-permute-start(f32[152,128]{1,0:T(8,128)} %get-tuple-element.18), channel_id=1, source_target_pairs={{1,0},{2,1},{3,2},{0,3},{5,4},{6,5},{7,6},{4,7},{9,8},{10,9},{11,1... | collective-permute-start | bytes 233480 | tf_op jit(solution)/shard_map/ppermute | solution.py:408
  42.5 0.6 copy-start.6
  42.5 0.7 copy-start.7
  42.5 0.7 copy-start.4
  42.5 0.8 copy-start.5
  51.4 1.1 %copy-start.11 = (bf16[125,512]{1,0:T(8,128)(2,1)S(1)}, bf16[125,512]{1,0:T(8,128)(2,1)}, u32[]{:S(2)}) copy-start(bf16[125,512]{1,0:T(8,128)(2,1)} %param.13) | copy-start | bytes 384004
  56.4 10.3 %collective-permute-start.8 = (f32[104,128]{1,0:T(8,128)}, f32[104,128]{1,0:T(8,128)S(1)}, u32[]{:S(2)}, u32[]{:S(2)}) collective-permute-start(f32[104,128]{1,0:T(8,128)} %get-tuple-element.22), channel_id=1, source_target_pairs={{0,4},{4,8},{8,12},{12,16},{16,20},{20,24},{24,28},{28,32},{32,36}... | collective-permute-start | bytes 159752 | tf_op jit(solution)/shard_map/ppermute | solution.py:405
  59.1 7.6 %collective-permute-start.9 = (f32[104,128]{1,0:T(8,128)}, f32[104,128]{1,0:T(8,128)S(1)}, u32[]{:S(2)}, u32[]{:S(2)}) collective-permute-start(f32[104,128]{1,0:T(8,128)} %get-tuple-element.23), channel_id=1, source_target_pairs={{4,0},{8,4},{12,8},{16,12},{20,16},{24,20},{28,24},{32,28},{36,32}... | collective-permute-start | bytes 159752 | tf_op jit(solution)/shard_map/ppermute | solution.py:406
  62.0 4.7 %collective-permute-start.10 = (f32[104,32]{1,0:T(8,128)}, f32[104,32]{1,0:T(8,128)S(1)}, u32[]{:S(2)}, u32[]{:S(2)}) collective-permute-start(f32[104,32]{1,0:T(8,128)} %get-tuple-element.24), channel_id=1, source_target_pairs={{0,1},{1,2},{2,3},{3,0},{4,5},{5,6},{6,7},{7,4},{8,9},{9,10},{10,1... | collective-permute-start | bytes 39944 | tf_op jit(solution)/shard_map/ppermute | solution.py:407
  62.4 4.3 %collective-permute-start.11 = (f32[104,32]{1,0:T(8,128)}, f32[104,32]{1,0:T(8,128)S(1)}, u32[]{:S(2)}, u32[]{:S(2)}) collective-permute-start(f32[104,32]{1,0:T(8,128)} %get-tuple-element.25), channel_id=1, source_target_pairs={{1,0},{2,1},{3,2},{0,3},{5,4},{6,5},{7,6},{4,7},{9,8},{10,9},{11,1... | collective-permute-start | bytes 39944 | tf_op jit(solution)/shard_map/ppermute | solution.py:408
  66.7 0.6 copy-start.14
  66.7 0.6 copy-start.15
  66.7 0.6 copy-start.12
  66.7 0.6 copy-start.13
  71.4 25.7 %copy-start.16 = (s32[1,128]{1,0:T(1,128)S(1)}, s32[1,128]{1,0:T(1,128)}, u32[]{:S(2)}) copy-start(s32[1,128]{1,0:T(1,128)} %param.16) | copy-start | bytes 1540

commit v15 on v14

--- a/solution.py
+++ b/solution.py
@@ -410,7 +410,6 @@
 
 
 def body(velocity, eddy_visc, projection, acoustic_state, route_send, route_place):
-    joint = halos(jnp.concatenate([velocity, eddy_visc[None]], axis=0), 1)
     flow_size = lax.axis_size("flow")
     grp_size = lax.axis_size("grp")
     slot_cap = route_send.shape[2]
@@ -422,12 +421,14 @@
     home_hot = (sending[:, None] == jnp.arange(elem_count, dtype=jnp.int32)[None, :]).astype(jnp.float32)
     padded_state = jnp.pad(acoustic_state, ((0, 0), (0, 3), (0, 0))).reshape(512, elem_count)
     outgoing = jnp.dot(padded_state, place_hot, precision=HIGH)
+    outgoing, vel_in, nu_in = lax.optimization_barrier((outgoing, velocity, eddy_visc))
+    joint = halos(jnp.concatenate([vel_in, nu_in[None]], axis=0), 1)
     arrived = lax.all_to_all(outgoing, ("flow", "grp"), split_axis=1, concat_axis=1, tiled=True)
     state = jnp.dot(arrived, home_hot, precision=HIGH)
 
     row_len = velocity.shape[3] // 8
     mats = [jnp.asarray(m) for m in dg_matrices()]
-    vel, mxup, mxdn, myup, mydn = les_section_first(velocity, eddy_visc, joint, state)
+    vel, mxup, mxdn, myup, mydn = les_section_first(vel_in, nu_in, joint, state)
     merged = exchange_faces((mxdn, mxup, mydn, myup))
     vel, lamb = les_section_last(vel, eddy_visc, merged, joint)
     source = project(lamb, projection)

time: 99 us -> 99.2 us (level)
    all_to_all x1 -> x2, local copies, waits for them, and re-layouts: 0.36 us -> 1.46 us  [body(): lax.all_to_all(outgoing, ('flow', 'grp'), split_axis=1, concat_axis=1, ti...]
    dot_general x1 -> x0, local copies, waits for them, and re-layouts: 1 us -> none  [body(): outgoing = jnp.dot(padded_state, place_hot, precision=HIGH)]
where the time goes in v15:
time: 99.2 us; the launch traced here: 98.8 us
  starting transfers between devices  27.9 us (28%)
  blocking collectives  24.8 us (25%)
  Pallas kernels  14.2 us (14%)
  waiting for transfers between devices  13.2 us (13%)
  local copies, waits for them, and re-layouts  11 us (11%)
  matrix products  6.68 us (7%)
    all_to_all x1, blocking collectives, body(): lax.all_to_all(leaving, ('flow', 'grp'), split_axis=1, concat_axis=1, til...  24.8 us
    all_to_all x1, starting transfers between devices, body(): lax.all_to_all(outgoing, ('flow', 'grp'), split_axis=1, concat_axis=1, ti...  11.5 us
    all_to_all x1, waiting for transfers between devices, body(): lax.all_to_all(outgoing, ('flow', 'grp'), split_axis=1, concat_axis=1, ti...  9.44 us
    pallas_call x2, Pallas kernels, dg_step(): pl.pallas_call(lambda *refs: dg_step_kernel(want_faces, xoff, yoff, row_l...  5.67 us
    ppermute x2, starting transfers between devices, exchange_faces(): lax.ppermute(sy0, 'grp', down_g)  4.92 us
    unnamed x39, local copies, waits for them, and re-layouts  4.68 us
    pallas_call x1, Pallas kernels, les_section_first(): pl.pallas_call(lambda *refs: les_kernel(0, lax.axis_size('flow'), lax.axi...  4.37 us
    pallas_call x1, Pallas kernels, les_section_last(): pl.pallas_call(lambda *refs: les_kernel(1, lax.axis_size('flow'), lax.axi...  4.13 us
  transfers between devices with their start and end apart: 13, of which 3 were waited for; matrix products, arithmetic and copies ran while one was open for 2% of the time, Pallas kernels for 0%

profile of v15, /device:TPU:1, one launch (start us, length us, event | category | flops | bytes accessed | tf_op | source)
XLA Modules:
  0.0 98.8 jit_solution(5136503497749105711)
XLA Ops:
  0.6 1.0 copy.22
  1.6 1.1 %fusion.8 = f32[512,256]{1,0:T(8,128)S(1)} fusion(f32[512,128]{1,0:T(8,128)S(1)} %bitcast.47, s32[128]{0:T(128)} %bitcast.49), kind=kOutput, calls=%fused_computation.14 | convolution fusion | flops 201359360 | bytes 786944 | tf_op jit(solution)/shard_map/dot_general | solution.py:423
  3.0 1.1 %all_to_all.14 = f32[512,128,2]{0,2,1:T(2,128)} reshape(f32[512,256]{0,1:T(8,128)S(1)} %copy.23) | data formatting | bytes 1048576 | tf_op jit(solution)/shard_map/all_to_all | solution.py:426
  4.1 11.5 %all-to-all-start = ((f32[512,128,2]{0,2,1:T(2,128)}), f32[512,128,2]{0,2,1:T(2,128)S(1)}, u32[]{:S(2)}, u32[]{:S(2)}) async-start(f32[512,128,2]{0,2,1:T(2,128)} %all_to_all.14), calls=%async_computation | async-start | bytes 1048576 | tf_op jit(solution)/shard_map/all_to_all | solution.py:426
  15.6 2.7 %collective-permute-start.3 = (f32[4,8,1,256]{3,2,1,0:T(1,128)S(1)}, f32[4,8,1,256]{3,2,1,0:T(1,128)S(1)}, u32[]{:S(2)}, u32[]{:S(2)}) collective-permute-start(f32[4,8,1,256]{3,2,1,0:T(1,128)S(1)} %get-tuple-element.38), channel_id=1, source_target_pairs={{1,0},{2,1},{3,2},{0,3},{5,4},{6,5},{7,6},{4,7},{9,8},{10,9},{11,1... | collective-permute-start | bytes 98312 | tf_op jit(solution)/shard_map/ppermute | solution.py:251
  18.3 0.7 collective-permute-start.1
  19.0 1.3 %collective-permute-start = (f32[4,32,256]{2,1,0:T(8,128)S(1)}, f32[4,32,256]{2,1,0:T(8,128)S(1)}, u32[]{:S(2)}, u32[]{:S(2)}) collective-permute-start(f32[4,32,256]{2,1,0:T(8,128)S(1)} %get-tuple-element.41), channel_id=1, source_target_pairs={{0,4},{4,8},{8,12},{12,16},{16,20},{20,24},{24,28},{28,32},{32,36}... | collective-permute-start | bytes 393224 | tf_op jit(solution)/shard_map/ppermute | solution.py:248
  20.6 9.4 %all-to-all-done = f32[512,128,2]{0,2,1:T(2,128)S(1)} async-done(((f32[512,128,2]{0,2,1:T(2,128)}), f32[512,128,2]{0,2,1:T(2,128)S(1)}, u32[]{:S(2)}, u32[]{:S(2)}) %all-to-all-start) | async-done | bytes 524320 | tf_op jit(solution)/shard_map/all_to_all | solution.py:426
  30.4 1.4 %fusion.6.refs_10_.refs_0_ = f32[512,128]{1,0:T(8,128)} fusion(f32[512,256]{0,1:T(8,128)S(1)} %all_to_all.16, s32[256]{0:T(256)S(1)} %eq.34), kind=kOutput, calls=%fused_computation.11 | convolution fusion | flops 201359360 | bytes 787456 | tf_op jit(solution)/shard_map/dot_general | solution.py:427
  31.8 0.6 copy-done.8
  32.5 0.6 copy-done.3
  33.1 4.4 %shard_map.122 = (f32[3,8,32,256]{3,2,1,0:T(8,128)}, f32[296,128]{1,0:T(8,128)}, f32[296,128]{1,0:T(8,128)}, f32[152,128]{1,0:T(8,128)}, f32[152,128]{1,0:T(8,128)}) custom-call(f32[3,8,32,256]{3,2,1,0:T(8,128)} %refs_0_, f32[8,32,256]{2,1,0:T(8,128)} %refs_1_.2, f32[4,32,256]{2,1,0:T(8,128)} %copy-done.3, f32[4,32,256]{2,1,0:T(8,128)} %copy-done.2, ...), custom_call_target="tpu_custom_call" | custom-call | tf_op jit(solution)/shard_map/pallas_call | solution.py:226
  38.3 2.4 %collective-permute-start.7 = (f32[152,128]{1,0:T(8,128)}, f32[152,128]{1,0:T(8,128)S(1)}, u32[]{:S(2)}, u32[]{:S(2)}) collective-permute-start(f32[152,128]{1,0:T(8,128)} %get-tuple-element.24), channel_id=1, source_target_pairs={{1,0},{2,1},{3,2},{0,3},{5,4},{6,5},{7,6},{4,7},{9,8},{10,9},{11,1... | collective-permute-start | bytes 233480 | tf_op jit(solution)/shard_map/ppermute | solution.py:408
  40.7 2.0 %collective-permute-done.6.refs_4_ = f32[152,128]{1,0:T(8,128)S(1)} collective-permute-done((f32[152,128]{1,0:T(8,128)}, f32[152,128]{1,0:T(8,128)S(1)}, u32[]{:S(2)}, u32[]{:S(2)}) %collective-permute-start.6) | collective-permute-done | bytes 77856 | tf_op jit(solution)/shard_map/ppermute | solution.py:407
  42.7 0.6 copy-done.6
  43.5 4.1 %shard_map.123 = (f32[3,8,32,256]{3,2,1,0:T(8,128)}, bf16[3,8,32,256]{3,2,1,0:T(8,128)(2,1)}) custom-call(f32[3,8,32,256]{3,2,1,0:T(8,128)} %get-tuple-element.20.refs_0_, f32[8,32,256]{2,1,0:T(8,128)} %refs_1_.2, f32[296,128]{1,0:T(8,128)} %copy-done.4, f32[296,128]{1,0:T(8,128)} %copy-done.5, f32[152,128]{1,0:T(8,128)} %copy-done.6, f32[152,128]{1,0:T(8,128)} %copy-done.7, ...), custom_call_target="tpu_custom_call" | custom-call | tf_op jit(solution)/shard_map/pallas_call | solution.py:234
  47.6 1.2 %convolution_convert_fusion = bf16[768,256]{1,0:T(8,128)(2,1)S(1)} fusion(bf16[768,256]{1,0:T(8,128)(2,1)} %bitcast.48, bf16[256,256]{1,0:T(8,128)(2,1)S(1)} %copy-done.10), kind=kOutput, calls=%fused_computation.1 | convolution fusion | flops 100859904 | bytes 917504 | tf_op jit(solution)/shard_map/dot_general | solution.py:263
  48.9 0.6 reshape.32
  49.5 2.0 %copy.33 = bf16[3,1,8,4,8,8,32]{6,3,0,5,4,2,1:T(4,128)(2,1)S(1)} copy(bf16[3,1,8,4,8,8,32]{6,5,4,3,2,0,1:T(8,128)(2,1)S(1)} %reshape.32) | data formatting | bytes 786432 | tf_op jit(solution)/shard_map/reshape | solution.py:265
  51.6 0.9 reshape.33
  52.6 1.0 fusion.2
  53.6 3.0 %shard_map.124 = (f32[512,128]{1,0:T(8,128)}, f32[104,128]{1,0:T(8,128)}, f32[104,128]{1,0:T(8,128)}, f32[104,32]{1,0:T(8,128)}, f32[104,32]{1,0:T(8,128)}) custom-call(f32[512,128]{1,0:T(8,128)} %fusion.6.refs_10_.refs_0_, f32[384,128]{1,0:T(8,128)} %bitcast.43, f32[296,128]{1,0:T(8,128)} %copy-done.4, f32[296,128]{1,0:T(8,128)} %copy-done.5, ...), custom_call_target="tpu_custom_call" | custom-call | tf_op jit(solution)/shard_map/pallas_call | solution.py:383
  56.6 2.7 %collective-permute-start.8 = (f32[104,128]{1,0:T(8,128)}, f32[104,128]{1,0:T(8,128)S(1)}, u32[]{:S(2)}, u32[]{:S(2)}) collective-permute-start(f32[104,128]{1,0:T(8,128)} %get-tuple-element.28), channel_id=1, source_target_pairs={{0,4},{4,8},{8,12},{12,16},{16,20},{20,24},{24,28},{28,32},{32,36}... | collective-permute-start | bytes 159752 | tf_op jit(solution)/shard_map/ppermute | solution.py:405
  59.3 2.9 %collective-permute-start.9 = (f32[104,128]{1,0:T(8,128)}, f32[104,128]{1,0:T(8,128)S(1)}, u32[]{:S(2)}, u32[]{:S(2)}) collective-permute-start(f32[104,128]{1,0:T(8,128)} %get-tuple-element.29), channel_id=1, source_target_pairs={{4,0},{8,4},{12,8},{16,12},{20,16},{24,20},{28,24},{32,28},{36,32}... | collective-permute-start | bytes 159752 | tf_op jit(solution)/shard_map/ppermute | solution.py:406
  62.6 2.5 %collective-permute-start.11 = (f32[104,32]{1,0:T(8,128)}, f32[104,32]{1,0:T(8,128)S(1)}, u32[]{:S(2)}, u32[]{:S(2)}) collective-permute-start(f32[104,32]{1,0:T(8,128)} %get-tuple-element.31), channel_id=1, source_target_pairs={{1,0},{2,1},{3,2},{0,3},{5,4},{6,5},{7,6},{4,7},{9,8},{10,9},{11,1... | collective-permute-start | bytes 39944 | tf_op jit(solution)/shard_map/ppermute | solution.py:408
  65.1 1.7 %collective-permute-done.10.refs_4_ = f32[104,32]{1,0:T(8,128)S(1)} collective-permute-done((f32[104,32]{1,0:T(8,128)}, f32[104,32]{1,0:T(8,128)S(1)}, u32[]{:S(2)}, u32[]{:S(2)}) %collective-permute-start.10) | collective-permute-done | bytes 13344 | tf_op jit(solution)/shard_map/ppermute | solution.py:407
  66.9 0.6 copy-done.14
  67.5 2.7 %shard_map.125 = f32[512,128]{1,0:T(8,128)} custom-call(f32[512,128]{1,0:T(8,128)} %get-tuple-element.27.refs_0_, f32[384,128]{1,0:T(8,128)} %bitcast.44, f32[104,128]{1,0:T(8,128)} %copy-done.12, f32[104,128]{1,0:T(8,128)} %copy-done.13, f32[104,32]{1,0:T(8,128)} %copy-done.14, f32[104,32]{1,0:T(8,128)} %copy-done.15, f32[128,384]{1,0:T(8,128)} %constant.15.clone.refs_6_, ...), custom_call_target="tpu_custom_call" | custom-call | tf_op jit(solution)/shard_map/pallas_call | solution.py:383
  70.2 1.4 %fusion.5 = f32[512,256]{0,1:T(8,128)S(1)} fusion(f32[512,128]{1,0:T(8,128)} %shard_map.125, s32[256]{0:T(256)S(1)} %eq.34), kind=kOutput, calls=%fused_computation.10 | convolution fusion | flops 201359360 | bytes 787456 | tf_op jit(solution)/shard_map/dot_general | solution.py:441
  71.9 24.8 %all_to_all.21 = f32[512,128,2]{0,2,1:T(2,128)S(1)} all-to-all(f32[512,128,2]{0,2,1:T(2,128)S(1)} %all_to_all.17), channel_id=1, replica_groups=mesh['flow'=32,'grp'=4] {'flow','grp'}, dimensions={1} | all-to-all | bytes 1048576 | tf_op jit(solution)/shard_map/all_to_all | solution.py:442
  97.3 0.6 fusion
  97.9 0.9 copy.28
  (57 shorter events, 3.5 us)
Async XLA Ops:
  2.7 12.8 %copy-start = (f32[3,8,32,256]{3,2,1,0:T(8,128)S(1)}, f32[3,8,32,256]{3,2,1,0:T(8,128)}, u32[]{:S(2)}) copy-start(f32[3,8,32,256]{3,2,1,0:T(8,128)} %refs_0_) | copy-start | bytes 2359300
  2.7 12.8 %copy-start.1 = (f32[8,32,256]{2,1,0:T(8,128)S(1)}, f32[8,32,256]{2,1,0:T(8,128)}, u32[]{:S(2)}) copy-start(f32[8,32,256]{2,1,0:T(8,128)} %refs_1_.2) | copy-start | bytes 786436
  4.1 16.3 %copy-start.17 = (s32[1,128,2]{1,2,0:T(2,128)S(1)}, s32[1,128,2]{1,2,0:T(2,128)}, u32[]{:S(2)}) copy-start(s32[1,128,2]{1,2,0:T(2,128)} %param.15) | copy-start | bytes 3076
  4.1 26.0 %all-to-all-start = ((f32[512,128,2]{0,2,1:T(2,128)}), f32[512,128,2]{0,2,1:T(2,128)S(1)}, u32[]{:S(2)}, u32[]{:S(2)}) async-start(f32[512,128,2]{0,2,1:T(2,128)} %all_to_all.14), calls=%async_computation | async-start | bytes 1048576 | tf_op jit(solution)/shard_map/all_to_all | solution.py:426
  15.6 16.2 %collective-permute-start.3 = (f32[4,8,1,256]{3,2,1,0:T(1,128)S(1)}, f32[4,8,1,256]{3,2,1,0:T(1,128)S(1)}, u32[]{:S(2)}, u32[]{:S(2)}) collective-permute-start(f32[4,8,1,256]{3,2,1,0:T(1,128)S(1)} %get-tuple-element.38), channel_id=1, source_target_pairs={{1,0},{2,1},{3,2},{0,3},{5,4},{6,5},{7,6},{4,7},{9,8},{10,9},{11,1... | collective-permute-start | bytes 98312 | tf_op jit(solution)/shard_map/ppermute | solution.py:251
  18.3 13.5 %collective-permute-start.2 = (f32[4,8,1,256]{3,2,1,0:T(1,128)S(1)}, f32[4,8,1,256]{3,2,1,0:T(1,128)S(1)}, u32[]{:S(2)}, u32[]{:S(2)}) collective-permute-start(f32[4,8,1,256]{3,2,1,0:T(1,128)S(1)} %get-tuple-element.39), channel_id=1, source_target_pairs={{0,1},{1,2},{2,3},{3,0},{4,5},{5,6},{6,7},{7,4},{8,9},{9,10},{10,1... | collective-permute-start | bytes 98312 | tf_op jit(solution)/shard_map/ppermute | solution.py:250
  18.3 13.5 %collective-permute-start.1 = (f32[4,32,256]{2,1,0:T(8,128)S(1)}, f32[4,32,256]{2,1,0:T(8,128)S(1)}, u32[]{:S(2)}, u32[]{:S(2)}) collective-permute-start(f32[4,32,256]{2,1,0:T(8,128)S(1)} %get-tuple-element.40), channel_id=1, source_target_pairs={{4,0},{8,4},{12,8},{16,12},{20,16},{24,20},{28,24},{32,28},{36,32}... | collective-permute-start | bytes 393224 | tf_op jit(solution)/shard_map/ppermute | solution.py:249
  19.0 12.8 %collective-permute-start = (f32[4,32,256]{2,1,0:T(8,128)S(1)}, f32[4,32,256]{2,1,0:T(8,128)S(1)}, u32[]{:S(2)}, u32[]{:S(2)}) collective-permute-start(f32[4,32,256]{2,1,0:T(8,128)S(1)} %get-tuple-element.41), channel_id=1, source_target_pairs={{0,4},{4,8},{8,12},{12,16},{16,20},{20,24},{24,28},{28,32},{32,36}... | collective-permute-start | bytes 393224 | tf_op jit(solution)/shard_map/ppermute | solution.py:248
  31.8 15.8 %copy-start.10 = (bf16[256,256]{1,0:T(8,128)(2,1)S(1)}, bf16[256,256]{1,0:T(8,128)(2,1)}, u32[]{:S(2)}) copy-start(bf16[256,256]{1,0:T(8,128)(2,1)} %constant.19.clone) | copy-start | bytes 393220
  31.8 0.6 copy-start.8
  31.8 0.6 copy-start.9
  31.8 0.7 copy-start.2
  32.5 0.7 copy-start.3
  37.5 5.2 %collective-permute-start.4 = (f32[296,128]{1,0:T(8,128)}, f32[296,128]{1,0:T(8,128)S(1)}, u32[]{:S(2)}, u32[]{:S(2)}) collective-permute-start(f32[296,128]{1,0:T(8,128)} %get-tuple-element.21), channel_id=1, source_target_pairs={{0,4},{4,8},{8,12},{12,16},{16,20},{20,24},{24,28},{28,32},{32,36}... | collective-permute-start | bytes 454664 | tf_op jit(solution)/shard_map/ppermute | solution.py:405
  37.8 4.9 %collective-permute-start.5 = (f32[296,128]{1,0:T(8,128)}, f32[296,128]{1,0:T(8,128)S(1)}, u32[]{:S(2)}, u32[]{:S(2)}) collective-permute-start(f32[296,128]{1,0:T(8,128)} %get-tuple-element.22), channel_id=1, source_target_pairs={{4,0},{8,4},{12,8},{16,12},{20,16},{24,20},{28,24},{32,28},{36,32}... | collective-permute-start | bytes 454664 | tf_op jit(solution)/shard_map/ppermute | solution.py:406
  38.0 4.7 %collective-permute-start.6 = (f32[152,128]{1,0:T(8,128)}, f32[152,128]{1,0:T(8,128)S(1)}, u32[]{:S(2)}, u32[]{:S(2)}) collective-permute-start(f32[152,128]{1,0:T(8,128)} %get-tuple-element.23), channel_id=1, source_target_pairs={{0,1},{1,2},{2,3},{3,0},{4,5},{5,6},{6,7},{7,4},{8,9},{9,10},{10,1... | collective-permute-start | bytes 233480 | tf_op jit(solution)/shard_map/ppermute | solution.py:407
  38.3 4.4 %collective-permute-start.7 = (f32[152,128]{1,0:T(8,128)}, f32[152,128]{1,0:T(8,128)S(1)}, u32[]{:S(2)}, u32[]{:S(2)}) collective-permute-start(f32[152,128]{1,0:T(8,128)} %get-tuple-element.24), channel_id=1, source_target_pairs={{1,0},{2,1},{3,2},{0,3},{5,4},{6,5},{7,6},{4,7},{9,8},{10,9},{11,1... | collective-permute-start | bytes 233480 | tf_op jit(solution)/shard_map/ppermute | solution.py:408
  42.7 0.6 copy-start.6
  42.7 0.7 copy-start.7
  42.7 0.7 copy-start.4
  42.7 0.8 copy-start.5
  51.6 1.1 %copy-start.11 = (bf16[125,512]{1,0:T(8,128)(2,1)S(1)}, bf16[125,512]{1,0:T(8,128)(2,1)}, u32[]{:S(2)}) copy-start(bf16[125,512]{1,0:T(8,128)(2,1)} %param.13) | copy-start | bytes 384004
  56.6 10.3 %collective-permute-start.8 = (f32[104,128]{1,0:T(8,128)}, f32[104,128]{1,0:T(8,128)S(1)}, u32[]{:S(2)}, u32[]{:S(2)}) collective-permute-start(f32[104,128]{1,0:T(8,128)} %get-tuple-element.28), channel_id=1, source_target_pairs={{0,4},{4,8},{8,12},{12,16},{16,20},{20,24},{24,28},{28,32},{32,36}... | collective-permute-start | bytes 159752 | tf_op jit(solution)/shard_map/ppermute | solution.py:405
  59.3 7.6 %collective-permute-start.9 = (f32[104,128]{1,0:T(8,128)}, f32[104,128]{1,0:T(8,128)S(1)}, u32[]{:S(2)}, u32[]{:S(2)}) collective-permute-start(f32[104,128]{1,0:T(8,128)} %get-tuple-element.29), channel_id=1, source_target_pairs={{4,0},{8,4},{12,8},{16,12},{20,16},{24,20},{28,24},{32,28},{36,32}... | collective-permute-start | bytes 159752 | tf_op jit(solution)/shard_map/ppermute | solution.py:406
  62.2 4.7 %collective-permute-start.10 = (f32[104,32]{1,0:T(8,128)}, f32[104,32]{1,0:T(8,128)S(1)}, u32[]{:S(2)}, u32[]{:S(2)}) collective-permute-start(f32[104,32]{1,0:T(8,128)} %get-tuple-element.30), channel_id=1, source_target_pairs={{0,1},{1,2},{2,3},{3,0},{4,5},{5,6},{6,7},{7,4},{8,9},{9,10},{10,1... | collective-permute-start | bytes 39944 | tf_op jit(solution)/shard_map/ppermute | solution.py:407
  62.6 4.3 %collective-permute-start.11 = (f32[104,32]{1,0:T(8,128)}, f32[104,32]{1,0:T(8,128)S(1)}, u32[]{:S(2)}, u32[]{:S(2)}) collective-permute-start(f32[104,32]{1,0:T(8,128)} %get-tuple-element.31), channel_id=1, source_target_pairs={{1,0},{2,1},{3,2},{0,3},{5,4},{6,5},{7,6},{4,7},{9,8},{10,9},{11,1... | collective-permute-start | bytes 39944 | tf_op jit(solution)/shard_map/ppermute | solution.py:408
  66.8 0.6 copy-start.14
  66.8 0.6 copy-start.15
  66.9 0.6 copy-start.12
  66.9 0.6 copy-start.13
  71.6 25.7 %copy-start.16 = (s32[1,128]{1,0:T(1,128)S(1)}, s32[1,128]{1,0:T(1,128)}, u32[]{:S(2)}) copy-start(s32[1,128]{1,0:T(1,128)} %param.16) | copy-start | bytes 1540

commit v16 on v14

--- a/solution.py
+++ b/solution.py
@@ -157,19 +157,19 @@
     def zm(f):
         return jnp.where(lane == 0, 0.0, pltpu.roll(f, 1, 1))
 
-    def step(x, carry):
-        lo = jnp.maximum(x - 1, 0)
-        hi = jnp.minimum(x + 1, size_x - 1)
+    def plane_step(x, first, last):
+        lo = x - 1
+        hi = x + 1
         u = [vel_ref[c, x] for c in range(3)]
-        uxm = [jnp.where(x == 0, xlo(c), vel_ref[c, lo]) for c in range(3)]
-        uxp = [jnp.where(x == size_x - 1, xhi(c), vel_ref[c, hi]) for c in range(3)]
+        uxm = [xlo(c) if first else vel_ref[c, lo] for c in range(3)]
+        uxp = [xhi(c) if last else vel_ref[c, hi] for c in range(3)]
         uym = [ym(u[c], ylo(c, x)) for c in range(3)]
         uyp = [yp(u[c], yhi(c, x)) for c in range(3)]
         uzm = [zm(u[c]) for c in range(3)]
         uzp = [zp(u[c]) for c in range(3)]
         nu = nu_ref[x]
-        nxm = jnp.where(x == 0, jnp.where(at_lo_f, 0.0, nxlo_ref[3]), nu_ref[lo])
-        nxp = jnp.where(x == size_x - 1, jnp.where(at_hi_f, 0.0, nxhi_ref[3]), nu_ref[hi])
+        nxm = jnp.where(at_lo_f, 0.0, nxlo_ref[3]) if first else nu_ref[lo]
+        nxp = jnp.where(at_hi_f, 0.0, nxhi_ref[3]) if last else nu_ref[hi]
         nym = ym(nu, jnp.where(at_lo_g, 0.0, nylo_ref[3, x]))
         nyp = yp(nu, jnp.where(at_hi_g, 0.0, nyhi_ref[3, x]))
         nzm = zm(nu)
@@ -194,9 +194,14 @@
             out_ref[c, x] = u[c] + TIME_STEP_LES * (total - lamb[c])
             if mode == 1:
                 lamb_ref[c, x] = lamb[c].astype(lamb_ref.dtype)
+
+    def step(x, carry):
+        plane_step(x, False, False)
         return carry
 
-    lax.fori_loop(0, size_x, step, 0)
+    plane_step(0, True, False)
+    lax.fori_loop(1, size_x - 1, step, 0)
+    plane_step(size_x - 1, False, True)
     if mode == 0:
         for c in range(3):
             for h in range(2):

time: 99 us -> 98.6 us (level)
  no operation moved by 1% of the time
where the time goes in v16:
time: 98.6 us; the launch traced here: 98.2 us
  starting transfers between devices  28.1 us (28%)
  blocking collectives  24.6 us (25%)
  Pallas kernels  13.7 us (14%)
  waiting for transfers between devices  13.2 us (13%)
  local copies, waits for them, and re-layouts  10.7 us (11%)
  matrix products  6.78 us (7%)
    all_to_all x1, blocking collectives, body(): lax.all_to_all(leaving, ('flow', 'grp'), split_axis=1, concat_axis=1, til...  24.6 us
    all_to_all x1, starting transfers between devices, body(): lax.all_to_all(outgoing, ('flow', 'grp'), split_axis=1, concat_axis=1, ti...  11.5 us
    all_to_all x1, waiting for transfers between devices, body(): lax.all_to_all(outgoing, ('flow', 'grp'), split_axis=1, concat_axis=1, ti...  9.44 us
    pallas_call x2, Pallas kernels, dg_step(): pl.pallas_call(lambda *refs: dg_step_kernel(want_faces, xoff, yoff, row_l...  5.67 us
    ppermute x2, starting transfers between devices, exchange_faces(): lax.ppermute(sy0, 'grp', down_g)  4.93 us
    unnamed x39, local copies, waits for them, and re-layouts  4.68 us
    pallas_call x1, Pallas kernels, les_section_first(): pl.pallas_call(lambda *refs: les_kernel(0, lax.axis_size('flow'), lax.axi...  4.13 us
    pallas_call x1, Pallas kernels, les_section_last(): pl.pallas_call(lambda *refs: les_kernel(1, lax.axis_size('flow'), lax.axi...  3.95 us
  transfers between devices with their start and end apart: 13, of which 3 were waited for; matrix products, arithmetic and copies ran while one was open for 2% of the time, Pallas kernels for 0%

profile of v16, /device:TPU:1, one launch (start us, length us, event | category | flops | bytes accessed | tf_op | source)
XLA Modules:
  0.0 98.2 jit_solution(7066916995859654659)
XLA Ops:
  0.6 1.0 copy.37
  1.7 1.2 %fusion.9 = f32[512,128,2]{1,0,2:T(8,128)S(1)} fusion(f32[512,128,1]{1,0,2:T(8,128)S(1)} %bitcast.47, s32[128,2]{0,1:T(2,128)S(1)} %multiply_add_fusion, s32[128]{0:T(128)} %bitcast.49), kind=kOutput, calls=%fused_computation.14 | convolution fusion | flops 201359360 | bytes 787968 | tf_op jit(solution)/shard_map/dot_general | solution.py:429
  2.9 1.0 %copy.31 = f32[512,128,2]{0,2,1:T(2,128)} copy(f32[512,128,2]{1,0,2:T(8,128)S(1)} %fusion.9) | data formatting | bytes 1048576 | tf_op jit(solution)/shard_map/dot_general | solution.py:429
  3.9 11.5 %all-to-all-start = ((f32[512,128,2]{0,2,1:T(2,128)}), f32[512,128,2]{0,2,1:T(2,128)S(1)}, u32[]{:S(2)}, u32[]{:S(2)}) async-start(f32[512,128,2]{0,2,1:T(2,128)} %copy.31), calls=%async_computation | async-start | bytes 1048576 | tf_op jit(solution)/shard_map/all_to_all | solution.py:430
  15.4 2.7 %collective-permute-start.3 = (f32[4,8,1,256]{3,2,1,0:T(1,128)S(1)}, f32[4,8,1,256]{3,2,1,0:T(1,128)S(1)}, u32[]{:S(2)}, u32[]{:S(2)}) collective-permute-start(f32[4,8,1,256]{3,2,1,0:T(1,128)S(1)} %get-tuple-element.34), channel_id=1, source_target_pairs={{1,0},{2,1},{3,2},{0,3},{5,4},{6,5},{7,6},{4,7},{9,8},{10,9},{11,1... | collective-permute-start | bytes 98312 | tf_op jit(solution)/shard_map/ppermute | solution.py:256
  18.1 0.7 collective-permute-start.1
  18.8 1.3 %collective-permute-start = (f32[4,32,256]{2,1,0:T(8,128)S(1)}, f32[4,32,256]{2,1,0:T(8,128)S(1)}, u32[]{:S(2)}, u32[]{:S(2)}) collective-permute-start(f32[4,32,256]{2,1,0:T(8,128)S(1)} %get-tuple-element.37), channel_id=1, source_target_pairs={{0,4},{4,8},{8,12},{12,16},{16,20},{20,24},{24,28},{28,32},{32,36}... | collective-permute-start | bytes 393224 | tf_op jit(solution)/shard_map/ppermute | solution.py:253
  20.4 9.4 %all-to-all-done = f32[512,128,2]{0,2,1:T(2,128)S(1)} async-done(((f32[512,128,2]{0,2,1:T(2,128)}), f32[512,128,2]{0,2,1:T(2,128)S(1)}, u32[]{:S(2)}, u32[]{:S(2)}) %all-to-all-start) | async-done | bytes 524320 | tf_op jit(solution)/shard_map/all_to_all | solution.py:430
  30.2 1.4 %fusion.6.refs_10_.refs_0_ = f32[512,128]{1,0:T(8,128)} fusion(f32[512,256]{0,1:T(8,128)S(1)} %all_to_all.13, s32[256]{0:T(256)S(1)} %eq.61), kind=kOutput, calls=%fused_computation.12 | convolution fusion | flops 201359360 | bytes 787456 | tf_op jit(solution)/shard_map/dot_general | solution.py:431
  31.6 0.6 copy-done.8
  32.3 0.6 copy-done.3
  33.0 4.1 %shard_map.122 = (f32[3,8,32,256]{3,2,1,0:T(8,128)}, f32[296,128]{1,0:T(8,128)}, f32[296,128]{1,0:T(8,128)}, f32[152,128]{1,0:T(8,128)}, f32[152,128]{1,0:T(8,128)}) custom-call(f32[3,8,32,256]{3,2,1,0:T(8,128)} %refs_0_.1, f32[8,32,256]{2,1,0:T(8,128)} %refs_1_.3, f32[4,32,256]{2,1,0:T(8,128)} %copy-done.3, f32[4,32,256]{2,1,0:T(8,128)} %copy-done.2, ...), custom_call_target="tpu_custom_call" | custom-call | tf_op jit(solution)/shard_map/pallas_call | solution.py:231
  37.9 2.4 %collective-permute-start.7 = (f32[152,128]{1,0:T(8,128)}, f32[152,128]{1,0:T(8,128)S(1)}, u32[]{:S(2)}, u32[]{:S(2)}) collective-permute-start(f32[152,128]{1,0:T(8,128)} %get-tuple-element.18), channel_id=1, source_target_pairs={{1,0},{2,1},{3,2},{0,3},{5,4},{6,5},{7,6},{4,7},{9,8},{10,9},{11,1... | collective-permute-start | bytes 233480 | tf_op jit(solution)/shard_map/ppermute | solution.py:413
  40.3 2.0 %collective-permute-done.6.refs_4_ = f32[152,128]{1,0:T(8,128)S(1)} collective-permute-done((f32[152,128]{1,0:T(8,128)}, f32[152,128]{1,0:T(8,128)S(1)}, u32[]{:S(2)}, u32[]{:S(2)}) %collective-permute-start.6) | collective-permute-done | bytes 77856 | tf_op jit(solution)/shard_map/ppermute | solution.py:412
  42.3 0.6 copy-done.6
  43.1 4.0 %shard_map.123 = (f32[3,8,32,256]{3,2,1,0:T(8,128)}, bf16[3,8,32,256]{3,2,1,0:T(8,128)(2,1)}) custom-call(f32[3,8,32,256]{3,2,1,0:T(8,128)} %get-tuple-element.14.refs_0_, f32[8,32,256]{2,1,0:T(8,128)} %refs_1_.3, f32[296,128]{1,0:T(8,128)} %copy-done.4, f32[296,128]{1,0:T(8,128)} %copy-done.5, f32[152,128]{1,0:T(8,128)} %copy-done.6, f32[152,128]{1,0:T(8,128)} %copy-done.7, ...), custom_call_target="tpu_custom_call" | custom-call | tf_op jit(solution)/shard_map/pallas_call | solution.py:239
  47.0 1.2 %convolution_convert_fusion = bf16[768,256]{1,0:T(8,128)(2,1)S(1)} fusion(bf16[768,256]{1,0:T(8,128)(2,1)} %bitcast.48, bf16[256,256]{1,0:T(8,128)(2,1)S(1)} %copy-done.10), kind=kOutput, calls=%fused_computation.1 | convolution fusion | flops 100859904 | bytes 917504 | tf_op jit(solution)/shard_map/dot_general | solution.py:268
  48.3 0.6 reshape.50
  48.9 2.0 %copy.42 = bf16[3,1,8,4,8,8,32]{6,3,0,5,4,2,1:T(4,128)(2,1)S(1)} copy(bf16[3,1,8,4,8,8,32]{6,5,4,3,2,0,1:T(8,128)(2,1)S(1)} %reshape.50) | data formatting | bytes 786432 | tf_op jit(solution)/shard_map/reshape | solution.py:270
  51.0 0.9 reshape.51
  52.0 1.0 fusion.2
  53.0 2.9 %shard_map.124 = (f32[512,128]{1,0:T(8,128)}, f32[104,128]{1,0:T(8,128)}, f32[104,128]{1,0:T(8,128)}, f32[104,32]{1,0:T(8,128)}, f32[104,32]{1,0:T(8,128)}) custom-call(f32[512,128]{1,0:T(8,128)} %fusion.6.refs_10_.refs_0_, f32[384,128]{1,0:T(8,128)} %bitcast.43, f32[296,128]{1,0:T(8,128)} %copy-done.4, f32[296,128]{1,0:T(8,128)} %copy-done.5, ...), custom_call_target="tpu_custom_call" | custom-call | tf_op jit(solution)/shard_map/pallas_call | solution.py:388
  55.9 2.7 %collective-permute-start.8 = (f32[104,128]{1,0:T(8,128)}, f32[104,128]{1,0:T(8,128)S(1)}, u32[]{:S(2)}, u32[]{:S(2)}) collective-permute-start(f32[104,128]{1,0:T(8,128)} %get-tuple-element.22), channel_id=1, source_target_pairs={{0,4},{4,8},{8,12},{12,16},{16,20},{20,24},{24,28},{28,32},{32,36}... | collective-permute-start | bytes 159752 | tf_op jit(solution)/shard_map/ppermute | solution.py:410
  58.7 3.1 %collective-permute-start.9 = (f32[104,128]{1,0:T(8,128)}, f32[104,128]{1,0:T(8,128)S(1)}, u32[]{:S(2)}, u32[]{:S(2)}) collective-permute-start(f32[104,128]{1,0:T(8,128)} %get-tuple-element.23), channel_id=1, source_target_pairs={{4,0},{8,4},{12,8},{16,12},{20,16},{24,20},{28,24},{32,28},{36,32}... | collective-permute-start | bytes 159752 | tf_op jit(solution)/shard_map/ppermute | solution.py:411
  62.2 2.5 %collective-permute-start.11 = (f32[104,32]{1,0:T(8,128)}, f32[104,32]{1,0:T(8,128)S(1)}, u32[]{:S(2)}, u32[]{:S(2)}) collective-permute-start(f32[104,32]{1,0:T(8,128)} %get-tuple-element.25), channel_id=1, source_target_pairs={{1,0},{2,1},{3,2},{0,3},{5,4},{6,5},{7,6},{4,7},{9,8},{10,9},{11,1... | collective-permute-start | bytes 39944 | tf_op jit(solution)/shard_map/ppermute | solution.py:413
  64.7 1.7 %collective-permute-done.10.refs_4_ = f32[104,32]{1,0:T(8,128)S(1)} collective-permute-done((f32[104,32]{1,0:T(8,128)}, f32[104,32]{1,0:T(8,128)S(1)}, u32[]{:S(2)}, u32[]{:S(2)}) %collective-permute-start.10) | collective-permute-done | bytes 13344 | tf_op jit(solution)/shard_map/ppermute | solution.py:412
  66.5 0.6 copy-done.14
  67.1 2.7 %shard_map.125 = f32[512,128]{1,0:T(8,128)} custom-call(f32[512,128]{1,0:T(8,128)} %get-tuple-element.21.refs_0_, f32[384,128]{1,0:T(8,128)} %bitcast.44, f32[104,128]{1,0:T(8,128)} %copy-done.12, f32[104,128]{1,0:T(8,128)} %copy-done.13, f32[104,32]{1,0:T(8,128)} %copy-done.14, f32[104,32]{1,0:T(8,128)} %copy-done.15, f32[128,384]{1,0:T(8,128)} %constant.17.clone.refs_6_, ...), custom_call_target="tpu_custom_call" | custom-call | tf_op jit(solution)/shard_map/pallas_call | solution.py:388
  69.8 1.4 %fusion.5 = f32[512,256]{0,1:T(8,128)S(1)} fusion(f32[512,128]{1,0:T(8,128)} %shard_map.125, s32[256]{0:T(256)S(1)} %eq.61), kind=kOutput, calls=%fused_computation.11 | convolution fusion | flops 201359360 | bytes 787456 | tf_op jit(solution)/shard_map/dot_general | solution.py:445
  71.5 24.6 %all_to_all.18 = f32[512,128,2]{0,2,1:T(2,128)S(1)} all-to-all(f32[512,128,2]{0,2,1:T(2,128)S(1)} %all_to_all.14), channel_id=1, replica_groups=mesh['flow'=32,'grp'=4] {'flow','grp'}, dimensions={1} | all-to-all | bytes 1048576 | tf_op jit(solution)/shard_map/all_to_all | solution.py:446
  96.7 0.6 fusion
  97.3 0.9 copy.36
  (57 shorter events, 3.3 us)
Async XLA Ops:
  1.6 13.7 %copy-start = (f32[3,8,32,256]{3,2,1,0:T(8,128)S(1)}, f32[3,8,32,256]{3,2,1,0:T(8,128)}, u32[]{:S(2)}) copy-start(f32[3,8,32,256]{3,2,1,0:T(8,128)} %refs_0_.1) | copy-start | bytes 2359300
  1.7 13.7 %copy-start.1 = (f32[8,32,256]{2,1,0:T(8,128)S(1)}, f32[8,32,256]{2,1,0:T(8,128)}, u32[]{:S(2)}) copy-start(f32[8,32,256]{2,1,0:T(8,128)} %refs_1_.3) | copy-start | bytes 786436
  3.9 16.3 %copy-start.17 = (s32[1,128,2]{1,2,0:T(2,128)S(1)}, s32[1,128,2]{1,2,0:T(2,128)}, u32[]{:S(2)}) copy-start(s32[1,128,2]{1,2,0:T(2,128)} %param.15) | copy-start | bytes 3076
  3.9 26.0 %all-to-all-start = ((f32[512,128,2]{0,2,1:T(2,128)}), f32[512,128,2]{0,2,1:T(2,128)S(1)}, u32[]{:S(2)}, u32[]{:S(2)}) async-start(f32[512,128,2]{0,2,1:T(2,128)} %copy.31), calls=%async_computation | async-start | bytes 1048576 | tf_op jit(solution)/shard_map/all_to_all | solution.py:430
  15.4 16.2 %collective-permute-start.3 = (f32[4,8,1,256]{3,2,1,0:T(1,128)S(1)}, f32[4,8,1,256]{3,2,1,0:T(1,128)S(1)}, u32[]{:S(2)}, u32[]{:S(2)}) collective-permute-start(f32[4,8,1,256]{3,2,1,0:T(1,128)S(1)} %get-tuple-element.34), channel_id=1, source_target_pairs={{1,0},{2,1},{3,2},{0,3},{5,4},{6,5},{7,6},{4,7},{9,8},{10,9},{11,1... | collective-permute-start | bytes 98312 | tf_op jit(solution)/shard_map/ppermute | solution.py:256
  18.1 13.5 %collective-permute-start.2 = (f32[4,8,1,256]{3,2,1,0:T(1,128)S(1)}, f32[4,8,1,256]{3,2,1,0:T(1,128)S(1)}, u32[]{:S(2)}, u32[]{:S(2)}) collective-permute-start(f32[4,8,1,256]{3,2,1,0:T(1,128)S(1)} %get-tuple-element.35), channel_id=1, source_target_pairs={{0,1},{1,2},{2,3},{3,0},{4,5},{5,6},{6,7},{7,4},{8,9},{9,10},{10,1... | collective-permute-start | bytes 98312 | tf_op jit(solution)/shard_map/ppermute | solution.py:255
  18.1 13.5 %collective-permute-start.1 = (f32[4,32,256]{2,1,0:T(8,128)S(1)}, f32[4,32,256]{2,1,0:T(8,128)S(1)}, u32[]{:S(2)}, u32[]{:S(2)}) collective-permute-start(f32[4,32,256]{2,1,0:T(8,128)S(1)} %get-tuple-element.36), channel_id=1, source_target_pairs={{4,0},{8,4},{12,8},{16,12},{20,16},{24,20},{28,24},{32,28},{36,32}... | collective-permute-start | bytes 393224 | tf_op jit(solution)/shard_map/ppermute | solution.py:254
  18.8 12.8 %collective-permute-start = (f32[4,32,256]{2,1,0:T(8,128)S(1)}, f32[4,32,256]{2,1,0:T(8,128)S(1)}, u32[]{:S(2)}, u32[]{:S(2)}) collective-permute-start(f32[4,32,256]{2,1,0:T(8,128)S(1)} %get-tuple-element.37), channel_id=1, source_target_pairs={{0,4},{4,8},{8,12},{12,16},{16,20},{20,24},{24,28},{28,32},{32,36}... | collective-permute-start | bytes 393224 | tf_op jit(solution)/shard_map/ppermute | solution.py:253
  31.6 15.4 %copy-start.10 = (bf16[256,256]{1,0:T(8,128)(2,1)S(1)}, bf16[256,256]{1,0:T(8,128)(2,1)}, u32[]{:S(2)}) copy-start(bf16[256,256]{1,0:T(8,128)(2,1)} %constant.21.clone) | copy-start | bytes 393220
  31.6 0.6 copy-start.8
  31.6 0.6 copy-start.9
  31.6 0.7 copy-start.2
  32.3 0.7 copy-start.3
  37.1 5.2 %collective-permute-start.4 = (f32[296,128]{1,0:T(8,128)}, f32[296,128]{1,0:T(8,128)S(1)}, u32[]{:S(2)}, u32[]{:S(2)}) collective-permute-start(f32[296,128]{1,0:T(8,128)} %get-tuple-element.15), channel_id=1, source_target_pairs={{0,4},{4,8},{8,12},{12,16},{16,20},{20,24},{24,28},{28,32},{32,36}... | collective-permute-start | bytes 454664 | tf_op jit(solution)/shard_map/ppermute | solution.py:410
  37.4 4.9 %collective-permute-start.5 = (f32[296,128]{1,0:T(8,128)}, f32[296,128]{1,0:T(8,128)S(1)}, u32[]{:S(2)}, u32[]{:S(2)}) collective-permute-start(f32[296,128]{1,0:T(8,128)} %get-tuple-element.16), channel_id=1, source_target_pairs={{4,0},{8,4},{12,8},{16,12},{20,16},{24,20},{28,24},{32,28},{36,32}... | collective-permute-start | bytes 454664 | tf_op jit(solution)/shard_map/ppermute | solution.py:411
  37.6 4.7 %collective-permute-start.6 = (f32[152,128]{1,0:T(8,128)}, f32[152,128]{1,0:T(8,128)S(1)}, u32[]{:S(2)}, u32[]{:S(2)}) collective-permute-start(f32[152,128]{1,0:T(8,128)} %get-tuple-element.17), channel_id=1, source_target_pairs={{0,1},{1,2},{2,3},{3,0},{4,5},{5,6},{6,7},{7,4},{8,9},{9,10},{10,1... | collective-permute-start | bytes 233480 | tf_op jit(solution)/shard_map/ppermute | solution.py:412
  37.9 4.4 %collective-permute-start.7 = (f32[152,128]{1,0:T(8,128)}, f32[152,128]{1,0:T(8,128)S(1)}, u32[]{:S(2)}, u32[]{:S(2)}) collective-permute-start(f32[152,128]{1,0:T(8,128)} %get-tuple-element.18), channel_id=1, source_target_pairs={{1,0},{2,1},{3,2},{0,3},{5,4},{6,5},{7,6},{4,7},{9,8},{10,9},{11,1... | collective-permute-start | bytes 233480 | tf_op jit(solution)/shard_map/ppermute | solution.py:413
  42.3 0.6 copy-start.6
  42.3 0.7 copy-start.7
  42.3 0.7 copy-start.4
  42.3 0.8 copy-start.5
  50.9 1.1 %copy-start.11 = (bf16[125,512]{1,0:T(8,128)(2,1)S(1)}, bf16[125,512]{1,0:T(8,128)(2,1)}, u32[]{:S(2)}) copy-start(bf16[125,512]{1,0:T(8,128)(2,1)} %param.13) | copy-start | bytes 384004
  55.9 10.5 %collective-permute-start.8 = (f32[104,128]{1,0:T(8,128)}, f32[104,128]{1,0:T(8,128)S(1)}, u32[]{:S(2)}, u32[]{:S(2)}) collective-permute-start(f32[104,128]{1,0:T(8,128)} %get-tuple-element.22), channel_id=1, source_target_pairs={{0,4},{4,8},{8,12},{12,16},{16,20},{20,24},{24,28},{28,32},{32,36}... | collective-permute-start | bytes 159752 | tf_op jit(solution)/shard_map/ppermute | solution.py:410
  58.7 7.8 %collective-permute-start.9 = (f32[104,128]{1,0:T(8,128)}, f32[104,128]{1,0:T(8,128)S(1)}, u32[]{:S(2)}, u32[]{:S(2)}) collective-permute-start(f32[104,128]{1,0:T(8,128)} %get-tuple-element.23), channel_id=1, source_target_pairs={{4,0},{8,4},{12,8},{16,12},{20,16},{24,20},{28,24},{32,28},{36,32}... | collective-permute-start | bytes 159752 | tf_op jit(solution)/shard_map/ppermute | solution.py:411
  61.8 4.7 %collective-permute-start.10 = (f32[104,32]{1,0:T(8,128)}, f32[104,32]{1,0:T(8,128)S(1)}, u32[]{:S(2)}, u32[]{:S(2)}) collective-permute-start(f32[104,32]{1,0:T(8,128)} %get-tuple-element.24), channel_id=1, source_target_pairs={{0,1},{1,2},{2,3},{3,0},{4,5},{5,6},{6,7},{7,4},{8,9},{9,10},{10,1... | collective-permute-start | bytes 39944 | tf_op jit(solution)/shard_map/ppermute | solution.py:412
  62.2 4.3 %collective-permute-start.11 = (f32[104,32]{1,0:T(8,128)}, f32[104,32]{1,0:T(8,128)S(1)}, u32[]{:S(2)}, u32[]{:S(2)}) collective-permute-start(f32[104,32]{1,0:T(8,128)} %get-tuple-element.25), channel_id=1, source_target_pairs={{1,0},{2,1},{3,2},{0,3},{5,4},{6,5},{7,6},{4,7},{9,8},{10,9},{11,1... | collective-permute-start | bytes 39944 | tf_op jit(solution)/shard_map/ppermute | solution.py:413
  66.4 0.6 copy-start.14
  66.5 0.6 copy-start.15
  66.5 0.6 copy-start.12
  66.5 0.6 copy-start.13
  71.2 25.5 %copy-start.16 = (s32[1,128]{1,0:T(1,128)S(1)}, s32[1,128]{1,0:T(1,128)}, u32[]{:S(2)}) copy-start(s32[1,128]{1,0:T(1,128)} %param.16) | copy-start | bytes 1540

commit v17 on v16

--- a/solution.py
+++ b/solution.py
@@ -228,11 +228,15 @@
     size_x, size_y, size_z = vel.shape[1], vel.shape[2], vel.shape[3]
     xbuf = jax.ShapeDtypeStruct((3 * 2 * size_y + FACE_ROWS, size_z // 2), jnp.float32)
     ybuf = jax.ShapeDtypeStruct((3 * 2 * size_x + FACE_ROWS, size_z // 2), jnp.float32)
+    def kernel(vel_ref, nu_ref, xlo_ref, xhi_ref, ylo_ref, yhi_ref, *rest):
+        halo_refs = (xlo_ref, xhi_ref, ylo_ref, yhi_ref)
+        les_kernel(0, lax.axis_size("flow"), lax.axis_size("grp"), vel_ref, nu_ref, *halo_refs, *halo_refs, *rest)
+
     return pl.pallas_call(
-        lambda *refs: les_kernel(0, lax.axis_size("flow"), lax.axis_size("grp"), *refs),
+        kernel,
         out_shape=(jax.ShapeDtypeStruct(vel.shape, jnp.float32), xbuf, xbuf, ybuf, ybuf),
         scratch_shapes=[pltpu.VMEM((6, FACE_ROWS, state.shape[1]), jnp.float32)],
-    )(vel, nu, *joint, *joint, state)
+    )(vel, nu, *joint, state)
 
 
 def les_section_last(vel, nu, merged, joint):

time: 98.6 us -> 98.5 us (level)
  no operation moved by 1% of the time
where the time goes in v17:
time: 98.5 us; the launch traced here: 98.1 us
  starting transfers between devices  28.2 us (29%)
  blocking collectives  24.6 us (25%)
  Pallas kernels  13.6 us (14%)
  waiting for transfers between devices  13.2 us (13%)
  local copies, waits for them, and re-layouts  10.7 us (11%)
  matrix products  6.77 us (7%)
    all_to_all x1, blocking collectives, body(): lax.all_to_all(leaving, ('flow', 'grp'), split_axis=1, concat_axis=1, til...  24.6 us
    all_to_all x1, starting transfers between devices, body(): lax.all_to_all(outgoing, ('flow', 'grp'), split_axis=1, concat_axis=1, ti...  11.5 us
    all_to_all x1, waiting for transfers between devices, body(): lax.all_to_all(outgoing, ('flow', 'grp'), split_axis=1, concat_axis=1, ti...  9.44 us
    pallas_call x2, Pallas kernels, dg_step(): pl.pallas_call(lambda *refs: dg_step_kernel(want_faces, xoff, yoff, row_l...  5.67 us
    ppermute x2, starting transfers between devices, exchange_faces(): lax.ppermute(sy0, 'grp', down_g)  4.92 us
    unnamed x39, local copies, waits for them, and re-layouts  4.68 us
    pallas_call x1, Pallas kernels, les_section_first(): pl.pallas_call(kernel, out_shape=(jax.ShapeDtypeStruct(vel.shape, jnp.flo...  4 us
    pallas_call x1, Pallas kernels, les_section_last(): pl.pallas_call(lambda *refs: les_kernel(1, lax.axis_size('flow'), lax.axi...  3.95 us
  transfers between devices with their start and end apart: 13, of which 3 were waited for; matrix products, arithmetic and copies ran while one was open for 2% of the time, Pallas kernels for 0%

profile of v17, /device:TPU:1, one launch (start us, length us, event | category | flops | bytes accessed | tf_op | source)
XLA Modules:
  0.0 98.1 jit_solution(3606101090958305495)
XLA Ops:
  0.6 1.0 copy.37
  1.7 1.2 %fusion.9 = f32[512,128,2]{1,0,2:T(8,128)S(1)} fusion(f32[512,128,1]{1,0,2:T(8,128)S(1)} %bitcast.47, s32[128,2]{0,1:T(2,128)S(1)} %multiply_add_fusion, s32[128]{0:T(128)} %bitcast.49), kind=kOutput, calls=%fused_computation.14 | convolution fusion | flops 201359360 | bytes 787968 | tf_op jit(solution)/shard_map/dot_general | solution.py:433
  2.9 1.0 %copy.31 = f32[512,128,2]{0,2,1:T(2,128)} copy(f32[512,128,2]{1,0,2:T(8,128)S(1)} %fusion.9) | data formatting | bytes 1048576 | tf_op jit(solution)/shard_map/dot_general | solution.py:433
  3.9 11.5 %all-to-all-start = ((f32[512,128,2]{0,2,1:T(2,128)}), f32[512,128,2]{0,2,1:T(2,128)S(1)}, u32[]{:S(2)}, u32[]{:S(2)}) async-start(f32[512,128,2]{0,2,1:T(2,128)} %copy.31), calls=%async_computation | async-start | bytes 1048576 | tf_op jit(solution)/shard_map/all_to_all | solution.py:434
  15.4 2.7 %collective-permute-start.3 = (f32[4,8,1,256]{3,2,1,0:T(1,128)S(1)}, f32[4,8,1,256]{3,2,1,0:T(1,128)S(1)}, u32[]{:S(2)}, u32[]{:S(2)}) collective-permute-start(f32[4,8,1,256]{3,2,1,0:T(1,128)S(1)} %get-tuple-element.34), channel_id=1, source_target_pairs={{1,0},{2,1},{3,2},{0,3},{5,4},{6,5},{7,6},{4,7},{9,8},{10,9},{11,1... | collective-permute-start | bytes 98312 | tf_op jit(solution)/shard_map/ppermute | solution.py:260
  18.1 0.7 collective-permute-start.1
  18.8 1.3 %collective-permute-start = (f32[4,32,256]{2,1,0:T(8,128)S(1)}, f32[4,32,256]{2,1,0:T(8,128)S(1)}, u32[]{:S(2)}, u32[]{:S(2)}) collective-permute-start(f32[4,32,256]{2,1,0:T(8,128)S(1)} %get-tuple-element.37), channel_id=1, source_target_pairs={{0,4},{4,8},{8,12},{12,16},{16,20},{20,24},{24,28},{28,32},{32,36}... | collective-permute-start | bytes 393224 | tf_op jit(solution)/shard_map/ppermute | solution.py:257
  20.4 9.4 %all-to-all-done = f32[512,128,2]{0,2,1:T(2,128)S(1)} async-done(((f32[512,128,2]{0,2,1:T(2,128)}), f32[512,128,2]{0,2,1:T(2,128)S(1)}, u32[]{:S(2)}, u32[]{:S(2)}) %all-to-all-start) | async-done | bytes 524320 | tf_op jit(solution)/shard_map/all_to_all | solution.py:434
  30.2 1.4 %fusion.6.rest_0_.refs_0_ = f32[512,128]{1,0:T(8,128)} fusion(f32[512,256]{0,1:T(8,128)S(1)} %all_to_all.13, s32[256]{0:T(256)S(1)} %eq.61), kind=kOutput, calls=%fused_computation.12 | convolution fusion | flops 201359360 | bytes 787456 | tf_op jit(solution)/shard_map/dot_general | solution.py:435
  31.6 0.6 copy-done.8
  32.3 0.6 copy-done.5
  33.0 4.0 %shard_map.122 = (f32[3,8,32,256]{3,2,1,0:T(8,128)}, f32[296,128]{1,0:T(8,128)}, f32[296,128]{1,0:T(8,128)}, f32[152,128]{1,0:T(8,128)}, f32[152,128]{1,0:T(8,128)}) custom-call(f32[3,8,32,256]{3,2,1,0:T(8,128)} %vel_ref.1, f32[8,32,256]{2,1,0:T(8,128)} %refs_1_.1, f32[4,32,256]{2,1,0:T(8,128)} %copy-done.5, f32[4,32,256]{2,1,0:T(8,128)} %copy-done.4, ...), custom_call_target="tpu_custom_call" | custom-call | tf_op jit(solution)/shard_map/pallas_call | solution.py:235
  37.8 2.4 %collective-permute-start.7 = (f32[152,128]{1,0:T(8,128)}, f32[152,128]{1,0:T(8,128)S(1)}, u32[]{:S(2)}, u32[]{:S(2)}) collective-permute-start(f32[152,128]{1,0:T(8,128)} %get-tuple-element.18), channel_id=1, source_target_pairs={{1,0},{2,1},{3,2},{0,3},{5,4},{6,5},{7,6},{4,7},{9,8},{10,9},{11,1... | collective-permute-start | bytes 233480 | tf_op jit(solution)/shard_map/ppermute | solution.py:417
  40.1 2.0 %collective-permute-done.6.refs_4_ = f32[152,128]{1,0:T(8,128)S(1)} collective-permute-done((f32[152,128]{1,0:T(8,128)}, f32[152,128]{1,0:T(8,128)S(1)}, u32[]{:S(2)}, u32[]{:S(2)}) %collective-permute-start.6) | collective-permute-done | bytes 77856 | tf_op jit(solution)/shard_map/ppermute | solution.py:416
  42.2 0.6 copy-done.6
  42.9 4.0 %shard_map.123 = (f32[3,8,32,256]{3,2,1,0:T(8,128)}, bf16[3,8,32,256]{3,2,1,0:T(8,128)(2,1)}) custom-call(f32[3,8,32,256]{3,2,1,0:T(8,128)} %get-tuple-element.14.refs_0_, f32[8,32,256]{2,1,0:T(8,128)} %refs_1_.1, f32[296,128]{1,0:T(8,128)} %copy-done.2, f32[296,128]{1,0:T(8,128)} %copy-done.3, f32[152,128]{1,0:T(8,128)} %copy-done.6, f32[152,128]{1,0:T(8,128)} %copy-done.7, ...), custom_call_target="tpu_custom_call" | custom-call | tf_op jit(solution)/shard_map/pallas_call | solution.py:243
  46.9 1.2 %convolution_convert_fusion = bf16[768,256]{1,0:T(8,128)(2,1)S(1)} fusion(bf16[768,256]{1,0:T(8,128)(2,1)} %bitcast.48, bf16[256,256]{1,0:T(8,128)(2,1)S(1)} %copy-done.10), kind=kOutput, calls=%fused_computation.1 | convolution fusion | flops 100859904 | bytes 917504 | tf_op jit(solution)/shard_map/dot_general | solution.py:272
  48.1 0.6 reshape.50
  48.8 2.0 %copy.42 = bf16[3,1,8,4,8,8,32]{6,3,0,5,4,2,1:T(4,128)(2,1)S(1)} copy(bf16[3,1,8,4,8,8,32]{6,5,4,3,2,0,1:T(8,128)(2,1)S(1)} %reshape.50) | data formatting | bytes 786432 | tf_op jit(solution)/shard_map/reshape | solution.py:274
  50.8 0.9 reshape.51
  51.9 1.0 fusion.2
  52.9 3.0 %shard_map.124 = (f32[512,128]{1,0:T(8,128)}, f32[104,128]{1,0:T(8,128)}, f32[104,128]{1,0:T(8,128)}, f32[104,32]{1,0:T(8,128)}, f32[104,32]{1,0:T(8,128)}) custom-call(f32[512,128]{1,0:T(8,128)} %fusion.6.rest_0_.refs_0_, f32[384,128]{1,0:T(8,128)} %bitcast.43, f32[296,128]{1,0:T(8,128)} %copy-done.2, f32[296,128]{1,0:T(8,128)} %copy-done.3, ...), custom_call_target="tpu_custom_call" | custom-call | tf_op jit(solution)/shard_map/pallas_call | solution.py:392
  55.8 2.7 %collective-permute-start.8 = (f32[104,128]{1,0:T(8,128)}, f32[104,128]{1,0:T(8,128)S(1)}, u32[]{:S(2)}, u32[]{:S(2)}) collective-permute-start(f32[104,128]{1,0:T(8,128)} %get-tuple-element.22), channel_id=1, source_target_pairs={{0,4},{4,8},{8,12},{12,16},{16,20},{20,24},{24,28},{28,32},{32,36}... | collective-permute-start | bytes 159752 | tf_op jit(solution)/shard_map/ppermute | solution.py:414
  58.5 3.1 %collective-permute-start.9 = (f32[104,128]{1,0:T(8,128)}, f32[104,128]{1,0:T(8,128)S(1)}, u32[]{:S(2)}, u32[]{:S(2)}) collective-permute-start(f32[104,128]{1,0:T(8,128)} %get-tuple-element.23), channel_id=1, source_target_pairs={{4,0},{8,4},{12,8},{16,12},{20,16},{24,20},{28,24},{32,28},{36,32}... | collective-permute-start | bytes 159752 | tf_op jit(solution)/shard_map/ppermute | solution.py:415
  62.1 2.5 %collective-permute-start.11 = (f32[104,32]{1,0:T(8,128)}, f32[104,32]{1,0:T(8,128)S(1)}, u32[]{:S(2)}, u32[]{:S(2)}) collective-permute-start(f32[104,32]{1,0:T(8,128)} %get-tuple-element.25), channel_id=1, source_target_pairs={{1,0},{2,1},{3,2},{0,3},{5,4},{6,5},{7,6},{4,7},{9,8},{10,9},{11,1... | collective-permute-start | bytes 39944 | tf_op jit(solution)/shard_map/ppermute | solution.py:417
  64.6 1.7 %collective-permute-done.10.refs_4_ = f32[104,32]{1,0:T(8,128)S(1)} collective-permute-done((f32[104,32]{1,0:T(8,128)}, f32[104,32]{1,0:T(8,128)S(1)}, u32[]{:S(2)}, u32[]{:S(2)}) %collective-permute-start.10) | collective-permute-done | bytes 13344 | tf_op jit(solution)/shard_map/ppermute | solution.py:416
  66.4 0.6 copy-done.14
  67.0 2.7 %shard_map.125 = f32[512,128]{1,0:T(8,128)} custom-call(f32[512,128]{1,0:T(8,128)} %get-tuple-element.21.refs_0_, f32[384,128]{1,0:T(8,128)} %bitcast.44, f32[104,128]{1,0:T(8,128)} %copy-done.12, f32[104,128]{1,0:T(8,128)} %copy-done.13, f32[104,32]{1,0:T(8,128)} %copy-done.14, f32[104,32]{1,0:T(8,128)} %copy-done.15, f32[128,384]{1,0:T(8,128)} %constant.17.clone.refs_6_, ...), custom_call_target="tpu_custom_call" | custom-call | tf_op jit(solution)/shard_map/pallas_call | solution.py:392
  69.7 1.4 %fusion.5 = f32[512,256]{0,1:T(8,128)S(1)} fusion(f32[512,128]{1,0:T(8,128)} %shard_map.125, s32[256]{0:T(256)S(1)} %eq.61), kind=kOutput, calls=%fused_computation.11 | convolution fusion | flops 201359360 | bytes 787456 | tf_op jit(solution)/shard_map/dot_general | solution.py:449
  71.4 24.6 %all_to_all.18 = f32[512,128,2]{0,2,1:T(2,128)S(1)} all-to-all(f32[512,128,2]{0,2,1:T(2,128)S(1)} %all_to_all.14), channel_id=1, replica_groups=mesh['flow'=32,'grp'=4] {'flow','grp'}, dimensions={1} | all-to-all | bytes 1048576 | tf_op jit(solution)/shard_map/all_to_all | solution.py:450
  96.6 0.6 fusion
  97.2 0.9 copy.36
  (57 shorter events, 3.3 us)
Async XLA Ops:
  1.6 13.7 %copy-start = (f32[3,8,32,256]{3,2,1,0:T(8,128)S(1)}, f32[3,8,32,256]{3,2,1,0:T(8,128)}, u32[]{:S(2)}) copy-start(f32[3,8,32,256]{3,2,1,0:T(8,128)} %vel_ref.1) | copy-start | bytes 2359300
  1.7 13.7 %copy-start.1 = (f32[8,32,256]{2,1,0:T(8,128)S(1)}, f32[8,32,256]{2,1,0:T(8,128)}, u32[]{:S(2)}) copy-start(f32[8,32,256]{2,1,0:T(8,128)} %refs_1_.1) | copy-start | bytes 786436
  3.9 16.3 %copy-start.17 = (s32[1,128,2]{1,2,0:T(2,128)S(1)}, s32[1,128,2]{1,2,0:T(2,128)}, u32[]{:S(2)}) copy-start(s32[1,128,2]{1,2,0:T(2,128)} %param.15) | copy-start | bytes 3076
  3.9 26.0 %all-to-all-start = ((f32[512,128,2]{0,2,1:T(2,128)}), f32[512,128,2]{0,2,1:T(2,128)S(1)}, u32[]{:S(2)}, u32[]{:S(2)}) async-start(f32[512,128,2]{0,2,1:T(2,128)} %copy.31), calls=%async_computation | async-start | bytes 1048576 | tf_op jit(solution)/shard_map/all_to_all | solution.py:434
  15.4 16.2 %collective-permute-start.3 = (f32[4,8,1,256]{3,2,1,0:T(1,128)S(1)}, f32[4,8,1,256]{3,2,1,0:T(1,128)S(1)}, u32[]{:S(2)}, u32[]{:S(2)}) collective-permute-start(f32[4,8,1,256]{3,2,1,0:T(1,128)S(1)} %get-tuple-element.34), channel_id=1, source_target_pairs={{1,0},{2,1},{3,2},{0,3},{5,4},{6,5},{7,6},{4,7},{9,8},{10,9},{11,1... | collective-permute-start | bytes 98312 | tf_op jit(solution)/shard_map/ppermute | solution.py:260
  18.1 13.5 %collective-permute-start.2 = (f32[4,8,1,256]{3,2,1,0:T(1,128)S(1)}, f32[4,8,1,256]{3,2,1,0:T(1,128)S(1)}, u32[]{:S(2)}, u32[]{:S(2)}) collective-permute-start(f32[4,8,1,256]{3,2,1,0:T(1,128)S(1)} %get-tuple-element.35), channel_id=1, source_target_pairs={{0,1},{1,2},{2,3},{3,0},{4,5},{5,6},{6,7},{7,4},{8,9},{9,10},{10,1... | collective-permute-start | bytes 98312 | tf_op jit(solution)/shard_map/ppermute | solution.py:259
  18.1 13.5 %collective-permute-start.1 = (f32[4,32,256]{2,1,0:T(8,128)S(1)}, f32[4,32,256]{2,1,0:T(8,128)S(1)}, u32[]{:S(2)}, u32[]{:S(2)}) collective-permute-start(f32[4,32,256]{2,1,0:T(8,128)S(1)} %get-tuple-element.36), channel_id=1, source_target_pairs={{4,0},{8,4},{12,8},{16,12},{20,16},{24,20},{28,24},{32,28},{36,32}... | collective-permute-start | bytes 393224 | tf_op jit(solution)/shard_map/ppermute | solution.py:258
  18.8 12.8 %collective-permute-start = (f32[4,32,256]{2,1,0:T(8,128)S(1)}, f32[4,32,256]{2,1,0:T(8,128)S(1)}, u32[]{:S(2)}, u32[]{:S(2)}) collective-permute-start(f32[4,32,256]{2,1,0:T(8,128)S(1)} %get-tuple-element.37), channel_id=1, source_target_pairs={{0,4},{4,8},{8,12},{12,16},{16,20},{20,24},{24,28},{28,32},{32,36}... | collective-permute-start | bytes 393224 | tf_op jit(solution)/shard_map/ppermute | solution.py:257
  31.6 15.3 %copy-start.10 = (bf16[256,256]{1,0:T(8,128)(2,1)S(1)}, bf16[256,256]{1,0:T(8,128)(2,1)}, u32[]{:S(2)}) copy-start(bf16[256,256]{1,0:T(8,128)(2,1)} %constant.21.clone) | copy-start | bytes 393220
  31.6 0.6 copy-start.8
  31.6 0.6 copy-start.9
  31.6 0.7 copy-start.4
  32.3 0.7 copy-start.5
  37.0 5.2 %collective-permute-start.4 = (f32[296,128]{1,0:T(8,128)}, f32[296,128]{1,0:T(8,128)S(1)}, u32[]{:S(2)}, u32[]{:S(2)}) collective-permute-start(f32[296,128]{1,0:T(8,128)} %get-tuple-element.15), channel_id=1, source_target_pairs={{0,4},{4,8},{8,12},{12,16},{16,20},{20,24},{24,28},{28,32},{32,36}... | collective-permute-start | bytes 454664 | tf_op jit(solution)/shard_map/ppermute | solution.py:414
  37.3 4.9 %collective-permute-start.5 = (f32[296,128]{1,0:T(8,128)}, f32[296,128]{1,0:T(8,128)S(1)}, u32[]{:S(2)}, u32[]{:S(2)}) collective-permute-start(f32[296,128]{1,0:T(8,128)} %get-tuple-element.16), channel_id=1, source_target_pairs={{4,0},{8,4},{12,8},{16,12},{20,16},{24,20},{28,24},{32,28},{36,32}... | collective-permute-start | bytes 454664 | tf_op jit(solution)/shard_map/ppermute | solution.py:415
  37.5 4.7 %collective-permute-start.6 = (f32[152,128]{1,0:T(8,128)}, f32[152,128]{1,0:T(8,128)S(1)}, u32[]{:S(2)}, u32[]{:S(2)}) collective-permute-start(f32[152,128]{1,0:T(8,128)} %get-tuple-element.17), channel_id=1, source_target_pairs={{0,1},{1,2},{2,3},{3,0},{4,5},{5,6},{6,7},{7,4},{8,9},{9,10},{10,1... | collective-permute-start | bytes 233480 | tf_op jit(solution)/shard_map/ppermute | solution.py:416
  37.8 4.4 %collective-permute-start.7 = (f32[152,128]{1,0:T(8,128)}, f32[152,128]{1,0:T(8,128)S(1)}, u32[]{:S(2)}, u32[]{:S(2)}) collective-permute-start(f32[152,128]{1,0:T(8,128)} %get-tuple-element.18), channel_id=1, source_target_pairs={{1,0},{2,1},{3,2},{0,3},{5,4},{6,5},{7,6},{4,7},{9,8},{10,9},{11,1... | collective-permute-start | bytes 233480 | tf_op jit(solution)/shard_map/ppermute | solution.py:417
  42.1 0.6 copy-start.6
  42.1 0.7 copy-start.7
  42.1 0.7 copy-start.2
  42.2 0.8 copy-start.3
  50.8 1.1 %copy-start.11 = (bf16[125,512]{1,0:T(8,128)(2,1)S(1)}, bf16[125,512]{1,0:T(8,128)(2,1)}, u32[]{:S(2)}) copy-start(bf16[125,512]{1,0:T(8,128)(2,1)} %param.13) | copy-start | bytes 384004
  55.8 10.5 %collective-permute-start.8 = (f32[104,128]{1,0:T(8,128)}, f32[104,128]{1,0:T(8,128)S(1)}, u32[]{:S(2)}, u32[]{:S(2)}) collective-permute-start(f32[104,128]{1,0:T(8,128)} %get-tuple-element.22), channel_id=1, source_target_pairs={{0,4},{4,8},{8,12},{12,16},{16,20},{20,24},{24,28},{28,32},{32,36}... | collective-permute-start | bytes 159752 | tf_op jit(solution)/shard_map/ppermute | solution.py:414
  58.5 7.8 %collective-permute-start.9 = (f32[104,128]{1,0:T(8,128)}, f32[104,128]{1,0:T(8,128)S(1)}, u32[]{:S(2)}, u32[]{:S(2)}) collective-permute-start(f32[104,128]{1,0:T(8,128)} %get-tuple-element.23), channel_id=1, source_target_pairs={{4,0},{8,4},{12,8},{16,12},{20,16},{24,20},{28,24},{32,28},{36,32}... | collective-permute-start | bytes 159752 | tf_op jit(solution)/shard_map/ppermute | solution.py:415
  61.7 4.7 %collective-permute-start.10 = (f32[104,32]{1,0:T(8,128)}, f32[104,32]{1,0:T(8,128)S(1)}, u32[]{:S(2)}, u32[]{:S(2)}) collective-permute-start(f32[104,32]{1,0:T(8,128)} %get-tuple-element.24), channel_id=1, source_target_pairs={{0,1},{1,2},{2,3},{3,0},{4,5},{5,6},{6,7},{7,4},{8,9},{9,10},{10,1... | collective-permute-start | bytes 39944 | tf_op jit(solution)/shard_map/ppermute | solution.py:416
  62.1 4.3 %collective-permute-start.11 = (f32[104,32]{1,0:T(8,128)}, f32[104,32]{1,0:T(8,128)S(1)}, u32[]{:S(2)}, u32[]{:S(2)}) collective-permute-start(f32[104,32]{1,0:T(8,128)} %get-tuple-element.25), channel_id=1, source_target_pairs={{1,0},{2,1},{3,2},{0,3},{5,4},{6,5},{7,6},{4,7},{9,8},{10,9},{11,1... | collective-permute-start | bytes 39944 | tf_op jit(solution)/shard_map/ppermute | solution.py:417
  66.3 0.6 copy-start.14
  66.3 0.6 copy-start.15
  66.3 0.6 copy-start.12
  66.4 0.6 copy-start.13
  71.1 25.5 %copy-start.16 = (s32[1,128]{1,0:T(1,128)S(1)}, s32[1,128]{1,0:T(1,128)}, u32[]{:S(2)}) copy-start(s32[1,128]{1,0:T(1,128)} %param.16) | copy-start | bytes 1540

commit v18 on v16

--- a/solution.py
+++ b/solution.py
@@ -426,9 +426,9 @@
     place_hot = (placing[:, None] == jnp.arange(total_slots, dtype=jnp.int32)[None, :]).astype(jnp.float32)
     home_hot = (sending[:, None] == jnp.arange(elem_count, dtype=jnp.int32)[None, :]).astype(jnp.float32)
     padded_state = jnp.pad(acoustic_state, ((0, 0), (0, 3), (0, 0))).reshape(512, elem_count)
-    outgoing = jnp.dot(padded_state, place_hot, precision=HIGH)
+    outgoing = jnp.dot(padded_state, place_hot, precision=THREE_PASS)
     arrived = lax.all_to_all(outgoing, ("flow", "grp"), split_axis=1, concat_axis=1, tiled=True)
-    state = jnp.dot(arrived, home_hot, precision=HIGH)
+    state = jnp.dot(arrived, home_hot, precision=THREE_PASS)
 
     row_len = velocity.shape[3] // 8
     mats = [jnp.asarray(m) for m in dg_matrices()]
@@ -442,9 +442,9 @@
     state = res[0]
     recv = exchange_faces(res[1:])
     state = dg_step(state, source, recv, mats, False, row_len)[0]
-    leaving = lax.dot_general(state, home_hot, (((1,), (1,)), ((), ())), precision=HIGH)
+    leaving = lax.dot_general(state, home_hot, (((1,), (1,)), ((), ())), precision=THREE_PASS)
     returned = lax.all_to_all(leaving, ("flow", "grp"), split_axis=1, concat_axis=1, tiled=True)
-    acoustic_out = lax.dot_general(returned, place_hot, (((1,), (1,)), ((), ())), precision=HIGH)
+    acoustic_out = lax.dot_general(returned, place_hot, (((1,), (1,)), ((), ())), precision=THREE_PASS)
     acoustic_out = acoustic_out.reshape(4, 128, elem_count)[:, :125]
     return (vel, acoustic_out)
 

time: 98.6 us -> 98.2 us (level)
  no operation moved by 1% of the time
where the time goes in v18:
time: 98.2 us; the launch traced here: 97.8 us
  starting transfers between devices  28.1 us (29%)
  blocking collectives  24.6 us (25%)
  Pallas kernels  13.7 us (14%)
  waiting for transfers between devices  13.2 us (13%)
  local copies, waits for them, and re-layouts  10.7 us (11%)
  matrix products  6.34 us (6%)
    all_to_all x1, blocking collectives, body(): lax.all_to_all(leaving, ('flow', 'grp'), split_axis=1, concat_axis=1, til...  24.6 us
    all_to_all x1, starting transfers between devices, body(): lax.all_to_all(outgoing, ('flow', 'grp'), split_axis=1, concat_axis=1, ti...  11.5 us
    all_to_all x1, waiting for transfers between devices, body(): lax.all_to_all(outgoing, ('flow', 'grp'), split_axis=1, concat_axis=1, ti...  9.44 us
    pallas_call x2, Pallas kernels, dg_step(): pl.pallas_call(lambda *refs: dg_step_kernel(want_faces, xoff, yoff, row_l...  5.67 us
    ppermute x2, starting transfers between devices, exchange_faces(): lax.ppermute(sy0, 'grp', down_g)  4.77 us
    unnamed x39, local copies, waits for them, and re-layouts  4.68 us
    pallas_call x1, Pallas kernels, les_section_first(): pl.pallas_call(lambda *refs: les_kernel(0, lax.axis_size('flow'), lax.axi...  4.13 us
    pallas_call x1, Pallas kernels, les_section_last(): pl.pallas_call(lambda *refs: les_kernel(1, lax.axis_size('flow'), lax.axi...  3.95 us
  transfers between devices with their start and end apart: 13, of which 3 were waited for; matrix products, arithmetic and copies ran while one was open for 2% of the time, Pallas kernels for 0%

profile of v18, /device:TPU:1, one launch (start us, length us, event | category | flops | bytes accessed | tf_op | source)
XLA Modules:
  0.0 97.8 jit_solution(11408965076287410853)
XLA Ops:
  0.6 1.0 copy.37
  1.7 1.1 %fusion.9 = f32[512,128,2]{1,0,2:T(8,128)S(1)} fusion(f32[512,128,1]{1,0,2:T(8,128)S(1)} %bitcast.47, s32[128,2]{0,1:T(2,128)S(1)} %multiply_add_fusion, s32[128]{0:T(128)} %bitcast.49), kind=kOutput, calls=%fused_computation.14 | convolution fusion | flops 100696064 | bytes 787968 | tf_op jit(solution)/shard_map/dot_general | solution.py:429
  2.8 1.0 %copy.31 = f32[512,128,2]{0,2,1:T(2,128)} copy(f32[512,128,2]{1,0,2:T(8,128)S(1)} %fusion.9) | data formatting | bytes 1048576 | tf_op jit(solution)/shard_map/dot_general | solution.py:429
  3.8 11.5 %all-to-all-start = ((f32[512,128,2]{0,2,1:T(2,128)}), f32[512,128,2]{0,2,1:T(2,128)S(1)}, u32[]{:S(2)}, u32[]{:S(2)}) async-start(f32[512,128,2]{0,2,1:T(2,128)} %copy.31), calls=%async_computation | async-start | bytes 1048576 | tf_op jit(solution)/shard_map/all_to_all | solution.py:430
  15.4 2.7 %collective-permute-start.3 = (f32[4,8,1,256]{3,2,1,0:T(1,128)S(1)}, f32[4,8,1,256]{3,2,1,0:T(1,128)S(1)}, u32[]{:S(2)}, u32[]{:S(2)}) collective-permute-start(f32[4,8,1,256]{3,2,1,0:T(1,128)S(1)} %get-tuple-element.34), channel_id=1, source_target_pairs={{1,0},{2,1},{3,2},{0,3},{5,4},{6,5},{7,6},{4,7},{9,8},{10,9},{11,1... | collective-permute-start | bytes 98312 | tf_op jit(solution)/shard_map/ppermute | solution.py:256
  18.1 0.7 collective-permute-start.1
  18.8 1.3 %collective-permute-start = (f32[4,32,256]{2,1,0:T(8,128)S(1)}, f32[4,32,256]{2,1,0:T(8,128)S(1)}, u32[]{:S(2)}, u32[]{:S(2)}) collective-permute-start(f32[4,32,256]{2,1,0:T(8,128)S(1)} %get-tuple-element.37), channel_id=1, source_target_pairs={{0,4},{4,8},{8,12},{12,16},{16,20},{20,24},{24,28},{28,32},{32,36}... | collective-permute-start | bytes 393224 | tf_op jit(solution)/shard_map/ppermute | solution.py:253
  20.4 9.4 %all-to-all-done = f32[512,128,2]{0,2,1:T(2,128)S(1)} async-done(((f32[512,128,2]{0,2,1:T(2,128)}), f32[512,128,2]{0,2,1:T(2,128)S(1)}, u32[]{:S(2)}, u32[]{:S(2)}) %all-to-all-start) | async-done | bytes 524320 | tf_op jit(solution)/shard_map/all_to_all | solution.py:430
  30.2 1.2 %fusion.6.refs_10_.refs_0_ = f32[512,128]{1,0:T(8,128)} fusion(f32[512,256]{0,1:T(8,128)S(1)} %all_to_all.13, s32[256]{0:T(256)S(1)} %eq.61), kind=kOutput, calls=%fused_computation.12 | convolution fusion | flops 100696064 | bytes 787456 | tf_op jit(solution)/shard_map/dot_general | solution.py:431
  31.4 0.6 copy-done.8
  32.1 0.6 copy-done.3
  32.7 4.1 %shard_map.122 = (f32[3,8,32,256]{3,2,1,0:T(8,128)}, f32[296,128]{1,0:T(8,128)}, f32[296,128]{1,0:T(8,128)}, f32[152,128]{1,0:T(8,128)}, f32[152,128]{1,0:T(8,128)}) custom-call(f32[3,8,32,256]{3,2,1,0:T(8,128)} %refs_0_.1, f32[8,32,256]{2,1,0:T(8,128)} %refs_1_.3, f32[4,32,256]{2,1,0:T(8,128)} %copy-done.3, f32[4,32,256]{2,1,0:T(8,128)} %copy-done.2, ...), custom_call_target="tpu_custom_call" | custom-call | tf_op jit(solution)/shard_map/pallas_call | solution.py:231
  37.7 2.4 %collective-permute-start.7 = (f32[152,128]{1,0:T(8,128)}, f32[152,128]{1,0:T(8,128)S(1)}, u32[]{:S(2)}, u32[]{:S(2)}) collective-permute-start(f32[152,128]{1,0:T(8,128)} %get-tuple-element.18), channel_id=1, source_target_pairs={{1,0},{2,1},{3,2},{0,3},{5,4},{6,5},{7,6},{4,7},{9,8},{10,9},{11,1... | collective-permute-start | bytes 233480 | tf_op jit(solution)/shard_map/ppermute | solution.py:413
  40.1 2.0 %collective-permute-done.6.refs_4_ = f32[152,128]{1,0:T(8,128)S(1)} collective-permute-done((f32[152,128]{1,0:T(8,128)}, f32[152,128]{1,0:T(8,128)S(1)}, u32[]{:S(2)}, u32[]{:S(2)}) %collective-permute-start.6) | collective-permute-done | bytes 77856 | tf_op jit(solution)/shard_map/ppermute | solution.py:412
  42.1 0.6 copy-done.6
  42.8 4.0 %shard_map.123 = (f32[3,8,32,256]{3,2,1,0:T(8,128)}, bf16[3,8,32,256]{3,2,1,0:T(8,128)(2,1)}) custom-call(f32[3,8,32,256]{3,2,1,0:T(8,128)} %get-tuple-element.14.refs_0_, f32[8,32,256]{2,1,0:T(8,128)} %refs_1_.3, f32[296,128]{1,0:T(8,128)} %copy-done.4, f32[296,128]{1,0:T(8,128)} %copy-done.5, f32[152,128]{1,0:T(8,128)} %copy-done.6, f32[152,128]{1,0:T(8,128)} %copy-done.7, ...), custom_call_target="tpu_custom_call" | custom-call | tf_op jit(solution)/shard_map/pallas_call | solution.py:239
  46.8 1.3 %convolution_convert_fusion = bf16[768,256]{1,0:T(8,128)(2,1)S(1)} fusion(bf16[768,256]{1,0:T(8,128)(2,1)} %bitcast.48, bf16[256,256]{1,0:T(8,128)(2,1)S(1)} %copy-done.10), kind=kOutput, calls=%fused_computation.1 | convolution fusion | flops 100859904 | bytes 917504 | tf_op jit(solution)/shard_map/dot_general | solution.py:268
  48.1 0.6 reshape.50
  48.7 2.0 %copy.42 = bf16[3,1,8,4,8,8,32]{6,3,0,5,4,2,1:T(4,128)(2,1)S(1)} copy(bf16[3,1,8,4,8,8,32]{6,5,4,3,2,0,1:T(8,128)(2,1)S(1)} %reshape.50) | data formatting | bytes 786432 | tf_op jit(solution)/shard_map/reshape | solution.py:270
  50.7 0.9 reshape.51
  51.8 1.0 fusion.2
  52.8 2.9 %shard_map.124 = (f32[512,128]{1,0:T(8,128)}, f32[104,128]{1,0:T(8,128)}, f32[104,128]{1,0:T(8,128)}, f32[104,32]{1,0:T(8,128)}, f32[104,32]{1,0:T(8,128)}) custom-call(f32[512,128]{1,0:T(8,128)} %fusion.6.refs_10_.refs_0_, f32[384,128]{1,0:T(8,128)} %bitcast.43, f32[296,128]{1,0:T(8,128)} %copy-done.4, f32[296,128]{1,0:T(8,128)} %copy-done.5, ...), custom_call_target="tpu_custom_call" | custom-call | tf_op jit(solution)/shard_map/pallas_call | solution.py:388
  55.7 2.7 %collective-permute-start.8 = (f32[104,128]{1,0:T(8,128)}, f32[104,128]{1,0:T(8,128)S(1)}, u32[]{:S(2)}, u32[]{:S(2)}) collective-permute-start(f32[104,128]{1,0:T(8,128)} %get-tuple-element.22), channel_id=1, source_target_pairs={{0,4},{4,8},{8,12},{12,16},{16,20},{20,24},{24,28},{28,32},{32,36}... | collective-permute-start | bytes 159752 | tf_op jit(solution)/shard_map/ppermute | solution.py:410
  58.4 3.1 %collective-permute-start.9 = (f32[104,128]{1,0:T(8,128)}, f32[104,128]{1,0:T(8,128)S(1)}, u32[]{:S(2)}, u32[]{:S(2)}) collective-permute-start(f32[104,128]{1,0:T(8,128)} %get-tuple-element.23), channel_id=1, source_target_pairs={{4,0},{8,4},{12,8},{16,12},{20,16},{24,20},{28,24},{32,28},{36,32}... | collective-permute-start | bytes 159752 | tf_op jit(solution)/shard_map/ppermute | solution.py:411
  61.6 0.5 collective-permute-start.10
  62.1 2.4 %collective-permute-start.11 = (f32[104,32]{1,0:T(8,128)}, f32[104,32]{1,0:T(8,128)S(1)}, u32[]{:S(2)}, u32[]{:S(2)}) collective-permute-start(f32[104,32]{1,0:T(8,128)} %get-tuple-element.25), channel_id=1, source_target_pairs={{1,0},{2,1},{3,2},{0,3},{5,4},{6,5},{7,6},{4,7},{9,8},{10,9},{11,1... | collective-permute-start | bytes 39944 | tf_op jit(solution)/shard_map/ppermute | solution.py:413
  64.5 1.7 %collective-permute-done.10.refs_4_ = f32[104,32]{1,0:T(8,128)S(1)} collective-permute-done((f32[104,32]{1,0:T(8,128)}, f32[104,32]{1,0:T(8,128)S(1)}, u32[]{:S(2)}, u32[]{:S(2)}) %collective-permute-start.10) | collective-permute-done | bytes 13344 | tf_op jit(solution)/shard_map/ppermute | solution.py:412
  66.3 0.6 copy-done.14
  66.9 2.7 %shard_map.125 = f32[512,128]{1,0:T(8,128)} custom-call(f32[512,128]{1,0:T(8,128)} %get-tuple-element.21.refs_0_, f32[384,128]{1,0:T(8,128)} %bitcast.44, f32[104,128]{1,0:T(8,128)} %copy-done.12, f32[104,128]{1,0:T(8,128)} %copy-done.13, f32[104,32]{1,0:T(8,128)} %copy-done.14, f32[104,32]{1,0:T(8,128)} %copy-done.15, f32[128,384]{1,0:T(8,128)} %constant.17.clone.refs_6_, ...), custom_call_target="tpu_custom_call" | custom-call | tf_op jit(solution)/shard_map/pallas_call | solution.py:388
  69.6 1.3 %fusion.5 = f32[512,256]{0,1:T(8,128)S(1)} fusion(f32[512,128]{1,0:T(8,128)} %shard_map.125, s32[256]{0:T(256)S(1)} %eq.61), kind=kOutput, calls=%fused_computation.11 | convolution fusion | flops 100696064 | bytes 787456 | tf_op jit(solution)/shard_map/dot_general | solution.py:445
  71.2 24.6 %all_to_all.18 = f32[512,128,2]{0,2,1:T(2,128)S(1)} all-to-all(f32[512,128,2]{0,2,1:T(2,128)S(1)} %all_to_all.14), channel_id=1, replica_groups=mesh['flow'=32,'grp'=4] {'flow','grp'}, dimensions={1} | all-to-all | bytes 1048576 | tf_op jit(solution)/shard_map/all_to_all | solution.py:446
  96.9 0.9 copy.36
  (57 shorter events, 3.4 us)
Async XLA Ops:
  1.6 13.7 %copy-start = (f32[3,8,32,256]{3,2,1,0:T(8,128)S(1)}, f32[3,8,32,256]{3,2,1,0:T(8,128)}, u32[]{:S(2)}) copy-start(f32[3,8,32,256]{3,2,1,0:T(8,128)} %refs_0_.1) | copy-start | bytes 2359300
  1.7 13.7 %copy-start.1 = (f32[8,32,256]{2,1,0:T(8,128)S(1)}, f32[8,32,256]{2,1,0:T(8,128)}, u32[]{:S(2)}) copy-start(f32[8,32,256]{2,1,0:T(8,128)} %refs_1_.3) | copy-start | bytes 786436
  3.8 16.3 %copy-start.17 = (s32[1,128,2]{1,2,0:T(2,128)S(1)}, s32[1,128,2]{1,2,0:T(2,128)}, u32[]{:S(2)}) copy-start(s32[1,128,2]{1,2,0:T(2,128)} %param.15) | copy-start | bytes 3076
  3.8 26.0 %all-to-all-start = ((f32[512,128,2]{0,2,1:T(2,128)}), f32[512,128,2]{0,2,1:T(2,128)S(1)}, u32[]{:S(2)}, u32[]{:S(2)}) async-start(f32[512,128,2]{0,2,1:T(2,128)} %copy.31), calls=%async_computation | async-start | bytes 1048576 | tf_op jit(solution)/shard_map/all_to_all | solution.py:430
  15.4 16.0 %collective-permute-start.3 = (f32[4,8,1,256]{3,2,1,0:T(1,128)S(1)}, f32[4,8,1,256]{3,2,1,0:T(1,128)S(1)}, u32[]{:S(2)}, u32[]{:S(2)}) collective-permute-start(f32[4,8,1,256]{3,2,1,0:T(1,128)S(1)} %get-tuple-element.34), channel_id=1, source_target_pairs={{1,0},{2,1},{3,2},{0,3},{5,4},{6,5},{7,6},{4,7},{9,8},{10,9},{11,1... | collective-permute-start | bytes 98312 | tf_op jit(solution)/shard_map/ppermute | solution.py:256
  18.0 13.3 %collective-permute-start.2 = (f32[4,8,1,256]{3,2,1,0:T(1,128)S(1)}, f32[4,8,1,256]{3,2,1,0:T(1,128)S(1)}, u32[]{:S(2)}, u32[]{:S(2)}) collective-permute-start(f32[4,8,1,256]{3,2,1,0:T(1,128)S(1)} %get-tuple-element.35), channel_id=1, source_target_pairs={{0,1},{1,2},{2,3},{3,0},{4,5},{5,6},{6,7},{7,4},{8,9},{9,10},{10,1... | collective-permute-start | bytes 98312 | tf_op jit(solution)/shard_map/ppermute | solution.py:255
  18.1 13.3 %collective-permute-start.1 = (f32[4,32,256]{2,1,0:T(8,128)S(1)}, f32[4,32,256]{2,1,0:T(8,128)S(1)}, u32[]{:S(2)}, u32[]{:S(2)}) collective-permute-start(f32[4,32,256]{2,1,0:T(8,128)S(1)} %get-tuple-element.36), channel_id=1, source_target_pairs={{4,0},{8,4},{12,8},{16,12},{20,16},{24,20},{28,24},{32,28},{36,32}... | collective-permute-start | bytes 393224 | tf_op jit(solution)/shard_map/ppermute | solution.py:254
  18.8 12.6 %collective-permute-start = (f32[4,32,256]{2,1,0:T(8,128)S(1)}, f32[4,32,256]{2,1,0:T(8,128)S(1)}, u32[]{:S(2)}, u32[]{:S(2)}) collective-permute-start(f32[4,32,256]{2,1,0:T(8,128)S(1)} %get-tuple-element.37), channel_id=1, source_target_pairs={{0,4},{4,8},{8,12},{12,16},{16,20},{20,24},{24,28},{28,32},{32,36}... | collective-permute-start | bytes 393224 | tf_op jit(solution)/shard_map/ppermute | solution.py:253
  31.4 15.4 %copy-start.10 = (bf16[256,256]{1,0:T(8,128)(2,1)S(1)}, bf16[256,256]{1,0:T(8,128)(2,1)}, u32[]{:S(2)}) copy-start(bf16[256,256]{1,0:T(8,128)(2,1)} %constant.21.clone) | copy-start | bytes 393220
  31.4 0.6 copy-start.8
  31.4 0.6 copy-start.9
  31.4 0.7 copy-start.2
  32.1 0.7 copy-start.3
  36.9 5.2 %collective-permute-start.4 = (f32[296,128]{1,0:T(8,128)}, f32[296,128]{1,0:T(8,128)S(1)}, u32[]{:S(2)}, u32[]{:S(2)}) collective-permute-start(f32[296,128]{1,0:T(8,128)} %get-tuple-element.15), channel_id=1, source_target_pairs={{0,4},{4,8},{8,12},{12,16},{16,20},{20,24},{24,28},{28,32},{32,36}... | collective-permute-start | bytes 454664 | tf_op jit(solution)/shard_map/ppermute | solution.py:410
  37.2 4.9 %collective-permute-start.5 = (f32[296,128]{1,0:T(8,128)}, f32[296,128]{1,0:T(8,128)S(1)}, u32[]{:S(2)}, u32[]{:S(2)}) collective-permute-start(f32[296,128]{1,0:T(8,128)} %get-tuple-element.16), channel_id=1, source_target_pairs={{4,0},{8,4},{12,8},{16,12},{20,16},{24,20},{28,24},{32,28},{36,32}... | collective-permute-start | bytes 454664 | tf_op jit(solution)/shard_map/ppermute | solution.py:411
  37.4 4.7 %collective-permute-start.6 = (f32[152,128]{1,0:T(8,128)}, f32[152,128]{1,0:T(8,128)S(1)}, u32[]{:S(2)}, u32[]{:S(2)}) collective-permute-start(f32[152,128]{1,0:T(8,128)} %get-tuple-element.17), channel_id=1, source_target_pairs={{0,1},{1,2},{2,3},{3,0},{4,5},{5,6},{6,7},{7,4},{8,9},{9,10},{10,1... | collective-permute-start | bytes 233480 | tf_op jit(solution)/shard_map/ppermute | solution.py:412
  37.7 4.4 %collective-permute-start.7 = (f32[152,128]{1,0:T(8,128)}, f32[152,128]{1,0:T(8,128)S(1)}, u32[]{:S(2)}, u32[]{:S(2)}) collective-permute-start(f32[152,128]{1,0:T(8,128)} %get-tuple-element.18), channel_id=1, source_target_pairs={{1,0},{2,1},{3,2},{0,3},{5,4},{6,5},{7,6},{4,7},{9,8},{10,9},{11,1... | collective-permute-start | bytes 233480 | tf_op jit(solution)/shard_map/ppermute | solution.py:413
  42.0 0.6 copy-start.6
  42.0 0.7 copy-start.7
  42.1 0.7 copy-start.4
  42.1 0.8 copy-start.5
  50.7 1.1 %copy-start.11 = (bf16[125,512]{1,0:T(8,128)(2,1)S(1)}, bf16[125,512]{1,0:T(8,128)(2,1)}, u32[]{:S(2)}) copy-start(bf16[125,512]{1,0:T(8,128)(2,1)} %param.13) | copy-start | bytes 384004
  55.7 10.5 %collective-permute-start.8 = (f32[104,128]{1,0:T(8,128)}, f32[104,128]{1,0:T(8,128)S(1)}, u32[]{:S(2)}, u32[]{:S(2)}) collective-permute-start(f32[104,128]{1,0:T(8,128)} %get-tuple-element.22), channel_id=1, source_target_pairs={{0,4},{4,8},{8,12},{12,16},{16,20},{20,24},{24,28},{28,32},{32,36}... | collective-permute-start | bytes 159752 | tf_op jit(solution)/shard_map/ppermute | solution.py:410
  58.4 7.8 %collective-permute-start.9 = (f32[104,128]{1,0:T(8,128)}, f32[104,128]{1,0:T(8,128)S(1)}, u32[]{:S(2)}, u32[]{:S(2)}) collective-permute-start(f32[104,128]{1,0:T(8,128)} %get-tuple-element.23), channel_id=1, source_target_pairs={{4,0},{8,4},{12,8},{16,12},{20,16},{24,20},{28,24},{32,28},{36,32}... | collective-permute-start | bytes 159752 | tf_op jit(solution)/shard_map/ppermute | solution.py:411
  61.6 4.7 %collective-permute-start.10 = (f32[104,32]{1,0:T(8,128)}, f32[104,32]{1,0:T(8,128)S(1)}, u32[]{:S(2)}, u32[]{:S(2)}) collective-permute-start(f32[104,32]{1,0:T(8,128)} %get-tuple-element.24), channel_id=1, source_target_pairs={{0,1},{1,2},{2,3},{3,0},{4,5},{5,6},{6,7},{7,4},{8,9},{9,10},{10,1... | collective-permute-start | bytes 39944 | tf_op jit(solution)/shard_map/ppermute | solution.py:412
  62.1 4.1 %collective-permute-start.11 = (f32[104,32]{1,0:T(8,128)}, f32[104,32]{1,0:T(8,128)S(1)}, u32[]{:S(2)}, u32[]{:S(2)}) collective-permute-start(f32[104,32]{1,0:T(8,128)} %get-tuple-element.25), channel_id=1, source_target_pairs={{1,0},{2,1},{3,2},{0,3},{5,4},{6,5},{7,6},{4,7},{9,8},{10,9},{11,1... | collective-permute-start | bytes 39944 | tf_op jit(solution)/shard_map/ppermute | solution.py:413
  66.2 0.6 copy-start.14
  66.2 0.6 copy-start.15
  66.2 0.6 copy-start.12
  66.3 0.6 copy-start.13
  70.9 25.5 %copy-start.16 = (s32[1,128]{1,0:T(1,128)S(1)}, s32[1,128]{1,0:T(1,128)}, u32[]{:S(2)}) copy-start(s32[1,128]{1,0:T(1,128)} %param.16) | copy-start | bytes 1540

commit v19 on v18

--- a/solution.py
+++ b/solution.py
@@ -215,7 +215,7 @@
         yrows = 3 * 2 * size_x
         elems = state_ref.shape[1]
         row_len = size_z // 8
-        face_ref[...] = jnp.zeros(face_ref.shape, jnp.float32)
+        face_ref[:, pl.ds(100, FACE_ROWS - 100), :] = jnp.zeros((6, FACE_ROWS - 100, face_ref.shape[2]), jnp.float32)
         extract_faces(state_ref, face_ref)
         mxup_ref[pl.ds(xrows, FACE_ROWS), :] = face_ref[1]
         mxdn_ref[pl.ds(xrows, FACE_ROWS), :] = face_ref[0]
@@ -301,7 +301,7 @@
 
 
 def dg_faces_kernel(state_ref, sx0_ref, sx4_ref, sy0_ref, sy4_ref, face_ref):
-    face_ref[...] = jnp.zeros(face_ref.shape, jnp.float32)
+    face_ref[:, pl.ds(100, FACE_ROWS - 100), :] = jnp.zeros((6, FACE_ROWS - 100, face_ref.shape[2]), jnp.float32)
     extract_faces(state_ref, face_ref)
     send_faces(face_ref, sx0_ref, sx4_ref, sy0_ref, sy4_ref, sy0_ref.shape[1])
 
@@ -315,8 +315,7 @@
     elems = state_ref.shape[1]
     lane = lax.broadcasted_iota(jnp.int32, (FACE_ROWS, elems), 1)
     ez = lane % row_len
-    face_ref[...] = jnp.zeros(face_ref.shape, jnp.float32)
-    oth_ref[...] = jnp.zeros(oth_ref.shape, jnp.float32)
+    face_ref[:, pl.ds(100, FACE_ROWS - 100), :] = jnp.zeros((6, FACE_ROWS - 100, face_ref.shape[2]), jnp.float32)
     extract_faces(state_ref, face_ref)
     flow_i = lax.axis_index("flow")
     grp_i = lax.axis_index("grp")

time: 98.2 us -> 98.2 us (level)
  no operation moved by 1% of the time
where the time goes in v19:
time: 98.2 us; the launch traced here: 97.7 us
  starting transfers between devices  28.2 us (29%)
  blocking collectives  24.6 us (25%)
  Pallas kernels  13.7 us (14%)
  waiting for transfers between devices  13.2 us (13%)
  local copies, waits for them, and re-layouts  10.7 us (11%)
  matrix products  6.33 us (6%)
    all_to_all x1, blocking collectives, body(): lax.all_to_all(leaving, ('flow', 'grp'), split_axis=1, concat_axis=1, til...  24.6 us
    all_to_all x1, starting transfers between devices, body(): lax.all_to_all(outgoing, ('flow', 'grp'), split_axis=1, concat_axis=1, ti...  11.5 us
    all_to_all x1, waiting for transfers between devices, body(): lax.all_to_all(outgoing, ('flow', 'grp'), split_axis=1, concat_axis=1, ti...  9.44 us
    pallas_call x2, Pallas kernels, dg_step(): pl.pallas_call(lambda *refs: dg_step_kernel(want_faces, xoff, yoff, row_l...  5.65 us
    ppermute x2, starting transfers between devices, exchange_faces(): lax.ppermute(sy0, 'grp', down_g)  4.79 us
    unnamed x39, local copies, waits for them, and re-layouts  4.68 us
    pallas_call x1, Pallas kernels, les_section_first(): pl.pallas_call(lambda *refs: les_kernel(0, lax.axis_size('flow'), lax.axi...  4.12 us
    pallas_call x1, Pallas kernels, les_section_last(): pl.pallas_call(lambda *refs: les_kernel(1, lax.axis_size('flow'), lax.axi...  3.95 us
  transfers between devices with their start and end apart: 13, of which 3 were waited for; matrix products, arithmetic and copies ran while one was open for 2% of the time, Pallas kernels for 0%

profile of v19, /device:TPU:1, one launch (start us, length us, event | category | flops | bytes accessed | tf_op | source)
XLA Modules:
  0.0 97.7 jit_solution(6737175540217064052)
XLA Ops:
  0.6 1.0 copy.37
  1.7 1.1 %fusion.9 = f32[512,128,2]{1,0,2:T(8,128)S(1)} fusion(f32[512,128,1]{1,0,2:T(8,128)S(1)} %bitcast.47, s32[128,2]{0,1:T(2,128)S(1)} %multiply_add_fusion, s32[128]{0:T(128)} %bitcast.49), kind=kOutput, calls=%fused_computation.14 | convolution fusion | flops 100696064 | bytes 787968 | tf_op jit(solution)/shard_map/dot_general | solution.py:428
  2.8 1.0 %copy.31 = f32[512,128,2]{0,2,1:T(2,128)} copy(f32[512,128,2]{1,0,2:T(8,128)S(1)} %fusion.9) | data formatting | bytes 1048576 | tf_op jit(solution)/shard_map/dot_general | solution.py:428
  3.8 11.5 %all-to-all-start = ((f32[512,128,2]{0,2,1:T(2,128)}), f32[512,128,2]{0,2,1:T(2,128)S(1)}, u32[]{:S(2)}, u32[]{:S(2)}) async-start(f32[512,128,2]{0,2,1:T(2,128)} %copy.31), calls=%async_computation | async-start | bytes 1048576 | tf_op jit(solution)/shard_map/all_to_all | solution.py:429
  15.4 2.7 %collective-permute-start.3 = (f32[4,8,1,256]{3,2,1,0:T(1,128)S(1)}, f32[4,8,1,256]{3,2,1,0:T(1,128)S(1)}, u32[]{:S(2)}, u32[]{:S(2)}) collective-permute-start(f32[4,8,1,256]{3,2,1,0:T(1,128)S(1)} %get-tuple-element.34), channel_id=1, source_target_pairs={{1,0},{2,1},{3,2},{0,3},{5,4},{6,5},{7,6},{4,7},{9,8},{10,9},{11,1... | collective-permute-start | bytes 98312 | tf_op jit(solution)/shard_map/ppermute | solution.py:256
  18.1 0.7 collective-permute-start.1
  18.8 1.3 %collective-permute-start = (f32[4,32,256]{2,1,0:T(8,128)S(1)}, f32[4,32,256]{2,1,0:T(8,128)S(1)}, u32[]{:S(2)}, u32[]{:S(2)}) collective-permute-start(f32[4,32,256]{2,1,0:T(8,128)S(1)} %get-tuple-element.37), channel_id=1, source_target_pairs={{0,4},{4,8},{8,12},{12,16},{16,20},{20,24},{24,28},{28,32},{32,36}... | collective-permute-start | bytes 393224 | tf_op jit(solution)/shard_map/ppermute | solution.py:253
  20.4 9.4 %all-to-all-done = f32[512,128,2]{0,2,1:T(2,128)S(1)} async-done(((f32[512,128,2]{0,2,1:T(2,128)}), f32[512,128,2]{0,2,1:T(2,128)S(1)}, u32[]{:S(2)}, u32[]{:S(2)}) %all-to-all-start) | async-done | bytes 524320 | tf_op jit(solution)/shard_map/all_to_all | solution.py:429
  30.2 1.2 %fusion.6.refs_10_.refs_0_ = f32[512,128]{1,0:T(8,128)} fusion(f32[512,256]{0,1:T(8,128)S(1)} %all_to_all.13, s32[256]{0:T(256)S(1)} %eq.61), kind=kOutput, calls=%fused_computation.12 | convolution fusion | flops 100696064 | bytes 787456 | tf_op jit(solution)/shard_map/dot_general | solution.py:430
  31.4 0.6 copy-done.8
  32.1 0.6 copy-done.3
  32.7 4.1 %shard_map.122 = (f32[3,8,32,256]{3,2,1,0:T(8,128)}, f32[296,128]{1,0:T(8,128)}, f32[296,128]{1,0:T(8,128)}, f32[152,128]{1,0:T(8,128)}, f32[152,128]{1,0:T(8,128)}) custom-call(f32[3,8,32,256]{3,2,1,0:T(8,128)} %refs_0_.1, f32[8,32,256]{2,1,0:T(8,128)} %refs_1_.3, f32[4,32,256]{2,1,0:T(8,128)} %copy-done.3, f32[4,32,256]{2,1,0:T(8,128)} %copy-done.2, ...), custom_call_target="tpu_custom_call" | custom-call | tf_op jit(solution)/shard_map/pallas_call | solution.py:231
  37.7 2.4 %collective-permute-start.7 = (f32[152,128]{1,0:T(8,128)}, f32[152,128]{1,0:T(8,128)S(1)}, u32[]{:S(2)}, u32[]{:S(2)}) collective-permute-start(f32[152,128]{1,0:T(8,128)} %get-tuple-element.18), channel_id=1, source_target_pairs={{1,0},{2,1},{3,2},{0,3},{5,4},{6,5},{7,6},{4,7},{9,8},{10,9},{11,1... | collective-permute-start | bytes 233480 | tf_op jit(solution)/shard_map/ppermute | solution.py:412
  40.0 2.0 %collective-permute-done.6.refs_4_ = f32[152,128]{1,0:T(8,128)S(1)} collective-permute-done((f32[152,128]{1,0:T(8,128)}, f32[152,128]{1,0:T(8,128)S(1)}, u32[]{:S(2)}, u32[]{:S(2)}) %collective-permute-start.6) | collective-permute-done | bytes 77856 | tf_op jit(solution)/shard_map/ppermute | solution.py:411
  42.1 0.6 copy-done.6
  42.8 4.0 %shard_map.123 = (f32[3,8,32,256]{3,2,1,0:T(8,128)}, bf16[3,8,32,256]{3,2,1,0:T(8,128)(2,1)}) custom-call(f32[3,8,32,256]{3,2,1,0:T(8,128)} %get-tuple-element.14.refs_0_, f32[8,32,256]{2,1,0:T(8,128)} %refs_1_.3, f32[296,128]{1,0:T(8,128)} %copy-done.4, f32[296,128]{1,0:T(8,128)} %copy-done.5, f32[152,128]{1,0:T(8,128)} %copy-done.6, f32[152,128]{1,0:T(8,128)} %copy-done.7, ...), custom_call_target="tpu_custom_call" | custom-call | tf_op jit(solution)/shard_map/pallas_call | solution.py:239
  46.8 1.3 %convolution_convert_fusion = bf16[768,256]{1,0:T(8,128)(2,1)S(1)} fusion(bf16[768,256]{1,0:T(8,128)(2,1)} %bitcast.48, bf16[256,256]{1,0:T(8,128)(2,1)S(1)} %copy-done.10), kind=kOutput, calls=%fused_computation.1 | convolution fusion | flops 100859904 | bytes 917504 | tf_op jit(solution)/shard_map/dot_general | solution.py:268
  48.1 0.6 reshape.50
  48.7 2.0 %copy.42 = bf16[3,1,8,4,8,8,32]{6,3,0,5,4,2,1:T(4,128)(2,1)S(1)} copy(bf16[3,1,8,4,8,8,32]{6,5,4,3,2,0,1:T(8,128)(2,1)S(1)} %reshape.50) | data formatting | bytes 786432 | tf_op jit(solution)/shard_map/reshape | solution.py:270
  50.7 0.9 reshape.51
  51.8 1.0 fusion.2
  52.8 2.9 %shard_map.124 = (f32[512,128]{1,0:T(8,128)}, f32[104,128]{1,0:T(8,128)}, f32[104,128]{1,0:T(8,128)}, f32[104,32]{1,0:T(8,128)}, f32[104,32]{1,0:T(8,128)}) custom-call(f32[512,128]{1,0:T(8,128)} %fusion.6.refs_10_.refs_0_, f32[384,128]{1,0:T(8,128)} %bitcast.43, f32[296,128]{1,0:T(8,128)} %copy-done.4, f32[296,128]{1,0:T(8,128)} %copy-done.5, ...), custom_call_target="tpu_custom_call" | custom-call | tf_op jit(solution)/shard_map/pallas_call | solution.py:387
  55.7 2.7 %collective-permute-start.8 = (f32[104,128]{1,0:T(8,128)}, f32[104,128]{1,0:T(8,128)S(1)}, u32[]{:S(2)}, u32[]{:S(2)}) collective-permute-start(f32[104,128]{1,0:T(8,128)} %get-tuple-element.22), channel_id=1, source_target_pairs={{0,4},{4,8},{8,12},{12,16},{16,20},{20,24},{24,28},{28,32},{32,36}... | collective-permute-start | bytes 159752 | tf_op jit(solution)/shard_map/ppermute | solution.py:409
  58.4 3.1 %collective-permute-start.9 = (f32[104,128]{1,0:T(8,128)}, f32[104,128]{1,0:T(8,128)S(1)}, u32[]{:S(2)}, u32[]{:S(2)}) collective-permute-start(f32[104,128]{1,0:T(8,128)} %get-tuple-element.23), channel_id=1, source_target_pairs={{4,0},{8,4},{12,8},{16,12},{20,16},{24,20},{28,24},{32,28},{36,32}... | collective-permute-start | bytes 159752 | tf_op jit(solution)/shard_map/ppermute | solution.py:410
  61.6 0.5 collective-permute-start.10
  62.1 2.4 %collective-permute-start.11 = (f32[104,32]{1,0:T(8,128)}, f32[104,32]{1,0:T(8,128)S(1)}, u32[]{:S(2)}, u32[]{:S(2)}) collective-permute-start(f32[104,32]{1,0:T(8,128)} %get-tuple-element.25), channel_id=1, source_target_pairs={{1,0},{2,1},{3,2},{0,3},{5,4},{6,5},{7,6},{4,7},{9,8},{10,9},{11,1... | collective-permute-start | bytes 39944 | tf_op jit(solution)/shard_map/ppermute | solution.py:412
  64.5 1.7 %collective-permute-done.10.refs_4_ = f32[104,32]{1,0:T(8,128)S(1)} collective-permute-done((f32[104,32]{1,0:T(8,128)}, f32[104,32]{1,0:T(8,128)S(1)}, u32[]{:S(2)}, u32[]{:S(2)}) %collective-permute-start.10) | collective-permute-done | bytes 13344 | tf_op jit(solution)/shard_map/ppermute | solution.py:411
  66.3 0.6 copy-done.14
  66.9 2.7 %shard_map.125 = f32[512,128]{1,0:T(8,128)} custom-call(f32[512,128]{1,0:T(8,128)} %get-tuple-element.21.refs_0_, f32[384,128]{1,0:T(8,128)} %bitcast.44, f32[104,128]{1,0:T(8,128)} %copy-done.12, f32[104,128]{1,0:T(8,128)} %copy-done.13, f32[104,32]{1,0:T(8,128)} %copy-done.14, f32[104,32]{1,0:T(8,128)} %copy-done.15, f32[128,384]{1,0:T(8,128)} %constant.17.clone.refs_6_, ...), custom_call_target="tpu_custom_call" | custom-call | tf_op jit(solution)/shard_map/pallas_call | solution.py:387
  69.6 1.3 %fusion.5 = f32[512,256]{0,1:T(8,128)S(1)} fusion(f32[512,128]{1,0:T(8,128)} %shard_map.125, s32[256]{0:T(256)S(1)} %eq.61), kind=kOutput, calls=%fused_computation.11 | convolution fusion | flops 100696064 | bytes 787456 | tf_op jit(solution)/shard_map/dot_general | solution.py:444
  71.2 24.6 %all_to_all.18 = f32[512,128,2]{0,2,1:T(2,128)S(1)} all-to-all(f32[512,128,2]{0,2,1:T(2,128)S(1)} %all_to_all.14), channel_id=1, replica_groups=mesh['flow'=32,'grp'=4] {'flow','grp'}, dimensions={1} | all-to-all | bytes 1048576 | tf_op jit(solution)/shard_map/all_to_all | solution.py:445
  96.9 0.9 copy.36
  (57 shorter events, 3.4 us)
Async XLA Ops:
  1.6 13.7 %copy-start = (f32[3,8,32,256]{3,2,1,0:T(8,128)S(1)}, f32[3,8,32,256]{3,2,1,0:T(8,128)}, u32[]{:S(2)}) copy-start(f32[3,8,32,256]{3,2,1,0:T(8,128)} %refs_0_.1) | copy-start | bytes 2359300
  1.7 13.7 %copy-start.1 = (f32[8,32,256]{2,1,0:T(8,128)S(1)}, f32[8,32,256]{2,1,0:T(8,128)}, u32[]{:S(2)}) copy-start(f32[8,32,256]{2,1,0:T(8,128)} %refs_1_.3) | copy-start | bytes 786436
  3.8 16.3 %copy-start.17 = (s32[1,128,2]{1,2,0:T(2,128)S(1)}, s32[1,128,2]{1,2,0:T(2,128)}, u32[]{:S(2)}) copy-start(s32[1,128,2]{1,2,0:T(2,128)} %param.15) | copy-start | bytes 3076
  3.8 26.0 %all-to-all-start = ((f32[512,128,2]{0,2,1:T(2,128)}), f32[512,128,2]{0,2,1:T(2,128)S(1)}, u32[]{:S(2)}, u32[]{:S(2)}) async-start(f32[512,128,2]{0,2,1:T(2,128)} %copy.31), calls=%async_computation | async-start | bytes 1048576 | tf_op jit(solution)/shard_map/all_to_all | solution.py:429
  15.4 16.0 %collective-permute-start.3 = (f32[4,8,1,256]{3,2,1,0:T(1,128)S(1)}, f32[4,8,1,256]{3,2,1,0:T(1,128)S(1)}, u32[]{:S(2)}, u32[]{:S(2)}) collective-permute-start(f32[4,8,1,256]{3,2,1,0:T(1,128)S(1)} %get-tuple-element.34), channel_id=1, source_target_pairs={{1,0},{2,1},{3,2},{0,3},{5,4},{6,5},{7,6},{4,7},{9,8},{10,9},{11,1... | collective-permute-start | bytes 98312 | tf_op jit(solution)/shard_map/ppermute | solution.py:256
  18.0 13.3 %collective-permute-start.2 = (f32[4,8,1,256]{3,2,1,0:T(1,128)S(1)}, f32[4,8,1,256]{3,2,1,0:T(1,128)S(1)}, u32[]{:S(2)}, u32[]{:S(2)}) collective-permute-start(f32[4,8,1,256]{3,2,1,0:T(1,128)S(1)} %get-tuple-element.35), channel_id=1, source_target_pairs={{0,1},{1,2},{2,3},{3,0},{4,5},{5,6},{6,7},{7,4},{8,9},{9,10},{10,1... | collective-permute-start | bytes 98312 | tf_op jit(solution)/shard_map/ppermute | solution.py:255
  18.1 13.3 %collective-permute-start.1 = (f32[4,32,256]{2,1,0:T(8,128)S(1)}, f32[4,32,256]{2,1,0:T(8,128)S(1)}, u32[]{:S(2)}, u32[]{:S(2)}) collective-permute-start(f32[4,32,256]{2,1,0:T(8,128)S(1)} %get-tuple-element.36), channel_id=1, source_target_pairs={{4,0},{8,4},{12,8},{16,12},{20,16},{24,20},{28,24},{32,28},{36,32}... | collective-permute-start | bytes 393224 | tf_op jit(solution)/shard_map/ppermute | solution.py:254
  18.8 12.6 %collective-permute-start = (f32[4,32,256]{2,1,0:T(8,128)S(1)}, f32[4,32,256]{2,1,0:T(8,128)S(1)}, u32[]{:S(2)}, u32[]{:S(2)}) collective-permute-start(f32[4,32,256]{2,1,0:T(8,128)S(1)} %get-tuple-element.37), channel_id=1, source_target_pairs={{0,4},{4,8},{8,12},{12,16},{16,20},{20,24},{24,28},{28,32},{32,36}... | collective-permute-start | bytes 393224 | tf_op jit(solution)/shard_map/ppermute | solution.py:253
  31.4 15.4 %copy-start.10 = (bf16[256,256]{1,0:T(8,128)(2,1)S(1)}, bf16[256,256]{1,0:T(8,128)(2,1)}, u32[]{:S(2)}) copy-start(bf16[256,256]{1,0:T(8,128)(2,1)} %constant.21.clone) | copy-start | bytes 393220
  31.4 0.6 copy-start.8
  31.4 0.6 copy-start.9
  31.4 0.7 copy-start.2
  32.1 0.7 copy-start.3
  36.9 5.2 %collective-permute-start.4 = (f32[296,128]{1,0:T(8,128)}, f32[296,128]{1,0:T(8,128)S(1)}, u32[]{:S(2)}, u32[]{:S(2)}) collective-permute-start(f32[296,128]{1,0:T(8,128)} %get-tuple-element.15), channel_id=1, source_target_pairs={{0,4},{4,8},{8,12},{12,16},{16,20},{20,24},{24,28},{28,32},{32,36}... | collective-permute-start | bytes 454664 | tf_op jit(solution)/shard_map/ppermute | solution.py:409
  37.2 4.9 %collective-permute-start.5 = (f32[296,128]{1,0:T(8,128)}, f32[296,128]{1,0:T(8,128)S(1)}, u32[]{:S(2)}, u32[]{:S(2)}) collective-permute-start(f32[296,128]{1,0:T(8,128)} %get-tuple-element.16), channel_id=1, source_target_pairs={{4,0},{8,4},{12,8},{16,12},{20,16},{24,20},{28,24},{32,28},{36,32}... | collective-permute-start | bytes 454664 | tf_op jit(solution)/shard_map/ppermute | solution.py:410
  37.4 4.7 %collective-permute-start.6 = (f32[152,128]{1,0:T(8,128)}, f32[152,128]{1,0:T(8,128)S(1)}, u32[]{:S(2)}, u32[]{:S(2)}) collective-permute-start(f32[152,128]{1,0:T(8,128)} %get-tuple-element.17), channel_id=1, source_target_pairs={{0,1},{1,2},{2,3},{3,0},{4,5},{5,6},{6,7},{7,4},{8,9},{9,10},{10,1... | collective-permute-start | bytes 233480 | tf_op jit(solution)/shard_map/ppermute | solution.py:411
  37.7 4.4 %collective-permute-start.7 = (f32[152,128]{1,0:T(8,128)}, f32[152,128]{1,0:T(8,128)S(1)}, u32[]{:S(2)}, u32[]{:S(2)}) collective-permute-start(f32[152,128]{1,0:T(8,128)} %get-tuple-element.18), channel_id=1, source_target_pairs={{1,0},{2,1},{3,2},{0,3},{5,4},{6,5},{7,6},{4,7},{9,8},{10,9},{11,1... | collective-permute-start | bytes 233480 | tf_op jit(solution)/shard_map/ppermute | solution.py:412
  42.0 0.6 copy-start.6
  42.0 0.7 copy-start.7
  42.1 0.7 copy-start.4
  42.1 0.8 copy-start.5
  50.7 1.1 %copy-start.11 = (bf16[125,512]{1,0:T(8,128)(2,1)S(1)}, bf16[125,512]{1,0:T(8,128)(2,1)}, u32[]{:S(2)}) copy-start(bf16[125,512]{1,0:T(8,128)(2,1)} %param.13) | copy-start | bytes 384004
  55.7 10.5 %collective-permute-start.8 = (f32[104,128]{1,0:T(8,128)}, f32[104,128]{1,0:T(8,128)S(1)}, u32[]{:S(2)}, u32[]{:S(2)}) collective-permute-start(f32[104,128]{1,0:T(8,128)} %get-tuple-element.22), channel_id=1, source_target_pairs={{0,4},{4,8},{8,12},{12,16},{16,20},{20,24},{24,28},{28,32},{32,36}... | collective-permute-start | bytes 159752 | tf_op jit(solution)/shard_map/ppermute | solution.py:409
  58.4 7.8 %collective-permute-start.9 = (f32[104,128]{1,0:T(8,128)}, f32[104,128]{1,0:T(8,128)S(1)}, u32[]{:S(2)}, u32[]{:S(2)}) collective-permute-start(f32[104,128]{1,0:T(8,128)} %get-tuple-element.23), channel_id=1, source_target_pairs={{4,0},{8,4},{12,8},{16,12},{20,16},{24,20},{28,24},{32,28},{36,32}... | collective-permute-start | bytes 159752 | tf_op jit(solution)/shard_map/ppermute | solution.py:410
  61.6 4.7 %collective-permute-start.10 = (f32[104,32]{1,0:T(8,128)}, f32[104,32]{1,0:T(8,128)S(1)}, u32[]{:S(2)}, u32[]{:S(2)}) collective-permute-start(f32[104,32]{1,0:T(8,128)} %get-tuple-element.24), channel_id=1, source_target_pairs={{0,1},{1,2},{2,3},{3,0},{4,5},{5,6},{6,7},{7,4},{8,9},{9,10},{10,1... | collective-permute-start | bytes 39944 | tf_op jit(solution)/shard_map/ppermute | solution.py:411
  62.1 4.1 %collective-permute-start.11 = (f32[104,32]{1,0:T(8,128)}, f32[104,32]{1,0:T(8,128)S(1)}, u32[]{:S(2)}, u32[]{:S(2)}) collective-permute-start(f32[104,32]{1,0:T(8,128)} %get-tuple-element.25), channel_id=1, source_target_pairs={{1,0},{2,1},{3,2},{0,3},{5,4},{6,5},{7,6},{4,7},{9,8},{10,9},{11,1... | collective-permute-start | bytes 39944 | tf_op jit(solution)/shard_map/ppermute | solution.py:412
  66.2 0.6 copy-start.14
  66.2 0.6 copy-start.15
  66.2 0.6 copy-start.12
  66.2 0.6 copy-start.13
  70.9 25.5 %copy-start.16 = (s32[1,128]{1,0:T(1,128)S(1)}, s32[1,128]{1,0:T(1,128)}, u32[]{:S(2)}) copy-start(s32[1,128]{1,0:T(1,128)} %param.16) | copy-start | bytes 1540

commit v20 on v18

--- a/solution.py
+++ b/solution.py
@@ -200,7 +200,7 @@
         return carry
 
     plane_step(0, True, False)
-    lax.fori_loop(1, size_x - 1, step, 0)
+    lax.fori_loop(1, size_x - 1, step, 0, unroll=True)
     plane_step(size_x - 1, False, True)
     if mode == 0:
         for c in range(3):

time: 98.2 us -> 97.8 us (level)
  no operation moved by 1% of the time
where the time goes in v20:
time: 97.8 us; the launch traced here: 97.4 us
  starting transfers between devices  28 us (29%)
  blocking collectives  24.8 us (25%)
  Pallas kernels  13.4 us (14%)
  waiting for transfers between devices  13.2 us (13%)
  local copies, waits for them, and re-layouts  10.7 us (11%)
  matrix products  6.34 us (6%)
    all_to_all x1, blocking collectives, body(): lax.all_to_all(leaving, ('flow', 'grp'), split_axis=1, concat_axis=1, til...  24.8 us
    all_to_all x1, starting transfers between devices, body(): lax.all_to_all(outgoing, ('flow', 'grp'), split_axis=1, concat_axis=1, ti...  11.5 us
    all_to_all x1, waiting for transfers between devices, body(): lax.all_to_all(outgoing, ('flow', 'grp'), split_axis=1, concat_axis=1, ti...  9.44 us
    pallas_call x2, Pallas kernels, dg_step(): pl.pallas_call(lambda *refs: dg_step_kernel(want_faces, xoff, yoff, row_l...  5.67 us
    ppermute x2, starting transfers between devices, exchange_faces(): lax.ppermute(sy0, 'grp', down_g)  4.77 us
    unnamed x39, local copies, waits for them, and re-layouts  4.68 us
    pallas_call x1, Pallas kernels, les_section_first(): pl.pallas_call(lambda *refs: les_kernel(0, lax.axis_size('flow'), lax.axi...  3.94 us
    pallas_call x1, Pallas kernels, les_section_last(): pl.pallas_call(lambda *refs: les_kernel(1, lax.axis_size('flow'), lax.axi...  3.76 us
  transfers between devices with their start and end apart: 13, of which 3 were waited for; matrix products, arithmetic and copies ran while one was open for 2% of the time, Pallas kernels for 0%

profile of v20, /device:TPU:1, one launch (start us, length us, event | category | flops | bytes accessed | tf_op | source)
XLA Modules:
  0.0 97.4 jit_solution(17228834126443872080)
XLA Ops:
  0.6 1.0 copy.37
  1.7 1.1 %fusion.9 = f32[512,128,2]{1,0,2:T(8,128)S(1)} fusion(f32[512,128,1]{1,0,2:T(8,128)S(1)} %bitcast.47, s32[128,2]{0,1:T(2,128)S(1)} %multiply_add_fusion, s32[128]{0:T(128)} %bitcast.49), kind=kOutput, calls=%fused_computation.14 | convolution fusion | flops 100696064 | bytes 787968 | tf_op jit(solution)/shard_map/dot_general | solution.py:429
  2.8 1.0 %copy.31 = f32[512,128,2]{0,2,1:T(2,128)} copy(f32[512,128,2]{1,0,2:T(8,128)S(1)} %fusion.9) | data formatting | bytes 1048576 | tf_op jit(solution)/shard_map/dot_general | solution.py:429
  3.8 11.5 %all-to-all-start = ((f32[512,128,2]{0,2,1:T(2,128)}), f32[512,128,2]{0,2,1:T(2,128)S(1)}, u32[]{:S(2)}, u32[]{:S(2)}) async-start(f32[512,128,2]{0,2,1:T(2,128)} %copy.31), calls=%async_computation | async-start | bytes 1048576 | tf_op jit(solution)/shard_map/all_to_all | solution.py:430
  15.4 2.7 %collective-permute-start.3 = (f32[4,8,1,256]{3,2,1,0:T(1,128)S(1)}, f32[4,8,1,256]{3,2,1,0:T(1,128)S(1)}, u32[]{:S(2)}, u32[]{:S(2)}) collective-permute-start(f32[4,8,1,256]{3,2,1,0:T(1,128)S(1)} %get-tuple-element.34), channel_id=1, source_target_pairs={{1,0},{2,1},{3,2},{0,3},{5,4},{6,5},{7,6},{4,7},{9,8},{10,9},{11,1... | collective-permute-start | bytes 98312 | tf_op jit(solution)/shard_map/ppermute | solution.py:256
  18.1 0.7 collective-permute-start.1
  18.8 1.3 %collective-permute-start = (f32[4,32,256]{2,1,0:T(8,128)S(1)}, f32[4,32,256]{2,1,0:T(8,128)S(1)}, u32[]{:S(2)}, u32[]{:S(2)}) collective-permute-start(f32[4,32,256]{2,1,0:T(8,128)S(1)} %get-tuple-element.37), channel_id=1, source_target_pairs={{0,4},{4,8},{8,12},{12,16},{16,20},{20,24},{24,28},{28,32},{32,36}... | collective-permute-start | bytes 393224 | tf_op jit(solution)/shard_map/ppermute | solution.py:253
  20.4 9.4 %all-to-all-done = f32[512,128,2]{0,2,1:T(2,128)S(1)} async-done(((f32[512,128,2]{0,2,1:T(2,128)}), f32[512,128,2]{0,2,1:T(2,128)S(1)}, u32[]{:S(2)}, u32[]{:S(2)}) %all-to-all-start) | async-done | bytes 524320 | tf_op jit(solution)/shard_map/all_to_all | solution.py:430
  30.2 1.2 %fusion.6.refs_10_.refs_0_ = f32[512,128]{1,0:T(8,128)} fusion(f32[512,256]{0,1:T(8,128)S(1)} %all_to_all.13, s32[256]{0:T(256)S(1)} %eq.61), kind=kOutput, calls=%fused_computation.12 | convolution fusion | flops 100696064 | bytes 787456 | tf_op jit(solution)/shard_map/dot_general | solution.py:431
  31.4 0.6 copy-done.8
  32.1 0.6 copy-done.3
  32.7 3.9 %shard_map.122 = (f32[3,8,32,256]{3,2,1,0:T(8,128)}, f32[296,128]{1,0:T(8,128)}, f32[296,128]{1,0:T(8,128)}, f32[152,128]{1,0:T(8,128)}, f32[152,128]{1,0:T(8,128)}) custom-call(f32[3,8,32,256]{3,2,1,0:T(8,128)} %refs_0_.1, f32[8,32,256]{2,1,0:T(8,128)} %refs_1_.3, f32[4,32,256]{2,1,0:T(8,128)} %copy-done.3, f32[4,32,256]{2,1,0:T(8,128)} %copy-done.2, ...), custom_call_target="tpu_custom_call" | custom-call | tf_op jit(solution)/shard_map/pallas_call | solution.py:231
  37.5 2.4 %collective-permute-start.7 = (f32[152,128]{1,0:T(8,128)}, f32[152,128]{1,0:T(8,128)S(1)}, u32[]{:S(2)}, u32[]{:S(2)}) collective-permute-start(f32[152,128]{1,0:T(8,128)} %get-tuple-element.18), channel_id=1, source_target_pairs={{1,0},{2,1},{3,2},{0,3},{5,4},{6,5},{7,6},{4,7},{9,8},{10,9},{11,1... | collective-permute-start | bytes 233480 | tf_op jit(solution)/shard_map/ppermute | solution.py:413
  39.9 2.0 %collective-permute-done.6.refs_4_ = f32[152,128]{1,0:T(8,128)S(1)} collective-permute-done((f32[152,128]{1,0:T(8,128)}, f32[152,128]{1,0:T(8,128)S(1)}, u32[]{:S(2)}, u32[]{:S(2)}) %collective-permute-start.6) | collective-permute-done | bytes 77856 | tf_op jit(solution)/shard_map/ppermute | solution.py:412
  41.9 0.6 copy-done.6
  42.7 3.8 %shard_map.123 = (f32[3,8,32,256]{3,2,1,0:T(8,128)}, bf16[3,8,32,256]{3,2,1,0:T(8,128)(2,1)}) custom-call(f32[3,8,32,256]{3,2,1,0:T(8,128)} %get-tuple-element.14.refs_0_, f32[8,32,256]{2,1,0:T(8,128)} %refs_1_.3, f32[296,128]{1,0:T(8,128)} %copy-done.4, f32[296,128]{1,0:T(8,128)} %copy-done.5, f32[152,128]{1,0:T(8,128)} %copy-done.6, f32[152,128]{1,0:T(8,128)} %copy-done.7, ...), custom_call_target="tpu_custom_call" | custom-call | tf_op jit(solution)/shard_map/pallas_call | solution.py:239
  46.4 1.3 %convolution_convert_fusion = bf16[768,256]{1,0:T(8,128)(2,1)S(1)} fusion(bf16[768,256]{1,0:T(8,128)(2,1)} %bitcast.48, bf16[256,256]{1,0:T(8,128)(2,1)S(1)} %copy-done.10), kind=kOutput, calls=%fused_computation.1 | convolution fusion | flops 100859904 | bytes 917504 | tf_op jit(solution)/shard_map/dot_general | solution.py:268
  47.7 0.6 reshape.50
  48.3 2.0 %copy.42 = bf16[3,1,8,4,8,8,32]{6,3,0,5,4,2,1:T(4,128)(2,1)S(1)} copy(bf16[3,1,8,4,8,8,32]{6,5,4,3,2,0,1:T(8,128)(2,1)S(1)} %reshape.50) | data formatting | bytes 786432 | tf_op jit(solution)/shard_map/reshape | solution.py:270
  50.4 0.9 reshape.51
  51.4 1.0 %fusion.2 = f32[128,3,128]{2,0,1:T(8,128)} fusion(bf16[3,128,512]{2,1,0:T(8,128)(2,1)S(1)} %bitcast.45, bf16[125,512]{1,0:T(8,128)(2,1)S(1)} %copy-done.11), kind=kOutput, calls=%fused_computation.6 | convolution fusion | flops 50331648 | bytes 717824 | tf_op jit(solution)/shard_map/dot_general | solution.py:272
  52.4 3.0 %shard_map.124 = (f32[512,128]{1,0:T(8,128)}, f32[104,128]{1,0:T(8,128)}, f32[104,128]{1,0:T(8,128)}, f32[104,32]{1,0:T(8,128)}, f32[104,32]{1,0:T(8,128)}) custom-call(f32[512,128]{1,0:T(8,128)} %fusion.6.refs_10_.refs_0_, f32[384,128]{1,0:T(8,128)} %bitcast.43, f32[296,128]{1,0:T(8,128)} %copy-done.4, f32[296,128]{1,0:T(8,128)} %copy-done.5, ...), custom_call_target="tpu_custom_call" | custom-call | tf_op jit(solution)/shard_map/pallas_call | solution.py:388
  55.4 2.7 %collective-permute-start.8 = (f32[104,128]{1,0:T(8,128)}, f32[104,128]{1,0:T(8,128)S(1)}, u32[]{:S(2)}, u32[]{:S(2)}) collective-permute-start(f32[104,128]{1,0:T(8,128)} %get-tuple-element.22), channel_id=1, source_target_pairs={{0,4},{4,8},{8,12},{12,16},{16,20},{20,24},{24,28},{28,32},{32,36}... | collective-permute-start | bytes 159752 | tf_op jit(solution)/shard_map/ppermute | solution.py:410
  58.1 2.9 %collective-permute-start.9 = (f32[104,128]{1,0:T(8,128)}, f32[104,128]{1,0:T(8,128)S(1)}, u32[]{:S(2)}, u32[]{:S(2)}) collective-permute-start(f32[104,128]{1,0:T(8,128)} %get-tuple-element.23), channel_id=1, source_target_pairs={{4,0},{8,4},{12,8},{16,12},{20,16},{24,20},{28,24},{32,28},{36,32}... | collective-permute-start | bytes 159752 | tf_op jit(solution)/shard_map/ppermute | solution.py:411
  61.0 0.6 collective-permute-start.10
  61.6 2.4 %collective-permute-start.11 = (f32[104,32]{1,0:T(8,128)}, f32[104,32]{1,0:T(8,128)S(1)}, u32[]{:S(2)}, u32[]{:S(2)}) collective-permute-start(f32[104,32]{1,0:T(8,128)} %get-tuple-element.25), channel_id=1, source_target_pairs={{1,0},{2,1},{3,2},{0,3},{5,4},{6,5},{7,6},{4,7},{9,8},{10,9},{11,1... | collective-permute-start | bytes 39944 | tf_op jit(solution)/shard_map/ppermute | solution.py:413
  63.9 1.7 %collective-permute-done.10.refs_4_ = f32[104,32]{1,0:T(8,128)S(1)} collective-permute-done((f32[104,32]{1,0:T(8,128)}, f32[104,32]{1,0:T(8,128)S(1)}, u32[]{:S(2)}, u32[]{:S(2)}) %collective-permute-start.10) | collective-permute-done | bytes 13344 | tf_op jit(solution)/shard_map/ppermute | solution.py:412
  65.7 0.6 copy-done.14
  66.3 2.7 %shard_map.125 = f32[512,128]{1,0:T(8,128)} custom-call(f32[512,128]{1,0:T(8,128)} %get-tuple-element.21.refs_0_, f32[384,128]{1,0:T(8,128)} %bitcast.44, f32[104,128]{1,0:T(8,128)} %copy-done.12, f32[104,128]{1,0:T(8,128)} %copy-done.13, f32[104,32]{1,0:T(8,128)} %copy-done.14, f32[104,32]{1,0:T(8,128)} %copy-done.15, f32[128,384]{1,0:T(8,128)} %constant.17.clone.refs_6_, ...), custom_call_target="tpu_custom_call" | custom-call | tf_op jit(solution)/shard_map/pallas_call | solution.py:388
  69.1 1.3 %fusion.5 = f32[512,256]{0,1:T(8,128)S(1)} fusion(f32[512,128]{1,0:T(8,128)} %shard_map.125, s32[256]{0:T(256)S(1)} %eq.61), kind=kOutput, calls=%fused_computation.11 | convolution fusion | flops 100696064 | bytes 787456 | tf_op jit(solution)/shard_map/dot_general | solution.py:445
  70.7 24.8 %all_to_all.18 = f32[512,128,2]{0,2,1:T(2,128)S(1)} all-to-all(f32[512,128,2]{0,2,1:T(2,128)S(1)} %all_to_all.14), channel_id=1, replica_groups=mesh['flow'=32,'grp'=4] {'flow','grp'}, dimensions={1} | all-to-all | bytes 1048576 | tf_op jit(solution)/shard_map/all_to_all | solution.py:446
  96.5 0.9 copy.36
  (57 shorter events, 3.4 us)
Async XLA Ops:
  1.6 13.7 %copy-start = (f32[3,8,32,256]{3,2,1,0:T(8,128)S(1)}, f32[3,8,32,256]{3,2,1,0:T(8,128)}, u32[]{:S(2)}) copy-start(f32[3,8,32,256]{3,2,1,0:T(8,128)} %refs_0_.1) | copy-start | bytes 2359300
  1.7 13.7 %copy-start.1 = (f32[8,32,256]{2,1,0:T(8,128)S(1)}, f32[8,32,256]{2,1,0:T(8,128)}, u32[]{:S(2)}) copy-start(f32[8,32,256]{2,1,0:T(8,128)} %refs_1_.3) | copy-start | bytes 786436
  3.8 16.3 %copy-start.17 = (s32[1,128,2]{1,2,0:T(2,128)S(1)}, s32[1,128,2]{1,2,0:T(2,128)}, u32[]{:S(2)}) copy-start(s32[1,128,2]{1,2,0:T(2,128)} %param.15) | copy-start | bytes 3076
  3.8 26.0 %all-to-all-start = ((f32[512,128,2]{0,2,1:T(2,128)}), f32[512,128,2]{0,2,1:T(2,128)S(1)}, u32[]{:S(2)}, u32[]{:S(2)}) async-start(f32[512,128,2]{0,2,1:T(2,128)} %copy.31), calls=%async_computation | async-start | bytes 1048576 | tf_op jit(solution)/shard_map/all_to_all | solution.py:430
  15.4 16.0 %collective-permute-start.3 = (f32[4,8,1,256]{3,2,1,0:T(1,128)S(1)}, f32[4,8,1,256]{3,2,1,0:T(1,128)S(1)}, u32[]{:S(2)}, u32[]{:S(2)}) collective-permute-start(f32[4,8,1,256]{3,2,1,0:T(1,128)S(1)} %get-tuple-element.34), channel_id=1, source_target_pairs={{1,0},{2,1},{3,2},{0,3},{5,4},{6,5},{7,6},{4,7},{9,8},{10,9},{11,1... | collective-permute-start | bytes 98312 | tf_op jit(solution)/shard_map/ppermute | solution.py:256
  18.0 13.3 %collective-permute-start.2 = (f32[4,8,1,256]{3,2,1,0:T(1,128)S(1)}, f32[4,8,1,256]{3,2,1,0:T(1,128)S(1)}, u32[]{:S(2)}, u32[]{:S(2)}) collective-permute-start(f32[4,8,1,256]{3,2,1,0:T(1,128)S(1)} %get-tuple-element.35), channel_id=1, source_target_pairs={{0,1},{1,2},{2,3},{3,0},{4,5},{5,6},{6,7},{7,4},{8,9},{9,10},{10,1... | collective-permute-start | bytes 98312 | tf_op jit(solution)/shard_map/ppermute | solution.py:255
  18.1 13.3 %collective-permute-start.1 = (f32[4,32,256]{2,1,0:T(8,128)S(1)}, f32[4,32,256]{2,1,0:T(8,128)S(1)}, u32[]{:S(2)}, u32[]{:S(2)}) collective-permute-start(f32[4,32,256]{2,1,0:T(8,128)S(1)} %get-tuple-element.36), channel_id=1, source_target_pairs={{4,0},{8,4},{12,8},{16,12},{20,16},{24,20},{28,24},{32,28},{36,32}... | collective-permute-start | bytes 393224 | tf_op jit(solution)/shard_map/ppermute | solution.py:254
  18.8 12.6 %collective-permute-start = (f32[4,32,256]{2,1,0:T(8,128)S(1)}, f32[4,32,256]{2,1,0:T(8,128)S(1)}, u32[]{:S(2)}, u32[]{:S(2)}) collective-permute-start(f32[4,32,256]{2,1,0:T(8,128)S(1)} %get-tuple-element.37), channel_id=1, source_target_pairs={{0,4},{4,8},{8,12},{12,16},{16,20},{20,24},{24,28},{28,32},{32,36}... | collective-permute-start | bytes 393224 | tf_op jit(solution)/shard_map/ppermute | solution.py:253
  31.4 15.0 %copy-start.10 = (bf16[256,256]{1,0:T(8,128)(2,1)S(1)}, bf16[256,256]{1,0:T(8,128)(2,1)}, u32[]{:S(2)}) copy-start(bf16[256,256]{1,0:T(8,128)(2,1)} %constant.21.clone) | copy-start | bytes 393220
  31.4 0.6 copy-start.8
  31.4 0.6 copy-start.9
  31.4 0.7 copy-start.2
  32.1 0.7 copy-start.3
  36.7 5.2 %collective-permute-start.4 = (f32[296,128]{1,0:T(8,128)}, f32[296,128]{1,0:T(8,128)S(1)}, u32[]{:S(2)}, u32[]{:S(2)}) collective-permute-start(f32[296,128]{1,0:T(8,128)} %get-tuple-element.15), channel_id=1, source_target_pairs={{0,4},{4,8},{8,12},{12,16},{16,20},{20,24},{24,28},{28,32},{32,36}... | collective-permute-start | bytes 454664 | tf_op jit(solution)/shard_map/ppermute | solution.py:410
  37.0 4.9 %collective-permute-start.5 = (f32[296,128]{1,0:T(8,128)}, f32[296,128]{1,0:T(8,128)S(1)}, u32[]{:S(2)}, u32[]{:S(2)}) collective-permute-start(f32[296,128]{1,0:T(8,128)} %get-tuple-element.16), channel_id=1, source_target_pairs={{4,0},{8,4},{12,8},{16,12},{20,16},{24,20},{28,24},{32,28},{36,32}... | collective-permute-start | bytes 454664 | tf_op jit(solution)/shard_map/ppermute | solution.py:411
  37.2 4.7 %collective-permute-start.6 = (f32[152,128]{1,0:T(8,128)}, f32[152,128]{1,0:T(8,128)S(1)}, u32[]{:S(2)}, u32[]{:S(2)}) collective-permute-start(f32[152,128]{1,0:T(8,128)} %get-tuple-element.17), channel_id=1, source_target_pairs={{0,1},{1,2},{2,3},{3,0},{4,5},{5,6},{6,7},{7,4},{8,9},{9,10},{10,1... | collective-permute-start | bytes 233480 | tf_op jit(solution)/shard_map/ppermute | solution.py:412
  37.5 4.4 %collective-permute-start.7 = (f32[152,128]{1,0:T(8,128)}, f32[152,128]{1,0:T(8,128)S(1)}, u32[]{:S(2)}, u32[]{:S(2)}) collective-permute-start(f32[152,128]{1,0:T(8,128)} %get-tuple-element.18), channel_id=1, source_target_pairs={{1,0},{2,1},{3,2},{0,3},{5,4},{6,5},{7,6},{4,7},{9,8},{10,9},{11,1... | collective-permute-start | bytes 233480 | tf_op jit(solution)/shard_map/ppermute | solution.py:413
  41.9 0.6 copy-start.6
  41.9 0.7 copy-start.7
  41.9 0.7 copy-start.4
  41.9 0.8 copy-start.5
  50.3 1.1 %copy-start.11 = (bf16[125,512]{1,0:T(8,128)(2,1)S(1)}, bf16[125,512]{1,0:T(8,128)(2,1)}, u32[]{:S(2)}) copy-start(bf16[125,512]{1,0:T(8,128)(2,1)} %param.13) | copy-start | bytes 384004
  55.4 10.3 %collective-permute-start.8 = (f32[104,128]{1,0:T(8,128)}, f32[104,128]{1,0:T(8,128)S(1)}, u32[]{:S(2)}, u32[]{:S(2)}) collective-permute-start(f32[104,128]{1,0:T(8,128)} %get-tuple-element.22), channel_id=1, source_target_pairs={{0,4},{4,8},{8,12},{12,16},{16,20},{20,24},{24,28},{28,32},{32,36}... | collective-permute-start | bytes 159752 | tf_op jit(solution)/shard_map/ppermute | solution.py:410
  58.1 7.6 %collective-permute-start.9 = (f32[104,128]{1,0:T(8,128)}, f32[104,128]{1,0:T(8,128)S(1)}, u32[]{:S(2)}, u32[]{:S(2)}) collective-permute-start(f32[104,128]{1,0:T(8,128)} %get-tuple-element.23), channel_id=1, source_target_pairs={{4,0},{8,4},{12,8},{16,12},{20,16},{24,20},{28,24},{32,28},{36,32}... | collective-permute-start | bytes 159752 | tf_op jit(solution)/shard_map/ppermute | solution.py:411
  61.0 4.7 %collective-permute-start.10 = (f32[104,32]{1,0:T(8,128)}, f32[104,32]{1,0:T(8,128)S(1)}, u32[]{:S(2)}, u32[]{:S(2)}) collective-permute-start(f32[104,32]{1,0:T(8,128)} %get-tuple-element.24), channel_id=1, source_target_pairs={{0,1},{1,2},{2,3},{3,0},{4,5},{5,6},{6,7},{7,4},{8,9},{9,10},{10,1... | collective-permute-start | bytes 39944 | tf_op jit(solution)/shard_map/ppermute | solution.py:412
  61.6 4.1 %collective-permute-start.11 = (f32[104,32]{1,0:T(8,128)}, f32[104,32]{1,0:T(8,128)S(1)}, u32[]{:S(2)}, u32[]{:S(2)}) collective-permute-start(f32[104,32]{1,0:T(8,128)} %get-tuple-element.25), channel_id=1, source_target_pairs={{1,0},{2,1},{3,2},{0,3},{5,4},{6,5},{7,6},{4,7},{9,8},{10,9},{11,1... | collective-permute-start | bytes 39944 | tf_op jit(solution)/shard_map/ppermute | solution.py:413
  65.7 0.6 copy-start.14
  65.7 0.6 copy-start.15
  65.7 0.6 copy-start.12
  65.7 0.6 copy-start.13
  70.4 25.7 %copy-start.16 = (s32[1,128]{1,0:T(1,128)S(1)}, s32[1,128]{1,0:T(1,128)}, u32[]{:S(2)}) copy-start(s32[1,128]{1,0:T(1,128)} %param.16) | copy-start | bytes 1540

commit v21 on v20

--- a/solution.py
+++ b/solution.py
@@ -228,11 +228,15 @@
     size_x, size_y, size_z = vel.shape[1], vel.shape[2], vel.shape[3]
     xbuf = jax.ShapeDtypeStruct((3 * 2 * size_y + FACE_ROWS, size_z // 2), jnp.float32)
     ybuf = jax.ShapeDtypeStruct((3 * 2 * size_x + FACE_ROWS, size_z // 2), jnp.float32)
+    def kernel(vel_ref, nu_ref, xlo_ref, xhi_ref, ylo_ref, yhi_ref, *rest):
+        halo_refs = (xlo_ref, xhi_ref, ylo_ref, yhi_ref)
+        les_kernel(0, lax.axis_size("flow"), lax.axis_size("grp"), vel_ref, nu_ref, *halo_refs, *halo_refs, *rest)
+
     return pl.pallas_call(
-        lambda *refs: les_kernel(0, lax.axis_size("flow"), lax.axis_size("grp"), *refs),
+        kernel,
         out_shape=(jax.ShapeDtypeStruct(vel.shape, jnp.float32), xbuf, xbuf, ybuf, ybuf),
         scratch_shapes=[pltpu.VMEM((6, FACE_ROWS, state.shape[1]), jnp.float32)],
-    )(vel, nu, *joint, *joint, state)
+    )(vel, nu, *joint, state)
 
 
 def les_section_last(vel, nu, merged, joint):

time: 97.8 us -> 97.7 us (level)
  no operation moved by 1% of the time
where the time goes in v21:
time: 97.7 us; the launch traced here: 97.2 us
  starting transfers between devices  28 us (29%)
  blocking collectives  24.8 us (25%)
  waiting for transfers between devices  13.2 us (14%)
  Pallas kernels  13.2 us (14%)
  local copies, waits for them, and re-layouts  10.7 us (11%)
  matrix products  6.33 us (6%)
    all_to_all x1, blocking collectives, body(): lax.all_to_all(leaving, ('flow', 'grp'), split_axis=1, concat_axis=1, til...  24.8 us
    all_to_all x1, starting transfers between devices, body(): lax.all_to_all(outgoing, ('flow', 'grp'), split_axis=1, concat_axis=1, ti...  11.5 us
    all_to_all x1, waiting for transfers between devices, body(): lax.all_to_all(outgoing, ('flow', 'grp'), split_axis=1, concat_axis=1, ti...  9.44 us
    pallas_call x2, Pallas kernels, dg_step(): pl.pallas_call(lambda *refs: dg_step_kernel(want_faces, xoff, yoff, row_l...  5.67 us
    ppermute x2, starting transfers between devices, exchange_faces(): lax.ppermute(sy0, 'grp', down_g)  4.78 us
    unnamed x39, local copies, waits for them, and re-layouts  4.68 us
    pallas_call x1, Pallas kernels, les_section_first(): pl.pallas_call(kernel, out_shape=(jax.ShapeDtypeStruct(vel.shape, jnp.flo...  3.81 us
    pallas_call x1, Pallas kernels, les_section_last(): pl.pallas_call(lambda *refs: les_kernel(1, lax.axis_size('flow'), lax.axi...  3.76 us
  transfers between devices with their start and end apart: 13, of which 3 were waited for; matrix products, arithmetic and copies ran while one was open for 2% of the time, Pallas kernels for 0%

profile of v21, /device:TPU:1, one launch (start us, length us, event | category | flops | bytes accessed | tf_op | source)
XLA Modules:
  0.0 97.2 jit_solution(5651938972924533493)
XLA Ops:
  0.6 1.0 copy.37
  1.7 1.1 %fusion.9 = f32[512,128,2]{1,0,2:T(8,128)S(1)} fusion(f32[512,128,1]{1,0,2:T(8,128)S(1)} %bitcast.47, s32[128,2]{0,1:T(2,128)S(1)} %multiply_add_fusion, s32[128]{0:T(128)} %bitcast.49), kind=kOutput, calls=%fused_computation.14 | convolution fusion | flops 100696064 | bytes 787968 | tf_op jit(solution)/shard_map/dot_general | solution.py:433
  2.8 1.0 %copy.31 = f32[512,128,2]{0,2,1:T(2,128)} copy(f32[512,128,2]{1,0,2:T(8,128)S(1)} %fusion.9) | data formatting | bytes 1048576 | tf_op jit(solution)/shard_map/dot_general | solution.py:433
  3.8 11.5 %all-to-all-start = ((f32[512,128,2]{0,2,1:T(2,128)}), f32[512,128,2]{0,2,1:T(2,128)S(1)}, u32[]{:S(2)}, u32[]{:S(2)}) async-start(f32[512,128,2]{0,2,1:T(2,128)} %copy.31), calls=%async_computation | async-start | bytes 1048576 | tf_op jit(solution)/shard_map/all_to_all | solution.py:434
  15.4 2.7 %collective-permute-start.3 = (f32[4,8,1,256]{3,2,1,0:T(1,128)S(1)}, f32[4,8,1,256]{3,2,1,0:T(1,128)S(1)}, u32[]{:S(2)}, u32[]{:S(2)}) collective-permute-start(f32[4,8,1,256]{3,2,1,0:T(1,128)S(1)} %get-tuple-element.34), channel_id=1, source_target_pairs={{1,0},{2,1},{3,2},{0,3},{5,4},{6,5},{7,6},{4,7},{9,8},{10,9},{11,1... | collective-permute-start | bytes 98312 | tf_op jit(solution)/shard_map/ppermute | solution.py:260
  18.1 0.7 collective-permute-start.1
  18.8 1.3 %collective-permute-start = (f32[4,32,256]{2,1,0:T(8,128)S(1)}, f32[4,32,256]{2,1,0:T(8,128)S(1)}, u32[]{:S(2)}, u32[]{:S(2)}) collective-permute-start(f32[4,32,256]{2,1,0:T(8,128)S(1)} %get-tuple-element.37), channel_id=1, source_target_pairs={{0,4},{4,8},{8,12},{12,16},{16,20},{20,24},{24,28},{28,32},{32,36}... | collective-permute-start | bytes 393224 | tf_op jit(solution)/shard_map/ppermute | solution.py:257
  20.4 9.4 %all-to-all-done = f32[512,128,2]{0,2,1:T(2,128)S(1)} async-done(((f32[512,128,2]{0,2,1:T(2,128)}), f32[512,128,2]{0,2,1:T(2,128)S(1)}, u32[]{:S(2)}, u32[]{:S(2)}) %all-to-all-start) | async-done | bytes 524320 | tf_op jit(solution)/shard_map/all_to_all | solution.py:434
  30.2 1.2 %fusion.6.rest_0_.refs_0_ = f32[512,128]{1,0:T(8,128)} fusion(f32[512,256]{0,1:T(8,128)S(1)} %all_to_all.13, s32[256]{0:T(256)S(1)} %eq.61), kind=kOutput, calls=%fused_computation.12 | convolution fusion | flops 100696064 | bytes 787456 | tf_op jit(solution)/shard_map/dot_general | solution.py:435
  31.4 0.6 copy-done.8
  32.1 0.6 copy-done.5
  32.7 3.8 %shard_map.122 = (f32[3,8,32,256]{3,2,1,0:T(8,128)}, f32[296,128]{1,0:T(8,128)}, f32[296,128]{1,0:T(8,128)}, f32[152,128]{1,0:T(8,128)}, f32[152,128]{1,0:T(8,128)}) custom-call(f32[3,8,32,256]{3,2,1,0:T(8,128)} %vel_ref.1, f32[8,32,256]{2,1,0:T(8,128)} %refs_1_.1, f32[4,32,256]{2,1,0:T(8,128)} %copy-done.5, f32[4,32,256]{2,1,0:T(8,128)} %copy-done.4, ...), custom_call_target="tpu_custom_call" | custom-call | tf_op jit(solution)/shard_map/pallas_call | solution.py:235
  37.4 2.4 %collective-permute-start.7 = (f32[152,128]{1,0:T(8,128)}, f32[152,128]{1,0:T(8,128)S(1)}, u32[]{:S(2)}, u32[]{:S(2)}) collective-permute-start(f32[152,128]{1,0:T(8,128)} %get-tuple-element.18), channel_id=1, source_target_pairs={{1,0},{2,1},{3,2},{0,3},{5,4},{6,5},{7,6},{4,7},{9,8},{10,9},{11,1... | collective-permute-start | bytes 233480 | tf_op jit(solution)/shard_map/ppermute | solution.py:417
  39.7 2.0 %collective-permute-done.6.refs_4_ = f32[152,128]{1,0:T(8,128)S(1)} collective-permute-done((f32[152,128]{1,0:T(8,128)}, f32[152,128]{1,0:T(8,128)S(1)}, u32[]{:S(2)}, u32[]{:S(2)}) %collective-permute-start.6) | collective-permute-done | bytes 77856 | tf_op jit(solution)/shard_map/ppermute | solution.py:416
  41.8 0.6 copy-done.6
  42.5 3.8 %shard_map.123 = (f32[3,8,32,256]{3,2,1,0:T(8,128)}, bf16[3,8,32,256]{3,2,1,0:T(8,128)(2,1)}) custom-call(f32[3,8,32,256]{3,2,1,0:T(8,128)} %get-tuple-element.14.refs_0_, f32[8,32,256]{2,1,0:T(8,128)} %refs_1_.1, f32[296,128]{1,0:T(8,128)} %copy-done.2, f32[296,128]{1,0:T(8,128)} %copy-done.3, f32[152,128]{1,0:T(8,128)} %copy-done.6, f32[152,128]{1,0:T(8,128)} %copy-done.7, ...), custom_call_target="tpu_custom_call" | custom-call | tf_op jit(solution)/shard_map/pallas_call | solution.py:243
  46.3 1.2 %convolution_convert_fusion = bf16[768,256]{1,0:T(8,128)(2,1)S(1)} fusion(bf16[768,256]{1,0:T(8,128)(2,1)} %bitcast.48, bf16[256,256]{1,0:T(8,128)(2,1)S(1)} %copy-done.10), kind=kOutput, calls=%fused_computation.1 | convolution fusion | flops 100859904 | bytes 917504 | tf_op jit(solution)/shard_map/dot_general | solution.py:272
  47.5 0.6 reshape.50
  48.2 2.0 %copy.42 = bf16[3,1,8,4,8,8,32]{6,3,0,5,4,2,1:T(4,128)(2,1)S(1)} copy(bf16[3,1,8,4,8,8,32]{6,5,4,3,2,0,1:T(8,128)(2,1)S(1)} %reshape.50) | data formatting | bytes 786432 | tf_op jit(solution)/shard_map/reshape | solution.py:274
  50.2 0.9 reshape.51
  51.3 1.0 %fusion.2 = f32[128,3,128]{2,0,1:T(8,128)} fusion(bf16[3,128,512]{2,1,0:T(8,128)(2,1)S(1)} %bitcast.45, bf16[125,512]{1,0:T(8,128)(2,1)S(1)} %copy-done.11), kind=kOutput, calls=%fused_computation.6 | convolution fusion | flops 50331648 | bytes 717824 | tf_op jit(solution)/shard_map/dot_general | solution.py:276
  52.3 3.0 %shard_map.124 = (f32[512,128]{1,0:T(8,128)}, f32[104,128]{1,0:T(8,128)}, f32[104,128]{1,0:T(8,128)}, f32[104,32]{1,0:T(8,128)}, f32[104,32]{1,0:T(8,128)}) custom-call(f32[512,128]{1,0:T(8,128)} %fusion.6.rest_0_.refs_0_, f32[384,128]{1,0:T(8,128)} %bitcast.43, f32[296,128]{1,0:T(8,128)} %copy-done.2, f32[296,128]{1,0:T(8,128)} %copy-done.3, ...), custom_call_target="tpu_custom_call" | custom-call | tf_op jit(solution)/shard_map/pallas_call | solution.py:392
  55.2 2.7 %collective-permute-start.8 = (f32[104,128]{1,0:T(8,128)}, f32[104,128]{1,0:T(8,128)S(1)}, u32[]{:S(2)}, u32[]{:S(2)}) collective-permute-start(f32[104,128]{1,0:T(8,128)} %get-tuple-element.22), channel_id=1, source_target_pairs={{0,4},{4,8},{8,12},{12,16},{16,20},{20,24},{24,28},{28,32},{32,36}... | collective-permute-start | bytes 159752 | tf_op jit(solution)/shard_map/ppermute | solution.py:414
  57.9 2.9 %collective-permute-start.9 = (f32[104,128]{1,0:T(8,128)}, f32[104,128]{1,0:T(8,128)S(1)}, u32[]{:S(2)}, u32[]{:S(2)}) collective-permute-start(f32[104,128]{1,0:T(8,128)} %get-tuple-element.23), channel_id=1, source_target_pairs={{4,0},{8,4},{12,8},{16,12},{20,16},{24,20},{28,24},{32,28},{36,32}... | collective-permute-start | bytes 159752 | tf_op jit(solution)/shard_map/ppermute | solution.py:415
  60.9 0.5 collective-permute-start.10
  61.4 2.4 %collective-permute-start.11 = (f32[104,32]{1,0:T(8,128)}, f32[104,32]{1,0:T(8,128)S(1)}, u32[]{:S(2)}, u32[]{:S(2)}) collective-permute-start(f32[104,32]{1,0:T(8,128)} %get-tuple-element.25), channel_id=1, source_target_pairs={{1,0},{2,1},{3,2},{0,3},{5,4},{6,5},{7,6},{4,7},{9,8},{10,9},{11,1... | collective-permute-start | bytes 39944 | tf_op jit(solution)/shard_map/ppermute | solution.py:417
  63.8 1.7 %collective-permute-done.10.refs_4_ = f32[104,32]{1,0:T(8,128)S(1)} collective-permute-done((f32[104,32]{1,0:T(8,128)}, f32[104,32]{1,0:T(8,128)S(1)}, u32[]{:S(2)}, u32[]{:S(2)}) %collective-permute-start.10) | collective-permute-done | bytes 13344 | tf_op jit(solution)/shard_map/ppermute | solution.py:416
  65.6 0.6 copy-done.14
  66.2 2.7 %shard_map.125 = f32[512,128]{1,0:T(8,128)} custom-call(f32[512,128]{1,0:T(8,128)} %get-tuple-element.21.refs_0_, f32[384,128]{1,0:T(8,128)} %bitcast.44, f32[104,128]{1,0:T(8,128)} %copy-done.12, f32[104,128]{1,0:T(8,128)} %copy-done.13, f32[104,32]{1,0:T(8,128)} %copy-done.14, f32[104,32]{1,0:T(8,128)} %copy-done.15, f32[128,384]{1,0:T(8,128)} %constant.17.clone.refs_6_, ...), custom_call_target="tpu_custom_call" | custom-call | tf_op jit(solution)/shard_map/pallas_call | solution.py:392
  68.9 1.3 %fusion.5 = f32[512,256]{0,1:T(8,128)S(1)} fusion(f32[512,128]{1,0:T(8,128)} %shard_map.125, s32[256]{0:T(256)S(1)} %eq.61), kind=kOutput, calls=%fused_computation.11 | convolution fusion | flops 100696064 | bytes 787456 | tf_op jit(solution)/shard_map/dot_general | solution.py:449
  70.6 24.8 %all_to_all.18 = f32[512,128,2]{0,2,1:T(2,128)S(1)} all-to-all(f32[512,128,2]{0,2,1:T(2,128)S(1)} %all_to_all.14), channel_id=1, replica_groups=mesh['flow'=32,'grp'=4] {'flow','grp'}, dimensions={1} | all-to-all | bytes 1048576 | tf_op jit(solution)/shard_map/all_to_all | solution.py:450
  96.4 0.9 copy.36
  (57 shorter events, 3.4 us)
Async XLA Ops:
  1.6 13.7 %copy-start = (f32[3,8,32,256]{3,2,1,0:T(8,128)S(1)}, f32[3,8,32,256]{3,2,1,0:T(8,128)}, u32[]{:S(2)}) copy-start(f32[3,8,32,256]{3,2,1,0:T(8,128)} %vel_ref.1) | copy-start | bytes 2359300
  1.7 13.7 %copy-start.1 = (f32[8,32,256]{2,1,0:T(8,128)S(1)}, f32[8,32,256]{2,1,0:T(8,128)}, u32[]{:S(2)}) copy-start(f32[8,32,256]{2,1,0:T(8,128)} %refs_1_.1) | copy-start | bytes 786436
  3.8 16.3 %copy-start.17 = (s32[1,128,2]{1,2,0:T(2,128)S(1)}, s32[1,128,2]{1,2,0:T(2,128)}, u32[]{:S(2)}) copy-start(s32[1,128,2]{1,2,0:T(2,128)} %param.15) | copy-start | bytes 3076
  3.8 26.0 %all-to-all-start = ((f32[512,128,2]{0,2,1:T(2,128)}), f32[512,128,2]{0,2,1:T(2,128)S(1)}, u32[]{:S(2)}, u32[]{:S(2)}) async-start(f32[512,128,2]{0,2,1:T(2,128)} %copy.31), calls=%async_computation | async-start | bytes 1048576 | tf_op jit(solution)/shard_map/all_to_all | solution.py:434
  15.4 16.0 %collective-permute-start.3 = (f32[4,8,1,256]{3,2,1,0:T(1,128)S(1)}, f32[4,8,1,256]{3,2,1,0:T(1,128)S(1)}, u32[]{:S(2)}, u32[]{:S(2)}) collective-permute-start(f32[4,8,1,256]{3,2,1,0:T(1,128)S(1)} %get-tuple-element.34), channel_id=1, source_target_pairs={{1,0},{2,1},{3,2},{0,3},{5,4},{6,5},{7,6},{4,7},{9,8},{10,9},{11,1... | collective-permute-start | bytes 98312 | tf_op jit(solution)/shard_map/ppermute | solution.py:260
  18.0 13.3 %collective-permute-start.2 = (f32[4,8,1,256]{3,2,1,0:T(1,128)S(1)}, f32[4,8,1,256]{3,2,1,0:T(1,128)S(1)}, u32[]{:S(2)}, u32[]{:S(2)}) collective-permute-start(f32[4,8,1,256]{3,2,1,0:T(1,128)S(1)} %get-tuple-element.35), channel_id=1, source_target_pairs={{0,1},{1,2},{2,3},{3,0},{4,5},{5,6},{6,7},{7,4},{8,9},{9,10},{10,1... | collective-permute-start | bytes 98312 | tf_op jit(solution)/shard_map/ppermute | solution.py:259
  18.1 13.3 %collective-permute-start.1 = (f32[4,32,256]{2,1,0:T(8,128)S(1)}, f32[4,32,256]{2,1,0:T(8,128)S(1)}, u32[]{:S(2)}, u32[]{:S(2)}) collective-permute-start(f32[4,32,256]{2,1,0:T(8,128)S(1)} %get-tuple-element.36), channel_id=1, source_target_pairs={{4,0},{8,4},{12,8},{16,12},{20,16},{24,20},{28,24},{32,28},{36,32}... | collective-permute-start | bytes 393224 | tf_op jit(solution)/shard_map/ppermute | solution.py:258
  18.8 12.6 %collective-permute-start = (f32[4,32,256]{2,1,0:T(8,128)S(1)}, f32[4,32,256]{2,1,0:T(8,128)S(1)}, u32[]{:S(2)}, u32[]{:S(2)}) collective-permute-start(f32[4,32,256]{2,1,0:T(8,128)S(1)} %get-tuple-element.37), channel_id=1, source_target_pairs={{0,4},{4,8},{8,12},{12,16},{16,20},{20,24},{24,28},{28,32},{32,36}... | collective-permute-start | bytes 393224 | tf_op jit(solution)/shard_map/ppermute | solution.py:257
  31.4 14.9 %copy-start.10 = (bf16[256,256]{1,0:T(8,128)(2,1)S(1)}, bf16[256,256]{1,0:T(8,128)(2,1)}, u32[]{:S(2)}) copy-start(bf16[256,256]{1,0:T(8,128)(2,1)} %constant.21.clone) | copy-start | bytes 393220
  31.4 0.6 copy-start.8
  31.4 0.6 copy-start.9
  31.4 0.7 copy-start.4
  32.1 0.7 copy-start.5
  36.5 5.2 %collective-permute-start.4 = (f32[296,128]{1,0:T(8,128)}, f32[296,128]{1,0:T(8,128)S(1)}, u32[]{:S(2)}, u32[]{:S(2)}) collective-permute-start(f32[296,128]{1,0:T(8,128)} %get-tuple-element.15), channel_id=1, source_target_pairs={{0,4},{4,8},{8,12},{12,16},{16,20},{20,24},{24,28},{28,32},{32,36}... | collective-permute-start | bytes 454664 | tf_op jit(solution)/shard_map/ppermute | solution.py:414
  36.9 4.9 %collective-permute-start.5 = (f32[296,128]{1,0:T(8,128)}, f32[296,128]{1,0:T(8,128)S(1)}, u32[]{:S(2)}, u32[]{:S(2)}) collective-permute-start(f32[296,128]{1,0:T(8,128)} %get-tuple-element.16), channel_id=1, source_target_pairs={{4,0},{8,4},{12,8},{16,12},{20,16},{24,20},{28,24},{32,28},{36,32}... | collective-permute-start | bytes 454664 | tf_op jit(solution)/shard_map/ppermute | solution.py:415
  37.1 4.7 %collective-permute-start.6 = (f32[152,128]{1,0:T(8,128)}, f32[152,128]{1,0:T(8,128)S(1)}, u32[]{:S(2)}, u32[]{:S(2)}) collective-permute-start(f32[152,128]{1,0:T(8,128)} %get-tuple-element.17), channel_id=1, source_target_pairs={{0,1},{1,2},{2,3},{3,0},{4,5},{5,6},{6,7},{7,4},{8,9},{9,10},{10,1... | collective-permute-start | bytes 233480 | tf_op jit(solution)/shard_map/ppermute | solution.py:416
  37.4 4.4 %collective-permute-start.7 = (f32[152,128]{1,0:T(8,128)}, f32[152,128]{1,0:T(8,128)S(1)}, u32[]{:S(2)}, u32[]{:S(2)}) collective-permute-start(f32[152,128]{1,0:T(8,128)} %get-tuple-element.18), channel_id=1, source_target_pairs={{1,0},{2,1},{3,2},{0,3},{5,4},{6,5},{7,6},{4,7},{9,8},{10,9},{11,1... | collective-permute-start | bytes 233480 | tf_op jit(solution)/shard_map/ppermute | solution.py:417
  41.7 0.6 copy-start.6
  41.7 0.7 copy-start.7
  41.7 0.7 copy-start.2
  41.8 0.8 copy-start.3
  50.2 1.1 %copy-start.11 = (bf16[125,512]{1,0:T(8,128)(2,1)S(1)}, bf16[125,512]{1,0:T(8,128)(2,1)}, u32[]{:S(2)}) copy-start(bf16[125,512]{1,0:T(8,128)(2,1)} %param.13) | copy-start | bytes 384004
  55.2 10.3 %collective-permute-start.8 = (f32[104,128]{1,0:T(8,128)}, f32[104,128]{1,0:T(8,128)S(1)}, u32[]{:S(2)}, u32[]{:S(2)}) collective-permute-start(f32[104,128]{1,0:T(8,128)} %get-tuple-element.22), channel_id=1, source_target_pairs={{0,4},{4,8},{8,12},{12,16},{16,20},{20,24},{24,28},{28,32},{32,36}... | collective-permute-start | bytes 159752 | tf_op jit(solution)/shard_map/ppermute | solution.py:414
  57.9 7.6 %collective-permute-start.9 = (f32[104,128]{1,0:T(8,128)}, f32[104,128]{1,0:T(8,128)S(1)}, u32[]{:S(2)}, u32[]{:S(2)}) collective-permute-start(f32[104,128]{1,0:T(8,128)} %get-tuple-element.23), channel_id=1, source_target_pairs={{4,0},{8,4},{12,8},{16,12},{20,16},{24,20},{28,24},{32,28},{36,32}... | collective-permute-start | bytes 159752 | tf_op jit(solution)/shard_map/ppermute | solution.py:415
  60.9 4.7 %collective-permute-start.10 = (f32[104,32]{1,0:T(8,128)}, f32[104,32]{1,0:T(8,128)S(1)}, u32[]{:S(2)}, u32[]{:S(2)}) collective-permute-start(f32[104,32]{1,0:T(8,128)} %get-tuple-element.24), channel_id=1, source_target_pairs={{0,1},{1,2},{2,3},{3,0},{4,5},{5,6},{6,7},{7,4},{8,9},{9,10},{10,1... | collective-permute-start | bytes 39944 | tf_op jit(solution)/shard_map/ppermute | solution.py:416
  61.4 4.1 %collective-permute-start.11 = (f32[104,32]{1,0:T(8,128)}, f32[104,32]{1,0:T(8,128)S(1)}, u32[]{:S(2)}, u32[]{:S(2)}) collective-permute-start(f32[104,32]{1,0:T(8,128)} %get-tuple-element.25), channel_id=1, source_target_pairs={{1,0},{2,1},{3,2},{0,3},{5,4},{6,5},{7,6},{4,7},{9,8},{10,9},{11,1... | collective-permute-start | bytes 39944 | tf_op jit(solution)/shard_map/ppermute | solution.py:417
  65.5 0.6 copy-start.14
  65.5 0.6 copy-start.15
  65.6 0.6 copy-start.12
  65.6 0.6 copy-start.13
  70.2 25.7 %copy-start.16 = (s32[1,128]{1,0:T(1,128)S(1)}, s32[1,128]{1,0:T(1,128)}, u32[]{:S(2)}) copy-start(s32[1,128]{1,0:T(1,128)} %param.16) | copy-start | bytes 1540
